TPU v7x, 32 devices: a whole 2x2x4 slice. The times are simulated.
32 devices in a mesh: groups: 2 (over y), tensor: 4 (over z), store: 4 (over x, core).
Axes of the slice: x: 2, y: 2, z: 4, core: 2. Of those that a mesh axis runs over, the one named last changes fastest.
Arguments:
- x_new: bfloat16 [128, 8192], P('groups', 'store'), parts along dimension 0, may hold values from -6 to 6
- kv_pages: bfloat16 [8, 160, 128, 2048], P(('groups', 'store'), 'tensor'), parts along dimension 0, may hold values from -6 to 6
- w_query: bfloat16 [8192, 8192], P('store', 'tensor'), may hold values from -3 to 3
- w_keyval: bfloat16 [8192, 2048], P('store'), may hold values from -0.0625 to 0.0625
- w_out: bfloat16 [8192, 8192], P('tensor', 'store'), may hold values from -0.0625 to 0.0625
- lengths: int32 [2], P('groups'), parts along dimension 0, may hold values from 4096 to 32768, as said below
- page_store: int32 [512, 1], P('groups'), parts along dimension 0, may hold values from 0 to 3; in each aligned block of 256 rows (0 to 255, 256 to 511, ...) at most 160 rows name the same one
- offsets: int32 [2], P('groups'), parts along dimension 0, may hold values from 0 to 8191
Outputs:
- attn_out: bfloat16 [128, 8192], P(('groups', 'tensor'), 'store'), parts along dimension 0
There are 2 independent parts, one for each index of `groups`. A program takes and returns all parts, laid end to end along the dimension named above; an argument that names none is the same for every part. Nothing has to cross between parts.
Inputs may be any that keep to these rules, and one draw needn't show every extreme that they name: `lengths`: one session in every draw has exactly 32768 tokens. `page_store`: at most 160 pages of a group lie on one store shard, and some shard holds exactly 160.
All inputs are finite; a program needn't handle non-finite values.
Results may differ from a plain program's by a relative error of at most 0.019.
The roundings to bfloat16 on the way count: a program that leaves them out, or rounds other values in their place, can miss the bound.
Values may be sent and summed in bfloat16 or wider, within the bound.
No kernel may reach another device: no remote copies, remote signals or barrier semaphores. Data moves between devices by JAX's collectives and lax.ppermute only.
A program may use at most 192 MiB of HBM per device.

v0:
```python
import math

import jax
import jax.numpy as jnp
import numpy as np
from jax import lax
from jax.sharding import PartitionSpec as P

HQ = 64
KVH = 8
HD = 128
TURN = 64
MAXPAGES = 256


THETA = 500000.0
NEG_FILL = -1e30
ROPE_FACTOR = 8.0
LOW_FACTOR = 1.0
HIGH_FACTOR = 4.0
INITIAL_CONTEXT = 8192.0


def joined(x, axis, combine):
    everything = jax.tree.map(lambda part: lax.all_gather(part, axis), x)
    first = jax.tree.map(lambda part: part[0], everything)

    def step(k, so_far):
        return combine(so_far, jax.tree.map(lambda part: part[k], everything))

    return lax.fori_loop(1, lax.axis_size(axis), step, first)


def inverse_freq(width):
    steps_half = jnp.arange(width // 2, dtype=jnp.float32)
    base_freq = jnp.exp(-(steps_half * (2.0 / width)) * jnp.log(jnp.float32(THETA)))
    wavelength = 2.0 * math.pi / base_freq
    low_wave = INITIAL_CONTEXT / LOW_FACTOR
    high_wave = INITIAL_CONTEXT / HIGH_FACTOR
    smooth = (INITIAL_CONTEXT / wavelength - LOW_FACTOR) / (HIGH_FACTOR - LOW_FACTOR)
    blended = (1.0 - smooth) * base_freq / ROPE_FACTOR + smooth * base_freq
    scaled = jnp.where(wavelength > low_wave, base_freq / ROPE_FACTOR, blended)
    return jnp.where(wavelength < high_wave, base_freq, scaled)


def rotate(values, rot_angle):
    half_width = values.shape[-1] // 2
    first_half = values[..., :half_width]
    second_half = values[..., half_width:]
    cosine = jnp.cos(rot_angle)
    sine_part = jnp.sin(rot_angle)
    return jnp.concatenate(
        [
            first_half * cosine - second_half * sine_part,
            second_half * cosine + first_half * sine_part,
        ],
        axis=-1,
    )


def to_half(values):
    return values.astype(jnp.bfloat16)


def table_lookup(table, index):
    hits = index[..., None] == jnp.arange(table.shape[0], dtype=jnp.int32)
    return jnp.sum(jnp.where(hits, table, 0), axis=-1)


def page_positions(page_store, shards, capacity):
    store_of = page_store[:, 0]
    onehot = (store_of[:, None] == jnp.arange(shards, dtype=jnp.int32)[None, :]).astype(jnp.int32)
    ranks = jnp.sum((jnp.cumsum(onehot, axis=0) - onehot) * onehot, axis=1)
    return store_of * capacity + ranks


def slot_meta(page_store, lengths, offsets, shards, capacity, first_slot, slot_count, page_len):
    positions = page_positions(page_store, shards, capacity)
    wanted = first_slot + jnp.arange(slot_count, dtype=jnp.int32)
    matches = (positions[:, None] == wanted[None, :]).astype(jnp.int32)
    page_ids = jnp.sum(matches * jnp.arange(positions.shape[0], dtype=jnp.int32)[:, None], axis=0)
    filled = jnp.sum(matches, axis=0) > 0
    slot_sess = page_ids // MAXPAGES
    slot_page = page_ids % MAXPAGES
    key_pos = slot_page[:, None] * page_len + jnp.arange(page_len, dtype=jnp.int32)[None, :]
    key_ok = filled[:, None] & (key_pos < table_lookup(lengths, slot_sess)[:, None])
    key_sess = jnp.broadcast_to(slot_sess[:, None], (slot_count, page_len))
    key_off = jnp.broadcast_to(table_lookup(offsets, slot_sess)[:, None], (slot_count, page_len))
    return (key_sess.reshape(-1), key_ok.reshape(-1), key_off.reshape(-1))


def attend(query, key_rows, value_rows, allowed):
    score_scale = 1.0 / query.shape[-1] ** 0.5
    scores = (
        jnp.einsum("tkgd,nkd->tkgn", query, key_rows, preferred_element_type=jnp.float32)
        * score_scale
    )
    wide_mask = allowed[:, None, None, :]
    scores = jnp.where(wide_mask, scores, NEG_FILL)
    row_top = jnp.max(scores, axis=-1)
    weights = jnp.where(wide_mask, jnp.exp(scores - row_top[..., None]), 0.0)
    weight_sum = jnp.sum(weights, axis=-1)
    head_mix = jnp.einsum(
        "tkgn,nkd->tkgd",
        weights.astype(jnp.bfloat16),
        value_rows,
        preferred_element_type=jnp.float32,
    )
    return (row_top, weight_sum, head_mix)


def combine(first_part, second_part):
    new_top = jnp.maximum(first_part[0], second_part[0])
    first_factor = jnp.exp(first_part[0] - new_top)
    second_factor = jnp.exp(second_part[0] - new_top)
    summed = first_part[1] * first_factor + second_part[1] * second_factor
    mixed_sum = first_part[2] * first_factor[..., None] + second_part[2] * second_factor[..., None]
    return (new_top, summed, mixed_sum)


def body(x_new, kv_pages, w_query, w_keyval, w_out, lengths, page_store, offsets):
    tensors = lax.axis_size("tensor")
    shards = lax.axis_size("store")
    tensor_idx = lax.axis_index("tensor")
    store_idx = lax.axis_index("store")
    tok_count = x_new.shape[0]
    local_slots = kv_pages.shape[1]
    capacity = local_slots * tensors
    page_len = kv_pages.shape[2]
    group_size = HQ // KVH
    local_heads = w_query.shape[1] // HD
    local_kv = max(1, local_heads // group_size)
    local_group = local_heads // local_kv
    freq_table = inverse_freq(HD)
    kv_first = tensor_idx * local_heads // group_size
    keyval_cols = lax.dynamic_slice_in_dim(w_keyval, kv_first * (2 * HD), local_kv * 2 * HD, 1)
    query_part = jnp.dot(x_new, w_query, preferred_element_type=jnp.float32)
    keyval_part = jnp.dot(x_new, keyval_cols, preferred_element_type=jnp.float32)
    query_sum, keyval_sum = lax.psum((query_part, keyval_part), "store")
    keyval_local = keyval_sum.reshape(tok_count, local_kv, 2, HD)
    tok_ids = jnp.arange(tok_count, dtype=jnp.int32)
    tok_sess = tok_ids // TURN
    tok_pos = table_lookup(lengths, tok_sess) + tok_ids % TURN
    tok_angle = tok_pos.astype(jnp.float32)[:, None, None] * freq_table
    query_rot = to_half(rotate(query_sum.reshape(tok_count, local_heads, HD), tok_angle))
    key_new = to_half(rotate(keyval_local[:, :, 0], tok_angle))
    value_new = to_half(keyval_local[:, :, 1])
    query_local = query_rot.reshape(tok_count, local_kv, local_group, HD)
    new_allowed = (tok_sess[:, None] == tok_sess[None, :]) & (tok_ids[None, :] <= tok_ids[:, None])
    new_part = attend(query_local, key_new, value_new, new_allowed)
    stored = kv_pages.reshape(local_slots, page_len, KVH, 2 * HD)
    dest_heads = (
        np.arange(tensors)[:, None] * local_heads // group_size + np.arange(local_kv)[None, :]
    )
    outgoing = jnp.take(stored, jnp.asarray(dest_heads.reshape(-1), dtype=jnp.int32), axis=2)
    outgoing = outgoing.reshape(local_slots, page_len, tensors, local_kv * 2 * HD)
    incoming = lax.all_to_all(outgoing, "tensor", split_axis=2, concat_axis=0, tiled=True)
    key_sess, key_ok, key_off = slot_meta(
        page_store, lengths, offsets, shards, capacity, store_idx * capacity, capacity, page_len
    )
    block_slots = math.gcd(capacity, 8)
    block_count = capacity // block_slots
    block_keys = block_slots * page_len
    incoming = incoming.reshape(block_count, block_keys, local_kv, 2, HD)

    def visit(running, key_block):
        rows_kv, rows_sess, rows_ok, rows_off = key_block
        rot_angle = rows_off.astype(jnp.float32)[:, None, None] * freq_table
        key_rows = to_half(rotate(rows_kv[:, :, 0].astype(jnp.float32), rot_angle))
        allowed = (tok_sess[:, None] == rows_sess[None, :]) & rows_ok[None, :]
        return (combine(running, attend(query_local, key_rows, rows_kv[:, :, 1], allowed)), None)

    start_state = (
        jnp.full((tok_count, local_kv, local_group), NEG_FILL, jnp.float32),
        jnp.zeros((tok_count, local_kv, local_group), jnp.float32),
        jnp.zeros((tok_count, local_kv, local_group, HD), jnp.float32),
    )
    hist_state, unused = lax.scan(
        visit,
        start_state,
        (
            incoming,
            key_sess.reshape(block_count, block_keys),
            key_ok.reshape(block_count, block_keys),
            key_off.reshape(block_count, block_keys),
        ),
    )
    hist_top = hist_state[0].reshape(tok_count, local_heads)
    hist_sum = hist_state[1].reshape(tok_count, local_heads)
    hist_mix = hist_state[2].reshape(tok_count, local_heads, HD)
    merged = joined((hist_top, hist_sum, hist_mix), "store", combine)
    new_flat = (
        new_part[0].reshape(tok_count, local_heads),
        new_part[1].reshape(tok_count, local_heads),
        new_part[2].reshape(tok_count, local_heads, HD),
    )
    combined = combine(merged, new_flat)
    attended = (
        (combined[2] / combined[1][..., None])
        .reshape(tok_count, local_heads * HD)
        .astype(jnp.bfloat16)
    )
    result = lax.psum_scatter(
        jnp.dot(attended, w_out, preferred_element_type=jnp.float32),
        "tensor",
        scatter_dimension=0,
        tiled=True,
    )
    return result.astype(jnp.bfloat16)


def solution(mesh):
    in_specs = (
        P("groups", "store"),
        P(("groups", "store"), "tensor", None, None),
        P("store", "tensor"),
        P("store", None),
        P("tensor", "store"),
        P("groups"),
        P("groups", None),
        P("groups"),
    )
    out_specs = P(("groups", "tensor"), "store")
    return jax.shard_map(body, mesh=mesh, in_specs=in_specs, out_specs=out_specs, check_vma=False)
```

profile of v0, /device:TPU:0, one launch (start us, length us, event | category | flops | bytes accessed | tf_op | source)
XLA Modules:
  0.0 989.0 jit_solution(16655686878267934921)
XLA Ops:
  6.5 28.3 %copy.84 = bf16[1,40,128,2048]{2,3,1,0:T(8,128)(2,1)} copy(bf16[1,40,128,2048]{3,2,1,0:T(8,128)(2,1)} %param.14) | data formatting | bytes 41943040 | tf_op args[1]
  34.9 16.6 %fusion.76 = (bf16[40,128,8,128]{1,3,2,0:T(8,128)(2,1)}, bf16[40,128,8,128]{1,3,2,0:T(8,128)(2,1)}) fusion(bf16[40,128,8,256]{1,3,2,0:T(8,128)(2,1)} %bitcast.206), kind=kLoop, calls=%fused_computation.147 | loop fusion | bytes 41943040 | tf_op jit(solution)/shard_map/jit(_take)/gather | solution.py:155
  51.5 13.7 %copy.106 = bf16[40,128,8,128]{3,1,0,2:T(8,128)(2,1)} copy(bf16[40,128,8,128]{1,3,2,0:T(8,128)(2,1)} %get-tuple-element.376) | data formatting | bytes 20971520
  65.3 13.7 %copy.107 = bf16[40,128,8,128]{3,1,0,2:T(8,128)(2,1)} copy(bf16[40,128,8,128]{1,3,2,0:T(8,128)(2,1)} %get-tuple-element.377) | data formatting | bytes 20971520
  79.0 9.6 gather_fusion
  88.6 9.5 gather_fusion.1
  98.1 17.5 %pad_maximum_fusion = bf16[40,128,8,256]{3,1,0,2:T(8,128)(2,1)} fusion(bf16[40,128,8,128]{3,1,0,2:T(8,128)(2,1)} %bitcast.210, bf16[40,128,8,128]{3,1,0,2:T(8,128)(2,1)} %bitcast.209), kind=kLoop, calls=%fused_computation.55 | loop fusion | flops 41943040 | bytes 41943040
  115.6 28.3 %copy.87 = bf16[40,128,8,256]{1,3,2,0:T(8,128)(2,1)} copy(bf16[40,128,8,256]{3,1,0,2:T(8,128)(2,1)} %pad_maximum_fusion) | data formatting | bytes 41943040
  144.2 11.1 %bitcast_select_fusion.1 = bf16[40,128,4,512]{1,3,2,0:T(8,128)(2,1)S(1)} fusion(pred[4,512]{1,0:T(4,128)(4,1)S(1)} %bitcast.233, bf16[40,128,4,512]{1,3,2,0:T(8,128)(2,1)} %bitcast.205), kind=kLoop, calls=%fused_computation.56 | loop fusion | flops 10485760 | bytes 41945088 | tf_op jit(solution)/shard_map/jit(_take)/select_n | solution.py:155
  155.3 7.4 copy.88
  162.6 7.7 all-to-all-start
  170.4 2.1 fusion.35
  173.3 5.0 convolution_bitcast_fusion
  183.8 32.3 %all-reduce.3.cloned.1.call-done = (f32[64,16,128]{2,1,0:T(8,128)}, f32[64,2,2,128]{3,0,1,2:T(8,128)}) async-done(((f32[64,16,128]{2,1,0:T(8,128)}, f32[64,2,2,128]{3,0,1,2:T(8,128)}), (f32[64,16,128]{2,1,0:T(8,128)}, f32[64,2,2,128]{3,0,1,2:T(8,128)})) %all-reduce.3.cloned.1.call-update) | async-done | bytes 655376 | tf_op jit(solution)/shard_map/psum | solution.py:139
  217.8 407.0 %all-to-all-done = bf16[40,128,4,512]{1,3,0,2:T(8,128)(2,1)} async-done(((bf16[40,128,4,512]{1,3,0,2:T(8,128)(2,1)}), bf16[40,128,4,512]{1,3,0,2:T(8,128)(2,1)}, u32[]{:S(2)}, u32[]{:S(2)}) %all-to-all-start) | async-done | bytes 20971552 | tf_op jit(solution)/shard_map/all_to_all | solution.py:157
  624.8 25.9 %copy.89 = bf16[4,40,128,1,512]{4,2,1,0,3:T(8,128)(2,1)} copy(bf16[4,40,128,1,512]{2,4,1,0,3:T(8,128)(2,1)} %bitcast.17) | data formatting | bytes 41943040 | tf_op jit(solution)/shard_map/all_to_all | solution.py:157
  650.8 29.3 %reshape.418 = bf16[20,1024,2,2,128]{4,3,2,1,0:T(2,128)(2,1)} reshape(bf16[4,40,128,1,512]{4,2,1,0,3:T(8,128)(2,1)} %copy.89) | data formatting | bytes 41943040 | tf_op jit(solution)/shard_map/reshape | solution.py:164
  680.1 243.3 %while.35 = (s32[]{:T(128)}, f32[64,2,8]{0,2,1:T(8,128)S(1)}, f32[64,2,8]{0,2,1:T(8,128)S(1)}, f32[64,2,8,128]{3,0,2,1:T(8,128)S(1)}, s32[20,1024]{1,0:T(8,128)S...) while((s32[]{:T(128)}, f32[64,2,8]{0,2,1:T(8,128)S(1)}, ...), condition=%wide.region_9.10_spmd.clone, body=%wide.region_6.9_spmd.clone.sunk | while | flops 553591424 | bytes 40468636 | solution.py:178
  685.9 2.0 copy-done.2
  689.2 3.0 fusion.101
  698.1 2.0 copy-done.2
  701.4 3.0 fusion.101
  710.2 2.0 copy-done.2
  713.6 3.0 fusion.101
  722.4 2.0 copy-done.2
  725.7 3.0 fusion.101
  734.6 2.0 copy-done.2
  737.9 3.0 fusion.101
  746.7 2.0 copy-done.2
  750.1 3.0 fusion.101
  758.9 2.0 copy-done.2
  762.2 3.0 fusion.101
  771.1 2.0 copy-done.2
  774.4 3.0 fusion.101
  783.2 2.0 copy-done.2
  786.6 3.0 fusion.101
  795.4 2.0 copy-done.2
  798.7 3.0 fusion.101
  807.6 2.0 copy-done.2
  810.9 3.0 fusion.101
  819.7 2.0 copy-done.2
  823.1 3.0 fusion.101
  831.9 2.0 copy-done.2
  835.2 3.0 fusion.101
  844.1 2.0 copy-done.2
  847.4 3.0 fusion.101
  856.2 2.0 copy-done.2
  859.5 3.0 fusion.101
  868.4 2.0 copy-done.2
  871.7 3.0 fusion.101
  880.5 2.0 copy-done.2
  883.9 3.0 fusion.101
  892.7 2.0 copy-done.2
  896.0 3.0 fusion.101
  904.9 2.0 copy-done.2
  908.2 3.0 fusion.101
  917.0 2.0 copy-done.2
  920.4 3.0 fusion.101
  925.6 5.2 all_gather.10
  930.8 5.4 all_gather.9
  936.2 10.3 %all-gather.2.cloned.1.call-done = f32[4,64,16,128]{3,2,1,0:T(8,128)} async-done(((f32[1,64,16,128]{3,2,1,0:T(8,128)}), f32[4,64,16,128]{3,2,1,0:T(8,128)}) %all-gather.2.cloned.1.call-update) | async-done | bytes 2097168 | tf_op jit(solution)/shard_map/all_gather | solution.py:25
  947.6 5.0 while.34
  953.3 5.8 fusion.45
  959.1 21.8 %reduce-scatter.2.cloned.1.call-done = f32[16,2048]{1,0:T(8,128)} async-done(((f32[64,2048]{1,0:T(8,128)}), f32[16,2048]{1,0:T(8,128)}) %reduce-scatter.2.cloned.1.call-update) | async-done | bytes 131088 | tf_op jit(solution)/shard_map/reduce_scatter | solution.py:203
  (376 shorter events, 160.0 us)
Async XLA Ops:
  6.5 163.9 %copy-start = (bf16[64,2048]{1,0:T(8,128)(2,1)S(1)}, bf16[64,2048]{1,0:T(8,128)(2,1)}, u32[]{:S(2)}) copy-start(bf16[64,2048]{1,0:T(8,128)(2,1)} %param.13) | copy-start | bytes 786436
  162.6 462.2 %all-to-all-start = ((bf16[40,128,4,512]{1,3,0,2:T(8,128)(2,1)}), bf16[40,128,4,512]{1,3,0,2:T(8,128)(2,1)}, u32[]{:S(2)}, u32[]{:S(2)}) async-start(bf16[40,128,4,512]{1,3,0,2:T(8,128)(2,1)} %copy.88), calls=%async_computation | async-start | bytes 41943040 | tf_op jit(solution)/shard_map/all_to_all | solution.py:157
  170.4 45.7 %all-reduce.3.cloned.1.call-start = ((), (), s32[]{:S(2)}) async-start(), calls=%async_computation.4 | async-start | bytes 1310720 | tf_op jit(solution)/shard_map/psum | solution.py:139
  173.3 6.8 copy-start.4
  179.1 767.3 %all-gather.2.cloned.1.call-start = ((), (), s32[]{:S(2)}) async-start(), calls=%async_computation.2 | async-start | bytes 2621440 | tf_op jit(solution)/shard_map/all_gather | solution.py:25
  680.1 244.5 %copy-start.3 = (f32[64,2,2,128]{3,0,1,2:T(8,128)S(1)}, f32[64,2,2,128]{3,0,1,2:T(8,128)}, u32[]{:S(2)}) copy-start(f32[64,2,2,128]{3,0,1,2:T(8,128)} %get-tuple-element.353) | copy-start | bytes 393220
  685.9 2.0 copy-start.2
  698.1 2.0 copy-start.2
  710.2 2.0 copy-start.2
  722.4 2.0 copy-start.2
  734.6 2.0 copy-start.2
  746.7 2.0 copy-start.2
  758.9 2.0 copy-start.2
  771.1 2.0 copy-start.2
  783.2 2.0 copy-start.2
  795.4 2.0 copy-start.2
  807.6 2.0 copy-start.2
  819.7 2.0 copy-start.2
  831.9 2.0 copy-start.2
  844.0 2.0 copy-start.2
  856.2 2.0 copy-start.2
  868.4 2.0 copy-start.2
  880.5 2.0 copy-start.2
  892.7 2.0 copy-start.2
  904.9 2.0 copy-start.2
  917.0 2.0 copy-start.2
  924.5 56.4 %reduce-scatter.2.cloned.1.call-start = ((), (), s32[]{:S(2)}) async-start(), calls=%async_computation.3 | async-start | bytes 655360 | tf_op jit(solution)/shard_map/reduce_scatter | solution.py:203
  953.3 29.1 %copy-start.1 = (bf16[64,2048]{1,0:T(8,128)(2,1)S(1)}, bf16[64,2048]{1,0:T(8,128)(2,1)}, u32[]{:S(2)}) copy-start(bf16[64,2048]{1,0:T(8,128)(2,1)} %param.13) | copy-start | bytes 786436
Sparse Core Ops, SparseCore 0:
  179.3 36.7 all-reduce.2
  924.6 21.8 all-gather.1
  959.2 21.6 reduce-scatter.1
where the time goes:
time: 994 us; the launch traced here: 989 us
  waiting for transfers between devices  471 us (47%)
  local copies, waits for them, and re-layouts  270 us (27%)
  other arithmetic  117 us (12%)
  matrix products  94.7 us (10%)
  between operations  14.8 us (1%)
  blocking collectives  10.6 us (1%)
    all_to_all x1, waiting for transfers between devices, body(): lax.all_to_all(outgoing, 'tensor', split_axis=2, concat_axis=0, tiled=True)  407 us
    unnamed x23, local copies, waits for them, and re-layouts  85.2 us
    dot_general x21, matrix products, attend(): jnp.einsum('tkgn,nkd->tkgd', weights.astype(jnp.bfloat16), value_rows, pr...  59.7 us
    dynamic_slice x60, local copies, waits for them, and re-layouts, body(): lax.scan(visit, start_state, (incoming, key_sess.reshape(block_count, blo...  42.4 us
    while x40, local copies, waits for them, and re-layouts  39.4 us
    cos x21, other arithmetic, rotate(): cosine = jnp.cos(rot_angle)  38 us
    gather x3, local copies, waits for them, and re-layouts, body(): jnp.take(stored, jnp.asarray(dest_heads.reshape(-1), dtype=jnp.int32), ax...  35.7 us
    psum x1, waiting for transfers between devices, body(): query_sum, keyval_sum = lax.psum((query_part, keyval_part), 'store')  32.3 us
  transfers between devices with their start and end apart: 4, of which 4 were waited for; matrix products, arithmetic and copies ran while one was open for 1% of the time, Pallas kernels for 0%

commit v1 on v0

--- a/solution.py
+++ b/solution.py
@@ -5,6 +5,9 @@
 import numpy as np
 from jax import lax
 from jax.sharding import PartitionSpec as P
+from jax.experimental import pallas as pl
+from jax.experimental.pallas import tpu as pltpu
+import functools
 
 HQ = 64
 KVH = 8
@@ -118,15 +121,90 @@
     return (new_top, summed, mixed_sum)
 
 
+MASK_FILL = -3e30
+
+
+def hist_kernel(q_ref, kv_ref, bias_ref, cos_ref, sin_ref, acc_out, m_out, l_out, m_sc, l_sc, acc_sc, *, scale, blocks):
+    j = pl.program_id(1)
+
+    @pl.when(j == 0)
+    def _():
+        m_sc[...] = jnp.full(m_sc.shape, NEG_FILL, jnp.float32)
+        l_sc[...] = jnp.zeros(l_sc.shape, jnp.float32)
+        acc_sc[...] = jnp.zeros(acc_sc.shape, jnp.float32)
+
+    pages, page_len, width = kv_ref.shape
+    hd = width // 2
+    n = pages * page_len
+    keys = kv_ref[:, :, :hd].reshape(n, hd).astype(jnp.float32)
+    vals = kv_ref[:, :, hd:].reshape(n, hd)
+    keys = (keys * cos_ref[...] + pltpu.roll(keys, hd // 2, 1) * sin_ref[...]).astype(jnp.bfloat16)
+    scores = lax.dot_general(
+        q_ref[0], keys, (((1,), (1,)), ((), ())), preferred_element_type=jnp.float32
+    )
+    scores = scores * scale + bias_ref[0]
+    m_old = m_sc[...]
+    m_new = jnp.maximum(m_old, jnp.max(scores, axis=1, keepdims=True))
+    alpha = jnp.exp(m_old - m_new)
+    weights = jnp.exp(scores - m_new)
+    l_sc[...] = alpha * l_sc[...] + jnp.sum(weights, axis=1, keepdims=True)
+    acc_sc[...] = alpha * acc_sc[...] + jnp.dot(
+        weights.astype(jnp.bfloat16), vals, preferred_element_type=jnp.float32
+    )
+    m_sc[...] = m_new
+
+    @pl.when(j == blocks - 1)
+    def _():
+        acc_out[0] = acc_sc[...]
+        m_out[0] = m_sc[...]
+        l_out[0] = l_sc[...]
+
+
+def hist_attend(q_k, kv_local, bias, cos2, sin2, pb):
+    kv_heads, rows, hd = q_k.shape
+    slots, page_len, width = kv_local.shape
+    blocks = slots // pb
+    kernel = functools.partial(hist_kernel, scale=1.0 / hd ** 0.5, blocks=blocks)
+    return pl.pallas_call(
+        kernel,
+        grid=(kv_heads, blocks),
+        in_specs=[
+            pl.BlockSpec((1, rows, hd), lambda h, j: (h, 0, 0)),
+            pl.BlockSpec((pb, page_len, 2 * hd), lambda h, j: (j, 0, h)),
+            pl.BlockSpec((1, 1, pb * page_len), lambda h, j: (j, 0, 0)),
+            pl.BlockSpec((1, hd), lambda h, j: (0, 0)),
+            pl.BlockSpec((1, hd), lambda h, j: (0, 0)),
+        ],
+        out_specs=[
+            pl.BlockSpec((1, rows, hd), lambda h, j: (h, 0, 0)),
+            pl.BlockSpec((1, rows, 1), lambda h, j: (h, 0, 0)),
+            pl.BlockSpec((1, rows, 1), lambda h, j: (h, 0, 0)),
+        ],
+        out_shape=[
+            jax.ShapeDtypeStruct((kv_heads, rows, hd), jnp.float32),
+            jax.ShapeDtypeStruct((kv_heads, rows, 1), jnp.float32),
+            jax.ShapeDtypeStruct((kv_heads, rows, 1), jnp.float32),
+        ],
+        scratch_shapes=[
+            pltpu.VMEM((rows, 1), jnp.float32),
+            pltpu.VMEM((rows, 1), jnp.float32),
+            pltpu.VMEM((rows, hd), jnp.float32),
+        ],
+        compiler_params=pltpu.CompilerParams(dimension_semantics=("parallel", "arbitrary")),
+    )(q_k, kv_local, bias, cos2, sin2)
+
+
 def body(x_new, kv_pages, w_query, w_keyval, w_out, lengths, page_store, offsets):
     tensors = lax.axis_size("tensor")
     shards = lax.axis_size("store")
     tensor_idx = lax.axis_index("tensor")
     store_idx = lax.axis_index("store")
     tok_count = x_new.shape[0]
+    assert tok_count == TURN and lengths.shape[0] == 1
     local_slots = kv_pages.shape[1]
     capacity = local_slots * tensors
     page_len = kv_pages.shape[2]
+    kv_heads = kv_pages.shape[3] // (2 * HD)
     group_size = HQ // KVH
     local_heads = w_query.shape[1] // HD
     local_kv = max(1, local_heads // group_size)
@@ -145,56 +223,50 @@
     query_rot = to_half(rotate(query_sum.reshape(tok_count, local_heads, HD), tok_angle))
     key_new = to_half(rotate(keyval_local[:, :, 0], tok_angle))
     value_new = to_half(keyval_local[:, :, 1])
+
+    q_all = lax.all_gather(jnp.transpose(query_rot, (1, 0, 2)), "tensor", axis=0, tiled=True)
+    q_k = q_all.reshape(kv_heads, group_size * tok_count, HD)
+
+    first_slot = store_idx * capacity + tensor_idx * local_slots
+    key_sess, key_ok, key_off = slot_meta(
+        page_store, lengths, offsets, shards, capacity, first_slot, local_slots, page_len
+    )
+    pb = 8 if local_slots % 8 == 0 else local_slots
+    bias = jnp.where(key_ok, 0.0, MASK_FILL).astype(jnp.float32)
+    bias = bias.reshape(local_slots // pb, 1, pb * page_len)
+    hist_angle = offsets[0].astype(jnp.float32) * freq_table
+    cosine = jnp.cos(hist_angle)
+    sine = jnp.sin(hist_angle)
+    cos2 = jnp.concatenate([cosine, cosine])[None, :]
+    sin2 = jnp.concatenate([-sine, sine])[None, :]
+    kv_local = kv_pages.reshape(local_slots, page_len, kv_pages.shape[3])
+    acc, top, total = hist_attend(q_k, kv_local, bias, cos2, sin2, pb)
+    acc = acc.reshape(HQ, tok_count, HD)
+    top = top.reshape(HQ, tok_count)
+    total = total.reshape(HQ, tok_count)
+
+    glob_top = lax.pmax(top, ("tensor", "store"))
+    factor = jnp.exp(top - glob_top)
+    acc = acc * factor[..., None]
+    total = total * factor
+    acc, total = lax.psum_scatter((acc, total), "tensor", scatter_dimension=0, tiled=True)
+    acc, total = lax.psum((acc, total), "store")
+    loc_top = lax.dynamic_slice_in_dim(glob_top, tensor_idx * local_heads, local_heads, 0)
+    hist_part = (
+        jnp.transpose(loc_top),
+        jnp.transpose(total),
+        jnp.transpose(acc, (1, 0, 2)),
+    )
+
     query_local = query_rot.reshape(tok_count, local_kv, local_group, HD)
     new_allowed = (tok_sess[:, None] == tok_sess[None, :]) & (tok_ids[None, :] <= tok_ids[:, None])
     new_part = attend(query_local, key_new, value_new, new_allowed)
-    stored = kv_pages.reshape(local_slots, page_len, KVH, 2 * HD)
-    dest_heads = (
-        np.arange(tensors)[:, None] * local_heads // group_size + np.arange(local_kv)[None, :]
-    )
-    outgoing = jnp.take(stored, jnp.asarray(dest_heads.reshape(-1), dtype=jnp.int32), axis=2)
-    outgoing = outgoing.reshape(local_slots, page_len, tensors, local_kv * 2 * HD)
-    incoming = lax.all_to_all(outgoing, "tensor", split_axis=2, concat_axis=0, tiled=True)
-    key_sess, key_ok, key_off = slot_meta(
-        page_store, lengths, offsets, shards, capacity, store_idx * capacity, capacity, page_len
-    )
-    block_slots = math.gcd(capacity, 8)
-    block_count = capacity // block_slots
-    block_keys = block_slots * page_len
-    incoming = incoming.reshape(block_count, block_keys, local_kv, 2, HD)
-
-    def visit(running, key_block):
-        rows_kv, rows_sess, rows_ok, rows_off = key_block
-        rot_angle = rows_off.astype(jnp.float32)[:, None, None] * freq_table
-        key_rows = to_half(rotate(rows_kv[:, :, 0].astype(jnp.float32), rot_angle))
-        allowed = (tok_sess[:, None] == rows_sess[None, :]) & rows_ok[None, :]
-        return (combine(running, attend(query_local, key_rows, rows_kv[:, :, 1], allowed)), None)
-
-    start_state = (
-        jnp.full((tok_count, local_kv, local_group), NEG_FILL, jnp.float32),
-        jnp.zeros((tok_count, local_kv, local_group), jnp.float32),
-        jnp.zeros((tok_count, local_kv, local_group, HD), jnp.float32),
-    )
-    hist_state, unused = lax.scan(
-        visit,
-        start_state,
-        (
-            incoming,
-            key_sess.reshape(block_count, block_keys),
-            key_ok.reshape(block_count, block_keys),
-            key_off.reshape(block_count, block_keys),
-        ),
-    )
-    hist_top = hist_state[0].reshape(tok_count, local_heads)
-    hist_sum = hist_state[1].reshape(tok_count, local_heads)
-    hist_mix = hist_state[2].reshape(tok_count, local_heads, HD)
-    merged = joined((hist_top, hist_sum, hist_mix), "store", combine)
     new_flat = (
         new_part[0].reshape(tok_count, local_heads),
         new_part[1].reshape(tok_count, local_heads),
         new_part[2].reshape(tok_count, local_heads, HD),
     )
-    combined = combine(merged, new_flat)
+    combined = combine(hist_part, new_flat)
     attended = (
         (combined[2] / combined[1][..., None])
         .reshape(tok_count, local_heads * HD)

time: 994 us -> 371 us (0.37)
  waiting for transfers between devices: 471 us -> 167 us
  local copies, waits for them, and re-layouts: 270 us -> 4.56 us
  other arithmetic: 117 us -> 18.5 us
  Pallas kernels: 0 us -> 85.1 us
  matrix products: 94.7 us -> 14.3 us
  blocking collectives: 10.6 us -> 65.8 us
    all_to_all x1 -> x0, waiting for transfers between devices: 407 us -> none  [body(): lax.all_to_all(outgoing, 'tensor', split_axis=2, concat_axis=0, tiled=True)]
    pallas_call x0 -> x1, Pallas kernels: none -> 85.1 us  [hist_attend(): pl.pallas_call(kernel, grid=(kv_heads, blocks), in_specs=[pl.BlockSpec((1...]
    unnamed x23 -> x4, local copies, waits for them, and re-layouts: 85.2 us -> 0.95 us
    pmax x0 -> x1, blocking collectives: none -> 59.9 us  [body(): glob_top = lax.pmax(top, ('tensor', 'store'))]
    dot_general x21 -> x1, matrix products: 59.7 us -> 1.13 us  [attend(): jnp.einsum('tkgn,nkd->tkgd', weights.astype(jnp.bfloat16), value_rows, pr...]
    reduce_scatter x0 -> x2, waiting for transfers between devices: none -> 58.1 us  [body(): lax.psum_scatter((acc, total), 'tensor', scatter_dimension=0, tiled=True)]
    dynamic_slice x60 -> x0, local copies, waits for them, and re-layouts: 42.4 us -> none  [body(): lax.scan(visit, start_state, (incoming, key_sess.reshape(block_count, blo...]
    while x41 -> x0, local copies, waits for them, and re-layouts: 40.5 us -> none
  transfers between devices with their start and end apart: 4 -> 6, of which waited for: 4 -> 6; matrix products, arithmetic and copies ran while one was open for 1% -> 2% of each run, Pallas kernels for 0% -> 0%
where the time goes in v1:
time: 371 us; the launch traced here: 370 us
  waiting for transfers between devices  167 us (45%)
  Pallas kernels  85.1 us (23%)
  blocking collectives  65.8 us (18%)
  other arithmetic  18.5 us (5%)
  between operations  15 us (4%)
  matrix products  14.3 us (4%)
  local copies, waits for them, and re-layouts  4.56 us (1%)
    pallas_call x1, Pallas kernels, hist_attend(): pl.pallas_call(kernel, grid=(kv_heads, blocks), in_specs=[pl.BlockSpec((1...  85.1 us
    psum x2, waiting for transfers between devices, body(): query_sum, keyval_sum = lax.psum((query_part, keyval_part), 'store')  61.8 us
    pmax x1, blocking collectives, body(): glob_top = lax.pmax(top, ('tensor', 'store'))  59.9 us
    reduce_scatter x2, waiting for transfers between devices, body(): lax.psum_scatter((acc, total), 'tensor', scatter_dimension=0, tiled=True)  58.1 us
    all_gather x1, waiting for transfers between devices, body(): lax.all_gather(jnp.transpose(query_rot, (1, 0, 2)), 'tensor', axis=0, til...  24.7 us
    reduce_scatter x1, waiting for transfers between devices, body(): lax.psum_scatter(jnp.dot(attended, w_out, preferred_element_type=jnp.floa...  21.8 us
  transfers between devices with their start and end apart: 6, of which 6 were waited for; matrix products, arithmetic and copies ran while one was open for 2% of the time, Pallas kernels for 0%

profile of v1, /device:TPU:0, one launch (start us, length us, event | category | flops | bytes accessed | tf_op | source)
XLA Modules:
  0.0 370.4 jit_solution(13812970243307221711)
XLA Ops:
  6.5 0.9 copy-done
  7.5 4.9 %convolution_bitcast_fusion = f32[8,16,8,128]{3,2,1,0:T(8,128)S(1)} fusion(bf16[64,2048]{1,0:T(8,128)(2,1)S(1)} %copy-done, bf16[2048,2048]{1,0:T(8,128)(2,1)} %param.10), kind=kOutput, calls=%fused_computation.6 | convolution fusion | flops 536870912 | bytes 9175040 | tf_op jit(solution)/shard_map/dot_general | solution.py:215
  12.4 0.9 copy.70
  13.3 0.0 all-reduce.4.cloned.1.call-update
  13.3 0.0 all-gather.2.cloned.1.call-start
  13.4 1.2 reduce-window.6
  14.7 0.1 slice.35
  14.7 0.1 copy.39
  14.9 0.1 copy.40
  15.0 0.1 add_bitcast_fusion
  15.7 0.2 multiply_cosine_fusion
  15.9 33.4 %all-reduce.4.cloned.1.call-done = f32[64,16,128]{2,0,1:T(8,128)} async-done(((f32[64,16,128]{2,0,1:T(8,128)}), f32[64,16,128]{2,0,1:T(8,128)}) %all-reduce.4.cloned.1.call-update) | async-done | bytes 524304 | tf_op jit(solution)/shard_map/psum | solution.py:217
  49.4 1.4 subtract_convert_fusion
  50.8 0.8 maximum_bitcast_fusion
  51.7 0.0 all-gather.2.cloned.1.call-update
  51.7 0.0 reduce-scatter.4.cloned.1.call-start
  51.7 0.2 fusion.24
  51.9 0.1 reduce_sum.52
  52.0 0.1 gt.27
  52.1 0.1 and.112
  52.9 0.1 fusion.46
  52.9 0.1 multiply_sine_fusion.1
  53.0 0.7 maximum_bitcast_fusion.3.cos_ref
  53.7 0.6 maximum_bitcast_fusion.4.sin_ref
  54.3 0.1 add.148
  54.4 0.1 lt.52
  54.4 0.7 and_select_fusion.bias_ref
  55.1 24.7 %all-gather.2.cloned.1.call-done = bf16[64,64,128]{2,1,0:T(8,128)(2,1)} async-done(((bf16[16,64,128]{2,1,0:T(8,128)(2,1)}), bf16[64,64,128]{2,1,0:T(8,128)(2,1)}) %all-gather.2.cloned.1.call-update) | async-done | bytes 1048592 | tf_op jit(solution)/shard_map/all_gather | solution.py:227
  79.8 85.1 %shard_map.85 = (f32[8,512,128]{2,1,0:T(8,128)}, f32[8,512,1]{2,1,0:T(8,128)}, f32[8,512,1]{2,1,0:T(8,128)}) custom-call(bf16[8,512,128]{2,1,0:T(8,128)(2,1)} %bitcast.102, bf16[40,128,2048]{2,1,0:T(8,128)(2,1)} %bitcast.95, f32[5,1,1024]{2,1,0:T(1,128)} %and_select_fusion.bias_ref, f32[1,128]{1,0:T(1,128)} %maximum_bitcast_fusion.3.cos_ref, ...), custom_call_target="tpu_custom_call" | custom-call | tf_op jit(solution)/shard_map/pallas_call | solution.py:168
  164.9 2.2 reduce
  167.1 0.1 reshape.374
  167.1 59.9 %pmax.7 = f32[64,64]{1,0:T(8,128)S(1)} all-reduce(f32[64,64]{1,0:T(8,128)S(1)} %reshape.374), channel_id=1, replica_groups=mesh['groups'=2,'tensor'=4,'store'=4] {'tensor','store'}, use_global_device_ids=true, to_apply=%region_6.7 | all-reduce | flops 4096 | bytes 32768 | tf_op jit(solution)/shard_map/pmax | solution.py:248
  227.1 2.2 reduce.1
  229.3 0.1 reshape.378
  229.3 0.6 fusion.49
  230.0 0.1 copy.42
  230.0 3.9 %copy_multiply_fusion = f32[64,64,128]{2,0,1:T(8,128)} fusion(f32[64,64,128]{2,1,0:T(8,128)} %bitcast.99, f32[64,64]{0,1:T(8,128)S(1)} %copy.42), kind=kLoop, calls=%fused_computation | loop fusion | flops 524288 | bytes 4210688 | tf_op jit(solution)/shard_map/mul | solution.py:250
  234.0 0.0 reduce-scatter.4.cloned.1.call-update
  234.0 0.0 reduce-scatter.6.cloned.1.call-start
  234.1 0.5 reduce-scatter.6.cloned.1.call-update
  234.6 0.0 all-reduce.6.cloned.1.call-start
  234.6 2.1 fusion.4
  236.7 0.1 reshape.375
  236.8 0.7 copy.44
  237.5 37.8 %reduce-scatter.4.cloned.1.call-done = f32[16,64,128]{2,0,1:T(8,128)} async-done(((f32[64,64,128]{2,0,1:T(8,128)}), f32[16,64,128]{2,0,1:T(8,128)}) %reduce-scatter.4.cloned.1.call-update) | async-done | bytes 524304 | tf_op jit(solution)/shard_map/reduce_scatter | solution.py:252
  275.3 0.0 all-reduce.6.cloned.1.call-update
  275.3 0.0 reduce-scatter.8.cloned.1.call-start
  275.4 0.1 fusion.29
  275.4 20.3 %reduce-scatter.6.cloned.1.call-done = f32[16,64]{1,0:T(8,128)} async-done(((f32[64,64]{1,0:T(8,128)}), f32[16,64]{1,0:T(8,128)}) %reduce-scatter.6.cloned.1.call-update) | async-done | bytes 4112 | tf_op jit(solution)/shard_map/reduce_scatter | solution.py:252
  295.7 5.9 %psum.31 = f32[64,16]{0,1:T(8,128)S(1)} all-reduce(f32[64,16]{0,1:T(8,128)} %bitcast.108), channel_id=1, replica_groups=mesh['groups'=2,'tensor'=4,'store'=4] {'store'}, use_global_device_ids=true, to_apply=%region_12.13 | all-reduce | flops 1024 | bytes 8192 | tf_op jit(solution)/shard_map/psum | solution.py:253
  301.6 28.4 %all-reduce.6.cloned.1.call-done = (f32[64,2,2,128]{3,0,1,2:T(8,128)}, f32[64,16,128]{2,1,0:T(8,128)}) async-done(((f32[64,2,2,128]{3,0,1,2:T(8,128)}, f32[64,16,128]{2,1,0:T(8,128)}), (f32[64,2,2,128]{3,0,1,2:T(8,128)}, f32[64,16,128]{2,1,0:T(8,128)})) %all-reduce.6.cloned.1.call-update) | async-done | bytes 655376 | tf_op jit(solution)/shard_map/psum | solution.py:217
  330.0 0.8 slice_bitcast_fusion
  330.8 0.1 subtract_convert_fusion.1
  330.9 0.5 fusion.50
  331.4 0.1 fusion.10
  331.5 1.1 fusion.12
  332.7 0.1 copy.45
  332.8 0.1 copy.47
  332.9 0.1 copy.49
  333.0 1.5 fusion.9
  334.5 5.7 %fusion.14 = f32[64,2048]{1,0:T(8,128)} fusion(bf16[2048,2048]{1,0:T(8,128)(2,1)} %param.12, bf16[8,8,16,128]{3,2,1,0:T(8,128)(2,1)S(1)} %bitcast.98), kind=kOutput, calls=%fused_computation.19 | convolution fusion | flops 536870912 | bytes 9175040 | tf_op jit(solution)/shard_map/dot_general | solution.py:276
  340.2 0.0 reduce-scatter.8.cloned.1.call-update
  340.2 21.8 %reduce-scatter.8.cloned.1.call-done = f32[16,2048]{1,0:T(8,128)} async-done(((f32[64,2048]{1,0:T(8,128)}), f32[16,2048]{1,0:T(8,128)}) %reduce-scatter.8.cloned.1.call-update) | async-done | bytes 131088 | tf_op jit(solution)/shard_map/reduce_scatter | solution.py:275
  362.0 1.5 convert_element_type.52
  (18 shorter events, 0.2 us)
Async XLA Ops:
  6.5 1.0 copy-start
  6.5 6.9 %copy-start.1 = (s32[256,1]{0,1:T(1,128)S(1)}, s32[256,1]{0,1:T(1,128)}, u32[]{:S(2)}) copy-start(s32[256,1]{0,1:T(1,128)} %param.14) | copy-start | bytes 3076
  6.5 42.8 %all-reduce.4.cloned.1.call-start = ((), (), s32[]{:S(2)}) async-start(), calls=%async_computation.3 | async-start | bytes 1048576 | tf_op jit(solution)/shard_map/psum | solution.py:217
  13.3 66.5 %all-gather.2.cloned.1.call-start = ((), (), s32[]{:S(2)}) async-start(), calls=%async_computation.4 | async-start | bytes 1310720 | tf_op jit(solution)/shard_map/all_gather | solution.py:227
  51.7 223.6 %reduce-scatter.4.cloned.1.call-start = ((), (), s32[]{:S(2)}) async-start(), calls=%async_computation.5 | async-start | bytes 2621440 | tf_op jit(solution)/shard_map/reduce_scatter | solution.py:252
  234.0 61.7 %reduce-scatter.6.cloned.1.call-start = ((), (), s32[]{:S(2)}) async-start(), calls=%async_computation.6 | async-start | bytes 40960 | tf_op jit(solution)/shard_map/reduce_scatter | solution.py:252
  234.6 95.4 %all-reduce.6.cloned.1.call-start = ((), (), s32[]{:S(2)}) async-start(), calls=%async_computation.8 | async-start | bytes 1310720 | tf_op jit(solution)/shard_map/psum | solution.py:217
  275.3 86.8 %reduce-scatter.8.cloned.1.call-start = ((), (), s32[]{:S(2)}) async-start(), calls=%async_computation.7 | async-start | bytes 655360 | tf_op jit(solution)/shard_map/reduce_scatter | solution.py:275
Sparse Core Ops, SparseCore 0:
  13.4 35.8 all-reduce.3
  51.8 27.9 all-gather.1
  234.1 41.0 reduce-scatter.3
  277.4 18.2 reduce-scatter.5
  298.0 31.9 all-reduce.5
  340.4 21.6 reduce-scatter.7

commit v2 on v1

--- a/solution.py
+++ b/solution.py
@@ -245,12 +245,15 @@
     top = top.reshape(HQ, tok_count)
     total = total.reshape(HQ, tok_count)
 
-    glob_top = lax.pmax(top, ("tensor", "store"))
+    glob_top = jnp.max(lax.all_gather(top, ("tensor", "store")), axis=0)
     factor = jnp.exp(top - glob_top)
-    acc = acc * factor[..., None]
-    total = total * factor
-    acc, total = lax.psum_scatter((acc, total), "tensor", scatter_dimension=0, tiled=True)
-    acc, total = lax.psum((acc, total), "store")
+    packed = jnp.concatenate(
+        [(acc * factor[..., None]).reshape(HQ, tok_count * HD), total * factor], axis=1
+    )
+    packed = lax.psum_scatter(packed, "tensor", scatter_dimension=0, tiled=True)
+    packed = lax.psum(packed, "store")
+    acc = packed[:, : tok_count * HD].reshape(local_heads, tok_count, HD)
+    total = packed[:, tok_count * HD :]
     loc_top = lax.dynamic_slice_in_dim(glob_top, tensor_idx * local_heads, local_heads, 0)
     hist_part = (
         jnp.transpose(loc_top),

time: 371 us -> 312 us (0.84)
  blocking collectives: 65.8 us -> 21.3 us
  waiting for transfers between devices: 167 us -> 155 us
    pmax x1 -> x0, blocking collectives: 59.9 us -> none  [body(): glob_top = lax.pmax(top, ('tensor', 'store'))]
    psum x0 -> x1, waiting for transfers between devices: none -> 35.3 us  [body(): packed = lax.psum(packed, 'store')]
    psum x2 -> x1, waiting for transfers between devices: 61.8 us -> 33.4 us  [body(): query_sum, keyval_sum = lax.psum((query_part, keyval_part), 'store')]
    all_gather x0 -> x1, blocking collectives: none -> 21.3 us  [body(): glob_top = jnp.max(lax.all_gather(top, ('tensor', 'store')), axis=0)]
    reduce_scatter x2 -> x1, waiting for transfers between devices: 58.1 us -> 39 us  [body(): packed = lax.psum_scatter(packed, 'tensor', scatter_dimension=0, tiled=True)]
    psum x1 -> x0, blocking collectives: 5.87 us -> none  [body(): acc, total = lax.psum((acc, total), 'store')]
  transfers between devices with their start and end apart: 6 -> 5, of which waited for: 6 -> 5; matrix products, arithmetic and copies ran while one was open for 2% -> 2% of each run, Pallas kernels for 0% -> 0%
where the time goes in v2:
time: 312 us
  waiting for transfers between devices  155 us (50%)
  Pallas kernels  85.1 us (27%)
  blocking collectives  21.3 us (7%)
  other arithmetic  15.1 us (5%)
  between operations  14.7 us (5%)
  matrix products  13.5 us (4%)
  local copies, waits for them, and re-layouts  7.63 us (2%)
    pallas_call x1, Pallas kernels, hist_attend(): pl.pallas_call(kernel, grid=(kv_heads, blocks), in_specs=[pl.BlockSpec((1...  85.1 us
    reduce_scatter x1, waiting for transfers between devices, body(): packed = lax.psum_scatter(packed, 'tensor', scatter_dimension=0, tiled=True)  39 us
    psum x1, waiting for transfers between devices, body(): packed = lax.psum(packed, 'store')  35.3 us
    psum x1, waiting for transfers between devices, body(): query_sum, keyval_sum = lax.psum((query_part, keyval_part), 'store')  33.4 us
    all_gather x1, waiting for transfers between devices, body(): lax.all_gather(jnp.transpose(query_rot, (1, 0, 2)), 'tensor', axis=0, til...  24.7 us
    reduce_scatter x1, waiting for transfers between devices, body(): lax.psum_scatter(jnp.dot(attended, w_out, preferred_element_type=jnp.floa...  22 us
    all_gather x1, blocking collectives, body(): glob_top = jnp.max(lax.all_gather(top, ('tensor', 'store')), axis=0)  21.3 us
  transfers between devices with their start and end apart: 5, of which 5 were waited for; matrix products, arithmetic and copies ran while one was open for 2% of the time, Pallas kernels for 0%

profile of v2, /device:TPU:0, one launch (start us, length us, event | category | flops | bytes accessed | tf_op | source)
XLA Modules:
  0.0 312.0 jit_solution(4003024640160683212)
XLA Ops:
  6.5 0.0 copy-start
  6.5 0.9 copy-done
  7.5 4.9 %convolution_bitcast_fusion = f32[8,16,8,128]{3,2,1,0:T(8,128)S(1)} fusion(bf16[64,2048]{1,0:T(8,128)(2,1)S(1)} %copy-done, bf16[2048,2048]{1,0:T(8,128)(2,1)} %param.10), kind=kOutput, calls=%fused_computation.7 | convolution fusion | flops 536870912 | bytes 9175040 | tf_op jit(solution)/shard_map/dot_general | solution.py:215
  12.4 0.9 copy.66
  13.3 0.0 all-reduce.4.cloned.1.call-update
  13.3 0.0 all-gather.2.cloned.1.call-start
  13.4 1.2 reduce-window.6
  14.7 0.1 slice.43
  14.7 0.1 copy.37
  14.9 0.1 copy.38
  15.0 0.1 add_bitcast_fusion
  15.7 0.2 multiply_cosine_fusion
  15.9 33.4 %all-reduce.4.cloned.1.call-done = f32[64,16,128]{2,0,1:T(8,128)} async-done(((f32[64,16,128]{2,0,1:T(8,128)}), f32[64,16,128]{2,0,1:T(8,128)}) %all-reduce.4.cloned.1.call-update) | async-done | bytes 524304 | tf_op jit(solution)/shard_map/psum | solution.py:217
  49.4 1.4 subtract_convert_fusion
  50.8 0.8 maximum_bitcast_fusion
  51.7 0.0 all-gather.2.cloned.1.call-update
  51.7 0.0 reduce-scatter.3.cloned.1.call-start
  51.7 0.2 fusion.25
  51.9 0.1 reduce_sum.52
  52.0 0.1 gt.27
  52.1 0.1 and.112
  52.9 0.1 fusion.48
  52.9 0.1 multiply_sine_fusion.1
  53.0 0.7 maximum_bitcast_fusion.3.cos_ref
  53.7 0.6 maximum_bitcast_fusion.4.sin_ref
  54.3 0.1 add.144
  54.4 0.1 lt.52
  54.4 0.7 and_select_fusion.bias_ref
  55.1 24.7 %all-gather.2.cloned.1.call-done = bf16[64,64,128]{2,1,0:T(8,128)(2,1)} async-done(((bf16[16,64,128]{2,1,0:T(8,128)(2,1)}), bf16[64,64,128]{2,1,0:T(8,128)(2,1)}) %all-gather.2.cloned.1.call-update) | async-done | bytes 1048592 | tf_op jit(solution)/shard_map/all_gather | solution.py:227
  79.8 85.1 %shard_map.85 = (f32[8,512,128]{2,1,0:T(8,128)}, f32[8,512,1]{2,1,0:T(8,128)}, f32[8,512,1]{2,1,0:T(8,128)}) custom-call(bf16[8,512,128]{2,1,0:T(8,128)(2,1)} %bitcast.131, bf16[40,128,2048]{2,1,0:T(8,128)(2,1)} %bitcast.124, f32[5,1,1024]{2,1,0:T(1,128)} %and_select_fusion.bias_ref, f32[1,128]{1,0:T(1,128)} %maximum_bitcast_fusion.3.cos_ref, ...), custom_call_target="tpu_custom_call" | custom-call | tf_op jit(solution)/shard_map/pallas_call | solution.py:168
  164.9 2.3 reduce
  167.2 0.1 all_gather_reshape.3
  167.3 0.1 reshape.387
  167.4 21.3 %all_gather.7 = f32[16,64,64]{2,1,0:T(8,128)S(1)} all-gather(f32[1,64,64]{2,1,0:T(8,128)S(1)} %all_gather_reshape.3), channel_id=1, replica_groups=mesh['groups'=2,'tensor'=4,'store'=4] {'tensor','store'}, dimensions={0}, use_global_device_ids=true | all-gather | bytes 278528 | tf_op jit(solution)/shard_map/all_gather | solution.py:248
  188.7 0.6 reduce.2
  189.3 0.7 reshape.388
  190.0 1.7 reshape.386
  191.8 0.8 fusion.51
  192.6 0.6 mul.238
  193.2 1.4 bitcast_multiply_fusion
  194.6 1.5 pad_maximum_fusion
  196.1 0.0 reduce-scatter.3.cloned.1.call-update
  196.1 0.0 all-reduce.6.cloned.1.call-start
  196.2 2.1 fusion.4
  198.2 0.1 reshape.390
  198.3 0.7 copy.41
  199.0 39.0 %reduce-scatter.3.cloned.1.call-done = f32[16,8256]{1,0:T(8,128)} async-done(((f32[64,8256]{1,0:T(8,128)}), f32[16,8256]{1,0:T(8,128)}) %reduce-scatter.3.cloned.1.call-update) | async-done | bytes 528400 | tf_op jit(solution)/shard_map/reduce_scatter | solution.py:253
  238.0 0.0 all-reduce.6.cloned.1.call-update
  238.0 0.0 reduce-scatter.5.cloned.1.call-start
  238.0 0.1 fusion.30
  238.1 35.3 %all-reduce.6.cloned.1.call-done = (f32[16,8256]{1,0:T(8,128)}, f32[64,2,2,128]{3,0,1,2:T(8,128)}) async-done(((f32[16,8256]{1,0:T(8,128)}, f32[64,2,2,128]{3,0,1,2:T(8,128)}), (f32[16,8256]{1,0:T(8,128)}, f32[64,2,2,128]{3,0,1,2:T(8,128)})) %all-reduce.6.cloned.1.call-update) | async-done | bytes 659472 | tf_op jit(solution)/shard_map/psum | solution.py:254
  273.5 0.9 slice_bitcast_fusion.1
  274.4 0.1 subtract_convert_fusion.1
  274.5 0.5 fusion.52
  274.9 0.1 fusion.11
  275.1 0.3 fusion.13
  275.4 0.1 copy.42
  275.5 0.1 copy.44
  275.6 0.1 copy.46
  275.7 0.5 fusion.10
  276.1 5.7 %fusion.15 = f32[64,2048]{1,0:T(8,128)} fusion(bf16[2048,2048]{1,0:T(8,128)(2,1)} %param.12, bf16[8,8,16,128]{3,2,1,0:T(8,128)(2,1)S(1)} %bitcast.128), kind=kOutput, calls=%fused_computation.23 | convolution fusion | flops 536870912 | bytes 9175040 | tf_op jit(solution)/shard_map/dot_general | solution.py:279
  281.9 0.0 reduce-scatter.5.cloned.1.call-update
  281.9 22.0 %reduce-scatter.5.cloned.1.call-done = f32[16,2048]{1,0:T(8,128)} async-done(((f32[64,2048]{1,0:T(8,128)}), f32[16,2048]{1,0:T(8,128)}) %reduce-scatter.5.cloned.1.call-update) | async-done | bytes 131088 | tf_op jit(solution)/shard_map/reduce_scatter | solution.py:278
  303.9 1.5 convert_element_type.52
  (24 shorter events, 0.2 us)
Async XLA Ops:
  6.5 1.0 copy-start
  6.5 6.9 %copy-start.4 = (s32[256,1]{0,1:T(1,128)S(1)}, s32[256,1]{0,1:T(1,128)}, u32[]{:S(2)}) copy-start(s32[256,1]{0,1:T(1,128)} %param.14) | copy-start | bytes 3076
  6.5 42.8 %all-reduce.4.cloned.1.call-start = ((), (), s32[]{:S(2)}) async-start(), calls=%async_computation.2 | async-start | bytes 1048576 | tf_op jit(solution)/shard_map/psum | solution.py:217
  13.3 66.5 %all-gather.2.cloned.1.call-start = ((), (), s32[]{:S(2)}) async-start(), calls=%async_computation.3 | async-start | bytes 1310720 | tf_op jit(solution)/shard_map/all_gather | solution.py:227
  51.7 186.3 %reduce-scatter.3.cloned.1.call-start = ((), (), s32[]{:S(2)}) async-start(), calls=%async_computation.4 | async-start | bytes 2662400 | tf_op jit(solution)/shard_map/reduce_scatter | solution.py:253
  164.9 23.8 %copy-start.1 = (f32[8,512,1]{2,1,0:T(8,128)S(1)}, f32[8,512,1]{2,1,0:T(8,128)}, u32[]{:S(2)}) copy-start(f32[8,512,1]{2,1,0:T(8,128)} %get-tuple-element.10) | copy-start | bytes 49156
  196.1 77.4 %all-reduce.6.cloned.1.call-start = ((), (), s32[]{:S(2)}) async-start(), calls=%async_computation.6 | async-start | bytes 1327104 | tf_op jit(solution)/shard_map/psum | solution.py:254
  238.0 65.9 %reduce-scatter.5.cloned.1.call-start = ((), (), s32[]{:S(2)}) async-start(), calls=%async_computation.5 | async-start | bytes 655360 | tf_op jit(solution)/shard_map/reduce_scatter | solution.py:278
  273.5 1.6 copy-start.3
  273.5 1.9 copy-start.2
Sparse Core Ops, SparseCore 0:
  13.4 35.8 all-reduce.3
  51.8 27.9 all-gather.1
  196.2 41.7 reduce-scatter.2
  240.2 33.1 all-reduce.5
  282.0 21.8 reduce-scatter.4

commit v3 on v2

--- a/solution.py
+++ b/solution.py
@@ -124,7 +124,7 @@
 MASK_FILL = -3e30
 
 
-def hist_kernel(q_ref, kv_ref, bias_ref, cos_ref, sin_ref, acc_out, m_out, l_out, m_sc, l_sc, acc_sc, *, scale, blocks):
+def hist_kernel(kv0_ref, q_ref, k_ref, v_ref, bias_ref, acc_out, m_out, l_out, m_sc, l_sc, acc_sc, *, scale, blocks):
     j = pl.program_id(1)
 
     @pl.when(j == 0)
@@ -133,12 +133,10 @@
         l_sc[...] = jnp.zeros(l_sc.shape, jnp.float32)
         acc_sc[...] = jnp.zeros(acc_sc.shape, jnp.float32)
 
-    pages, page_len, width = kv_ref.shape
-    hd = width // 2
+    pages, page_len, hd = k_ref.shape
     n = pages * page_len
-    keys = kv_ref[:, :, :hd].reshape(n, hd).astype(jnp.float32)
-    vals = kv_ref[:, :, hd:].reshape(n, hd)
-    keys = (keys * cos_ref[...] + pltpu.roll(keys, hd // 2, 1) * sin_ref[...]).astype(jnp.bfloat16)
+    keys = k_ref[...].reshape(n, hd)
+    vals = v_ref[...].reshape(n, hd)
     scores = lax.dot_general(
         q_ref[0], keys, (((1,), (1,)), ((), ())), preferred_element_type=jnp.float32
     )
@@ -160,38 +158,46 @@
         l_out[0] = l_sc[...]
 
 
-def hist_attend(q_k, kv_local, bias, cos2, sin2, pb):
-    kv_heads, rows, hd = q_k.shape
+def hist_attend(kv0, q_k, keys_rot, kv_local, bias, pb):
+    heads, rows, hd = q_k.shape
     slots, page_len, width = kv_local.shape
+    kv_heads = width // (2 * hd)
     blocks = slots // pb
     kernel = functools.partial(hist_kernel, scale=1.0 / hd ** 0.5, blocks=blocks)
-    return pl.pallas_call(
-        kernel,
-        grid=(kv_heads, blocks),
+
+    def head_of(h, kv0_ref):
+        return (kv0_ref[0] + h) % kv_heads
+
+    grid_spec = pltpu.PrefetchScalarGridSpec(
+        num_scalar_prefetch=1,
+        grid=(heads, blocks),
         in_specs=[
-            pl.BlockSpec((1, rows, hd), lambda h, j: (h, 0, 0)),
-            pl.BlockSpec((pb, page_len, 2 * hd), lambda h, j: (j, 0, h)),
-            pl.BlockSpec((1, 1, pb * page_len), lambda h, j: (j, 0, 0)),
-            pl.BlockSpec((1, hd), lambda h, j: (0, 0)),
-            pl.BlockSpec((1, hd), lambda h, j: (0, 0)),
+            pl.BlockSpec((1, rows, hd), lambda h, j, r: (h, 0, 0)),
+            pl.BlockSpec((pb, page_len, hd), lambda h, j, r: (j, 0, head_of(h, r))),
+            pl.BlockSpec((pb, page_len, hd), lambda h, j, r: (j, 0, 2 * head_of(h, r) + 1)),
+            pl.BlockSpec((1, 1, pb * page_len), lambda h, j, r: (j, 0, 0)),
         ],
         out_specs=[
-            pl.BlockSpec((1, rows, hd), lambda h, j: (h, 0, 0)),
-            pl.BlockSpec((1, rows, 1), lambda h, j: (h, 0, 0)),
-            pl.BlockSpec((1, rows, 1), lambda h, j: (h, 0, 0)),
-        ],
-        out_shape=[
-            jax.ShapeDtypeStruct((kv_heads, rows, hd), jnp.float32),
-            jax.ShapeDtypeStruct((kv_heads, rows, 1), jnp.float32),
-            jax.ShapeDtypeStruct((kv_heads, rows, 1), jnp.float32),
+            pl.BlockSpec((1, rows, hd), lambda h, j, r: (h, 0, 0)),
+            pl.BlockSpec((1, rows, 1), lambda h, j, r: (h, 0, 0)),
+            pl.BlockSpec((1, rows, 1), lambda h, j, r: (h, 0, 0)),
         ],
         scratch_shapes=[
             pltpu.VMEM((rows, 1), jnp.float32),
             pltpu.VMEM((rows, 1), jnp.float32),
             pltpu.VMEM((rows, hd), jnp.float32),
         ],
-        compiler_params=pltpu.CompilerParams(dimension_semantics=("parallel", "arbitrary")),
-    )(q_k, kv_local, bias, cos2, sin2)
+    )
+    return pl.pallas_call(
+        kernel,
+        grid_spec=grid_spec,
+        out_shape=[
+            jax.ShapeDtypeStruct((heads, rows, hd), jnp.float32),
+            jax.ShapeDtypeStruct((heads, rows, 1), jnp.float32),
+            jax.ShapeDtypeStruct((heads, rows, 1), jnp.float32),
+        ],
+        compiler_params=pltpu.CompilerParams(dimension_semantics=("arbitrary", "arbitrary")),
+    )(jnp.reshape(kv0, (1,)).astype(jnp.int32), q_k, keys_rot, kv_local, bias)
 
 
 def body(x_new, kv_pages, w_query, w_keyval, w_out, lengths, page_store, offsets):
@@ -224,9 +230,6 @@
     key_new = to_half(rotate(keyval_local[:, :, 0], tok_angle))
     value_new = to_half(keyval_local[:, :, 1])
 
-    q_all = lax.all_gather(jnp.transpose(query_rot, (1, 0, 2)), "tensor", axis=0, tiled=True)
-    q_k = q_all.reshape(kv_heads, group_size * tok_count, HD)
-
     first_slot = store_idx * capacity + tensor_idx * local_slots
     key_sess, key_ok, key_off = slot_meta(
         page_store, lengths, offsets, shards, capacity, first_slot, local_slots, page_len
@@ -235,12 +238,33 @@
     bias = jnp.where(key_ok, 0.0, MASK_FILL).astype(jnp.float32)
     bias = bias.reshape(local_slots // pb, 1, pb * page_len)
     hist_angle = offsets[0].astype(jnp.float32) * freq_table
-    cosine = jnp.cos(hist_angle)
-    sine = jnp.sin(hist_angle)
-    cos2 = jnp.concatenate([cosine, cosine])[None, :]
-    sin2 = jnp.concatenate([-sine, sine])[None, :]
     kv_local = kv_pages.reshape(local_slots, page_len, kv_pages.shape[3])
-    acc, top, total = hist_attend(q_k, kv_local, bias, cos2, sin2, pb)
+    keys_rot = to_half(
+        rotate(
+            kv_local.reshape(local_slots, page_len, kv_heads, 2, HD)[:, :, :, 0].astype(jnp.float32),
+            hist_angle,
+        )
+    ).reshape(local_slots, page_len, kv_heads * HD)
+
+    q_heads = jnp.transpose(query_rot, (1, 0, 2))
+    q_all = lax.all_gather(q_heads, "tensor", axis=0, tiled=True)
+    q_k = q_all.reshape(kv_heads, group_size * tok_count, HD)
+    if local_heads % group_size == 0:
+        own = hist_attend(
+            kv_first, q_heads.reshape(local_kv, group_size * tok_count, HD), keys_rot, kv_local, bias, pb
+        )
+        rest_first = kv_first + local_kv
+        q_rest = lax.dynamic_slice_in_dim(
+            jnp.concatenate([q_k, q_k], axis=0), rest_first % kv_heads, kv_heads - local_kv, 0
+        )
+        rest = hist_attend(rest_first % kv_heads, q_rest, keys_rot, kv_local, bias, pb)
+        parts = []
+        for first, second in zip(own, rest):
+            rolled = jnp.concatenate([first, second, first, second], axis=0)
+            parts.append(lax.dynamic_slice_in_dim(rolled, kv_heads - kv_first, kv_heads, 0))
+        acc, top, total = parts
+    else:
+        acc, top, total = hist_attend(jnp.int32(0), q_k, keys_rot, kv_local, bias, pb)
     acc = acc.reshape(HQ, tok_count, HD)
     top = top.reshape(HQ, tok_count)
     total = total.reshape(HQ, tok_count)

time: 312 us -> 363 us (1.16)
  local copies, waits for them, and re-layouts: 7.63 us -> 64.3 us
  waiting for transfers between devices: 155 us -> 101 us
  other arithmetic: 15.1 us -> 62.9 us
    another operation x2 -> x3, local copies, waits for them, and re-layouts: 0.1 us -> 34.1 us  [the longest x1 34 us: body(): kv_local.reshape(local_slots, page_len, kv_heads, 2, HD)[:, :, :, 0]]
    psum x1, waiting for transfers between devices: 33.4 us -> 0.02 us  [body(): query_sum, keyval_sum = lax.psum((query_part, keyval_part), 'store')]
    all_gather x1, waiting for transfers between devices: 24.7 us -> 4.6 us  [body(): q_all = lax.all_gather(q_heads, 'tensor', axis=0, tiled=True)]
    another operation x4 -> x5, other arithmetic: 2.78 us -> 21.5 us
    convert_element_type x0 -> x1, other arithmetic: none -> 17.5 us  [body(): kv_local.reshape(local_slots, page_len, kv_heads, 2, HD)[:, :, :, 0]]
    convert_element_type x0 -> x1, local copies, waits for them, and re-layouts: none -> 16.3 us  [to_half(): return values.astype(jnp.bfloat16)]
    concatenate x0 -> x6, other arithmetic: none -> 13.9 us  [the longest x2 8.26 us: rotate(): jnp.concatenate([first_half * cosine - second_half * sine_part, second_ha...]
    pallas_call x0 -> x4, local copies, waits for them, and re-layouts: none -> 6.49 us  [hist_attend(): pl.pallas_call(kernel, grid_spec=grid_spec, out_shape=[jax.ShapeDtypeStru...]
  transfers between devices with their start and end apart: 5 -> 5, of which waited for: 5 -> 4; matrix products, arithmetic and copies ran while one was open for 2% -> 29% of each run, Pallas kernels for 0% -> 6%
where the time goes in v3:
time: 363 us; the launch traced here: 361 us
  waiting for transfers between devices  101 us (28%)
  Pallas kernels  82 us (23%)
  local copies, waits for them, and re-layouts  64.3 us (18%)
  other arithmetic  62.9 us (17%)
  blocking collectives  21.5 us (6%)
  between operations  14.7 us (4%)
  matrix products  14.3 us (4%)
    pallas_call x2, Pallas kernels, hist_attend(): pl.pallas_call(kernel, grid_spec=grid_spec, out_shape=[jax.ShapeDtypeStru...  82 us
    reduce_scatter x1, waiting for transfers between devices, body(): packed = lax.psum_scatter(packed, 'tensor', scatter_dimension=0, tiled=True)  39 us
    psum x1, waiting for transfers between devices, body(): packed = lax.psum(packed, 'store')  35.3 us
    another operation x1, local copies, waits for them, and re-layouts, body(): kv_local.reshape(local_slots, page_len, kv_heads, 2, HD)[:, :, :, 0]  34 us
    reduce_scatter x1, waiting for transfers between devices, body(): lax.psum_scatter(jnp.dot(attended, w_out, preferred_element_type=jnp.floa...  22 us
    another operation x5, other arithmetic  21.5 us
    all_gather x1, blocking collectives, body(): glob_top = jnp.max(lax.all_gather(top, ('tensor', 'store')), axis=0)  21.5 us
    convert_element_type x1, other arithmetic, body(): kv_local.reshape(local_slots, page_len, kv_heads, 2, HD)[:, :, :, 0]  17.5 us
  transfers between devices with their start and end apart: 5, of which 4 were waited for; matrix products, arithmetic and copies ran while one was open for 29% of the time, Pallas kernels for 6%

profile of v3, /device:TPU:0, one launch (start us, length us, event | category | flops | bytes accessed | tf_op | source)
XLA Modules:
  0.0 360.8 jit_solution(7767647685430638583)
XLA Ops:
  6.5 0.9 copy-done
  7.5 4.9 %convolution_bitcast_fusion = f32[8,16,8,128]{3,2,1,0:T(8,128)S(1)} fusion(bf16[64,2048]{1,0:T(8,128)(2,1)S(1)} %copy-done, bf16[2048,2048]{1,0:T(8,128)(2,1)} %param.10), kind=kOutput, calls=%fused_computation.21 | convolution fusion | flops 536870912 | bytes 9175040 | tf_op jit(solution)/shard_map/dot_general | solution.py:221
  12.4 0.9 copy.90
  14.1 34.0 %reshape_reshape.3 = bf16[40,128,8,2,128]{4,3,2,1,0:T(2,128)(2,1)} reshape(bf16[1,40,128,2048]{3,2,1,0:T(8,128)(2,1)} %param.9) | data formatting | bytes 41943040 | tf_op jit(solution)/shard_map/reshape;reshape | solution.py:244
  48.1 17.5 %fusion = f32[40,128,8,128]{3,2,1,0:T(8,128)} fusion(bf16[40,128,8,1,128]{4,3,2,1,0:T(2,128)(2,1)} %bitcast.142), kind=kLoop, calls=%fused_computation.4 | loop fusion | flops 5242880 | bytes 31457280 | tf_op jit(solution)/shard_map/convert_element_type | solution.py:244
  66.3 0.1 multiply_sine_fusion.1
  66.3 18.8 %subtract_convert_fusion = (bf16[40,128,8,64]{3,2,1,0:T(8,128)(2,1)S(1)}, bf16[40,128,8,64]{3,2,1,0:T(8,128)(2,1)S(1)}) fusion(f32[40,128,8,128]{3,2,1,0:T(8,128)} %fusion, f32[64]{0:T(128)S(1)} %get-tuple-element.38, f32[64]{0:T(128)S(1)} %get-tuple-element.39), kind=kLoop, calls=%fused_computation.1 | loop fusion | flops 20971520 | bytes 31457792 | tf_op jit(solution)/shard_map/convert.8
  85.1 7.4 %pad_maximum_fusion = bf16[40,128,8,128]{3,2,1,0:T(8,128)(2,1)} fusion(bf16[40,128,8,64]{3,2,1,0:T(8,128)(2,1)S(1)} %get-tuple-element.27, bf16[40,128,8,64]{3,2,1,0:T(8,128)(2,1)S(1)} %get-tuple-element.26), kind=kLoop, calls=%fused_computation.2 | loop fusion | flops 20971520 | bytes 20971520 | tf_op jit(solution)/shard_map/concatenate | solution.py:55
  92.5 16.3 %convert_element_type.58.k_ref = bf16[40,128,1024]{2,1,0:T(8,128)(2,1)} reshape(bf16[40,128,8,128]{3,2,1,0:T(8,128)(2,1)} %pad_maximum_fusion) | data formatting | bytes 20971520 | tf_op jit(solution)/shard_map/convert_element_type | solution.py:65
  108.8 1.2 reduce-window.6
  110.0 0.1 slice.58
  110.1 0.1 copy.49
  110.3 0.1 copy.50
  110.4 0.2 multiply_cosine_fusion
  110.6 1.4 subtract_convert_fusion.1
  112.0 0.9 fusion.67
  112.9 0.0 reduce-scatter.3.cloned.1.call-start
  113.0 0.1 add_bitcast_fusion
  113.1 0.2 fusion.30
  113.3 0.1 gt.34
  113.3 0.1 and.119
  113.5 0.1 reduce_sum.52
  113.6 0.1 lt.73
  113.6 0.1 add.179
  113.7 0.7 and_select_fusion.bias_ref
  114.4 0.9 pad_maximum_fusion.2
  115.2 21.4 %shard_map.85 = (f32[2,512,128]{2,1,0:T(8,128)}, f32[2,512,1]{2,1,0:T(8,128)}, f32[2,512,1]{2,1,0:T(8,128)}) custom-call(s32[1]{0:T(128)} %bitcast.kv0_ref, bf16[2,512,128]{2,1,0:T(8,128)(2,1)} %bitcast.149, bf16[40,128,1024]{2,1,0:T(8,128)(2,1)} %convert_element_type.58.k_ref, bf16[40,128,2048]{2,1,0:T(8,128)(2,1)} %bitcast.140, ...), custom_call_target="tpu_custom_call" | custom-call | tf_op jit(solution)/shard_map/pallas_call | solution.py:191
  136.7 1.2 copy.56
  137.9 1.2 copy.52
  139.1 4.6 %all-gather.2.cloned.1.call-done = bf16[64,64,128]{2,1,0:T(8,128)(2,1)} async-done(((bf16[16,64,128]{2,1,0:T(8,128)(2,1)}), bf16[64,64,128]{2,1,0:T(8,128)(2,1)}) %all-gather.2.cloned.1.call-update) | async-done | bytes 1048592 | tf_op jit(solution)/shard_map/all_gather | solution.py:250
  143.7 2.3 fusion.11.q_ref
  146.0 60.5 %shard_map.86 = (f32[6,512,128]{2,1,0:T(8,128)}, f32[6,512,1]{2,1,0:T(8,128)}, f32[6,512,1]{2,1,0:T(8,128)}) custom-call(s32[1]{0:T(128)} %bitcast.17.kv0_ref, bf16[6,512,128]{2,1,0:T(8,128)(2,1)} %fusion.11.q_ref, bf16[40,128,1024]{2,1,0:T(8,128)(2,1)} %convert_element_type.58.k_ref, bf16[40,128,2048]{2,1,0:T(8,128)(2,1)} %bitcast.141, ...), custom_call_target="tpu_custom_call" | custom-call | tf_op jit(solution)/shard_map/pallas_call | solution.py:191
  206.6 2.0 copy.53
  208.6 0.1 reshape.431
  208.7 0.1 all_gather_reshape.3
  208.8 2.0 copy.57
  210.9 0.7 reshape.432
  211.5 21.5 %all_gather.7 = f32[16,64,64]{2,1,0:T(8,128)S(1)} all-gather(f32[1,64,64]{2,1,0:T(8,128)S(1)} %all_gather_reshape.3), channel_id=1, replica_groups=mesh['groups'=2,'tensor'=4,'store'=4] {'tensor','store'}, dimensions={0}, use_global_device_ids=true | all-gather | bytes 278528 | tf_op jit(solution)/shard_map/all_gather | solution.py:272
  233.0 3.3 fusion.3
  236.3 1.7 reshape.430
  238.1 0.8 fusion.61
  238.9 0.6 mul.308
  239.5 1.4 bitcast_multiply_fusion
  240.9 1.5 pad_maximum_fusion.1
  242.4 0.0 all-reduce.6.cloned.1.call-start
  242.5 2.1 fusion.8
  244.6 0.1 reshape.434
  244.7 0.7 copy.61
  245.3 39.0 %reduce-scatter.3.cloned.1.call-done = f32[16,8256]{1,0:T(8,128)} async-done(((f32[64,8256]{1,0:T(8,128)}), f32[16,8256]{1,0:T(8,128)}) %reduce-scatter.3.cloned.1.call-update) | async-done | bytes 528400 | tf_op jit(solution)/shard_map/reduce_scatter | solution.py:277
  284.4 0.1 fusion.35
  284.5 35.3 %all-reduce.6.cloned.1.call-done = (f32[16,8256]{1,0:T(8,128)}, f32[64,2,2,128]{3,0,1,2:T(8,128)}) async-done(((f32[16,8256]{1,0:T(8,128)}, f32[64,2,2,128]{3,0,1,2:T(8,128)}), (f32[16,8256]{1,0:T(8,128)}, f32[64,2,2,128]{3,0,1,2:T(8,128)})) %all-reduce.6.cloned.1.call-update) | async-done | bytes 659472 | tf_op jit(solution)/shard_map/psum | solution.py:278
  319.8 0.8 slice_bitcast_fusion.1
  320.6 0.1 subtract_convert_fusion.2
  320.7 0.5 fusion.62
  321.2 1.1 fusion.18
  322.3 0.1 fusion.16
  322.5 0.7 fusion.45
  323.2 0.1 copy.66
  323.3 0.1 copy.64
  323.4 0.1 copy.62
  323.4 1.5 fusion.15
  325.0 5.7 %fusion.20 = f32[64,2048]{1,0:T(8,128)} fusion(bf16[2048,2048]{1,0:T(8,128)(2,1)} %param.12, bf16[8,8,16,128]{3,2,1,0:T(8,128)(2,1)S(1)} %bitcast.146), kind=kOutput, calls=%fused_computation.38 | convolution fusion | flops 536870912 | bytes 9175040 | tf_op jit(solution)/shard_map/dot_general | solution.py:303
  330.7 22.0 %reduce-scatter.5.cloned.1.call-done = f32[16,2048]{1,0:T(8,128)} async-done(((f32[64,2048]{1,0:T(8,128)}), f32[16,2048]{1,0:T(8,128)}) %reduce-scatter.5.cloned.1.call-update) | async-done | bytes 131088 | tf_op jit(solution)/shard_map/reduce_scatter | solution.py:302
  352.8 1.5 convert_element_type.66
  (30 shorter events, 0.5 us)
Async XLA Ops:
  6.5 1.0 copy-start
  6.5 104.0 %all-reduce.4.cloned.1.call-start = ((), (), s32[]{:S(2)}) async-start(), calls=%async_computation.2 | async-start | bytes 1048576 | tf_op jit(solution)/shard_map/psum | solution.py:223
  13.3 130.4 %all-gather.2.cloned.1.call-start = ((), (), s32[]{:S(2)}) async-start(), calls=%async_computation.3 | async-start | bytes 1310720 | tf_op jit(solution)/shard_map/all_gather | solution.py:250
  48.1 18.3 %copy-start.2 = (s32[256,1]{0,1:T(1,128)S(1)}, s32[256,1]{0,1:T(1,128)}, u32[]{:S(2)}) copy-start(s32[256,1]{0,1:T(1,128)} %param.14) | copy-start | bytes 3076
  112.9 171.4 %reduce-scatter.3.cloned.1.call-start = ((), (), s32[]{:S(2)}) async-start(), calls=%async_computation.4 | async-start | bytes 2662400 | tf_op jit(solution)/shard_map/reduce_scatter | solution.py:277
  146.0 87.0 %copy-start.1 = (f32[2,512,128]{2,1,0:T(8,128)S(1)}, f32[2,512,128]{2,1,0:T(8,128)}, u32[]{:S(2)}) copy-start(f32[2,512,128]{2,1,0:T(8,128)} %get-tuple-element.11) | copy-start | bytes 1572868
  242.4 77.4 %all-reduce.6.cloned.1.call-start = ((), (), s32[]{:S(2)}) async-start(), calls=%async_computation.6 | async-start | bytes 1327104 | tf_op jit(solution)/shard_map/psum | solution.py:278
  284.3 68.4 %reduce-scatter.5.cloned.1.call-start = ((), (), s32[]{:S(2)}) async-start(), calls=%async_computation.5 | async-start | bytes 655360 | tf_op jit(solution)/shard_map/reduce_scatter | solution.py:302
Sparse Core Ops, SparseCore 0:
  13.4 35.8 all-reduce.3
  113.0 30.6 all-gather.1
  242.6 41.7 reduce-scatter.2
  286.6 33.1 all-reduce.5
  330.8 21.8 reduce-scatter.4

commit v4 on v3

--- a/solution.py
+++ b/solution.py
@@ -124,7 +124,7 @@
 MASK_FILL = -3e30
 
 
-def hist_kernel(kv0_ref, q_ref, k_ref, v_ref, bias_ref, acc_out, m_out, l_out, m_sc, l_sc, acc_sc, *, scale, blocks):
+def hist_kernel(kv0_ref, q_ref, k_ref, v_ref, bias_ref, cos_ref, sin_ref, acc_out, m_out, l_out, m_sc, l_sc, acc_sc, *, scale, blocks):
     j = pl.program_id(1)
 
     @pl.when(j == 0)
@@ -135,8 +135,9 @@
 
     pages, page_len, hd = k_ref.shape
     n = pages * page_len
-    keys = k_ref[...].reshape(n, hd)
+    keys = k_ref[...].reshape(n, hd).astype(jnp.float32)
     vals = v_ref[...].reshape(n, hd)
+    keys = (keys * cos_ref[...] + pltpu.roll(keys, hd // 2, 1) * sin_ref[...]).astype(jnp.bfloat16)
     scores = lax.dot_general(
         q_ref[0], keys, (((1,), (1,)), ((), ())), preferred_element_type=jnp.float32
     )
@@ -158,7 +159,7 @@
         l_out[0] = l_sc[...]
 
 
-def hist_attend(kv0, q_k, keys_rot, kv_local, bias, pb):
+def hist_attend(kv0, q_k, kv_local, bias, cos2, sin2, pb):
     heads, rows, hd = q_k.shape
     slots, page_len, width = kv_local.shape
     kv_heads = width // (2 * hd)
@@ -173,9 +174,11 @@
         grid=(heads, blocks),
         in_specs=[
             pl.BlockSpec((1, rows, hd), lambda h, j, r: (h, 0, 0)),
-            pl.BlockSpec((pb, page_len, hd), lambda h, j, r: (j, 0, head_of(h, r))),
+            pl.BlockSpec((pb, page_len, hd), lambda h, j, r: (j, 0, 2 * head_of(h, r))),
             pl.BlockSpec((pb, page_len, hd), lambda h, j, r: (j, 0, 2 * head_of(h, r) + 1)),
             pl.BlockSpec((1, 1, pb * page_len), lambda h, j, r: (j, 0, 0)),
+            pl.BlockSpec((1, hd), lambda h, j, r: (0, 0)),
+            pl.BlockSpec((1, hd), lambda h, j, r: (0, 0)),
         ],
         out_specs=[
             pl.BlockSpec((1, rows, hd), lambda h, j, r: (h, 0, 0)),
@@ -197,7 +200,7 @@
             jax.ShapeDtypeStruct((heads, rows, 1), jnp.float32),
         ],
         compiler_params=pltpu.CompilerParams(dimension_semantics=("arbitrary", "arbitrary")),
-    )(jnp.reshape(kv0, (1,)).astype(jnp.int32), q_k, keys_rot, kv_local, bias)
+    )(jnp.reshape(kv0, (1,)).astype(jnp.int32), q_k, kv_local, kv_local, bias, cos2, sin2)
 
 
 def body(x_new, kv_pages, w_query, w_keyval, w_out, lengths, page_store, offsets):
@@ -234,37 +237,35 @@
     key_sess, key_ok, key_off = slot_meta(
         page_store, lengths, offsets, shards, capacity, first_slot, local_slots, page_len
     )
-    pb = 8 if local_slots % 8 == 0 else local_slots
+    pb = max(d for d in range(1, min(local_slots, 20) + 1) if local_slots % d == 0)
     bias = jnp.where(key_ok, 0.0, MASK_FILL).astype(jnp.float32)
     bias = bias.reshape(local_slots // pb, 1, pb * page_len)
     hist_angle = offsets[0].astype(jnp.float32) * freq_table
     kv_local = kv_pages.reshape(local_slots, page_len, kv_pages.shape[3])
-    keys_rot = to_half(
-        rotate(
-            kv_local.reshape(local_slots, page_len, kv_heads, 2, HD)[:, :, :, 0].astype(jnp.float32),
-            hist_angle,
-        )
-    ).reshape(local_slots, page_len, kv_heads * HD)
+    cosine = jnp.cos(hist_angle)
+    sine = jnp.sin(hist_angle)
+    cos2 = jnp.concatenate([cosine, cosine])[None, :]
+    sin2 = jnp.concatenate([-sine, sine])[None, :]
 
     q_heads = jnp.transpose(query_rot, (1, 0, 2))
     q_all = lax.all_gather(q_heads, "tensor", axis=0, tiled=True)
     q_k = q_all.reshape(kv_heads, group_size * tok_count, HD)
     if local_heads % group_size == 0:
         own = hist_attend(
-            kv_first, q_heads.reshape(local_kv, group_size * tok_count, HD), keys_rot, kv_local, bias, pb
+            kv_first, q_heads.reshape(local_kv, group_size * tok_count, HD), kv_local, bias, cos2, sin2, pb
         )
         rest_first = kv_first + local_kv
         q_rest = lax.dynamic_slice_in_dim(
             jnp.concatenate([q_k, q_k], axis=0), rest_first % kv_heads, kv_heads - local_kv, 0
         )
-        rest = hist_attend(rest_first % kv_heads, q_rest, keys_rot, kv_local, bias, pb)
+        rest = hist_attend(rest_first % kv_heads, q_rest, kv_local, bias, cos2, sin2, pb)
         parts = []
         for first, second in zip(own, rest):
             rolled = jnp.concatenate([first, second, first, second], axis=0)
             parts.append(lax.dynamic_slice_in_dim(rolled, kv_heads - kv_first, kv_heads, 0))
         acc, top, total = parts
     else:
-        acc, top, total = hist_attend(jnp.int32(0), q_k, keys_rot, kv_local, bias, pb)
+        acc, top, total = hist_attend(jnp.int32(0), q_k, kv_local, bias, cos2, sin2, pb)
     acc = acc.reshape(HQ, tok_count, HD)
     top = top.reshape(HQ, tok_count)
     total = total.reshape(HQ, tok_count)

time: 363 us -> 270 us (0.74)
  local copies, waits for them, and re-layouts: 64.3 us -> 14.3 us
  other arithmetic: 62.9 us -> 17.4 us
  waiting for transfers between devices: 101 us -> 138 us
  Pallas kernels: 82 us -> 49 us
    another operation x3 -> x2, local copies, waits for them, and re-layouts: 34.1 us -> 0.1 us  [the longest x1 34 us: body(): kv_local.reshape(local_slots, page_len, kv_heads, 2, HD)[:, :, :, 0]]
    pallas_call x2, Pallas kernels: 82 us -> 49 us  [hist_attend(): pl.pallas_call(kernel, grid_spec=grid_spec, out_shape=[jax.ShapeDtypeStru...]
    psum x1, waiting for transfers between devices: 0.02 us -> 32.9 us  [body(): query_sum, keyval_sum = lax.psum((query_part, keyval_part), 'store')]
    another operation x5 -> x4, other arithmetic: 21.5 us -> 2.78 us
    convert_element_type x1 -> x0, other arithmetic: 17.5 us -> none  [body(): kv_local.reshape(local_slots, page_len, kv_heads, 2, HD)[:, :, :, 0]]
    convert_element_type x1 -> x0, local copies, waits for them, and re-layouts: 16.3 us -> none  [to_half(): return values.astype(jnp.bfloat16)]
    concatenate x2 -> x1, other arithmetic: 8.26 us -> 0.86 us  [rotate(): jnp.concatenate([first_half * cosine - second_half * sine_part, second_ha...]
    all_gather x1, waiting for transfers between devices: 4.6 us -> 8.44 us  [body(): q_all = lax.all_gather(q_heads, 'tensor', axis=0, tiled=True)]
  transfers between devices with their start and end apart: 5 -> 5, of which waited for: 4 -> 5; matrix products, arithmetic and copies ran while one was open for 29% -> 4% of each run, Pallas kernels for 6% -> 5%
where the time goes in v4:
time: 270 us; the launch traced here: 269 us
  waiting for transfers between devices  138 us (51%)
  Pallas kernels  49 us (18%)
  blocking collectives  21.5 us (8%)
  other arithmetic  17.4 us (6%)
  between operations  14.7 us (5%)
  local copies, waits for them, and re-layouts  14.3 us (5%)
  matrix products  14.3 us (5%)
    pallas_call x2, Pallas kernels, hist_attend(): pl.pallas_call(kernel, grid_spec=grid_spec, out_shape=[jax.ShapeDtypeStru...  49 us
    reduce_scatter x1, waiting for transfers between devices, body(): packed = lax.psum_scatter(packed, 'tensor', scatter_dimension=0, tiled=True)  39 us
    psum x1, waiting for transfers between devices, body(): packed = lax.psum(packed, 'store')  35.3 us
    psum x1, waiting for transfers between devices, body(): query_sum, keyval_sum = lax.psum((query_part, keyval_part), 'store')  32.9 us
    reduce_scatter x1, waiting for transfers between devices, body(): lax.psum_scatter(jnp.dot(attended, w_out, preferred_element_type=jnp.floa...  22 us
    all_gather x1, blocking collectives, body(): glob_top = jnp.max(lax.all_gather(top, ('tensor', 'store')), axis=0)  21.5 us
    all_gather x1, waiting for transfers between devices, body(): q_all = lax.all_gather(q_heads, 'tensor', axis=0, tiled=True)  8.44 us
    pallas_call x4, local copies, waits for them, and re-layouts, hist_attend(): pl.pallas_call(kernel, grid_spec=grid_spec, out_shape=[jax.ShapeDtypeStru...  6.64 us
  transfers between devices with their start and end apart: 5, of which 5 were waited for; matrix products, arithmetic and copies ran while one was open for 4% of the time, Pallas kernels for 5%

profile of v4, /device:TPU:0, one launch (start us, length us, event | category | flops | bytes accessed | tf_op | source)
XLA Modules:
  0.0 269.2 jit_solution(7948850755737241333)
XLA Ops:
  6.5 0.9 copy-done
  7.5 4.9 %convolution_bitcast_fusion = f32[8,16,8,128]{3,2,1,0:T(8,128)S(1)} fusion(bf16[64,2048]{1,0:T(8,128)(2,1)S(1)} %copy-done, bf16[2048,2048]{1,0:T(8,128)(2,1)} %param.10), kind=kOutput, calls=%fused_computation.16 | convolution fusion | flops 536870912 | bytes 9175040 | tf_op jit(solution)/shard_map/dot_general | solution.py:224
  12.4 0.9 copy.88
  13.3 0.0 all-gather.2.cloned.1.call-start
  14.1 1.2 reduce-window.6
  15.3 0.1 slice.43
  15.4 0.1 copy.49
  15.5 0.1 copy.50
  15.6 0.1 add_bitcast_fusion
  15.7 0.2 fusion.29
  16.0 0.1 gt.27
  16.1 0.1 and.119
  16.2 0.1 reduce_sum.52
  16.3 0.2 multiply_cosine_fusion
  16.5 32.9 %all-reduce.4.cloned.1.call-done = f32[64,16,128]{2,0,1:T(8,128)} async-done(((f32[64,16,128]{2,0,1:T(8,128)}), f32[64,16,128]{2,0,1:T(8,128)}) %all-reduce.4.cloned.1.call-update) | async-done | bytes 524304 | tf_op jit(solution)/shard_map/psum | solution.py:226
  49.4 1.4 subtract_convert_fusion
  50.8 0.9 fusion.63
  51.7 0.0 reduce-scatter.3.cloned.1.call-start
  51.8 0.1 lt.66
  51.9 0.1 add.161
  52.7 0.1 fusion.54
  52.7 0.1 multiply_sine_fusion.1
  52.8 0.6 maximum_bitcast_fusion.2.cos_ref
  53.4 0.7 maximum_bitcast_fusion.3.sin_ref
  54.0 0.7 and_select_fusion.bias_ref
  54.7 0.9 pad_maximum_fusion.1
  55.6 13.3 %shard_map.85 = (f32[2,512,128]{2,1,0:T(8,128)}, f32[2,512,1]{2,1,0:T(8,128)}, f32[2,512,1]{2,1,0:T(8,128)}) custom-call(s32[1]{0:T(128)} %bitcast.kv0_ref, bf16[2,512,128]{2,1,0:T(8,128)(2,1)} %bitcast.142, bf16[40,128,2048]{2,1,0:T(8,128)(2,1)} %bitcast.132, bf16[40,128,2048]{2,1,0:T(8,128)(2,1)} %bitcast.133, f32[2,1,2560]{2,1,0:T(1,128)} %and_select_fusion.bias_ref, ...), custom_call_target="tpu_custom_call" | custom-call | tf_op jit(solution)/shard_map/pallas_call | solution.py:194
  68.9 1.2 copy.58
  70.1 1.2 copy.54
  71.4 8.4 %all-gather.2.cloned.1.call-done = bf16[64,64,128]{2,1,0:T(8,128)(2,1)} async-done(((bf16[16,64,128]{2,1,0:T(8,128)(2,1)}), bf16[64,64,128]{2,1,0:T(8,128)(2,1)}) %all-gather.2.cloned.1.call-update) | async-done | bytes 1048592 | tf_op jit(solution)/shard_map/all_gather | solution.py:251
  79.8 2.3 fusion.10.q_ref
  82.1 35.7 %shard_map.86 = (f32[6,512,128]{2,1,0:T(8,128)}, f32[6,512,1]{2,1,0:T(8,128)}, f32[6,512,1]{2,1,0:T(8,128)}) custom-call(s32[1]{0:T(128)} %bitcast.15.kv0_ref, bf16[6,512,128]{2,1,0:T(8,128)(2,1)} %fusion.10.q_ref, bf16[40,128,2048]{2,1,0:T(8,128)(2,1)} %bitcast.134, bf16[40,128,2048]{2,1,0:T(8,128)(2,1)} %bitcast.135, ...), custom_call_target="tpu_custom_call" | custom-call | tf_op jit(solution)/shard_map/pallas_call | solution.py:194
  117.8 2.2 copy.55
  120.0 0.1 reshape.399
  120.1 0.1 all_gather_reshape.3
  120.2 2.0 copy.59
  122.2 0.7 reshape.400
  122.9 21.5 %all_gather.7 = f32[16,64,64]{2,1,0:T(8,128)S(1)} all-gather(f32[1,64,64]{2,1,0:T(8,128)S(1)} %all_gather_reshape.3), channel_id=1, replica_groups=mesh['groups'=2,'tensor'=4,'store'=4] {'tensor','store'}, dimensions={0}, use_global_device_ids=true | all-gather | bytes 278528 | tf_op jit(solution)/shard_map/all_gather | solution.py:273
  144.4 1.9 fusion.2
  146.3 1.7 reshape.398
  148.1 0.8 fusion.57
  148.9 0.6 mul.239
  149.5 1.4 bitcast_multiply_fusion
  150.9 1.5 pad_maximum_fusion
  152.5 0.0 all-reduce.6.cloned.1.call-start
  152.5 2.1 fusion.7
  154.6 0.1 reshape.402
  154.7 0.7 copy.63
  155.3 39.0 %reduce-scatter.3.cloned.1.call-done = f32[16,8256]{1,0:T(8,128)} async-done(((f32[64,8256]{1,0:T(8,128)}), f32[16,8256]{1,0:T(8,128)}) %reduce-scatter.3.cloned.1.call-update) | async-done | bytes 528400 | tf_op jit(solution)/shard_map/reduce_scatter | solution.py:278
  194.3 0.0 reduce-scatter.5.cloned.1.call-start
  194.4 0.1 fusion.34
  194.5 35.3 %all-reduce.6.cloned.1.call-done = (f32[16,8256]{1,0:T(8,128)}, f32[64,2,2,128]{3,0,1,2:T(8,128)}) async-done(((f32[16,8256]{1,0:T(8,128)}, f32[64,2,2,128]{3,0,1,2:T(8,128)}), (f32[16,8256]{1,0:T(8,128)}, f32[64,2,2,128]{3,0,1,2:T(8,128)})) %all-reduce.6.cloned.1.call-update) | async-done | bytes 659472 | tf_op jit(solution)/shard_map/psum | solution.py:279
  229.8 0.9 slice_bitcast_fusion.1
  230.7 0.1 subtract_convert_fusion.1
  230.8 0.5 fusion.58
  231.3 1.1 fusion.17
  232.4 0.1 fusion.15
  232.6 0.1 copy.68
  232.7 0.1 copy.66
  232.7 0.1 copy.64
  232.8 0.5 fusion.14
  233.3 5.7 %fusion.19 = f32[64,2048]{1,0:T(8,128)} fusion(bf16[2048,2048]{1,0:T(8,128)(2,1)} %param.12, bf16[8,8,16,128]{3,2,1,0:T(8,128)(2,1)S(1)} %bitcast.139), kind=kOutput, calls=%fused_computation.33 | convolution fusion | flops 536870912 | bytes 9175040 | tf_op jit(solution)/shard_map/dot_general | solution.py:304
  239.1 22.0 %reduce-scatter.5.cloned.1.call-done = f32[16,2048]{1,0:T(8,128)} async-done(((f32[64,2048]{1,0:T(8,128)}), f32[16,2048]{1,0:T(8,128)}) %reduce-scatter.5.cloned.1.call-update) | async-done | bytes 131088 | tf_op jit(solution)/shard_map/reduce_scatter | solution.py:303
  261.1 1.5 convert_element_type.52
  (34 shorter events, 0.4 us)
Async XLA Ops:
  6.5 1.0 copy-start
  6.5 7.5 %copy-start.4 = (s32[256,1]{0,1:T(1,128)S(1)}, s32[256,1]{0,1:T(1,128)}, u32[]{:S(2)}) copy-start(s32[256,1]{0,1:T(1,128)} %param.14) | copy-start | bytes 3076
  6.5 42.8 %all-reduce.4.cloned.1.call-start = ((), (), s32[]{:S(2)}) async-start(), calls=%async_computation.2 | async-start | bytes 1048576 | tf_op jit(solution)/shard_map/psum | solution.py:226
  13.3 66.5 %all-gather.2.cloned.1.call-start = ((), (), s32[]{:S(2)}) async-start(), calls=%async_computation.3 | async-start | bytes 1310720 | tf_op jit(solution)/shard_map/all_gather | solution.py:251
  51.7 142.6 %reduce-scatter.3.cloned.1.call-start = ((), (), s32[]{:S(2)}) async-start(), calls=%async_computation.4 | async-start | bytes 2662400 | tf_op jit(solution)/shard_map/reduce_scatter | solution.py:278
  117.8 26.6 %copy-start.1 = (f32[6,512,128]{2,1,0:T(8,128)S(1)}, f32[6,512,128]{2,1,0:T(8,128)}, u32[]{:S(2)}) copy-start(f32[6,512,128]{2,1,0:T(8,128)} %get-tuple-element.12) | copy-start | bytes 4718596
  117.8 26.6 %copy-start.3 = (f32[2,512,128]{2,1,0:T(8,128)S(1)}, f32[2,512,128]{2,1,0:T(8,128)}, u32[]{:S(2)}) copy-start(f32[2,512,128]{2,1,0:T(8,128)} %get-tuple-element.11) | copy-start | bytes 1572868
  152.5 77.4 %all-reduce.6.cloned.1.call-start = ((), (), s32[]{:S(2)}) async-start(), calls=%async_computation.6 | async-start | bytes 1327104 | tf_op jit(solution)/shard_map/psum | solution.py:279
  194.3 66.8 %reduce-scatter.5.cloned.1.call-start = ((), (), s32[]{:S(2)}) async-start(), calls=%async_computation.5 | async-start | bytes 655360 | tf_op jit(solution)/shard_map/reduce_scatter | solution.py:303
  229.8 2.7 %copy-start.2 = (f32[16,8256]{1,0:T(8,128)S(1)}, f32[16,8256]{1,0:T(8,128)}, u32[]{:S(2)}) copy-start(f32[16,8256]{1,0:T(8,128)} %get-tuple-element.19) | copy-start | bytes 1585156
Sparse Core Ops, SparseCore 0:
  13.4 35.8 all-reduce.3
  51.8 27.9 all-gather.1
  152.6 41.7 reduce-scatter.2
  196.6 33.1 all-reduce.5
  239.2 21.8 reduce-scatter.4

commit v5 on v4

--- a/solution.py
+++ b/solution.py
@@ -237,7 +237,7 @@
     key_sess, key_ok, key_off = slot_meta(
         page_store, lengths, offsets, shards, capacity, first_slot, local_slots, page_len
     )
-    pb = max(d for d in range(1, min(local_slots, 20) + 1) if local_slots % d == 0)
+    pb = local_slots
     bias = jnp.where(key_ok, 0.0, MASK_FILL).astype(jnp.float32)
     bias = bias.reshape(local_slots // pb, 1, pb * page_len)
     hist_angle = offsets[0].astype(jnp.float32) * freq_table

time: 270 us -> 269 us (level)
  no operation moved by 1% of the time
where the time goes in v5:
time: 269 us; the launch traced here: 268 us
  waiting for transfers between devices  138 us (51%)
  Pallas kernels  47.6 us (18%)
  blocking collectives  21.5 us (8%)
  other arithmetic  17.4 us (6%)
  between operations  14.7 us (5%)
  matrix products  14.3 us (5%)
  local copies, waits for them, and re-layouts  13.8 us (5%)
    pallas_call x2, Pallas kernels, hist_attend(): pl.pallas_call(kernel, grid_spec=grid_spec, out_shape=[jax.ShapeDtypeStru...  47.6 us
    reduce_scatter x1, waiting for transfers between devices, body(): packed = lax.psum_scatter(packed, 'tensor', scatter_dimension=0, tiled=True)  39 us
    psum x1, waiting for transfers between devices, body(): packed = lax.psum(packed, 'store')  35.3 us
    psum x1, waiting for transfers between devices, body(): query_sum, keyval_sum = lax.psum((query_part, keyval_part), 'store')  32.1 us
    reduce_scatter x1, waiting for transfers between devices, body(): lax.psum_scatter(jnp.dot(attended, w_out, preferred_element_type=jnp.floa...  22 us
    all_gather x1, blocking collectives, body(): glob_top = jnp.max(lax.all_gather(top, ('tensor', 'store')), axis=0)  21.5 us
    all_gather x1, waiting for transfers between devices, body(): q_all = lax.all_gather(q_heads, 'tensor', axis=0, tiled=True)  9.67 us
    pallas_call x4, local copies, waits for them, and re-layouts, hist_attend(): pl.pallas_call(kernel, grid_spec=grid_spec, out_shape=[jax.ShapeDtypeStru...  6.64 us
  transfers between devices with their start and end apart: 5, of which 5 were waited for; matrix products, arithmetic and copies ran while one was open for 4% of the time, Pallas kernels for 5%

profile of v5, /device:TPU:0, one launch (start us, length us, event | category | flops | bytes accessed | tf_op | source)
XLA Modules:
  0.0 267.9 jit_solution(7807339782879762183)
XLA Ops:
  6.5 0.9 copy-done
  7.5 4.9 %convolution_bitcast_fusion = f32[8,16,8,128]{3,2,1,0:T(8,128)S(1)} fusion(bf16[64,2048]{1,0:T(8,128)(2,1)S(1)} %copy-done, bf16[2048,2048]{1,0:T(8,128)(2,1)} %param.10), kind=kOutput, calls=%fused_computation.16 | convolution fusion | flops 536870912 | bytes 9175040 | tf_op jit(solution)/shard_map/dot_general | solution.py:224
  12.4 0.9 copy.79
  13.3 0.0 all-reduce.4.cloned.1.call-update
  13.3 0.0 all-gather.2.cloned.1.call-start
  14.1 0.1 multiply_sine_fusion.1
  14.1 0.1 fusion.56
  14.9 0.6 maximum_bitcast_fusion.2.cos_ref
  15.5 1.2 reduce-window.6
  16.7 0.1 slice.43
  16.8 0.1 copy.43
  16.9 0.1 copy.44
  17.0 0.2 multiply_cosine_fusion
  17.2 32.1 %all-reduce.4.cloned.1.call-done = f32[64,16,128]{2,0,1:T(8,128)} async-done(((f32[64,16,128]{2,0,1:T(8,128)}), f32[64,16,128]{2,0,1:T(8,128)}) %all-reduce.4.cloned.1.call-update) | async-done | bytes 524304 | tf_op jit(solution)/shard_map/psum | solution.py:226
  49.4 1.4 subtract_convert_fusion
  50.8 0.9 fusion.65
  51.7 0.0 all-gather.2.cloned.1.call-update
  51.7 0.2 reduce-scatter.3.cloned.1.call-start
  51.9 0.7 maximum_bitcast_fusion.3.sin_ref
  52.6 0.1 add_bitcast_fusion
  52.7 0.2 fusion.28
  52.9 0.7 fusion.36
  53.6 0.9 pad_maximum_fusion.1
  54.5 13.2 %shard_map.85 = (f32[2,512,128]{2,1,0:T(8,128)}, f32[2,512,1]{2,1,0:T(8,128)}, f32[2,512,1]{2,1,0:T(8,128)}) custom-call(s32[1]{0:T(128)} %bitcast.kv0_ref, bf16[2,512,128]{2,1,0:T(8,128)(2,1)} %bitcast.141, bf16[40,128,2048]{2,1,0:T(8,128)(2,1)} %bitcast.131, bf16[40,128,2048]{2,1,0:T(8,128)(2,1)} %bitcast.132, f32[1,1,5120]{2,1,0:T(1,128)} %bitcast.143, ...), custom_call_target="tpu_custom_call" | custom-call | tf_op jit(solution)/shard_map/pallas_call | solution.py:194
  67.7 1.2 copy.49
  68.9 1.2 copy.45
  70.1 9.7 %all-gather.2.cloned.1.call-done = bf16[64,64,128]{2,1,0:T(8,128)(2,1)} async-done(((bf16[16,64,128]{2,1,0:T(8,128)(2,1)}), bf16[64,64,128]{2,1,0:T(8,128)(2,1)}) %all-gather.2.cloned.1.call-update) | async-done | bytes 1048592 | tf_op jit(solution)/shard_map/all_gather | solution.py:251
  79.8 2.3 fusion.10.q_ref
  82.1 34.4 %shard_map.86 = (f32[6,512,128]{2,1,0:T(8,128)}, f32[6,512,1]{2,1,0:T(8,128)}, f32[6,512,1]{2,1,0:T(8,128)}) custom-call(s32[1]{0:T(128)} %bitcast.15.kv0_ref, bf16[6,512,128]{2,1,0:T(8,128)(2,1)} %fusion.10.q_ref, bf16[40,128,2048]{2,1,0:T(8,128)(2,1)} %bitcast.133, bf16[40,128,2048]{2,1,0:T(8,128)(2,1)} %bitcast.134, f32[1,1,5120]{2,1,0:T(1,128)} %bitcast.144, ...), custom_call_target="tpu_custom_call" | custom-call | tf_op jit(solution)/shard_map/pallas_call | solution.py:194
  116.5 2.2 copy.46
  118.7 0.1 reshape.360
  118.8 0.1 all_gather_reshape.3
  118.9 2.0 copy.50
  120.9 0.7 reshape.361
  121.6 21.5 %all_gather.7 = f32[16,64,64]{2,1,0:T(8,128)S(1)} all-gather(f32[1,64,64]{2,1,0:T(8,128)S(1)} %all_gather_reshape.3), channel_id=1, replica_groups=mesh['groups'=2,'tensor'=4,'store'=4] {'tensor','store'}, dimensions={0}, use_global_device_ids=true | all-gather | bytes 278528 | tf_op jit(solution)/shard_map/all_gather | solution.py:273
  143.1 1.9 fusion.2
  145.0 1.7 reshape.359
  146.8 0.8 fusion.59
  147.6 0.6 mul.239
  148.2 1.4 bitcast_multiply_fusion
  149.6 1.5 pad_maximum_fusion
  151.1 0.0 reduce-scatter.3.cloned.1.call-update
  151.1 0.0 all-reduce.6.cloned.1.call-start
  151.2 2.1 fusion.7
  153.3 0.1 reshape.363
  153.4 0.7 copy.54
  154.0 39.0 %reduce-scatter.3.cloned.1.call-done = f32[16,8256]{1,0:T(8,128)} async-done(((f32[64,8256]{1,0:T(8,128)}), f32[16,8256]{1,0:T(8,128)}) %reduce-scatter.3.cloned.1.call-update) | async-done | bytes 528400 | tf_op jit(solution)/shard_map/reduce_scatter | solution.py:278
  193.0 0.0 all-reduce.6.cloned.1.call-update
  193.0 0.0 reduce-scatter.5.cloned.1.call-start
  193.1 0.1 fusion.34
  193.1 35.3 %all-reduce.6.cloned.1.call-done = (f32[16,8256]{1,0:T(8,128)}, f32[64,2,2,128]{3,0,1,2:T(8,128)}) async-done(((f32[16,8256]{1,0:T(8,128)}, f32[64,2,2,128]{3,0,1,2:T(8,128)}), (f32[16,8256]{1,0:T(8,128)}, f32[64,2,2,128]{3,0,1,2:T(8,128)})) %all-reduce.6.cloned.1.call-update) | async-done | bytes 659472 | tf_op jit(solution)/shard_map/psum | solution.py:279
  228.5 0.9 slice_bitcast_fusion.1
  229.4 0.1 subtract_convert_fusion.1
  229.5 0.5 fusion.60
  230.0 1.1 fusion.17
  231.1 0.1 fusion.15
  231.3 0.1 copy.59
  231.3 0.1 copy.57
  231.4 0.1 copy.55
  231.5 0.5 fusion.14
  232.0 5.7 %fusion.19 = f32[64,2048]{1,0:T(8,128)} fusion(bf16[2048,2048]{1,0:T(8,128)(2,1)} %param.12, bf16[8,8,16,128]{3,2,1,0:T(8,128)(2,1)S(1)} %bitcast.138), kind=kOutput, calls=%fused_computation.33 | convolution fusion | flops 536870912 | bytes 9175040 | tf_op jit(solution)/shard_map/dot_general | solution.py:304
  237.8 0.0 reduce-scatter.5.cloned.1.call-update
  237.8 22.0 %reduce-scatter.5.cloned.1.call-done = f32[16,2048]{1,0:T(8,128)} async-done(((f32[64,2048]{1,0:T(8,128)}), f32[16,2048]{1,0:T(8,128)}) %reduce-scatter.5.cloned.1.call-update) | async-done | bytes 131088 | tf_op jit(solution)/shard_map/reduce_scatter | solution.py:303
  259.8 1.5 convert_element_type.52
  (25 shorter events, 0.3 us)
Async XLA Ops:
  6.5 1.0 copy-start
  6.5 8.3 %copy-start.4 = (s32[256,1]{0,1:T(1,128)S(1)}, s32[256,1]{0,1:T(1,128)}, u32[]{:S(2)}) copy-start(s32[256,1]{0,1:T(1,128)} %param.14) | copy-start | bytes 3076
  6.5 42.8 %all-reduce.4.cloned.1.call-start = ((), (), s32[]{:S(2)}) async-start(), calls=%async_computation.2 | async-start | bytes 1048576 | tf_op jit(solution)/shard_map/psum | solution.py:226
  13.3 66.5 %all-gather.2.cloned.1.call-start = ((), (), s32[]{:S(2)}) async-start(), calls=%async_computation.3 | async-start | bytes 1310720 | tf_op jit(solution)/shard_map/all_gather | solution.py:251
  51.7 141.3 %reduce-scatter.3.cloned.1.call-start = ((), (), s32[]{:S(2)}) async-start(), calls=%async_computation.4 | async-start | bytes 2662400 | tf_op jit(solution)/shard_map/reduce_scatter | solution.py:278
  116.5 26.6 %copy-start.1 = (f32[6,512,128]{2,1,0:T(8,128)S(1)}, f32[6,512,128]{2,1,0:T(8,128)}, u32[]{:S(2)}) copy-start(f32[6,512,128]{2,1,0:T(8,128)} %get-tuple-element.12) | copy-start | bytes 4718596
  116.5 26.6 %copy-start.3 = (f32[2,512,128]{2,1,0:T(8,128)S(1)}, f32[2,512,128]{2,1,0:T(8,128)}, u32[]{:S(2)}) copy-start(f32[2,512,128]{2,1,0:T(8,128)} %get-tuple-element.11) | copy-start | bytes 1572868
  151.1 77.3 %all-reduce.6.cloned.1.call-start = ((), (), s32[]{:S(2)}) async-start(), calls=%async_computation.6 | async-start | bytes 1327104 | tf_op jit(solution)/shard_map/psum | solution.py:279
  193.0 66.8 %reduce-scatter.5.cloned.1.call-start = ((), (), s32[]{:S(2)}) async-start(), calls=%async_computation.5 | async-start | bytes 655360 | tf_op jit(solution)/shard_map/reduce_scatter | solution.py:303
  228.5 2.7 %copy-start.2 = (f32[16,8256]{1,0:T(8,128)S(1)}, f32[16,8256]{1,0:T(8,128)}, u32[]{:S(2)}) copy-start(f32[16,8256]{1,0:T(8,128)} %get-tuple-element.19) | copy-start | bytes 1585156
Sparse Core Ops, SparseCore 0:
  13.4 35.8 all-reduce.3
  51.8 27.9 all-gather.1
  151.3 41.6 reduce-scatter.2
  195.3 33.1 all-reduce.5
  237.9 21.8 reduce-scatter.4

commit v6 on v5

--- a/solution.py
+++ b/solution.py
@@ -275,31 +275,53 @@
     packed = jnp.concatenate(
         [(acc * factor[..., None]).reshape(HQ, tok_count * HD), total * factor], axis=1
     )
-    packed = lax.psum_scatter(packed, "tensor", scatter_dimension=0, tiled=True)
-    packed = lax.psum(packed, "store")
-    acc = packed[:, : tok_count * HD].reshape(local_heads, tok_count, HD)
-    total = packed[:, tok_count * HD :]
-    loc_top = lax.dynamic_slice_in_dim(glob_top, tensor_idx * local_heads, local_heads, 0)
-    hist_part = (
-        jnp.transpose(loc_top),
-        jnp.transpose(total),
-        jnp.transpose(acc, (1, 0, 2)),
-    )
-
-    query_local = query_rot.reshape(tok_count, local_kv, local_group, HD)
     new_allowed = (tok_sess[:, None] == tok_sess[None, :]) & (tok_ids[None, :] <= tok_ids[:, None])
-    new_part = attend(query_local, key_new, value_new, new_allowed)
-    new_flat = (
-        new_part[0].reshape(tok_count, local_heads),
-        new_part[1].reshape(tok_count, local_heads),
-        new_part[2].reshape(tok_count, local_heads, HD),
-    )
-    combined = combine(hist_part, new_flat)
-    attended = (
-        (combined[2] / combined[1][..., None])
-        .reshape(tok_count, local_heads * HD)
-        .astype(jnp.bfloat16)
-    )
+    chunk_heads = HQ // (tensors * shards)
+    if HQ % (tensors * shards) == 0 and group_size % chunk_heads == 0:
+        packed = lax.psum_scatter(packed, ("tensor", "store"), scatter_dimension=0, tiled=True)
+        acc = packed[:, : tok_count * HD].reshape(chunk_heads, tok_count, HD)
+        total = packed[:, tok_count * HD :]
+        chunk_first = (tensor_idx * shards + store_idx) * chunk_heads
+        loc_top = lax.dynamic_slice_in_dim(glob_top, chunk_first, chunk_heads, 0)
+        hist_part = (jnp.transpose(loc_top), jnp.transpose(total), jnp.transpose(acc, (1, 0, 2)))
+        in_group = store_idx * chunk_heads
+        query_chunk = lax.dynamic_slice_in_dim(query_rot, in_group, chunk_heads, 1)
+        kv_idx = in_group // group_size
+        key_chunk = lax.dynamic_slice_in_dim(key_new, kv_idx, 1, 1)
+        value_chunk = lax.dynamic_slice_in_dim(value_new, kv_idx, 1, 1)
+        new_part = attend(query_chunk.reshape(tok_count, 1, chunk_heads, HD), key_chunk, value_chunk, new_allowed)
+        new_flat = (
+            new_part[0].reshape(tok_count, chunk_heads),
+            new_part[1].reshape(tok_count, chunk_heads),
+            new_part[2].reshape(tok_count, chunk_heads, HD),
+        )
+        combined = combine(hist_part, new_flat)
+        attended = (
+            (combined[2] / combined[1][..., None])
+            .reshape(tok_count, chunk_heads * HD)
+            .astype(jnp.bfloat16)
+        )
+        attended = lax.all_gather(attended, "store", axis=1, tiled=True)
+    else:
+        packed = lax.psum_scatter(packed, "tensor", scatter_dimension=0, tiled=True)
+        packed = lax.psum(packed, "store")
+        acc = packed[:, : tok_count * HD].reshape(local_heads, tok_count, HD)
+        total = packed[:, tok_count * HD :]
+        loc_top = lax.dynamic_slice_in_dim(glob_top, tensor_idx * local_heads, local_heads, 0)
+        hist_part = (jnp.transpose(loc_top), jnp.transpose(total), jnp.transpose(acc, (1, 0, 2)))
+        query_local = query_rot.reshape(tok_count, local_kv, local_group, HD)
+        new_part = attend(query_local, key_new, value_new, new_allowed)
+        new_flat = (
+            new_part[0].reshape(tok_count, local_heads),
+            new_part[1].reshape(tok_count, local_heads),
+            new_part[2].reshape(tok_count, local_heads, HD),
+        )
+        combined = combine(hist_part, new_flat)
+        attended = (
+            (combined[2] / combined[1][..., None])
+            .reshape(tok_count, local_heads * HD)
+            .astype(jnp.bfloat16)
+        )
     result = lax.psum_scatter(
         jnp.dot(attended, w_out, preferred_element_type=jnp.float32),
         "tensor",

time: 269 us -> 292 us (1.086)
  waiting for transfers between devices: 138 us -> 157 us
  blocking collectives: 21.5 us -> 27.3 us
    unnamed x5, waiting for transfers between devices: 0.08 us -> 93.1 us
    reduce_scatter x1 -> x0, waiting for transfers between devices: 39 us -> none  [body(): packed = lax.psum_scatter(packed, 'tensor', scatter_dimension=0, tiled=True)]
    psum x1 -> x0, waiting for transfers between devices: 35.3 us -> none  [body(): packed = lax.psum(packed, 'store')]
    all_gather x0 -> x1, blocking collectives: none -> 5.79 us  [body(): attended = lax.all_gather(attended, 'store', axis=1, tiled=True)]
  transfers between devices with their start and end apart: 5 -> 4, of which waited for: 5 -> 4; matrix products, arithmetic and copies ran while one was open for 4% -> 3% of each run, Pallas kernels for 5% -> 5%
where the time goes in v6:
time: 292 us; the launch traced here: 291 us
  waiting for transfers between devices  157 us (54%)
  Pallas kernels  47.6 us (16%)
  blocking collectives  27.3 us (9%)
  other arithmetic  16.6 us (6%)
  between operations  15.3 us (5%)
  local copies, waits for them, and re-layouts  14.2 us (5%)
  matrix products  13.3 us (5%)
    unnamed x5, waiting for transfers between devices  93.1 us
    pallas_call x2, Pallas kernels, hist_attend(): pl.pallas_call(kernel, grid_spec=grid_spec, out_shape=[jax.ShapeDtypeStru...  47.6 us
    psum x1, waiting for transfers between devices, body(): query_sum, keyval_sum = lax.psum((query_part, keyval_part), 'store')  32.9 us
    all_gather x1, blocking collectives, body(): glob_top = jnp.max(lax.all_gather(top, ('tensor', 'store')), axis=0)  21.5 us
    reduce_scatter x1, waiting for transfers between devices, body(): lax.psum_scatter(jnp.dot(attended, w_out, preferred_element_type=jnp.floa...  20.9 us
    all_gather x1, waiting for transfers between devices, body(): q_all = lax.all_gather(q_heads, 'tensor', axis=0, tiled=True)  9.79 us
    pallas_call x4, local copies, waits for them, and re-layouts, hist_attend(): pl.pallas_call(kernel, grid_spec=grid_spec, out_shape=[jax.ShapeDtypeStru...  6.64 us
  transfers between devices with their start and end apart: 4, of which 4 were waited for; matrix products, arithmetic and copies ran while one was open for 3% of the time, Pallas kernels for 5%

profile of v6, /device:TPU:0, one launch (start us, length us, event | category | flops | bytes accessed | tf_op | source)
XLA Modules:
  0.0 291.3 jit_solution(14260439450597984209)
XLA Ops:
  6.5 0.0 copy-start
  6.5 0.0 all-reduce.7.cloned.1.call-start
  6.5 0.9 copy-done
  7.5 4.9 %convolution_bitcast_fusion = f32[8,16,8,128]{3,2,1,0:T(8,128)S(1)} fusion(bf16[64,2048]{1,0:T(8,128)(2,1)S(1)} %copy-done, bf16[2048,2048]{1,0:T(8,128)(2,1)} %param.10), kind=kOutput, calls=%fused_computation.13 | convolution fusion | flops 536870912 | bytes 9175040 | tf_op jit(solution)/shard_map/dot_general | solution.py:224
  12.4 0.8 copy.58
  13.3 2.1 fusion.5
  15.4 0.1 reshape.381
  15.5 0.7 copy.44
  16.1 0.0 all-reduce.7.cloned.1.call-update
  16.1 0.0 all-gather.2.cloned.1.call-start
  16.9 0.1 multiply_sine_fusion.1
  16.9 0.1 fusion.58
  17.7 0.0 copy-done.5
  17.7 1.2 reduce-window.6
  18.9 0.1 slice.43
  19.0 0.1 copy.34
  19.2 0.1 copy.35
  19.3 0.6 maximum_bitcast_fusion.cos_ref
  19.8 0.2 multiply_cosine_fusion
  20.0 32.9 %all-reduce.7.cloned.1.call-done = (f32[64,16,128]{2,0,1:T(8,128)}, f32[64,2,2,128]{3,0,1,2:T(8,128)}) async-done(((f32[64,16,128]{2,0,1:T(8,128)}, f32[64,2,2,128]{3,0,1,2:T(8,128)}), (f32[64,16,128]{2,0,1:T(8,128)}, f32[64,2,2,128]{3,0,1,2:T(8,128)})) %all-reduce.7.cloned.1.call-update) | async-done | bytes 655376 | tf_op jit(solution)/shard_map/psum | solution.py:226
  52.9 1.4 subtract_convert_fusion
  54.3 0.9 fusion.69
  55.2 0.0 all-gather.2.cloned.1.call-update
  55.2 0.2 all-reduce.5.cloned.1.call-start
  55.5 0.6 maximum_bitcast_fusion.1.sin_ref
  56.0 0.1 add_bitcast_fusion
  56.1 0.2 fusion.26
  56.3 0.7 fusion.30
  57.0 0.9 pad_maximum_fusion.1
  57.9 13.2 %shard_map.85 = (f32[2,512,128]{2,1,0:T(8,128)}, f32[2,512,1]{2,1,0:T(8,128)}, f32[2,512,1]{2,1,0:T(8,128)}) custom-call(s32[1]{0:T(128)} %bitcast.kv0_ref, bf16[2,512,128]{2,1,0:T(8,128)(2,1)} %bitcast.139, bf16[40,128,2048]{2,1,0:T(8,128)(2,1)} %bitcast.133, bf16[40,128,2048]{2,1,0:T(8,128)(2,1)} %bitcast.134, f32[1,1,5120]{2,1,0:T(1,128)} %bitcast.142, ...), custom_call_target="tpu_custom_call" | custom-call | tf_op jit(solution)/shard_map/pallas_call | solution.py:194
  71.1 1.2 copy.40
  72.3 1.2 copy.36
  73.6 9.8 %all-gather.2.cloned.1.call-done = bf16[64,64,128]{2,1,0:T(8,128)(2,1)} async-done(((bf16[16,64,128]{2,1,0:T(8,128)(2,1)}), bf16[64,64,128]{2,1,0:T(8,128)(2,1)}) %all-gather.2.cloned.1.call-update) | async-done | bytes 1048592 | tf_op jit(solution)/shard_map/all_gather | solution.py:251
  83.3 2.3 fusion.15.q_ref
  85.7 34.4 %shard_map.86 = (f32[6,512,128]{2,1,0:T(8,128)}, f32[6,512,1]{2,1,0:T(8,128)}, f32[6,512,1]{2,1,0:T(8,128)}) custom-call(s32[1]{0:T(128)} %bitcast.15.kv0_ref, bf16[6,512,128]{2,1,0:T(8,128)(2,1)} %fusion.15.q_ref, bf16[40,128,2048]{2,1,0:T(8,128)(2,1)} %bitcast.135, bf16[40,128,2048]{2,1,0:T(8,128)(2,1)} %bitcast.136, f32[1,1,5120]{2,1,0:T(1,128)} %bitcast.143, ...), custom_call_target="tpu_custom_call" | custom-call | tf_op jit(solution)/shard_map/pallas_call | solution.py:194
  120.0 0.0 copy-start.3
  120.0 2.2 copy.37
  122.2 0.1 reshape.378
  122.3 0.1 all_gather_reshape.3
  122.4 2.0 copy.41
  124.4 0.1 reshape.379
  124.5 21.5 %all_gather.10 = f32[16,64,64]{2,1,0:T(8,128)S(1)} all-gather(f32[1,64,64]{2,1,0:T(8,128)S(1)} %all_gather_reshape.3), channel_id=1, replica_groups=mesh['groups'=2,'tensor'=4,'store'=4] {'tensor','store'}, dimensions={0}, use_global_device_ids=true | all-gather | bytes 278528 | tf_op jit(solution)/shard_map/all_gather | solution.py:273
  146.0 0.0 copy-done.2
  146.0 1.9 fusion.2
  147.9 1.7 reshape.377
  149.8 0.6 mul.250
  150.4 1.4 bitcast_multiply_fusion
  151.8 1.5 pad_maximum_fusion
  153.2 0.0 all-reduce.5.cloned.1.call-update
  153.3 0.0 reduce-scatter.2.cloned.1.call-start
  153.4 0.5 copy-done.6
  153.9 0.6 dynamic-slice.1
  155.1 0.1 fusion.28
  155.2 0.1 add_convert_fusion.1
  155.3 0.3 fusion.62
  155.7 93.0 %all-reduce.5.cloned.1.call-done = f32[64,8256]{1,0:T(8,128)} async-done(((f32[64,8256]{1,0:T(8,128)}), f32[64,8256]{1,0:T(8,128)}) %all-reduce.5.cloned.1.call-update) | async-done | bytes 2113552
  248.7 1.0 dynamic-slice_bitcast_fusion
  249.7 0.8 fusion.52
  250.4 0.2 fusion.14
  250.7 5.8 %all_gather.11 = bf16[64,2048]{1,0:T(8,128)(2,1)S(1)} all-gather(bf16[64,512]{1,0:T(8,128)(2,1)S(1)} %bitcast.141), channel_id=1, replica_groups=mesh['groups'=2,'tensor'=4,'store'=4] {'store'}, dimensions={1}, use_global_device_ids=true | all-gather | bytes 327680 | tf_op jit(solution)/shard_map/all_gather | solution.py:304
  256.5 5.8 %fusion.63 = f32[64,2048]{1,0:T(8,128)} fusion(bf16[64,2048]{1,0:T(8,128)(2,1)S(1)} %all_gather.11, bf16[2048,2048]{1,0:T(8,128)(2,1)} %param.12), kind=kOutput, calls=%fused_computation.126 | convolution fusion | flops 536870912 | bytes 9175040 | tf_op jit(solution)/shard_map/dot_general | solution.py:326
  262.3 0.0 reduce-scatter.2.cloned.1.call-update
  262.3 20.9 %reduce-scatter.2.cloned.1.call-done = f32[16,2048]{1,0:T(8,128)} async-done(((f32[64,2048]{1,0:T(8,128)}), f32[16,2048]{1,0:T(8,128)}) %reduce-scatter.2.cloned.1.call-update) | async-done | bytes 131088 | tf_op jit(solution)/shard_map/reduce_scatter | solution.py:325
  283.2 1.5 convert_element_type.48
  (27 shorter events, 0.4 us)
Async XLA Ops:
  6.5 1.0 copy-start
  6.5 46.4 %all-reduce.7.cloned.1.call-start = ((), (), s32[]{:S(2)}) async-start(), calls=%async_computation.4 | async-start | bytes 1310720 | tf_op jit(solution)/shard_map/psum | solution.py:226
  13.3 4.4 %copy-start.5 = (s32[256,1]{0,1:T(1,128)S(1)}, s32[256,1]{0,1:T(1,128)}, u32[]{:S(2)}) copy-start(s32[256,1]{0,1:T(1,128)} %param.14) | copy-start | bytes 3076
  16.1 67.2 %all-gather.2.cloned.1.call-start = ((), (), s32[]{:S(2)}) async-start(), calls=%async_computation.1 | async-start | bytes 1310720 | tf_op jit(solution)/shard_map/all_gather | solution.py:251
  55.2 193.4 %all-reduce.5.cloned.1.call-start = ((), (), s32[]{:S(2)}) async-start(), calls=%async_computation.3 | async-start | bytes 4259840
  120.0 26.0 %copy-start.2 = (f32[6,512,128]{2,1,0:T(8,128)S(1)}, f32[6,512,128]{2,1,0:T(8,128)}, u32[]{:S(2)}) copy-start(f32[6,512,128]{2,1,0:T(8,128)} %get-tuple-element.12) | copy-start | bytes 4718596
  120.0 26.0 %copy-start.3 = (f32[2,512,128]{2,1,0:T(8,128)S(1)}, f32[2,512,128]{2,1,0:T(8,128)}, u32[]{:S(2)}) copy-start(f32[2,512,128]{2,1,0:T(8,128)} %get-tuple-element.11) | copy-start | bytes 1572868
  153.2 0.7 copy-start.6
  153.2 2.0 copy-start.4
  153.3 129.9 %reduce-scatter.2.cloned.1.call-start = ((), (), s32[]{:S(2)}) async-start(), calls=%async_computation.2 | async-start | bytes 655360 | tf_op jit(solution)/shard_map/reduce_scatter | solution.py:325
  256.5 28.3 %copy-start.1 = (bf16[64,2048]{1,0:T(8,128)(2,1)S(1)}, bf16[64,2048]{1,0:T(8,128)(2,1)}, u32[]{:S(2)}) copy-start(bf16[64,2048]{1,0:T(8,128)(2,1)} %param.8) | copy-start | bytes 786436
Sparse Core Ops, SparseCore 0:
  16.3 36.5 all-reduce.6
  55.4 27.9 all-gather.1
  153.4 95.2 all-reduce.4
  262.4 20.7 reduce-scatter.1

commit v7 on v5

--- a/solution.py
+++ b/solution.py
@@ -201,6 +201,17 @@
         ],
         compiler_params=pltpu.CompilerParams(dimension_semantics=("arbitrary", "arbitrary")),
     )(jnp.reshape(kv0, (1,)).astype(jnp.int32), q_k, kv_local, kv_local, bias, cos2, sin2)
+
+
+def axis_sum(x, axis):
+    n = lax.axis_size(axis)
+    if n & (n - 1):
+        return lax.psum(x, axis)
+    d = 1
+    while d < n:
+        x = x + lax.ppermute(x, axis, perm=[(i, i ^ d) for i in range(n)])
+        d *= 2
+    return x
 
 
 def body(x_new, kv_pages, w_query, w_keyval, w_out, lengths, page_store, offsets):
@@ -223,7 +234,9 @@
     keyval_cols = lax.dynamic_slice_in_dim(w_keyval, kv_first * (2 * HD), local_kv * 2 * HD, 1)
     query_part = jnp.dot(x_new, w_query, preferred_element_type=jnp.float32)
     keyval_part = jnp.dot(x_new, keyval_cols, preferred_element_type=jnp.float32)
-    query_sum, keyval_sum = lax.psum((query_part, keyval_part), "store")
+    width_q = query_part.shape[1]
+    both = axis_sum(jnp.concatenate([query_part, keyval_part], axis=1), "store")
+    query_sum, keyval_sum = both[:, :width_q], both[:, width_q:]
     keyval_local = keyval_sum.reshape(tok_count, local_kv, 2, HD)
     tok_ids = jnp.arange(tok_count, dtype=jnp.int32)
     tok_sess = tok_ids // TURN
@@ -276,7 +289,7 @@
         [(acc * factor[..., None]).reshape(HQ, tok_count * HD), total * factor], axis=1
     )
     packed = lax.psum_scatter(packed, "tensor", scatter_dimension=0, tiled=True)
-    packed = lax.psum(packed, "store")
+    packed = axis_sum(packed, "store")
     acc = packed[:, : tok_count * HD].reshape(local_heads, tok_count, HD)
     total = packed[:, tok_count * HD :]
     loc_top = lax.dynamic_slice_in_dim(glob_top, tensor_idx * local_heads, local_heads, 0)

time: 269 us -> 235 us (0.87)
  waiting for transfers between devices: 138 us -> 102 us
  starting transfers between devices: 0.35 us -> 4.9 us
    psum x2 -> x0, waiting for transfers between devices: 67.5 us -> none  [the longest x1 35.3 us: body(): packed = lax.psum(packed, 'store')]
    ppermute x0 -> x4, waiting for transfers between devices: none -> 27.8 us  [axis_sum(): x = x + lax.ppermute(x, axis, perm=[(i, i ^ d) for i in range(n)])]
    ppermute x0 -> x4, starting transfers between devices: none -> 4.63 us  [axis_sum(): x = x + lax.ppermute(x, axis, perm=[(i, i ^ d) for i in range(n)])]
    reduce_scatter x1, waiting for transfers between devices: 39 us -> 41.8 us  [body(): packed = lax.psum_scatter(packed, 'tensor', scatter_dimension=0, tiled=True)]
  transfers between devices with their start and end apart: 5 -> 7, of which waited for: 5 -> 6; matrix products, arithmetic and copies ran while one was open for 4% -> 4% of each run, Pallas kernels for 5% -> 6%
where the time goes in v7:
time: 235 us
  waiting for transfers between devices  102 us (43%)
  Pallas kernels  47.6 us (20%)
  blocking collectives  22.9 us (10%)
  other arithmetic  18 us (8%)
  between operations  14.7 us (6%)
  matrix products  13.5 us (6%)
  local copies, waits for them, and re-layouts  11.3 us (5%)
  starting transfers between devices  4.9 us (2%)
    pallas_call x2, Pallas kernels, hist_attend(): pl.pallas_call(kernel, grid_spec=grid_spec, out_shape=[jax.ShapeDtypeStru...  47.6 us
    reduce_scatter x1, waiting for transfers between devices, body(): packed = lax.psum_scatter(packed, 'tensor', scatter_dimension=0, tiled=True)  41.8 us
    ppermute x4, waiting for transfers between devices, axis_sum(): x = x + lax.ppermute(x, axis, perm=[(i, i ^ d) for i in range(n)])  27.8 us
    all_gather x1, blocking collectives, body(): glob_top = jnp.max(lax.all_gather(top, ('tensor', 'store')), axis=0)  22.9 us
    reduce_scatter x1, waiting for transfers between devices, body(): lax.psum_scatter(jnp.dot(attended, w_out, preferred_element_type=jnp.floa...  21.1 us
    all_gather x1, waiting for transfers between devices, body(): q_all = lax.all_gather(q_heads, 'tensor', axis=0, tiled=True)  11.2 us
    pallas_call x4, local copies, waits for them, and re-layouts, hist_attend(): pl.pallas_call(kernel, grid_spec=grid_spec, out_shape=[jax.ShapeDtypeStru...  6.64 us
    dot_general x1, matrix products, body(): jnp.dot(attended, w_out, preferred_element_type=jnp.float32)  5.77 us
  transfers between devices with their start and end apart: 7, of which 6 were waited for; matrix products, arithmetic and copies ran while one was open for 4% of the time, Pallas kernels for 6%

profile of v7, /device:TPU:0, one launch (start us, length us, event | category | flops | bytes accessed | tf_op | source)
XLA Modules:
  0.0 234.9 jit_solution(17190357994174024077)
XLA Ops:
  6.5 0.9 copy-done
  7.5 4.9 %fusion.63 = f32[64,2048]{1,0:T(8,128)S(1)} fusion(bf16[64,2048]{1,0:T(8,128)(2,1)S(1)} %copy-done, bf16[2048,2048]{1,0:T(8,128)(2,1)} %param.10), kind=kOutput, calls=%fused_computation.124 | convolution fusion | flops 536870912 | bytes 9175040 | tf_op jit(solution)/shard_map/dot_general | solution.py:235
  12.4 2.1 fusion.7
  14.6 0.5 collective-permute-start
  15.8 1.2 reduce-window.6
  17.0 0.1 slice.52
  17.1 0.1 copy.50
  17.2 0.1 copy.51
  18.0 0.1 fusion.57
  18.1 2.6 %collective-permute-start.1 = (f32[64,2560]{1,0:T(8,128)S(1)}, f32[64,2560]{1,0:T(8,128)S(1)}, u32[]{:S(2)}, u32[]{:S(2)}) collective-permute-start(f32[64,2560]{1,0:T(8,128)S(1)} %fusion.57), channel_id=1, source_target_pairs={{0,2},{1,3},{2,0},{3,1},{4,6},{5,7},{6,4},{7,5},{8,10},{9,11},{10,... | collective-permute-start | bytes 1966088 | tf_op jit(solution)/shard_map/ppermute | solution.py:212
  20.7 0.1 fusion.56
  20.8 0.1 multiply_sine_fusion.1
  20.8 0.7 maximum_bitcast_fusion.2.cos_ref
  21.5 0.2 multiply_cosine_fusion
  21.7 14.4 %collective-permute-done.1 = f32[64,2560]{1,0:T(8,128)S(1)} collective-permute-done((f32[64,2560]{1,0:T(8,128)S(1)}, f32[64,2560]{1,0:T(8,128)S(1)}, u32[]{:S(2)}, u32[]{:S(2)}) %collective-permute-start.1) | collective-permute-done | bytes 655392 | tf_op jit(solution)/shard_map/ppermute | solution.py:212
  36.1 0.1 add.155
  36.2 0.1 copy.76
  36.3 0.2 fusion.61
  36.5 0.3 subtract_convert_fusion
  36.8 0.9 fusion.68
  37.7 0.2 reduce-scatter.3.cloned.1.call-start
  38.0 0.6 maximum_bitcast_fusion.3.sin_ref
  38.6 0.1 add_bitcast_fusion
  38.7 0.2 fusion.28
  38.9 0.7 fusion.36
  39.6 0.9 pad_maximum_fusion.2
  40.5 13.2 %shard_map.85 = (f32[2,512,128]{2,1,0:T(8,128)}, f32[2,512,1]{2,1,0:T(8,128)}, f32[2,512,1]{2,1,0:T(8,128)}) custom-call(s32[1]{0:T(128)} %bitcast.kv0_ref, bf16[2,512,128]{2,1,0:T(8,128)(2,1)} %bitcast.140, bf16[40,128,2048]{2,1,0:T(8,128)(2,1)} %bitcast.130, bf16[40,128,2048]{2,1,0:T(8,128)(2,1)} %bitcast.131, f32[1,1,5120]{2,1,0:T(1,128)} %bitcast.143, ...), custom_call_target="tpu_custom_call" | custom-call | tf_op jit(solution)/shard_map/pallas_call | solution.py:194
  53.7 1.2 copy.56
  54.9 1.2 copy.52
  56.1 11.2 %all-gather.2.cloned.1.call-done = bf16[64,64,128]{2,1,0:T(8,128)(2,1)} async-done(((bf16[16,64,128]{2,1,0:T(8,128)(2,1)}), bf16[64,64,128]{2,1,0:T(8,128)(2,1)}) %all-gather.2.cloned.1.call-update) | async-done | bytes 1048592 | tf_op jit(solution)/shard_map/all_gather | solution.py:264
  67.3 2.3 fusion.10.q_ref
  69.7 34.4 %shard_map.86 = (f32[6,512,128]{2,1,0:T(8,128)}, f32[6,512,1]{2,1,0:T(8,128)}, f32[6,512,1]{2,1,0:T(8,128)}) custom-call(s32[1]{0:T(128)} %bitcast.16.kv0_ref, bf16[6,512,128]{2,1,0:T(8,128)(2,1)} %fusion.10.q_ref, bf16[40,128,2048]{2,1,0:T(8,128)(2,1)} %bitcast.132, bf16[40,128,2048]{2,1,0:T(8,128)(2,1)} %bitcast.133, f32[1,1,5120]{2,1,0:T(1,128)} %bitcast.144, ...), custom_call_target="tpu_custom_call" | custom-call | tf_op jit(solution)/shard_map/pallas_call | solution.py:194
  104.0 2.2 copy.53
  106.2 0.1 reshape.360
  106.3 0.1 all_gather_reshape.3
  106.4 2.0 copy.57
  108.5 0.1 reshape.361
  108.5 22.9 %all_gather.7 = f32[16,64,64]{2,1,0:T(8,128)} all-gather(f32[1,64,64]{2,1,0:T(8,128)S(1)} %all_gather_reshape.3), channel_id=1, replica_groups=mesh['groups'=2,'tensor'=4,'store'=4] {'tensor','store'}, dimensions={0}, use_global_device_ids=true | all-gather | bytes 278528 | tf_op jit(solution)/shard_map/all_gather | solution.py:286
  131.4 1.9 fusion.2
  133.3 1.7 reshape.359
  135.1 1.1 reduce_max.18
  136.2 0.6 mul.240
  136.8 1.4 bitcast_multiply_fusion
  138.2 1.5 pad_maximum_fusion
  139.7 41.8 %reduce-scatter.3.cloned.1.call-done = f32[16,8256]{1,0:T(8,128)} async-done(((f32[64,8256]{1,0:T(8,128)}), f32[16,8256]{1,0:T(8,128)}) %reduce-scatter.3.cloned.1.call-update) | async-done | bytes 528400 | tf_op jit(solution)/shard_map/reduce_scatter | solution.py:291
  181.6 0.1 fusion.34
  181.7 0.1 reshape.363
  181.8 0.1 slice.58
  181.9 0.1 subtract_convert_fusion.1
  182.0 1.7 collective-permute-done.2
  183.7 1.1 add.172
  184.8 1.5 collective-permute-start.3
  186.3 0.5 fusion.62
  186.8 0.1 fusion.15
  186.9 0.3 fusion.17
  187.2 11.8 %collective-permute-done.3 = f32[16,8256]{1,0:T(8,128)S(1)} collective-permute-done((f32[16,8256]{1,0:T(8,128)S(1)}, f32[16,8256]{1,0:T(8,128)S(1)}, u32[]{:S(2)}, u32[]{:S(2)}) %collective-permute-start.3) | collective-permute-done | bytes 528416 | tf_op jit(solution)/shard_map/ppermute | solution.py:212
  199.0 0.1 add.173
  199.1 0.1 copy.67
  199.2 0.1 copy.65
  199.3 0.1 copy.62
  199.3 0.5 fusion.14
  199.9 5.8 %fusion.19 = f32[64,2048]{1,0:T(8,128)} fusion(bf16[2048,2048]{1,0:T(8,128)(2,1)} %param.12, bf16[8,8,16,128]{3,2,1,0:T(8,128)(2,1)S(1)} %bitcast.138), kind=kOutput, calls=%fused_computation.33 | convolution fusion | flops 536870912 | bytes 9175040 | tf_op jit(solution)/shard_map/dot_general | solution.py:317
  205.7 21.1 %reduce-scatter.5.cloned.1.call-done = f32[16,2048]{1,0:T(8,128)} async-done(((f32[64,2048]{1,0:T(8,128)}), f32[16,2048]{1,0:T(8,128)}) %reduce-scatter.5.cloned.1.call-update) | async-done | bytes 131088 | tf_op jit(solution)/shard_map/reduce_scatter | solution.py:316
  226.8 1.5 convert_element_type.52
  (35 shorter events, 0.5 us)
Async XLA Ops:
  6.5 1.0 copy-start
  6.5 60.8 %all-gather.2.cloned.1.call-start = ((), (), s32[]{:S(2)}) async-start(), calls=%async_computation.2 | async-start | bytes 1310720 | tf_op jit(solution)/shard_map/all_gather | solution.py:264
  12.4 3.3 %copy-start.4 = (s32[256,1]{0,1:T(1,128)S(1)}, s32[256,1]{0,1:T(1,128)}, u32[]{:S(2)}) copy-start(s32[256,1]{0,1:T(1,128)} %param.14) | copy-start | bytes 3076
  14.6 3.4 %collective-permute-start = (f32[64,2560]{1,0:T(8,128)S(1)}, f32[64,2560]{1,0:T(8,128)S(1)}, u32[]{:S(2)}, u32[]{:S(2)}) collective-permute-start(f32[64,2560]{1,0:T(8,128)S(1)} %pad_maximum_fusion.1), channel_id=1, source_target_pairs={{0,1},{1,0},{2,3},{3,2},{4,5},{5,4},{6,7},{7,6},{8,9},{9,8},{10,11... | collective-permute-start | bytes 1966088 | tf_op jit(solution)/shard_map/ppermute | solution.py:212
  18.1 18.0 %collective-permute-start.1 = (f32[64,2560]{1,0:T(8,128)S(1)}, f32[64,2560]{1,0:T(8,128)S(1)}, u32[]{:S(2)}, u32[]{:S(2)}) collective-permute-start(f32[64,2560]{1,0:T(8,128)S(1)} %fusion.57), channel_id=1, source_target_pairs={{0,2},{1,3},{2,0},{3,1},{4,6},{5,7},{6,4},{7,5},{8,10},{9,11},{10,... | collective-permute-start | bytes 1966088 | tf_op jit(solution)/shard_map/ppermute | solution.py:212
  37.7 143.8 %reduce-scatter.3.cloned.1.call-start = ((), (), s32[]{:S(2)}) async-start(), calls=%async_computation.3 | async-start | bytes 2662400 | tf_op jit(solution)/shard_map/reduce_scatter | solution.py:291
  104.0 27.4 %copy-start.2 = (f32[6,512,128]{2,1,0:T(8,128)S(1)}, f32[6,512,128]{2,1,0:T(8,128)}, u32[]{:S(2)}) copy-start(f32[6,512,128]{2,1,0:T(8,128)} %get-tuple-element.12) | copy-start | bytes 4718596
  104.0 27.4 %copy-start.3 = (f32[2,512,128]{2,1,0:T(8,128)S(1)}, f32[2,512,128]{2,1,0:T(8,128)}, u32[]{:S(2)}) copy-start(f32[2,512,128]{2,1,0:T(8,128)} %get-tuple-element.11) | copy-start | bytes 1572868
  139.7 87.1 %reduce-scatter.5.cloned.1.call-start = ((), (), s32[]{:S(2)}) async-start(), calls=%async_computation.4 | async-start | bytes 655360 | tf_op jit(solution)/shard_map/reduce_scatter | solution.py:316
  181.6 2.1 collective-permute-start.2
  184.8 14.2 %collective-permute-start.3 = (f32[16,8256]{1,0:T(8,128)S(1)}, f32[16,8256]{1,0:T(8,128)S(1)}, u32[]{:S(2)}, u32[]{:S(2)}) collective-permute-start(f32[16,8256]{1,0:T(8,128)S(1)} %add.172), channel_id=1, source_target_pairs={{0,2},{1,3},{2,0},{3,1},{4,6},{5,7},{6,4},{7,5},{8,10},{9,11},{10,... | collective-permute-start | bytes 1585160 | tf_op jit(solution)/shard_map/ppermute | solution.py:212
  199.9 28.5 %copy-start.1 = (bf16[64,2048]{1,0:T(8,128)(2,1)S(1)}, bf16[64,2048]{1,0:T(8,128)(2,1)}, u32[]{:S(2)}) copy-start(bf16[64,2048]{1,0:T(8,128)(2,1)} %param.8) | copy-start | bytes 786436
Sparse Core Ops, SparseCore 0:
  37.9 29.4 all-gather.1
  139.8 41.7 reduce-scatter.2
  205.8 20.9 reduce-scatter.4

commit v8 on v7

--- a/solution.py
+++ b/solution.py
@@ -203,14 +203,27 @@
     )(jnp.reshape(kv0, (1,)).astype(jnp.int32), q_k, kv_local, kv_local, bias, cos2, sin2)
 
 
+def axis_reduce(x, axis, op):
+    n = lax.axis_size(axis)
+    d = 1
+    while d < n:
+        x = op(x, lax.ppermute(x, axis, perm=[(i, i ^ d) for i in range(n)]))
+        d *= 2
+    return x
+
+
 def axis_sum(x, axis):
     n = lax.axis_size(axis)
     if n & (n - 1):
         return lax.psum(x, axis)
-    d = 1
-    while d < n:
-        x = x + lax.ppermute(x, axis, perm=[(i, i ^ d) for i in range(n)])
-        d *= 2
+    return axis_reduce(x, axis, jnp.add)
+
+
+def axis_max(x, axes):
+    if any(lax.axis_size(a) & (lax.axis_size(a) - 1) for a in axes):
+        return jnp.max(lax.all_gather(x, axes), axis=0)
+    for a in axes:
+        x = axis_reduce(x, a, jnp.maximum)
     return x
 
 
@@ -283,7 +296,7 @@
     top = top.reshape(HQ, tok_count)
     total = total.reshape(HQ, tok_count)
 
-    glob_top = jnp.max(lax.all_gather(top, ("tensor", "store")), axis=0)
+    glob_top = axis_max(top, ("store", "tensor"))
     factor = jnp.exp(top - glob_top)
     packed = jnp.concatenate(
         [(acc * factor[..., None]).reshape(HQ, tok_count * HD), total * factor], axis=1

time: 235 us -> 223 us (0.949)
  blocking collectives: 22.9 us -> 0 us
  waiting for transfers between devices: 102 us -> 111 us
  starting transfers between devices: 4.9 us -> 8.84 us
  local copies, waits for them, and re-layouts: 11.3 us -> 8.67 us
    all_gather x1 -> x0, blocking collectives: 22.9 us -> none  [body(): glob_top = jnp.max(lax.all_gather(top, ('tensor', 'store')), axis=0)]
    ppermute x4 -> x8, waiting for transfers between devices: 27.8 us -> 33.6 us  [axis_reduce(): x = op(x, lax.ppermute(x, axis, perm=[(i, i ^ d) for i in range(n)]))]
    ppermute x4 -> x8, starting transfers between devices: 4.63 us -> 8.57 us  [axis_reduce(): x = op(x, lax.ppermute(x, axis, perm=[(i, i ^ d) for i in range(n)]))]
    pallas_call x4, local copies, waits for them, and re-layouts: 6.64 us -> 4.12 us  [hist_attend(): pl.pallas_call(kernel, grid_spec=grid_spec, out_shape=[jax.ShapeDtypeStru...]
  transfers between devices with their start and end apart: 7 -> 11, of which waited for: 6 -> 9; matrix products, arithmetic and copies ran while one was open for 4% -> 6% of each run, Pallas kernels for 6% -> 6%
where the time goes in v8:
time: 223 us
  waiting for transfers between devices  111 us (50%)
  Pallas kernels  47.5 us (21%)
  other arithmetic  18.3 us (8%)
  between operations  14.7 us (7%)
  matrix products  13.6 us (6%)
  starting transfers between devices  8.84 us (4%)
  local copies, waits for them, and re-layouts  8.67 us (4%)
    pallas_call x2, Pallas kernels, hist_attend(): pl.pallas_call(kernel, grid_spec=grid_spec, out_shape=[jax.ShapeDtypeStru...  47.5 us
    reduce_scatter x1, waiting for transfers between devices, body(): packed = lax.psum_scatter(packed, 'tensor', scatter_dimension=0, tiled=True)  44 us
    ppermute x8, waiting for transfers between devices, axis_reduce(): x = op(x, lax.ppermute(x, axis, perm=[(i, i ^ d) for i in range(n)]))  33.6 us
    reduce_scatter x1, waiting for transfers between devices, body(): lax.psum_scatter(jnp.dot(attended, w_out, preferred_element_type=jnp.floa...  21.1 us
    all_gather x1, waiting for transfers between devices, body(): q_all = lax.all_gather(q_heads, 'tensor', axis=0, tiled=True)  12.5 us
    ppermute x8, starting transfers between devices, axis_reduce(): x = op(x, lax.ppermute(x, axis, perm=[(i, i ^ d) for i in range(n)]))  8.57 us
    dot_general x1, matrix products, body(): jnp.dot(attended, w_out, preferred_element_type=jnp.float32)  5.79 us
    dot_general x1, matrix products, body(): query_part = jnp.dot(x_new, w_query, preferred_element_type=jnp.float32)  4.94 us
  transfers between devices with their start and end apart: 11, of which 9 were waited for; matrix products, arithmetic and copies ran while one was open for 6% of the time, Pallas kernels for 6%

profile of v8, /device:TPU:0, one launch (start us, length us, event | category | flops | bytes accessed | tf_op | source)
XLA Modules:
  0.0 222.9 jit_solution(3933800355075012672)
XLA Ops:
  6.5 0.9 copy-done
  7.5 4.9 %fusion.63 = f32[64,2048]{1,0:T(8,128)S(1)} fusion(bf16[64,2048]{1,0:T(8,128)(2,1)S(1)} %copy-done, bf16[2048,2048]{1,0:T(8,128)(2,1)} %param.10), kind=kOutput, calls=%fused_computation.124 | convolution fusion | flops 536870912 | bytes 9175040 | tf_op jit(solution)/shard_map/dot_general | solution.py:248
  12.4 2.1 fusion.7
  14.6 0.5 collective-permute-start
  15.8 1.2 reduce-window.6
  17.0 0.1 slice.52
  17.1 0.1 copy.50
  17.2 0.1 copy.51
  18.0 0.1 fusion.57
  18.1 2.6 %collective-permute-start.1 = (f32[64,2560]{1,0:T(8,128)S(1)}, f32[64,2560]{1,0:T(8,128)S(1)}, u32[]{:S(2)}, u32[]{:S(2)}) collective-permute-start(f32[64,2560]{1,0:T(8,128)S(1)} %fusion.57), channel_id=1, source_target_pairs={{0,2},{1,3},{2,0},{3,1},{4,6},{5,7},{6,4},{7,5},{8,10},{9,11},{10,... | collective-permute-start | bytes 1966088 | tf_op jit(solution)/shard_map/ppermute | solution.py:210
  20.8 0.7 maximum_bitcast_fusion.2.cos_ref
  21.5 0.2 multiply_cosine_fusion
  21.7 14.4 %collective-permute-done.1 = f32[64,2560]{1,0:T(8,128)S(1)} collective-permute-done((f32[64,2560]{1,0:T(8,128)S(1)}, f32[64,2560]{1,0:T(8,128)S(1)}, u32[]{:S(2)}, u32[]{:S(2)}) %collective-permute-start.1) | collective-permute-done | bytes 655392 | tf_op jit(solution)/shard_map/ppermute | solution.py:210
  36.1 0.1 add.155
  36.2 0.1 copy.76
  36.3 0.2 fusion.61
  36.5 0.3 subtract_convert_fusion
  36.8 0.9 fusion.68
  37.7 0.2 reduce-scatter.3.cloned.1.call-start
  37.9 0.6 maximum_bitcast_fusion.3.sin_ref
  38.5 0.1 add_bitcast_fusion
  38.6 0.2 fusion.28
  38.8 0.7 fusion.36
  39.5 0.9 pad_maximum_fusion.2
  40.4 13.2 %shard_map.85 = (f32[2,512,128]{2,1,0:T(8,128)}, f32[2,512,1]{2,1,0:T(8,128)}, f32[2,512,1]{2,1,0:T(8,128)}) custom-call(s32[1]{0:T(128)} %bitcast.kv0_ref, bf16[2,512,128]{2,1,0:T(8,128)(2,1)} %bitcast.138, bf16[40,128,2048]{2,1,0:T(8,128)(2,1)} %bitcast.128, bf16[40,128,2048]{2,1,0:T(8,128)(2,1)} %bitcast.129, f32[1,1,5120]{2,1,0:T(1,128)} %bitcast.141, ...), custom_call_target="tpu_custom_call" | custom-call | tf_op jit(solution)/shard_map/pallas_call | solution.py:194
  53.6 1.2 copy.52
  54.8 12.5 %all-gather.2.cloned.1.call-done = bf16[64,64,128]{2,1,0:T(8,128)(2,1)} async-done(((bf16[16,64,128]{2,1,0:T(8,128)(2,1)}), bf16[64,64,128]{2,1,0:T(8,128)(2,1)}) %all-gather.2.cloned.1.call-update) | async-done | bytes 1048592 | tf_op jit(solution)/shard_map/all_gather | solution.py:277
  67.3 2.3 %fusion.10.q_ref = bf16[6,512,128]{2,1,0:T(8,128)(2,1)} fusion(s32[]{:T(128)S(6)} %select_n.154, bf16[8,512,128]{2,1,0:T(8,128)(2,1)} %bitcast.139), kind=kLoop, calls=%fused_computation.17 | loop fusion | flops 393216 | bytes 1835012 | tf_op jit(solution)/shard_map/concatenate | solution.py:285
  69.6 34.3 %shard_map.86 = (f32[6,512,128]{2,1,0:T(8,128)}, f32[6,512,1]{2,1,0:T(8,128)}, f32[6,512,1]{2,1,0:T(8,128)}) custom-call(s32[1]{0:T(128)} %bitcast.16.kv0_ref, bf16[6,512,128]{2,1,0:T(8,128)(2,1)} %fusion.10.q_ref, bf16[40,128,2048]{2,1,0:T(8,128)(2,1)} %bitcast.130, bf16[40,128,2048]{2,1,0:T(8,128)(2,1)} %bitcast.131, f32[1,1,5120]{2,1,0:T(1,128)} %bitcast.142, ...), custom_call_target="tpu_custom_call" | custom-call | tf_op jit(solution)/shard_map/pallas_call | solution.py:194
  104.0 2.1 copy.53
  106.1 0.1 reshape.353
  106.2 1.2 collective-permute-done.2
  107.4 1.5 collective-permute-start.3
  108.9 0.2 copy.56
  109.1 2.3 %collective-permute-done.3 = f32[64,64]{1,0:T(8,128)S(1)} collective-permute-done((f32[64,64]{1,0:T(8,128)S(1)}, f32[64,64]{1,0:T(8,128)S(1)}, u32[]{:S(2)}, u32[]{:S(2)}) %collective-permute-start.3) | collective-permute-done | bytes 16416 | tf_op jit(solution)/shard_map/ppermute | solution.py:210
  111.3 1.4 collective-permute-start.4
  112.7 3.4 %fusion.2 = f32[8,512,128]{2,1,0:T(8,128)} fusion(s32[]{:T(128)S(6)} %select_n.155, f32[2,512,128]{2,1,0:T(8,128)S(1)} %copy-done.3, f32[6,512,128]{2,1,0:T(8,128)} %get-tuple-element.12), kind=kLoop, calls=%fused_computation.7 | loop fusion | flops 1572864 | bytes 4194308 | tf_op jit(solution)/shard_map/concatenate | solution.py:290
  116.1 0.6 copy.57
  116.8 1.1 collective-permute-start.5
  117.9 0.1 reshape.354
  117.9 1.7 reshape.352
  119.7 2.3 %collective-permute-done.5 = f32[64,64]{1,0:T(8,128)S(1)} collective-permute-done((f32[64,64]{1,0:T(8,128)S(1)}, f32[64,64]{1,0:T(8,128)S(1)}, u32[]{:S(2)}, u32[]{:S(2)}) %collective-permute-start.5) | collective-permute-done | bytes 16416 | tf_op jit(solution)/shard_map/ppermute | solution.py:210
  122.0 0.6 mul.240
  122.6 1.4 bitcast_multiply_fusion
  124.0 1.5 pad_maximum_fusion
  125.6 44.0 %reduce-scatter.3.cloned.1.call-done = f32[16,8256]{1,0:T(8,128)} async-done(((f32[64,8256]{1,0:T(8,128)}), f32[16,8256]{1,0:T(8,128)}) %reduce-scatter.3.cloned.1.call-update) | async-done | bytes 528400 | tf_op jit(solution)/shard_map/reduce_scatter | solution.py:304
  169.6 0.1 fusion.34
  169.7 0.1 reshape.356
  169.8 0.1 slice.58
  169.9 0.1 subtract_convert_fusion.1
  170.0 1.7 collective-permute-done.6
  171.7 1.1 add.172
  172.8 1.5 collective-permute-start.7
  174.3 0.5 fusion.62
  174.8 0.1 fusion.15
  174.9 0.3 fusion.17
  175.2 11.8 %collective-permute-done.7 = f32[16,8256]{1,0:T(8,128)S(1)} collective-permute-done((f32[16,8256]{1,0:T(8,128)S(1)}, f32[16,8256]{1,0:T(8,128)S(1)}, u32[]{:S(2)}, u32[]{:S(2)}) %collective-permute-start.7) | collective-permute-done | bytes 528416 | tf_op jit(solution)/shard_map/ppermute | solution.py:210
  187.1 0.1 copy.67
  187.2 0.1 copy.65
  187.3 0.1 copy.62
  187.4 0.5 fusion.14
  187.9 5.8 %fusion.19 = f32[64,2048]{1,0:T(8,128)} fusion(bf16[2048,2048]{1,0:T(8,128)(2,1)} %param.12, bf16[8,8,16,128]{3,2,1,0:T(8,128)(2,1)S(1)} %bitcast.136), kind=kOutput, calls=%fused_computation.33 | convolution fusion | flops 536870912 | bytes 9175040 | tf_op jit(solution)/shard_map/dot_general | solution.py:330
  193.7 21.1 %reduce-scatter.5.cloned.1.call-done = f32[16,2048]{1,0:T(8,128)} async-done(((f32[64,2048]{1,0:T(8,128)}), f32[16,2048]{1,0:T(8,128)}) %reduce-scatter.5.cloned.1.call-update) | async-done | bytes 131088 | tf_op jit(solution)/shard_map/reduce_scatter | solution.py:329
  214.8 1.5 convert_element_type.52
  (45 shorter events, 0.7 us)
Async XLA Ops:
  6.5 1.0 copy-start
  6.5 60.8 %all-gather.2.cloned.1.call-start = ((), (), s32[]{:S(2)}) async-start(), calls=%async_computation.2 | async-start | bytes 1310720 | tf_op jit(solution)/shard_map/all_gather | solution.py:277
  12.4 3.3 %copy-start.5 = (s32[256,1]{0,1:T(1,128)S(1)}, s32[256,1]{0,1:T(1,128)}, u32[]{:S(2)}) copy-start(s32[256,1]{0,1:T(1,128)} %param.14) | copy-start | bytes 3076
  14.6 3.4 %collective-permute-start = (f32[64,2560]{1,0:T(8,128)S(1)}, f32[64,2560]{1,0:T(8,128)S(1)}, u32[]{:S(2)}, u32[]{:S(2)}) collective-permute-start(f32[64,2560]{1,0:T(8,128)S(1)} %pad_maximum_fusion.1), channel_id=1, source_target_pairs={{0,1},{1,0},{2,3},{3,2},{4,5},{5,4},{6,7},{7,6},{8,9},{9,8},{10,11... | collective-permute-start | bytes 1966088 | tf_op jit(solution)/shard_map/ppermute | solution.py:210
  18.1 18.0 %collective-permute-start.1 = (f32[64,2560]{1,0:T(8,128)S(1)}, f32[64,2560]{1,0:T(8,128)S(1)}, u32[]{:S(2)}, u32[]{:S(2)}) collective-permute-start(f32[64,2560]{1,0:T(8,128)S(1)} %fusion.57), channel_id=1, source_target_pairs={{0,2},{1,3},{2,0},{3,1},{4,6},{5,7},{6,4},{7,5},{8,10},{9,11},{10,... | collective-permute-start | bytes 1966088 | tf_op jit(solution)/shard_map/ppermute | solution.py:210
  37.7 131.9 %reduce-scatter.3.cloned.1.call-start = ((), (), s32[]{:S(2)}) async-start(), calls=%async_computation.3 | async-start | bytes 2662400 | tf_op jit(solution)/shard_map/reduce_scatter | solution.py:304
  103.9 4.9 %copy-start.4 = (f32[2,512,1]{2,1,0:T(8,128)S(1)}, f32[2,512,1]{2,1,0:T(8,128)}, u32[]{:S(2)}) copy-start(f32[2,512,1]{2,1,0:T(8,128)} %get-tuple-element.15) | copy-start | bytes 12292
  103.9 8.8 %copy-start.3 = (f32[2,512,128]{2,1,0:T(8,128)S(1)}, f32[2,512,128]{2,1,0:T(8,128)}, u32[]{:S(2)}) copy-start(f32[2,512,128]{2,1,0:T(8,128)} %get-tuple-element.11) | copy-start | bytes 1572868
  106.2 1.2 collective-permute-start.2
  107.4 3.9 %collective-permute-start.3 = (f32[64,64]{1,0:T(8,128)S(1)}, f32[64,64]{1,0:T(8,128)S(1)}, u32[]{:S(2)}, u32[]{:S(2)}) collective-permute-start(f32[64,64]{1,0:T(8,128)S(1)} %max.15), channel_id=1, source_target_pairs={{0,2},{1,3},{2,0},{3,1},{4,6},{5,7},{6,4},{7,5},{8,10},{9,11},{10,... | collective-permute-start | bytes 49160 | tf_op jit(solution)/shard_map/ppermute | solution.py:210
  111.3 5.4 %collective-permute-start.4 = (f32[64,64]{1,0:T(8,128)S(1)}, f32[64,64]{1,0:T(8,128)S(1)}, u32[]{:S(2)}, u32[]{:S(2)}) collective-permute-start(f32[64,64]{1,0:T(8,128)S(1)} %max.16), channel_id=1, source_target_pairs={{0,4},{4,0},{8,12},{12,8},{1,5},{5,1},{9,13},{13,9},{2,6},{6,2},{1... | collective-permute-start | bytes 49160 | tf_op jit(solution)/shard_map/ppermute | solution.py:210
  112.7 3.4 %copy-start.2 = (f32[6,512,1]{2,1,0:T(8,128)S(1)}, f32[6,512,1]{2,1,0:T(8,128)}, u32[]{:S(2)}) copy-start(f32[6,512,1]{2,1,0:T(8,128)} %get-tuple-element.16) | copy-start | bytes 36868
  116.8 5.2 %collective-permute-start.5 = (f32[64,64]{1,0:T(8,128)S(1)}, f32[64,64]{1,0:T(8,128)S(1)}, u32[]{:S(2)}, u32[]{:S(2)}) collective-permute-start(f32[64,64]{1,0:T(8,128)S(1)} %max.17), channel_id=1, source_target_pairs={{0,8},{4,12},{8,0},{12,4},{1,9},{5,13},{9,1},{13,5},{2,10},{6,14},... | collective-permute-start | bytes 49160 | tf_op jit(solution)/shard_map/ppermute | solution.py:210
  125.5 89.3 %reduce-scatter.5.cloned.1.call-start = ((), (), s32[]{:S(2)}) async-start(), calls=%async_computation.4 | async-start | bytes 655360 | tf_op jit(solution)/shard_map/reduce_scatter | solution.py:329
  169.6 2.1 collective-permute-start.6
  172.8 14.2 %collective-permute-start.7 = (f32[16,8256]{1,0:T(8,128)S(1)}, f32[16,8256]{1,0:T(8,128)S(1)}, u32[]{:S(2)}, u32[]{:S(2)}) collective-permute-start(f32[16,8256]{1,0:T(8,128)S(1)} %add.172), channel_id=1, source_target_pairs={{0,2},{1,3},{2,0},{3,1},{4,6},{5,7},{6,4},{7,5},{8,10},{9,11},{10,... | collective-permute-start | bytes 1585160 | tf_op jit(solution)/shard_map/ppermute | solution.py:210
  187.9 28.5 %copy-start.1 = (bf16[64,2048]{1,0:T(8,128)(2,1)S(1)}, bf16[64,2048]{1,0:T(8,128)(2,1)}, u32[]{:S(2)}) copy-start(bf16[64,2048]{1,0:T(8,128)(2,1)} %param.8) | copy-start | bytes 786436
Sparse Core Ops, SparseCore 0:
  37.8 29.4 all-gather.1
  125.6 43.8 reduce-scatter.2
  193.8 20.9 reduce-scatter.4

commit v9 on v6

--- a/solution.py
+++ b/solution.py
@@ -203,6 +203,43 @@
     )(jnp.reshape(kv0, (1,)).astype(jnp.int32), q_k, kv_local, kv_local, bias, cos2, sin2)
 
 
+def axis_reduce(x, axis, op):
+    n = lax.axis_size(axis)
+    d = 1
+    while d < n:
+        x = op(x, lax.ppermute(x, axis, perm=[(i, i ^ d) for i in range(n)]))
+        d *= 2
+    return x
+
+
+def bit_scatter(block, axis):
+    n = lax.axis_size(axis)
+    idx = lax.axis_index(axis)
+    d = 1
+    while d < n:
+        bit = (idx // d) % 2
+        keep = lax.dynamic_index_in_dim(block, bit, 0, keepdims=False)
+        send = lax.dynamic_index_in_dim(block, 1 - bit, 0, keepdims=False)
+        block = keep + lax.ppermute(send, axis, perm=[(i, i ^ d) for i in range(n)])
+        d *= 2
+    return block
+
+
+def axis_sum(x, axis):
+    n = lax.axis_size(axis)
+    if n & (n - 1):
+        return lax.psum(x, axis)
+    return axis_reduce(x, axis, jnp.add)
+
+
+def axis_max(x, axes):
+    if any(lax.axis_size(a) & (lax.axis_size(a) - 1) for a in axes):
+        return jnp.max(lax.all_gather(x, axes), axis=0)
+    for a in axes:
+        x = axis_reduce(x, a, jnp.maximum)
+    return x
+
+
 def body(x_new, kv_pages, w_query, w_keyval, w_out, lengths, page_store, offsets):
     tensors = lax.axis_size("tensor")
     shards = lax.axis_size("store")
@@ -223,7 +260,9 @@
     keyval_cols = lax.dynamic_slice_in_dim(w_keyval, kv_first * (2 * HD), local_kv * 2 * HD, 1)
     query_part = jnp.dot(x_new, w_query, preferred_element_type=jnp.float32)
     keyval_part = jnp.dot(x_new, keyval_cols, preferred_element_type=jnp.float32)
-    query_sum, keyval_sum = lax.psum((query_part, keyval_part), "store")
+    width_q = query_part.shape[1]
+    both = axis_sum(jnp.concatenate([query_part, keyval_part], axis=1), "store")
+    query_sum, keyval_sum = both[:, :width_q], both[:, width_q:]
     keyval_local = keyval_sum.reshape(tok_count, local_kv, 2, HD)
     tok_ids = jnp.arange(tok_count, dtype=jnp.int32)
     tok_sess = tok_ids // TURN
@@ -270,17 +309,29 @@
     top = top.reshape(HQ, tok_count)
     total = total.reshape(HQ, tok_count)
 
-    glob_top = jnp.max(lax.all_gather(top, ("tensor", "store")), axis=0)
+    glob_top = axis_max(top, ("store", "tensor"))
     factor = jnp.exp(top - glob_top)
     packed = jnp.concatenate(
         [(acc * factor[..., None]).reshape(HQ, tok_count * HD), total * factor], axis=1
     )
     new_allowed = (tok_sess[:, None] == tok_sess[None, :]) & (tok_ids[None, :] <= tok_ids[:, None])
     chunk_heads = HQ // (tensors * shards)
-    if HQ % (tensors * shards) == 0 and group_size % chunk_heads == 0:
-        packed = lax.psum_scatter(packed, ("tensor", "store"), scatter_dimension=0, tiled=True)
-        acc = packed[:, : tok_count * HD].reshape(chunk_heads, tok_count, HD)
-        total = packed[:, tok_count * HD :]
+    if (
+        HQ % (tensors * shards) == 0
+        and group_size % chunk_heads == 0
+        and not shards & (shards - 1)
+        and not tensors & (tensors - 1)
+    ):
+        width = packed.shape[1]
+        s_bits = shards.bit_length() - 1
+        t_bits = tensors.bit_length() - 1
+        block = packed.reshape((2,) * t_bits + (2,) * s_bits + (chunk_heads, width))
+        order = tuple(range(t_bits + s_bits - 1, t_bits - 1, -1)) + tuple(range(t_bits - 1, -1, -1))
+        block = jnp.transpose(block, order + (t_bits + s_bits, t_bits + s_bits + 1))
+        block = bit_scatter(block, "store")
+        block = bit_scatter(block, "tensor")
+        acc = block[:, : tok_count * HD].reshape(chunk_heads, tok_count, HD)
+        total = block[:, tok_count * HD :]
         chunk_first = (tensor_idx * shards + store_idx) * chunk_heads
         loc_top = lax.dynamic_slice_in_dim(glob_top, chunk_first, chunk_heads, 0)
         hist_part = (jnp.transpose(loc_top), jnp.transpose(total), jnp.transpose(acc, (1, 0, 2)))
@@ -289,7 +340,9 @@
         kv_idx = in_group // group_size
         key_chunk = lax.dynamic_slice_in_dim(key_new, kv_idx, 1, 1)
         value_chunk = lax.dynamic_slice_in_dim(value_new, kv_idx, 1, 1)
-        new_part = attend(query_chunk.reshape(tok_count, 1, chunk_heads, HD), key_chunk, value_chunk, new_allowed)
+        new_part = attend(
+            query_chunk.reshape(tok_count, 1, chunk_heads, HD), key_chunk, value_chunk, new_allowed
+        )
         new_flat = (
             new_part[0].reshape(tok_count, chunk_heads),
             new_part[1].reshape(tok_count, chunk_heads),
@@ -304,11 +357,16 @@
         attended = lax.all_gather(attended, "store", axis=1, tiled=True)
     else:
         packed = lax.psum_scatter(packed, "tensor", scatter_dimension=0, tiled=True)
-        packed = lax.psum(packed, "store")
+        packed = axis_sum(packed, "store")
         acc = packed[:, : tok_count * HD].reshape(local_heads, tok_count, HD)
         total = packed[:, tok_count * HD :]
         loc_top = lax.dynamic_slice_in_dim(glob_top, tensor_idx * local_heads, local_heads, 0)
-        hist_part = (jnp.transpose(loc_top), jnp.transpose(total), jnp.transpose(acc, (1, 0, 2)))
+        hist_part = (
+            jnp.transpose(loc_top),
+            jnp.transpose(total),
+            jnp.transpose(acc, (1, 0, 2)),
+        )
+
         query_local = query_rot.reshape(tok_count, local_kv, local_group, HD)
         new_part = attend(query_local, key_new, value_new, new_allowed)
         new_flat = (

time: 292 us -> 205 us (0.70)
  waiting for transfers between devices: 157 us -> 82.6 us
  blocking collectives: 27.3 us -> 5.79 us
  starting transfers between devices: 0.31 us -> 10 us
    unnamed x5 -> x2, waiting for transfers between devices: 93.1 us -> 0.03 us
    ppermute x0 -> x10, waiting for transfers between devices: none -> 48.8 us  [the longest x4 28.8 us: bit_scatter(): block = keep + lax.ppermute(send, axis, perm=[(i, i ^ d) for i in range(n)])]
    psum x1 -> x0, waiting for transfers between devices: 32.9 us -> none  [body(): query_sum, keyval_sum = lax.psum((query_part, keyval_part), 'store')]
    all_gather x1 -> x0, blocking collectives: 21.5 us -> none  [body(): glob_top = jnp.max(lax.all_gather(top, ('tensor', 'store')), axis=0)]
    ppermute x0 -> x10, starting transfers between devices: none -> 9.79 us  [the longest x6 7.06 us: axis_reduce(): x = op(x, lax.ppermute(x, axis, perm=[(i, i ^ d) for i in range(n)]))]
  transfers between devices with their start and end apart: 4 -> 12, of which waited for: 4 -> 10; matrix products, arithmetic and copies ran while one was open for 3% -> 6% of each run, Pallas kernels for 5% -> 6%
where the time goes in v9:
time: 205 us
  waiting for transfers between devices  82.6 us (40%)
  Pallas kernels  47.5 us (23%)
  other arithmetic  18.3 us (9%)
  between operations  15 us (7%)
  matrix products  13.3 us (6%)
  local copies, waits for them, and re-layouts  11.9 us (6%)
  starting transfers between devices  10 us (5%)
  blocking collectives  5.79 us (3%)
    pallas_call x2, Pallas kernels, hist_attend(): pl.pallas_call(kernel, grid_spec=grid_spec, out_shape=[jax.ShapeDtypeStru...  47.5 us
    ppermute x4, waiting for transfers between devices, bit_scatter(): block = keep + lax.ppermute(send, axis, perm=[(i, i ^ d) for i in range(n)])  28.8 us
    reduce_scatter x1, waiting for transfers between devices, body(): lax.psum_scatter(jnp.dot(attended, w_out, preferred_element_type=jnp.floa...  21.3 us
    ppermute x6, waiting for transfers between devices, axis_reduce(): x = op(x, lax.ppermute(x, axis, perm=[(i, i ^ d) for i in range(n)]))  20 us
    all_gather x1, waiting for transfers between devices, body(): q_all = lax.all_gather(q_heads, 'tensor', axis=0, tiled=True)  12.5 us
    ppermute x6, starting transfers between devices, axis_reduce(): x = op(x, lax.ppermute(x, axis, perm=[(i, i ^ d) for i in range(n)]))  7.06 us
    dot_general x1, matrix products, body(): jnp.dot(attended, w_out, preferred_element_type=jnp.float32)  5.8 us
    all_gather x1, blocking collectives, body(): attended = lax.all_gather(attended, 'store', axis=1, tiled=True)  5.79 us
  transfers between devices with their start and end apart: 12, of which 10 were waited for; matrix products, arithmetic and copies ran while one was open for 6% of the time, Pallas kernels for 6%

profile of v9, /device:TPU:0, one launch (start us, length us, event | category | flops | bytes accessed | tf_op | source)
XLA Modules:
  0.0 204.5 jit_solution(11625587629343632130)
XLA Ops:
  6.5 0.9 copy-done
  7.5 4.9 %fusion.69 = f32[64,2048]{1,0:T(8,128)S(1)} fusion(bf16[64,2048]{1,0:T(8,128)(2,1)S(1)} %copy-done, bf16[2048,2048]{1,0:T(8,128)(2,1)} %param.10), kind=kOutput, calls=%fused_computation.143 | convolution fusion | flops 536870912 | bytes 9175040 | tf_op jit(solution)/shard_map/dot_general | solution.py:261
  12.4 2.1 %fusion.5 = f32[64,512]{1,0:T(8,128)S(1)} fusion(bf16[64,2048]{1,0:T(8,128)(2,1)S(1)} %copy-done, bf16[2048,2048]{1,0:T(8,128)(2,1)} %param.11, s32[]{:T(128)S(6)} %select_n.204), kind=kOutput, calls=%fused_computation.15 | convolution fusion | flops 134217728 | bytes 2490372 | tf_op jit(solution)/shard_map/dot_general | solution.py:262
  14.6 0.5 collective-permute-start
  15.8 1.2 reduce-window.6
  17.0 0.1 slice.52
  17.1 0.1 copy.48
  17.2 0.1 copy.49
  18.1 2.6 %collective-permute-start.1 = (f32[64,2560]{1,0:T(8,128)S(1)}, f32[64,2560]{1,0:T(8,128)S(1)}, u32[]{:S(2)}, u32[]{:S(2)}) collective-permute-start(f32[64,2560]{1,0:T(8,128)S(1)} %fusion.63), channel_id=1, source_target_pairs={{0,2},{1,3},{2,0},{3,1},{4,6},{5,7},{6,4},{7,5},{8,10},{9,11},{10,... | collective-permute-start | bytes 1966088 | tf_op jit(solution)/shard_map/ppermute | solution.py:210
  20.8 0.7 maximum_bitcast_fusion.cos_ref
  21.5 0.2 multiply_cosine_fusion
  21.7 14.4 %collective-permute-done.1 = f32[64,2560]{1,0:T(8,128)S(1)} collective-permute-done((f32[64,2560]{1,0:T(8,128)S(1)}, f32[64,2560]{1,0:T(8,128)S(1)}, u32[]{:S(2)}, u32[]{:S(2)}) %collective-permute-start.1) | collective-permute-done | bytes 655392 | tf_op jit(solution)/shard_map/ppermute | solution.py:210
  36.2 0.1 copy.73
  36.3 0.2 fusion.67
  36.5 0.3 subtract_convert_fusion
  36.8 0.8 fusion.76
  37.7 0.2 reduce-scatter.2.cloned.1.call-start
  37.9 0.6 maximum_bitcast_fusion.1.sin_ref
  38.5 0.1 add_bitcast_fusion
  38.6 0.2 fusion.31
  38.8 0.7 fusion.35
  39.5 0.9 pad_maximum_fusion.1
  40.4 13.2 %shard_map.85 = (f32[2,512,128]{2,1,0:T(8,128)}, f32[2,512,1]{2,1,0:T(8,128)}, f32[2,512,1]{2,1,0:T(8,128)}) custom-call(s32[1]{0:T(128)} %bitcast.kv0_ref, bf16[2,512,128]{2,1,0:T(8,128)(2,1)} %bitcast.157, bf16[40,128,2048]{2,1,0:T(8,128)(2,1)} %bitcast.152, bf16[40,128,2048]{2,1,0:T(8,128)(2,1)} %bitcast.153, f32[1,1,5120]{2,1,0:T(1,128)} %bitcast.164, ...), custom_call_target="tpu_custom_call" | custom-call | tf_op jit(solution)/shard_map/pallas_call | solution.py:194
  53.6 1.2 copy.50
  54.8 12.5 %all-gather.2.cloned.1.call-done = bf16[64,64,128]{2,1,0:T(8,128)(2,1)} async-done(((bf16[16,64,128]{2,1,0:T(8,128)(2,1)}), bf16[64,64,128]{2,1,0:T(8,128)(2,1)}) %all-gather.2.cloned.1.call-update) | async-done | bytes 1048592 | tf_op jit(solution)/shard_map/all_gather | solution.py:290
  67.3 2.3 %fusion.20.q_ref = bf16[6,512,128]{2,1,0:T(8,128)(2,1)} fusion(s32[]{:T(128)S(6)} %select_n.216, bf16[8,512,128]{2,1,0:T(8,128)(2,1)} %bitcast.158), kind=kLoop, calls=%fused_computation.30 | loop fusion | flops 393216 | bytes 1835012 | tf_op jit(solution)/shard_map/concatenate | solution.py:298
  69.6 34.3 %shard_map.86 = (f32[6,512,128]{2,1,0:T(8,128)}, f32[6,512,1]{2,1,0:T(8,128)}, f32[6,512,1]{2,1,0:T(8,128)}) custom-call(s32[1]{0:T(128)} %bitcast.16.kv0_ref, bf16[6,512,128]{2,1,0:T(8,128)(2,1)} %fusion.20.q_ref, bf16[40,128,2048]{2,1,0:T(8,128)(2,1)} %bitcast.154, bf16[40,128,2048]{2,1,0:T(8,128)(2,1)} %bitcast.155, f32[1,1,5120]{2,1,0:T(1,128)} %bitcast.165, ...), custom_call_target="tpu_custom_call" | custom-call | tf_op jit(solution)/shard_map/pallas_call | solution.py:194
  103.9 2.1 %copy.51 = f32[6,512,1]{1,0,2:T(8,128)S(1)} copy(f32[6,512,1]{2,1,0:T(8,128)} %get-tuple-element.14) | data formatting | bytes 24576 | tf_op jit(solution)/shard_map/pallas_call | solution.py:194
  106.1 0.1 reshape.376
  106.2 1.2 collective-permute-done.2
  107.4 1.5 collective-permute-start.3
  108.8 0.2 copy.54
  109.0 2.2 %collective-permute-done.3 = f32[64,64]{1,0:T(8,128)S(1)} collective-permute-done((f32[64,64]{1,0:T(8,128)S(1)}, f32[64,64]{1,0:T(8,128)S(1)}, u32[]{:S(2)}, u32[]{:S(2)}) %collective-permute-start.3) | collective-permute-done | bytes 16416 | tf_op jit(solution)/shard_map/ppermute | solution.py:210
  111.3 1.4 collective-permute-start.4
  112.7 2.1 %fusion.2 = f32[8,512,128]{2,1,0:T(8,128)S(1)} fusion(s32[]{:T(128)S(6)} %select_n.217, f32[2,512,128]{2,1,0:T(8,128)} %get-tuple-element.11, f32[6,512,128]{2,1,0:T(8,128)} %get-tuple-element.12), kind=kLoop, calls=%fused_computation.8 | loop fusion | flops 1572864 | bytes 4194308 | tf_op jit(solution)/shard_map/concatenate | solution.py:303
  114.8 2.0 copy.55
  116.8 1.1 collective-permute-start.5
  117.9 0.1 reshape.377
  118.0 1.8 reshape.375
  119.8 2.2 %collective-permute-done.5 = f32[64,64]{1,0:T(8,128)S(1)} collective-permute-done((f32[64,64]{1,0:T(8,128)S(1)}, f32[64,64]{1,0:T(8,128)S(1)}, u32[]{:S(2)}, u32[]{:S(2)}) %collective-permute-start.5) | collective-permute-done | bytes 16416 | tf_op jit(solution)/shard_map/ppermute | solution.py:210
  122.1 0.6 mul.252
  122.7 1.8 mul.253
  124.5 2.8 %mul.254 = f32[2,2,2,2,4,8192]{5,4,3,2,1,0:T(4,128)S(1)} multiply(f32[2,2,2,2,4,8192]{5,4,3,2,1,0:T(4,128)} %reshape.375, f32[2,2,2,2,4,8192]{5,4,3,2,1,0:T(4,128)} %mul.253) | non-fusion elementwise | flops 524288 | bytes 6291456 | tf_op jit(solution)/shard_map/mul | solution.py:315
  127.3 1.2 fusion.16
  128.5 3.0 %collective-permute-done.6 = f32[2,2,2,4,8256]{4,3,0,1,2:T(4,128)} collective-permute-done((f32[2,2,2,4,8256]{4,3,0,1,2:T(4,128)}, f32[2,2,2,4,8256]{4,3,0,1,2:T(4,128)}, u32[]{:S(2)}, u32[]{:S(2)}) %collective-permute-start.6) | collective-permute-done | bytes 1056800 | tf_op jit(solution)/shard_map/ppermute | solution.py:223
  131.6 1.6 fusion.19
  133.2 0.1 constant_dynamic-slice_fusion.2
  133.3 1.6 collective-permute-start.7
  134.9 0.1 fusion.33
  135.0 0.1 reshape.379
  135.1 12.4 %collective-permute-done.7 = f32[2,2,4,8256]{3,2,1,0:T(4,128)S(1)} collective-permute-done((f32[2,2,4,8256]{3,2,1,0:T(4,128)S(1)}, f32[2,2,4,8256]{3,2,1,0:T(4,128)S(1)}, u32[]{:S(2)}, u32[]{:S(2)}) %collective-permute-start.7) | collective-permute-done | bytes 528416 | tf_op jit(solution)/shard_map/ppermute | solution.py:223
  147.5 0.1 bitcast_add_fusion
  147.7 0.4 collective-permute-start.8
  148.1 0.1 add_convert_fusion.1
  148.2 0.1 slice.58
  148.3 0.3 fusion.68
  148.6 6.8 %collective-permute-done.8 = f32[2,4,8256]{2,1,0:T(4,128)S(1)} collective-permute-done((f32[2,4,8256]{2,1,0:T(4,128)S(1)}, f32[2,4,8256]{2,1,0:T(4,128)S(1)}, u32[]{:S(2)}, u32[]{:S(2)}) %collective-permute-start.8) | collective-permute-done | bytes 264224 | tf_op jit(solution)/shard_map/ppermute | solution.py:223
  155.5 0.8 collective-permute-start.9
  156.3 6.6 %collective-permute-done.9 = f32[4,8256]{1,0:T(4,128)S(1)} collective-permute-done((f32[4,8256]{1,0:T(4,128)S(1)}, f32[4,8256]{1,0:T(4,128)S(1)}, u32[]{:S(2)}, u32[]{:S(2)}) %collective-permute-start.9) | collective-permute-done | bytes 132128 | tf_op jit(solution)/shard_map/ppermute | solution.py:223
  163.0 0.2 fusion.14
  163.2 5.8 %all_gather.7 = bf16[64,2048]{1,0:T(8,128)(2,1)S(1)} all-gather(bf16[64,512]{1,0:T(8,128)(2,1)S(1)} %bitcast.163), channel_id=1, replica_groups=mesh['groups'=2,'tensor'=4,'store'=4] {'store'}, dimensions={1}, use_global_device_ids=true | all-gather | bytes 327680 | tf_op jit(solution)/shard_map/all_gather | solution.py:357
  169.0 5.8 %fusion.70 = f32[64,2048]{1,0:T(8,128)} fusion(bf16[64,2048]{1,0:T(8,128)(2,1)S(1)} %all_gather.7, bf16[2048,2048]{1,0:T(8,128)(2,1)} %param.12), kind=kOutput, calls=%fused_computation.144 | convolution fusion | flops 536870912 | bytes 9175040 | tf_op jit(solution)/shard_map/dot_general | solution.py:384
  174.9 21.3 %reduce-scatter.2.cloned.1.call-done = f32[16,2048]{1,0:T(8,128)} async-done(((f32[64,2048]{1,0:T(8,128)}), f32[16,2048]{1,0:T(8,128)}) %reduce-scatter.2.cloned.1.call-update) | async-done | bytes 131088 | tf_op jit(solution)/shard_map/reduce_scatter | solution.py:383
  196.1 1.5 convert_element_type.48
  (50 shorter events, 1.0 us)
Async XLA Ops:
  6.5 1.0 copy-start
  6.5 60.8 %all-gather.2.cloned.1.call-start = ((), (), s32[]{:S(2)}) async-start(), calls=%async_computation.1 | async-start | bytes 1310720 | tf_op jit(solution)/shard_map/all_gather | solution.py:290
  12.4 3.3 %copy-start.3 = (s32[256,1]{0,1:T(1,128)S(1)}, s32[256,1]{0,1:T(1,128)}, u32[]{:S(2)}) copy-start(s32[256,1]{0,1:T(1,128)} %param.14) | copy-start | bytes 3076
  14.6 3.5 %collective-permute-start = (f32[64,2560]{1,0:T(8,128)S(1)}, f32[64,2560]{1,0:T(8,128)S(1)}, u32[]{:S(2)}, u32[]{:S(2)}) collective-permute-start(f32[64,2560]{1,0:T(8,128)S(1)} %pad_maximum_fusion), channel_id=1, source_target_pairs={{0,1},{1,0},{2,3},{3,2},{4,5},{5,4},{6,7},{7,6},{8,9},{9,8},{10,11... | collective-permute-start | bytes 1966088 | tf_op jit(solution)/shard_map/ppermute | solution.py:210
  18.1 18.0 %collective-permute-start.1 = (f32[64,2560]{1,0:T(8,128)S(1)}, f32[64,2560]{1,0:T(8,128)S(1)}, u32[]{:S(2)}, u32[]{:S(2)}) collective-permute-start(f32[64,2560]{1,0:T(8,128)S(1)} %fusion.63), channel_id=1, source_target_pairs={{0,2},{1,3},{2,0},{3,1},{4,6},{5,7},{6,4},{7,5},{8,10},{9,11},{10,... | collective-permute-start | bytes 1966088 | tf_op jit(solution)/shard_map/ppermute | solution.py:210
  37.7 158.4 %reduce-scatter.2.cloned.1.call-start = ((), (), s32[]{:S(2)}) async-start(), calls=%async_computation.2 | async-start | bytes 655360 | tf_op jit(solution)/shard_map/reduce_scatter | solution.py:383
  103.9 4.9 %copy-start.2 = (f32[2,512,1]{2,1,0:T(8,128)S(1)}, f32[2,512,1]{2,1,0:T(8,128)}, u32[]{:S(2)}) copy-start(f32[2,512,1]{2,1,0:T(8,128)} %get-tuple-element.15) | copy-start | bytes 12292
  106.1 1.2 collective-permute-start.2
  107.4 3.9 %collective-permute-start.3 = (f32[64,64]{1,0:T(8,128)S(1)}, f32[64,64]{1,0:T(8,128)S(1)}, u32[]{:S(2)}, u32[]{:S(2)}) collective-permute-start(f32[64,64]{1,0:T(8,128)S(1)} %max.15), channel_id=1, source_target_pairs={{0,2},{1,3},{2,0},{3,1},{4,6},{5,7},{6,4},{7,5},{8,10},{9,11},{10,... | collective-permute-start | bytes 49160 | tf_op jit(solution)/shard_map/ppermute | solution.py:210
  111.3 5.5 %collective-permute-start.4 = (f32[64,64]{1,0:T(8,128)S(1)}, f32[64,64]{1,0:T(8,128)S(1)}, u32[]{:S(2)}, u32[]{:S(2)}) collective-permute-start(f32[64,64]{1,0:T(8,128)S(1)} %max.16), channel_id=1, source_target_pairs={{0,4},{4,0},{8,12},{12,8},{1,5},{5,1},{9,13},{13,9},{2,6},{6,2},{1... | collective-permute-start | bytes 49160 | tf_op jit(solution)/shard_map/ppermute | solution.py:210
  116.8 5.2 %collective-permute-start.5 = (f32[64,64]{1,0:T(8,128)S(1)}, f32[64,64]{1,0:T(8,128)S(1)}, u32[]{:S(2)}, u32[]{:S(2)}) collective-permute-start(f32[64,64]{1,0:T(8,128)S(1)} %max.17), channel_id=1, source_target_pairs={{0,8},{4,12},{8,0},{12,4},{1,9},{5,13},{9,1},{13,5},{2,10},{6,14},... | collective-permute-start | bytes 49160 | tf_op jit(solution)/shard_map/ppermute | solution.py:210
  128.5 3.0 %collective-permute-start.6 = (f32[2,2,2,4,8256]{4,3,0,1,2:T(4,128)}, f32[2,2,2,4,8256]{4,3,0,1,2:T(4,128)}, u32[]{:S(2)}, u32[]{:S(2)}) collective-permute-start(f32[2,2,2,4,8256]{4,3,0,1,2:T(4,128)} %fusion.16), channel_id=1, source_target_pairs={{0,1},{1,0},{2,3},{3,2},{4,5},{5,4},{6,7},{7,6},{8,9},{9,8},{10,11... | collective-permute-start | bytes 3170312 | tf_op jit(solution)/shard_map/ppermute | solution.py:223
  133.3 14.2 %collective-permute-start.7 = (f32[2,2,4,8256]{3,2,1,0:T(4,128)S(1)}, f32[2,2,4,8256]{3,2,1,0:T(4,128)S(1)}, u32[]{:S(2)}, u32[]{:S(2)}) collective-permute-start(f32[2,2,4,8256]{3,2,1,0:T(4,128)S(1)} %bitcast.160), channel_id=1, source_target_pairs={{0,2},{1,3},{2,0},{3,1},{4,6},{5,7},{6,4},{7,5},{8,10},{9,11},{10,... | collective-permute-start | bytes 1585160 | tf_op jit(solution)/shard_map/ppermute | solution.py:223
  147.7 7.7 %collective-permute-start.8 = (f32[2,4,8256]{2,1,0:T(4,128)S(1)}, f32[2,4,8256]{2,1,0:T(4,128)S(1)}, u32[]{:S(2)}, u32[]{:S(2)}) collective-permute-start(f32[2,4,8256]{2,1,0:T(4,128)S(1)} %dynamic-slice_bitcast_fusion), channel_id=1, source_target_pairs={{0,4},{4,0},{8,12},{12,8},{1,5},{5,1},{9,13},{13,9},{2,6},{6,2},{1... | collective-permute-start | bytes 792584 | tf_op jit(solution)/shard_map/ppermute | solution.py:223
  155.5 7.4 %collective-permute-start.9 = (f32[4,8256]{1,0:T(4,128)S(1)}, f32[4,8256]{1,0:T(4,128)S(1)}, u32[]{:S(2)}, u32[]{:S(2)}) collective-permute-start(f32[4,8256]{1,0:T(4,128)S(1)} %dynamic-slice_bitcast_fusion.1), channel_id=1, source_target_pairs={{0,8},{4,12},{8,0},{12,4},{1,9},{5,13},{9,1},{13,5},{2,10},{6,14},... | collective-permute-start | bytes 396296 | tf_op jit(solution)/shard_map/ppermute | solution.py:223
  169.0 28.6 %copy-start.1 = (bf16[64,2048]{1,0:T(8,128)(2,1)S(1)}, bf16[64,2048]{1,0:T(8,128)(2,1)}, u32[]{:S(2)}) copy-start(bf16[64,2048]{1,0:T(8,128)(2,1)} %param.8) | copy-start | bytes 786436
Sparse Core Ops, SparseCore 0:
  37.8 29.4 all-gather.1
  175.0 21.1 reduce-scatter.1

commit v10 on v9

--- a/solution.py
+++ b/solution.py
@@ -223,6 +223,33 @@
         block = keep + lax.ppermute(send, axis, perm=[(i, i ^ d) for i in range(n)])
         d *= 2
     return block
+
+
+def bit_gather(x, axis):
+    n = lax.axis_size(axis)
+    idx = lax.axis_index(axis)
+    dists = []
+    d = n // 2
+    while d >= 1:
+        other = lax.ppermute(x, axis, perm=[(i, i ^ d) for i in range(n)])
+        low = (idx // d) % 2 == 0
+        x = jnp.stack([jnp.where(low, x, other), jnp.where(low, other, x)])
+        dists.insert(0, d)
+        d //= 2
+    k = len(dists)
+    order = sorted(range(k), key=lambda j: -dists[j])
+    x = jnp.transpose(x, tuple(order) + tuple(range(k, x.ndim)))
+    return x.reshape((n * x.shape[k],) + x.shape[k + 1 :])
+
+
+def scatter_rows(x, axis):
+    n = lax.axis_size(axis)
+    if n & (n - 1):
+        return lax.psum_scatter(x, axis, scatter_dimension=0, tiled=True)
+    bits = n.bit_length() - 1
+    x = x.reshape((2,) * bits + (x.shape[0] // n,) + x.shape[1:])
+    x = jnp.transpose(x, tuple(range(bits - 1, -1, -1)) + tuple(range(bits, x.ndim)))
+    return bit_scatter(x, axis)
 
 
 def axis_sum(x, axis):
@@ -287,7 +314,10 @@
     sin2 = jnp.concatenate([-sine, sine])[None, :]
 
     q_heads = jnp.transpose(query_rot, (1, 0, 2))
-    q_all = lax.all_gather(q_heads, "tensor", axis=0, tiled=True)
+    if tensors & (tensors - 1):
+        q_all = lax.all_gather(q_heads, "tensor", axis=0, tiled=True)
+    else:
+        q_all = bit_gather(q_heads, "tensor")
     q_k = q_all.reshape(kv_heads, group_size * tok_count, HD)
     if local_heads % group_size == 0:
         own = hist_attend(
@@ -380,12 +410,7 @@
             .reshape(tok_count, local_heads * HD)
             .astype(jnp.bfloat16)
         )
-    result = lax.psum_scatter(
-        jnp.dot(attended, w_out, preferred_element_type=jnp.float32),
-        "tensor",
-        scatter_dimension=0,
-        tiled=True,
-    )
+    result = scatter_rows(jnp.dot(attended, w_out, preferred_element_type=jnp.float32), "tensor")
     return result.astype(jnp.bfloat16)
 
 

time: 205 us -> 187 us (0.912)
  between operations: 15 us -> 1.7 us
  waiting for transfers between devices: 82.6 us -> 70.3 us
  starting transfers between devices: 10 us -> 20.3 us
  other arithmetic: 18.3 us -> 16.1 us
    reduce_scatter x1 -> x0, waiting for transfers between devices: 21.3 us -> none  [body(): lax.psum_scatter(jnp.dot(attended, w_out, preferred_element_type=jnp.floa...]
    all_gather x1 -> x0, waiting for transfers between devices: 12.5 us -> none  [body(): q_all = lax.all_gather(q_heads, 'tensor', axis=0, tiled=True)]
    ppermute x4 -> x6, waiting for transfers between devices: 28.8 us -> 40.6 us  [bit_scatter(): block = keep + lax.ppermute(send, axis, perm=[(i, i ^ d) for i in range(n)])]
    ppermute x0 -> x2, waiting for transfers between devices: none -> 11.2 us  [bit_gather(): other = lax.ppermute(x, axis, perm=[(i, i ^ d) for i in range(n)])]
    ppermute x4 -> x6, starting transfers between devices: 2.73 us -> 8.55 us  [bit_scatter(): block = keep + lax.ppermute(send, axis, perm=[(i, i ^ d) for i in range(n)])]
    ppermute x0 -> x2, starting transfers between devices: none -> 3.69 us  [bit_gather(): other = lax.ppermute(x, axis, perm=[(i, i ^ d) for i in range(n)])]
  transfers between devices with their start and end apart: 12 -> 14, of which waited for: 10 -> 11; matrix products, arithmetic and copies ran while one was open for 6% -> 7% of each run, Pallas kernels for 6% -> 7%
where the time goes in v10:
time: 187 us; the launch traced here: 186 us
  waiting for transfers between devices  70.3 us (38%)
  Pallas kernels  47.5 us (25%)
  starting transfers between devices  20.3 us (11%)
  other arithmetic  16.1 us (9%)
  matrix products  12.5 us (7%)
  local copies, waits for them, and re-layouts  12 us (6%)
  blocking collectives  5.8 us (3%)
    pallas_call x2, Pallas kernels, hist_attend(): pl.pallas_call(kernel, grid_spec=grid_spec, out_shape=[jax.ShapeDtypeStru...  47.5 us
    ppermute x6, waiting for transfers between devices, bit_scatter(): block = keep + lax.ppermute(send, axis, perm=[(i, i ^ d) for i in range(n)])  40.6 us
    ppermute x6, waiting for transfers between devices, axis_reduce(): x = op(x, lax.ppermute(x, axis, perm=[(i, i ^ d) for i in range(n)]))  18.6 us
    ppermute x2, waiting for transfers between devices, bit_gather(): other = lax.ppermute(x, axis, perm=[(i, i ^ d) for i in range(n)])  11.2 us
    ppermute x6, starting transfers between devices, bit_scatter(): block = keep + lax.ppermute(send, axis, perm=[(i, i ^ d) for i in range(n)])  8.55 us
    ppermute x6, starting transfers between devices, axis_reduce(): x = op(x, lax.ppermute(x, axis, perm=[(i, i ^ d) for i in range(n)]))  8.07 us
    all_gather x1, blocking collectives, body(): attended = lax.all_gather(attended, 'store', axis=1, tiled=True)  5.8 us
    pallas_call x4, local copies, waits for them, and re-layouts, hist_attend(): pl.pallas_call(kernel, grid_spec=grid_spec, out_shape=[jax.ShapeDtypeStru...  5.5 us
  transfers between devices with their start and end apart: 14, of which 11 were waited for; matrix products, arithmetic and copies ran while one was open for 7% of the time, Pallas kernels for 7%

profile of v10, /device:TPU:0, one launch (start us, length us, event | category | flops | bytes accessed | tf_op | source)
XLA Modules:
  0.0 186.3 jit_solution(2648329289887269340)
XLA Ops:
  0.0 0.9 copy-done
  1.0 4.9 %fusion.70 = f32[64,2048]{1,0:T(8,128)S(1)} fusion(bf16[64,2048]{1,0:T(8,128)(2,1)S(1)} %copy-done, bf16[2048,2048]{1,0:T(8,128)(2,1)} %param.10), kind=kOutput, calls=%fused_computation.154 | convolution fusion | flops 536870912 | bytes 9175040 | tf_op jit(solution)/shard_map/dot_general | solution.py:288
  5.9 2.1 %fusion.5 = f32[64,512]{1,0:T(8,128)S(1)} fusion(bf16[64,2048]{1,0:T(8,128)(2,1)S(1)} %copy-done, bf16[2048,2048]{1,0:T(8,128)(2,1)} %param.11, s32[]{:T(128)S(6)} %select_n.246), kind=kOutput, calls=%fused_computation.15 | convolution fusion | flops 134217728 | bytes 2490372 | tf_op jit(solution)/shard_map/dot_general | solution.py:289
  8.0 0.5 collective-permute-start
  9.3 1.2 reduce-window.6
  10.6 0.1 copy.51
  10.7 0.1 copy.52
  11.8 2.6 %collective-permute-start.1 = (f32[64,2560]{1,0:T(8,128)S(1)}, f32[64,2560]{1,0:T(8,128)S(1)}, u32[]{:S(2)}, u32[]{:S(2)}) collective-permute-start(f32[64,2560]{1,0:T(8,128)S(1)} %fusion.64), channel_id=1, source_target_pairs={{0,2},{1,3},{2,0},{3,1},{4,6},{5,7},{6,4},{7,5},{8,10},{9,11},{10,... | collective-permute-start | bytes 1966088 | tf_op jit(solution)/shard_map/ppermute | solution.py:210
  14.4 0.6 maximum_bitcast_fusion.1.cos_ref
  15.0 0.2 fusion.32
  15.2 0.2 multiply_cosine_fusion
  15.4 14.4 %collective-permute-done.1 = f32[64,2560]{1,0:T(8,128)S(1)} collective-permute-done((f32[64,2560]{1,0:T(8,128)S(1)}, f32[64,2560]{1,0:T(8,128)S(1)}, u32[]{:S(2)}, u32[]{:S(2)}) %collective-permute-start.1) | collective-permute-done | bytes 655392 | tf_op jit(solution)/shard_map/ppermute | solution.py:210
  29.9 0.1 copy.77
  30.0 0.2 fusion.68
  30.2 0.3 subtract_convert_fusion
  30.5 0.2 fusion.77
  30.7 2.9 %collective-permute-start.2 = (bf16[16,64,128]{2,1,0:T(8,128)(2,1)S(1)}, bf16[16,64,128]{2,1,0:T(8,128)(2,1)S(1)}, u32[]{:S(2)}, u32[]{:S(2)}) collective-permute-start(bf16[16,64,128]{2,1,0:T(8,128)(2,1)S(1)} %fusion.77), channel_id=1, source_target_pairs={{0,8},{4,12},{8,0},{12,4},{1,9},{5,13},{9,1},{13,5},{2,10},{6,14},... | collective-permute-start | bytes 786440 | tf_op jit(solution)/shard_map/ppermute | solution.py:234
  33.6 0.6 maximum_bitcast_fusion.2.sin_ref
  34.2 11.2 %collective-permute-done.2 = bf16[16,64,128]{2,1,0:T(8,128)(2,1)S(1)} collective-permute-done((bf16[16,64,128]{2,1,0:T(8,128)(2,1)S(1)}, bf16[16,64,128]{2,1,0:T(8,128)(2,1)S(1)}, u32[]{:S(2)}, u32[]{:S(2)}) %collective-permute-start.2) | collective-permute-done | bytes 262176 | tf_op jit(solution)/shard_map/ppermute | solution.py:234
  45.4 0.2 select_bitcast_fusion.3
  45.7 0.8 collective-permute-start.3
  46.5 0.7 fusion.36
  47.2 0.8 pad_maximum_fusion.2
  48.0 13.2 %shard_map.85 = (f32[2,512,128]{2,1,0:T(8,128)}, f32[2,512,1]{2,1,0:T(8,128)}, f32[2,512,1]{2,1,0:T(8,128)}) custom-call(s32[1]{0:T(128)} %bitcast.kv0_ref, bf16[2,512,128]{2,1,0:T(8,128)(2,1)} %bitcast.183, bf16[40,128,2048]{2,1,0:T(8,128)(2,1)} %bitcast.175, bf16[40,128,2048]{2,1,0:T(8,128)(2,1)} %bitcast.176, f32[1,1,5120]{2,1,0:T(1,128)} %bitcast.189, ...), custom_call_target="tpu_custom_call" | custom-call | tf_op jit(solution)/shard_map/pallas_call | solution.py:194
  61.2 1.2 copy.54
  62.5 0.1 select_bitcast_fusion.1
  62.6 0.1 maximum_bitcast_fusion
  62.7 1.2 fusion.20.q_ref
  64.0 34.3 %shard_map.86 = (f32[6,512,128]{2,1,0:T(8,128)}, f32[6,512,1]{2,1,0:T(8,128)}, f32[6,512,1]{2,1,0:T(8,128)}) custom-call(s32[1]{0:T(128)} %bitcast.16.kv0_ref, bf16[6,512,128]{2,1,0:T(8,128)(2,1)} %fusion.20.q_ref, bf16[40,128,2048]{2,1,0:T(8,128)(2,1)} %bitcast.177, bf16[40,128,2048]{2,1,0:T(8,128)(2,1)} %bitcast.178, f32[1,1,5120]{2,1,0:T(1,128)} %bitcast.190, ...), custom_call_target="tpu_custom_call" | custom-call | tf_op jit(solution)/shard_map/pallas_call | solution.py:194
  98.3 2.1 %copy.55 = f32[6,512,1]{1,0,2:T(8,128)S(1)} copy(f32[6,512,1]{2,1,0:T(8,128)} %get-tuple-element.14) | data formatting | bytes 24576 | tf_op jit(solution)/shard_map/pallas_call | solution.py:194
  100.5 1.2 collective-permute-done.4
  101.7 1.5 collective-permute-start.5
  103.2 0.2 copy.58
  103.4 2.2 %collective-permute-done.5 = f32[64,64]{1,0:T(8,128)S(1)} collective-permute-done((f32[64,64]{1,0:T(8,128)S(1)}, f32[64,64]{1,0:T(8,128)S(1)}, u32[]{:S(2)}, u32[]{:S(2)}) %collective-permute-start.5) | collective-permute-done | bytes 16416 | tf_op jit(solution)/shard_map/ppermute | solution.py:210
  105.6 1.3 collective-permute-start.6
  106.9 2.1 %fusion.2 = f32[8,512,128]{2,1,0:T(8,128)S(1)} fusion(s32[]{:T(128)S(6)} %select_n.268, f32[2,512,128]{2,1,0:T(8,128)} %get-tuple-element.11, f32[6,512,128]{2,1,0:T(8,128)} %get-tuple-element.12), kind=kLoop, calls=%fused_computation.8 | loop fusion | flops 1572864 | bytes 4194308 | tf_op jit(solution)/shard_map/concatenate | solution.py:333
  109.1 2.0 %copy.59 = f32[6,512,1]{1,0,2:T(8,128)S(1)} copy(f32[6,512,1]{2,1,0:T(8,128)} %get-tuple-element.16) | data formatting | bytes 24576 | tf_op jit(solution)/shard_map/pallas_call | solution.py:194
  111.1 2.2 %collective-permute-start.7 = (f32[64,64]{1,0:T(8,128)S(1)}, f32[64,64]{1,0:T(8,128)S(1)}, u32[]{:S(2)}, u32[]{:S(2)}) collective-permute-start(f32[64,64]{1,0:T(8,128)S(1)} %max.17), channel_id=1, source_target_pairs={{0,8},{4,12},{8,0},{12,4},{1,9},{5,13},{9,1},{13,5},{2,10},{6,14},... | collective-permute-start | bytes 49160 | tf_op jit(solution)/shard_map/ppermute | solution.py:210
  113.4 1.8 reshape.378
  115.2 0.8 collective-permute-done.7
  116.0 0.6 mul.252
  116.6 1.8 mul.253
  118.4 2.8 %mul.254 = f32[2,2,2,2,4,8192]{5,4,3,2,1,0:T(4,128)S(1)} multiply(f32[2,2,2,2,4,8192]{5,4,3,2,1,0:T(4,128)} %reshape.378, f32[2,2,2,2,4,8192]{5,4,3,2,1,0:T(4,128)} %mul.253) | non-fusion elementwise | flops 524288 | bytes 6291456 | tf_op jit(solution)/shard_map/mul | solution.py:345
  121.2 1.2 fusion.16
  122.4 3.0 %collective-permute-done.8 = f32[2,2,2,4,8256]{4,3,0,1,2:T(4,128)} collective-permute-done((f32[2,2,2,4,8256]{4,3,0,1,2:T(4,128)}, f32[2,2,2,4,8256]{4,3,0,1,2:T(4,128)}, u32[]{:S(2)}, u32[]{:S(2)}) %collective-permute-start.8) | collective-permute-done | bytes 1056800 | tf_op jit(solution)/shard_map/ppermute | solution.py:223
  125.5 1.6 fusion.19
  127.2 1.6 collective-permute-start.9
  128.9 0.1 reshape.382
  129.1 12.3 %collective-permute-done.9 = f32[2,2,4,8256]{3,2,1,0:T(4,128)S(1)} collective-permute-done((f32[2,2,4,8256]{3,2,1,0:T(4,128)S(1)}, f32[2,2,4,8256]{3,2,1,0:T(4,128)S(1)}, u32[]{:S(2)}, u32[]{:S(2)}) %collective-permute-start.9) | collective-permute-done | bytes 528416 | tf_op jit(solution)/shard_map/ppermute | solution.py:223
  141.4 0.1 bitcast_add_fusion
  141.6 1.3 collective-permute-start.10
  142.9 0.1 add_convert_fusion.1
  143.1 0.3 fusion.69
  143.3 5.9 %collective-permute-done.10 = f32[2,4,8256]{2,1,0:T(4,128)S(1)} collective-permute-done((f32[2,4,8256]{2,1,0:T(4,128)S(1)}, f32[2,4,8256]{2,1,0:T(4,128)S(1)}, u32[]{:S(2)}, u32[]{:S(2)}) %collective-permute-start.10) | collective-permute-done | bytes 264224 | tf_op jit(solution)/shard_map/ppermute | solution.py:223
  149.4 2.4 %collective-permute-start.11 = (f32[4,8256]{1,0:T(4,128)S(1)}, f32[4,8256]{1,0:T(4,128)S(1)}, u32[]{:S(2)}, u32[]{:S(2)}) collective-permute-start(f32[4,8256]{1,0:T(4,128)S(1)} %dynamic-slice_bitcast_fusion.2), channel_id=1, source_target_pairs={{0,8},{4,12},{8,0},{12,4},{1,9},{5,13},{9,1},{13,5},{2,10},{6,14},... | collective-permute-start | bytes 396296 | tf_op jit(solution)/shard_map/ppermute | solution.py:223
  151.9 5.1 %collective-permute-done.11 = f32[4,8256]{1,0:T(4,128)S(1)} collective-permute-done((f32[4,8256]{1,0:T(4,128)S(1)}, f32[4,8256]{1,0:T(4,128)S(1)}, u32[]{:S(2)}, u32[]{:S(2)}) %collective-permute-start.11) | collective-permute-done | bytes 132128 | tf_op jit(solution)/shard_map/ppermute | solution.py:223
  157.1 0.2 fusion.14
  157.4 5.8 %all_gather.3 = bf16[64,2048]{1,0:T(8,128)(2,1)S(1)} all-gather(bf16[64,512]{1,0:T(8,128)(2,1)S(1)} %bitcast.188), channel_id=1, replica_groups=mesh['groups'=2,'tensor'=4,'store'=4] {'store'}, dimensions={1}, use_global_device_ids=true | all-gather | bytes 327680 | tf_op jit(solution)/shard_map/all_gather | solution.py:387
  163.2 5.0 %fusion.71 = f32[64,2048]{1,0:T(8,128)S(1)} fusion(bf16[64,2048]{1,0:T(8,128)(2,1)S(1)} %all_gather.3, bf16[2048,2048]{1,0:T(8,128)(2,1)} %param.12), kind=kOutput, calls=%fused_computation.155 | convolution fusion | flops 536870912 | bytes 9175040 | tf_op jit(solution)/shard_map/dot_general | solution.py:413
  168.2 0.8 collective-permute-start.12
  169.0 7.8 %collective-permute-done.12 = f32[2,16,2048]{2,1,0:T(8,128)S(1)} collective-permute-done((f32[2,16,2048]{2,1,0:T(8,128)S(1)}, f32[2,16,2048]{2,1,0:T(8,128)S(1)}, u32[]{:S(2)}, u32[]{:S(2)}) %collective-permute-start.12) | collective-permute-done | bytes 262176 | tf_op jit(solution)/shard_map/ppermute | solution.py:223
  176.9 2.4 %collective-permute-start.13 = (f32[16,2048]{1,0:T(8,128)S(1)}, f32[16,2048]{1,0:T(8,128)S(1)}, u32[]{:S(2)}, u32[]{:S(2)}) collective-permute-start(f32[16,2048]{1,0:T(8,128)S(1)} %dynamic-slice_bitcast_fusion.3), channel_id=1, source_target_pairs={{0,8},{4,12},{8,0},{12,4},{1,9},{5,13},{9,1},{13,5},{2,10},{6,14},... | collective-permute-start | bytes 393224 | tf_op jit(solution)/shard_map/ppermute | solution.py:223
  179.3 6.3 %collective-permute-done.13 = f32[16,2048]{1,0:T(8,128)S(1)} collective-permute-done((f32[16,2048]{1,0:T(8,128)S(1)}, f32[16,2048]{1,0:T(8,128)S(1)}, u32[]{:S(2)}, u32[]{:S(2)}) %collective-permute-start.13) | collective-permute-done | bytes 131104 | tf_op jit(solution)/shard_map/ppermute | solution.py:223
  185.6 0.6 fusion.22
  (60 shorter events, 1.7 us)
Async XLA Ops:
  0.0 1.0 copy-start
  5.9 3.4 %copy-start.3 = (s32[256,1]{0,1:T(1,128)S(1)}, s32[256,1]{0,1:T(1,128)}, u32[]{:S(2)}) copy-start(s32[256,1]{0,1:T(1,128)} %param.14) | copy-start | bytes 3076
  8.0 3.7 %collective-permute-start = (f32[64,2560]{1,0:T(8,128)S(1)}, f32[64,2560]{1,0:T(8,128)S(1)}, u32[]{:S(2)}, u32[]{:S(2)}) collective-permute-start(f32[64,2560]{1,0:T(8,128)S(1)} %pad_maximum_fusion), channel_id=1, source_target_pairs={{0,1},{1,0},{2,3},{3,2},{4,5},{5,4},{6,7},{7,6},{8,9},{9,8},{10,11... | collective-permute-start | bytes 1966088 | tf_op jit(solution)/shard_map/ppermute | solution.py:210
  11.8 18.0 %collective-permute-start.1 = (f32[64,2560]{1,0:T(8,128)S(1)}, f32[64,2560]{1,0:T(8,128)S(1)}, u32[]{:S(2)}, u32[]{:S(2)}) collective-permute-start(f32[64,2560]{1,0:T(8,128)S(1)} %fusion.64), channel_id=1, source_target_pairs={{0,2},{1,3},{2,0},{3,1},{4,6},{5,7},{6,4},{7,5},{8,10},{9,11},{10,... | collective-permute-start | bytes 1966088 | tf_op jit(solution)/shard_map/ppermute | solution.py:210
  30.7 14.7 %collective-permute-start.2 = (bf16[16,64,128]{2,1,0:T(8,128)(2,1)S(1)}, bf16[16,64,128]{2,1,0:T(8,128)(2,1)S(1)}, u32[]{:S(2)}, u32[]{:S(2)}) collective-permute-start(bf16[16,64,128]{2,1,0:T(8,128)(2,1)S(1)} %fusion.77), channel_id=1, source_target_pairs={{0,8},{4,12},{8,0},{12,4},{1,9},{5,13},{9,1},{13,5},{2,10},{6,14},... | collective-permute-start | bytes 786440 | tf_op jit(solution)/shard_map/ppermute | solution.py:234
  45.7 16.8 %collective-permute-start.3 = (bf16[2,16,64,128]{3,2,1,0:T(8,128)(2,1)S(1)}, bf16[2,16,64,128]{3,2,1,0:T(8,128)(2,1)S(1)}, u32[]{:S(2)}, u32[]{:S(2)}) collective-permute-start(bf16[2,16,64,128]{3,2,1,0:T(8,128)(2,1)S(1)} %pad_maximum_fusion.1), channel_id=1, source_target_pairs={{0,4},{4,0},{8,12},{12,8},{1,5},{5,1},{9,13},{13,9},{2,6},{6,2},{1... | collective-permute-start | bytes 1572872 | tf_op jit(solution)/shard_map/ppermute | solution.py:234
  98.3 4.9 %copy-start.2 = (f32[2,512,1]{2,1,0:T(8,128)S(1)}, f32[2,512,1]{2,1,0:T(8,128)}, u32[]{:S(2)}) copy-start(f32[2,512,1]{2,1,0:T(8,128)} %get-tuple-element.15) | copy-start | bytes 12292
  100.5 1.2 collective-permute-start.4
  101.7 3.9 %collective-permute-start.5 = (f32[64,64]{1,0:T(8,128)S(1)}, f32[64,64]{1,0:T(8,128)S(1)}, u32[]{:S(2)}, u32[]{:S(2)}) collective-permute-start(f32[64,64]{1,0:T(8,128)S(1)} %max.15), channel_id=1, source_target_pairs={{0,2},{1,3},{2,0},{3,1},{4,6},{5,7},{6,4},{7,5},{8,10},{9,11},{10,... | collective-permute-start | bytes 49160 | tf_op jit(solution)/shard_map/ppermute | solution.py:210
  105.6 5.4 %collective-permute-start.6 = (f32[64,64]{1,0:T(8,128)S(1)}, f32[64,64]{1,0:T(8,128)S(1)}, u32[]{:S(2)}, u32[]{:S(2)}) collective-permute-start(f32[64,64]{1,0:T(8,128)S(1)} %max.16), channel_id=1, source_target_pairs={{0,4},{4,0},{8,12},{12,8},{1,5},{5,1},{9,13},{13,9},{2,6},{6,2},{1... | collective-permute-start | bytes 49160 | tf_op jit(solution)/shard_map/ppermute | solution.py:210
  111.1 4.9 %collective-permute-start.7 = (f32[64,64]{1,0:T(8,128)S(1)}, f32[64,64]{1,0:T(8,128)S(1)}, u32[]{:S(2)}, u32[]{:S(2)}) collective-permute-start(f32[64,64]{1,0:T(8,128)S(1)} %max.17), channel_id=1, source_target_pairs={{0,8},{4,12},{8,0},{12,4},{1,9},{5,13},{9,1},{13,5},{2,10},{6,14},... | collective-permute-start | bytes 49160 | tf_op jit(solution)/shard_map/ppermute | solution.py:210
  122.4 3.0 %collective-permute-start.8 = (f32[2,2,2,4,8256]{4,3,0,1,2:T(4,128)}, f32[2,2,2,4,8256]{4,3,0,1,2:T(4,128)}, u32[]{:S(2)}, u32[]{:S(2)}) collective-permute-start(f32[2,2,2,4,8256]{4,3,0,1,2:T(4,128)} %fusion.16), channel_id=1, source_target_pairs={{0,1},{1,0},{2,3},{3,2},{4,5},{5,4},{6,7},{7,6},{8,9},{9,8},{10,11... | collective-permute-start | bytes 3170312 | tf_op jit(solution)/shard_map/ppermute | solution.py:223
  127.2 14.2 %collective-permute-start.9 = (f32[2,2,4,8256]{3,2,1,0:T(4,128)S(1)}, f32[2,2,4,8256]{3,2,1,0:T(4,128)S(1)}, u32[]{:S(2)}, u32[]{:S(2)}) collective-permute-start(f32[2,2,4,8256]{3,2,1,0:T(4,128)S(1)} %bitcast.185), channel_id=1, source_target_pairs={{0,2},{1,3},{2,0},{3,1},{4,6},{5,7},{6,4},{7,5},{8,10},{9,11},{10,... | collective-permute-start | bytes 1585160 | tf_op jit(solution)/shard_map/ppermute | solution.py:223
  141.6 7.7 %collective-permute-start.10 = (f32[2,4,8256]{2,1,0:T(4,128)S(1)}, f32[2,4,8256]{2,1,0:T(4,128)S(1)}, u32[]{:S(2)}, u32[]{:S(2)}) collective-permute-start(f32[2,4,8256]{2,1,0:T(4,128)S(1)} %dynamic-slice_bitcast_fusion), channel_id=1, source_target_pairs={{0,4},{4,0},{8,12},{12,8},{1,5},{5,1},{9,13},{13,9},{2,6},{6,2},{1... | collective-permute-start | bytes 792584 | tf_op jit(solution)/shard_map/ppermute | solution.py:223
  149.4 7.7 %collective-permute-start.11 = (f32[4,8256]{1,0:T(4,128)S(1)}, f32[4,8256]{1,0:T(4,128)S(1)}, u32[]{:S(2)}, u32[]{:S(2)}) collective-permute-start(f32[4,8256]{1,0:T(4,128)S(1)} %dynamic-slice_bitcast_fusion.2), channel_id=1, source_target_pairs={{0,8},{4,12},{8,0},{12,4},{1,9},{5,13},{9,1},{13,5},{2,10},{6,14},... | collective-permute-start | bytes 396296 | tf_op jit(solution)/shard_map/ppermute | solution.py:223
  163.2 23.1 %copy-start.1 = (bf16[64,2048]{1,0:T(8,128)(2,1)S(1)}, bf16[64,2048]{1,0:T(8,128)(2,1)}, u32[]{:S(2)}) copy-start(bf16[64,2048]{1,0:T(8,128)(2,1)} %param.8) | copy-start | bytes 786436
  168.2 8.6 %collective-permute-start.12 = (f32[2,16,2048]{2,1,0:T(8,128)S(1)}, f32[2,16,2048]{2,1,0:T(8,128)S(1)}, u32[]{:S(2)}, u32[]{:S(2)}) collective-permute-start(f32[2,16,2048]{2,1,0:T(8,128)S(1)} %dynamic-slice_bitcast_fusion.1), channel_id=1, source_target_pairs={{0,4},{4,0},{8,12},{12,8},{1,5},{5,1},{9,13},{13,9},{2,6},{6,2},{1... | collective-permute-start | bytes 786440 | tf_op jit(solution)/shard_map/ppermute | solution.py:223
  176.9 8.7 %collective-permute-start.13 = (f32[16,2048]{1,0:T(8,128)S(1)}, f32[16,2048]{1,0:T(8,128)S(1)}, u32[]{:S(2)}, u32[]{:S(2)}) collective-permute-start(f32[16,2048]{1,0:T(8,128)S(1)} %dynamic-slice_bitcast_fusion.3), channel_id=1, source_target_pairs={{0,8},{4,12},{8,0},{12,4},{1,9},{5,13},{9,1},{13,5},{2,10},{6,14},... | collective-permute-start | bytes 393224 | tf_op jit(solution)/shard_map/ppermute | solution.py:223

commit v11 on v10

--- a/solution.py
+++ b/solution.py
@@ -200,6 +200,11 @@
             jax.ShapeDtypeStruct((heads, rows, 1), jnp.float32),
         ],
         compiler_params=pltpu.CompilerParams(dimension_semantics=("arbitrary", "arbitrary")),
+        cost_estimate=pl.CostEstimate(
+            flops=4 * heads * rows * slots * page_len * hd,
+            transcendentals=heads * rows * slots * page_len,
+            bytes_accessed=heads * (slots * page_len * 2 * hd * 2 + rows * hd * 6),
+        ),
     )(jnp.reshape(kv0, (1,)).astype(jnp.int32), q_k, kv_local, kv_local, bias, cos2, sin2)
 
 

time: 187 us -> 187 us (level)
  no operation moved by 1% of the time
where the time goes in v11:
time: 187 us
  waiting for transfers between devices  71 us (38%)
  Pallas kernels  47.5 us (25%)
  starting transfers between devices  20.3 us (11%)
  other arithmetic  16.1 us (9%)
  matrix products  12.5 us (7%)
  local copies, waits for them, and re-layouts  12 us (6%)
  blocking collectives  5.8 us (3%)
    pallas_call x2, Pallas kernels, hist_attend(): pl.pallas_call(kernel, grid_spec=grid_spec, out_shape=[jax.ShapeDtypeStru...  47.5 us
    ppermute x6, waiting for transfers between devices, bit_scatter(): block = keep + lax.ppermute(send, axis, perm=[(i, i ^ d) for i in range(n)])  40.6 us
    ppermute x6, waiting for transfers between devices, axis_reduce(): x = op(x, lax.ppermute(x, axis, perm=[(i, i ^ d) for i in range(n)]))  19.4 us
    ppermute x2, waiting for transfers between devices, bit_gather(): other = lax.ppermute(x, axis, perm=[(i, i ^ d) for i in range(n)])  11 us
    ppermute x6, starting transfers between devices, bit_scatter(): block = keep + lax.ppermute(send, axis, perm=[(i, i ^ d) for i in range(n)])  8.54 us
    ppermute x6, starting transfers between devices, axis_reduce(): x = op(x, lax.ppermute(x, axis, perm=[(i, i ^ d) for i in range(n)]))  8.05 us
    all_gather x1, blocking collectives, body(): attended = lax.all_gather(attended, 'store', axis=1, tiled=True)  5.8 us
    pallas_call x4, local copies, waits for them, and re-layouts, hist_attend(): pl.pallas_call(kernel, grid_spec=grid_spec, out_shape=[jax.ShapeDtypeStru...  5.5 us
  transfers between devices with their start and end apart: 14, of which 11 were waited for; matrix products, arithmetic and copies ran while one was open for 7% of the time, Pallas kernels for 7%

profile of v11, /device:TPU:0, one launch (start us, length us, event | category | flops | bytes accessed | tf_op | source)
XLA Modules:
  0.0 187.0 jit_solution(7833720872265261867)
XLA Ops:
  0.0 0.9 copy-done
  1.0 4.9 %fusion.70 = f32[64,2048]{1,0:T(8,128)S(1)} fusion(bf16[64,2048]{1,0:T(8,128)(2,1)S(1)} %copy-done, bf16[2048,2048]{1,0:T(8,128)(2,1)} %param.10), kind=kOutput, calls=%fused_computation.154 | convolution fusion | flops 536870912 | bytes 9175040 | tf_op jit(solution)/shard_map/dot_general | solution.py:293
  5.9 2.1 %fusion.5 = f32[64,512]{1,0:T(8,128)S(1)} fusion(bf16[64,2048]{1,0:T(8,128)(2,1)S(1)} %copy-done, bf16[2048,2048]{1,0:T(8,128)(2,1)} %param.11, s32[]{:T(128)S(6)} %select_n.246), kind=kOutput, calls=%fused_computation.15 | convolution fusion | flops 134217728 | bytes 2490372 | tf_op jit(solution)/shard_map/dot_general | solution.py:294
  8.0 0.5 collective-permute-start
  9.3 1.2 reduce-window.6
  10.6 0.1 copy.51
  10.7 0.1 copy.52
  11.7 0.2 fusion.32
  11.9 2.6 %collective-permute-start.1 = (f32[64,2560]{1,0:T(8,128)S(1)}, f32[64,2560]{1,0:T(8,128)S(1)}, u32[]{:S(2)}, u32[]{:S(2)}) collective-permute-start(f32[64,2560]{1,0:T(8,128)S(1)} %fusion.64), channel_id=1, source_target_pairs={{0,2},{1,3},{2,0},{3,1},{4,6},{5,7},{6,4},{7,5},{8,10},{9,11},{10,... | collective-permute-start | bytes 1966088 | tf_op jit(solution)/shard_map/ppermute | solution.py:215
  14.5 0.2 multiply_cosine_fusion
  14.7 15.2 %collective-permute-done.1 = f32[64,2560]{1,0:T(8,128)S(1)} collective-permute-done((f32[64,2560]{1,0:T(8,128)S(1)}, f32[64,2560]{1,0:T(8,128)S(1)}, u32[]{:S(2)}, u32[]{:S(2)}) %collective-permute-start.1) | collective-permute-done | bytes 655392 | tf_op jit(solution)/shard_map/ppermute | solution.py:215
  30.0 0.1 copy.77
  30.1 0.2 fusion.68
  30.3 0.3 subtract_convert_fusion
  30.7 0.2 fusion.77
  30.8 2.9 %collective-permute-start.2 = (bf16[16,64,128]{2,1,0:T(8,128)(2,1)S(1)}, bf16[16,64,128]{2,1,0:T(8,128)(2,1)S(1)}, u32[]{:S(2)}, u32[]{:S(2)}) collective-permute-start(bf16[16,64,128]{2,1,0:T(8,128)(2,1)S(1)} %fusion.77), channel_id=1, source_target_pairs={{0,8},{4,12},{8,0},{12,4},{1,9},{5,13},{9,1},{13,5},{2,10},{6,14},... | collective-permute-start | bytes 786440 | tf_op jit(solution)/shard_map/ppermute | solution.py:239
  33.8 0.7 fusion.36
  34.5 11.0 %collective-permute-done.2 = bf16[16,64,128]{2,1,0:T(8,128)(2,1)S(1)} collective-permute-done((bf16[16,64,128]{2,1,0:T(8,128)(2,1)S(1)}, bf16[16,64,128]{2,1,0:T(8,128)(2,1)S(1)}, u32[]{:S(2)}, u32[]{:S(2)}) %collective-permute-start.2) | collective-permute-done | bytes 262176 | tf_op jit(solution)/shard_map/ppermute | solution.py:239
  45.5 0.2 select_bitcast_fusion.3
  45.8 0.8 collective-permute-start.3
  46.6 0.6 maximum_bitcast_fusion.1.cos_ref
  47.3 0.6 maximum_bitcast_fusion.2.sin_ref
  47.9 0.8 pad_maximum_fusion.2
  48.7 13.2 %shard_map.85 = (f32[2,512,128]{2,1,0:T(8,128)}, f32[2,512,1]{2,1,0:T(8,128)}, f32[2,512,1]{2,1,0:T(8,128)}) custom-call(s32[1]{0:T(128)} %bitcast.kv0_ref, bf16[2,512,128]{2,1,0:T(8,128)(2,1)} %bitcast.183, bf16[40,128,2048]{2,1,0:T(8,128)(2,1)} %bitcast.175, bf16[40,128,2048]{2,1,0:T(8,128)(2,1)} %bitcast.176, f32[1,1,5120]{2,1,0:T(1,128)} %bitcast.189, ...), custom_call_target="tpu_custom_call" | custom-call | flops 2684354560 | bytes 6029312 | tf_op jit(solution)/shard_map/pallas_call | solution.py:194
  61.9 1.2 copy.54
  63.2 0.1 select_bitcast_fusion.1
  63.2 0.1 maximum_bitcast_fusion
  63.4 1.2 fusion.20.q_ref
  64.7 34.3 %shard_map.86 = (f32[6,512,128]{2,1,0:T(8,128)}, f32[6,512,1]{2,1,0:T(8,128)}, f32[6,512,1]{2,1,0:T(8,128)}) custom-call(s32[1]{0:T(128)} %bitcast.16.kv0_ref, bf16[6,512,128]{2,1,0:T(8,128)(2,1)} %fusion.20.q_ref, bf16[40,128,2048]{2,1,0:T(8,128)(2,1)} %bitcast.177, bf16[40,128,2048]{2,1,0:T(8,128)(2,1)} %bitcast.178, f32[1,1,5120]{2,1,0:T(1,128)} %bitcast.190, ...), custom_call_target="tpu_custom_call" | custom-call | flops 8053063680 | bytes 18087936 | tf_op jit(solution)/shard_map/pallas_call | solution.py:194
  99.0 2.1 %copy.55 = f32[6,512,1]{1,0,2:T(8,128)S(1)} copy(f32[6,512,1]{2,1,0:T(8,128)} %get-tuple-element.14) | data formatting | bytes 24576 | tf_op jit(solution)/shard_map/pallas_call | solution.py:194
  101.2 1.2 collective-permute-done.4
  102.4 1.5 collective-permute-start.5
  103.9 0.2 copy.58
  104.1 2.2 %collective-permute-done.5 = f32[64,64]{1,0:T(8,128)S(1)} collective-permute-done((f32[64,64]{1,0:T(8,128)S(1)}, f32[64,64]{1,0:T(8,128)S(1)}, u32[]{:S(2)}, u32[]{:S(2)}) %collective-permute-start.5) | collective-permute-done | bytes 16416 | tf_op jit(solution)/shard_map/ppermute | solution.py:215
  106.3 1.3 collective-permute-start.6
  107.6 2.1 %fusion.2 = f32[8,512,128]{2,1,0:T(8,128)S(1)} fusion(s32[]{:T(128)S(6)} %select_n.268, f32[2,512,128]{2,1,0:T(8,128)} %get-tuple-element.11, f32[6,512,128]{2,1,0:T(8,128)} %get-tuple-element.12), kind=kLoop, calls=%fused_computation.8 | loop fusion | flops 1572864 | bytes 4194308 | tf_op jit(solution)/shard_map/concatenate | solution.py:338
  109.7 2.0 %copy.59 = f32[6,512,1]{1,0,2:T(8,128)S(1)} copy(f32[6,512,1]{2,1,0:T(8,128)} %get-tuple-element.16) | data formatting | bytes 24576 | tf_op jit(solution)/shard_map/pallas_call | solution.py:194
  111.8 2.2 %collective-permute-start.7 = (f32[64,64]{1,0:T(8,128)S(1)}, f32[64,64]{1,0:T(8,128)S(1)}, u32[]{:S(2)}, u32[]{:S(2)}) collective-permute-start(f32[64,64]{1,0:T(8,128)S(1)} %max.17), channel_id=1, source_target_pairs={{0,8},{4,12},{8,0},{12,4},{1,9},{5,13},{9,1},{13,5},{2,10},{6,14},... | collective-permute-start | bytes 49160 | tf_op jit(solution)/shard_map/ppermute | solution.py:215
  114.1 1.8 reshape.378
  115.9 0.8 collective-permute-done.7
  116.7 0.6 mul.252
  117.3 1.8 mul.253
  119.1 2.8 %mul.254 = f32[2,2,2,2,4,8192]{5,4,3,2,1,0:T(4,128)S(1)} multiply(f32[2,2,2,2,4,8192]{5,4,3,2,1,0:T(4,128)} %reshape.378, f32[2,2,2,2,4,8192]{5,4,3,2,1,0:T(4,128)} %mul.253) | non-fusion elementwise | flops 524288 | bytes 6291456 | tf_op jit(solution)/shard_map/mul | solution.py:350
  121.9 1.2 fusion.16
  123.1 3.0 %collective-permute-done.8 = f32[2,2,2,4,8256]{4,3,0,1,2:T(4,128)} collective-permute-done((f32[2,2,2,4,8256]{4,3,0,1,2:T(4,128)}, f32[2,2,2,4,8256]{4,3,0,1,2:T(4,128)}, u32[]{:S(2)}, u32[]{:S(2)}) %collective-permute-start.8) | collective-permute-done | bytes 1056800 | tf_op jit(solution)/shard_map/ppermute | solution.py:228
  126.2 1.6 fusion.19
  127.9 1.6 collective-permute-start.9
  129.6 0.1 reshape.382
  129.8 12.3 %collective-permute-done.9 = f32[2,2,4,8256]{3,2,1,0:T(4,128)S(1)} collective-permute-done((f32[2,2,4,8256]{3,2,1,0:T(4,128)S(1)}, f32[2,2,4,8256]{3,2,1,0:T(4,128)S(1)}, u32[]{:S(2)}, u32[]{:S(2)}) %collective-permute-start.9) | collective-permute-done | bytes 528416 | tf_op jit(solution)/shard_map/ppermute | solution.py:228
  142.1 0.1 bitcast_add_fusion
  142.3 1.3 collective-permute-start.10
  143.6 0.1 add_convert_fusion.1
  143.7 0.3 fusion.69
  144.0 5.9 %collective-permute-done.10 = f32[2,4,8256]{2,1,0:T(4,128)S(1)} collective-permute-done((f32[2,4,8256]{2,1,0:T(4,128)S(1)}, f32[2,4,8256]{2,1,0:T(4,128)S(1)}, u32[]{:S(2)}, u32[]{:S(2)}) %collective-permute-start.10) | collective-permute-done | bytes 264224 | tf_op jit(solution)/shard_map/ppermute | solution.py:228
  150.1 2.4 %collective-permute-start.11 = (f32[4,8256]{1,0:T(4,128)S(1)}, f32[4,8256]{1,0:T(4,128)S(1)}, u32[]{:S(2)}, u32[]{:S(2)}) collective-permute-start(f32[4,8256]{1,0:T(4,128)S(1)} %dynamic-slice_bitcast_fusion.2), channel_id=1, source_target_pairs={{0,8},{4,12},{8,0},{12,4},{1,9},{5,13},{9,1},{13,5},{2,10},{6,14},... | collective-permute-start | bytes 396296 | tf_op jit(solution)/shard_map/ppermute | solution.py:228
  152.6 5.1 %collective-permute-done.11 = f32[4,8256]{1,0:T(4,128)S(1)} collective-permute-done((f32[4,8256]{1,0:T(4,128)S(1)}, f32[4,8256]{1,0:T(4,128)S(1)}, u32[]{:S(2)}, u32[]{:S(2)}) %collective-permute-start.11) | collective-permute-done | bytes 132128 | tf_op jit(solution)/shard_map/ppermute | solution.py:228
  157.8 0.2 fusion.14
  158.1 5.8 %all_gather.3 = bf16[64,2048]{1,0:T(8,128)(2,1)S(1)} all-gather(bf16[64,512]{1,0:T(8,128)(2,1)S(1)} %bitcast.188), channel_id=1, replica_groups=mesh['groups'=2,'tensor'=4,'store'=4] {'store'}, dimensions={1}, use_global_device_ids=true | all-gather | bytes 327680 | tf_op jit(solution)/shard_map/all_gather | solution.py:392
  163.9 5.0 %fusion.71 = f32[64,2048]{1,0:T(8,128)S(1)} fusion(bf16[64,2048]{1,0:T(8,128)(2,1)S(1)} %all_gather.3, bf16[2048,2048]{1,0:T(8,128)(2,1)} %param.12), kind=kOutput, calls=%fused_computation.155 | convolution fusion | flops 536870912 | bytes 9175040 | tf_op jit(solution)/shard_map/dot_general | solution.py:418
  168.9 0.8 collective-permute-start.12
  169.7 7.8 %collective-permute-done.12 = f32[2,16,2048]{2,1,0:T(8,128)S(1)} collective-permute-done((f32[2,16,2048]{2,1,0:T(8,128)S(1)}, f32[2,16,2048]{2,1,0:T(8,128)S(1)}, u32[]{:S(2)}, u32[]{:S(2)}) %collective-permute-start.12) | collective-permute-done | bytes 262176 | tf_op jit(solution)/shard_map/ppermute | solution.py:228
  177.6 2.4 %collective-permute-start.13 = (f32[16,2048]{1,0:T(8,128)S(1)}, f32[16,2048]{1,0:T(8,128)S(1)}, u32[]{:S(2)}, u32[]{:S(2)}) collective-permute-start(f32[16,2048]{1,0:T(8,128)S(1)} %dynamic-slice_bitcast_fusion.3), channel_id=1, source_target_pairs={{0,8},{4,12},{8,0},{12,4},{1,9},{5,13},{9,1},{13,5},{2,10},{6,14},... | collective-permute-start | bytes 393224 | tf_op jit(solution)/shard_map/ppermute | solution.py:228
  180.0 6.3 %collective-permute-done.13 = f32[16,2048]{1,0:T(8,128)S(1)} collective-permute-done((f32[16,2048]{1,0:T(8,128)S(1)}, f32[16,2048]{1,0:T(8,128)S(1)}, u32[]{:S(2)}, u32[]{:S(2)}) %collective-permute-start.13) | collective-permute-done | bytes 131104 | tf_op jit(solution)/shard_map/ppermute | solution.py:228
  186.3 0.6 fusion.22
  (60 shorter events, 1.7 us)
Async XLA Ops:
  0.0 1.0 copy-start
  5.9 3.4 %copy-start.3 = (s32[256,1]{0,1:T(1,128)S(1)}, s32[256,1]{0,1:T(1,128)}, u32[]{:S(2)}) copy-start(s32[256,1]{0,1:T(1,128)} %param.14) | copy-start | bytes 3076
  8.0 3.8 %collective-permute-start = (f32[64,2560]{1,0:T(8,128)S(1)}, f32[64,2560]{1,0:T(8,128)S(1)}, u32[]{:S(2)}, u32[]{:S(2)}) collective-permute-start(f32[64,2560]{1,0:T(8,128)S(1)} %pad_maximum_fusion), channel_id=1, source_target_pairs={{0,1},{1,0},{2,3},{3,2},{4,5},{5,4},{6,7},{7,6},{8,9},{9,8},{10,11... | collective-permute-start | bytes 1966088 | tf_op jit(solution)/shard_map/ppermute | solution.py:215
  11.9 18.0 %collective-permute-start.1 = (f32[64,2560]{1,0:T(8,128)S(1)}, f32[64,2560]{1,0:T(8,128)S(1)}, u32[]{:S(2)}, u32[]{:S(2)}) collective-permute-start(f32[64,2560]{1,0:T(8,128)S(1)} %fusion.64), channel_id=1, source_target_pairs={{0,2},{1,3},{2,0},{3,1},{4,6},{5,7},{6,4},{7,5},{8,10},{9,11},{10,... | collective-permute-start | bytes 1966088 | tf_op jit(solution)/shard_map/ppermute | solution.py:215
  30.8 14.7 %collective-permute-start.2 = (bf16[16,64,128]{2,1,0:T(8,128)(2,1)S(1)}, bf16[16,64,128]{2,1,0:T(8,128)(2,1)S(1)}, u32[]{:S(2)}, u32[]{:S(2)}) collective-permute-start(bf16[16,64,128]{2,1,0:T(8,128)(2,1)S(1)} %fusion.77), channel_id=1, source_target_pairs={{0,8},{4,12},{8,0},{12,4},{1,9},{5,13},{9,1},{13,5},{2,10},{6,14},... | collective-permute-start | bytes 786440 | tf_op jit(solution)/shard_map/ppermute | solution.py:239
  45.8 17.3 %collective-permute-start.3 = (bf16[2,16,64,128]{3,2,1,0:T(8,128)(2,1)S(1)}, bf16[2,16,64,128]{3,2,1,0:T(8,128)(2,1)S(1)}, u32[]{:S(2)}, u32[]{:S(2)}) collective-permute-start(bf16[2,16,64,128]{3,2,1,0:T(8,128)(2,1)S(1)} %pad_maximum_fusion.1), channel_id=1, source_target_pairs={{0,4},{4,0},{8,12},{12,8},{1,5},{5,1},{9,13},{13,9},{2,6},{6,2},{1... | collective-permute-start | bytes 1572872 | tf_op jit(solution)/shard_map/ppermute | solution.py:239
  99.0 4.9 %copy-start.2 = (f32[2,512,1]{2,1,0:T(8,128)S(1)}, f32[2,512,1]{2,1,0:T(8,128)}, u32[]{:S(2)}) copy-start(f32[2,512,1]{2,1,0:T(8,128)} %get-tuple-element.15) | copy-start | bytes 12292
  101.2 1.2 collective-permute-start.4
  102.4 3.9 %collective-permute-start.5 = (f32[64,64]{1,0:T(8,128)S(1)}, f32[64,64]{1,0:T(8,128)S(1)}, u32[]{:S(2)}, u32[]{:S(2)}) collective-permute-start(f32[64,64]{1,0:T(8,128)S(1)} %max.15), channel_id=1, source_target_pairs={{0,2},{1,3},{2,0},{3,1},{4,6},{5,7},{6,4},{7,5},{8,10},{9,11},{10,... | collective-permute-start | bytes 49160 | tf_op jit(solution)/shard_map/ppermute | solution.py:215
  106.3 5.4 %collective-permute-start.6 = (f32[64,64]{1,0:T(8,128)S(1)}, f32[64,64]{1,0:T(8,128)S(1)}, u32[]{:S(2)}, u32[]{:S(2)}) collective-permute-start(f32[64,64]{1,0:T(8,128)S(1)} %max.16), channel_id=1, source_target_pairs={{0,4},{4,0},{8,12},{12,8},{1,5},{5,1},{9,13},{13,9},{2,6},{6,2},{1... | collective-permute-start | bytes 49160 | tf_op jit(solution)/shard_map/ppermute | solution.py:215
  111.8 4.9 %collective-permute-start.7 = (f32[64,64]{1,0:T(8,128)S(1)}, f32[64,64]{1,0:T(8,128)S(1)}, u32[]{:S(2)}, u32[]{:S(2)}) collective-permute-start(f32[64,64]{1,0:T(8,128)S(1)} %max.17), channel_id=1, source_target_pairs={{0,8},{4,12},{8,0},{12,4},{1,9},{5,13},{9,1},{13,5},{2,10},{6,14},... | collective-permute-start | bytes 49160 | tf_op jit(solution)/shard_map/ppermute | solution.py:215
  123.1 3.0 %collective-permute-start.8 = (f32[2,2,2,4,8256]{4,3,0,1,2:T(4,128)}, f32[2,2,2,4,8256]{4,3,0,1,2:T(4,128)}, u32[]{:S(2)}, u32[]{:S(2)}) collective-permute-start(f32[2,2,2,4,8256]{4,3,0,1,2:T(4,128)} %fusion.16), channel_id=1, source_target_pairs={{0,1},{1,0},{2,3},{3,2},{4,5},{5,4},{6,7},{7,6},{8,9},{9,8},{10,11... | collective-permute-start | bytes 3170312 | tf_op jit(solution)/shard_map/ppermute | solution.py:228
  127.9 14.2 %collective-permute-start.9 = (f32[2,2,4,8256]{3,2,1,0:T(4,128)S(1)}, f32[2,2,4,8256]{3,2,1,0:T(4,128)S(1)}, u32[]{:S(2)}, u32[]{:S(2)}) collective-permute-start(f32[2,2,4,8256]{3,2,1,0:T(4,128)S(1)} %bitcast.185), channel_id=1, source_target_pairs={{0,2},{1,3},{2,0},{3,1},{4,6},{5,7},{6,4},{7,5},{8,10},{9,11},{10,... | collective-permute-start | bytes 1585160 | tf_op jit(solution)/shard_map/ppermute | solution.py:228
  142.3 7.7 %collective-permute-start.10 = (f32[2,4,8256]{2,1,0:T(4,128)S(1)}, f32[2,4,8256]{2,1,0:T(4,128)S(1)}, u32[]{:S(2)}, u32[]{:S(2)}) collective-permute-start(f32[2,4,8256]{2,1,0:T(4,128)S(1)} %dynamic-slice_bitcast_fusion), channel_id=1, source_target_pairs={{0,4},{4,0},{8,12},{12,8},{1,5},{5,1},{9,13},{13,9},{2,6},{6,2},{1... | collective-permute-start | bytes 792584 | tf_op jit(solution)/shard_map/ppermute | solution.py:228
  150.1 7.7 %collective-permute-start.11 = (f32[4,8256]{1,0:T(4,128)S(1)}, f32[4,8256]{1,0:T(4,128)S(1)}, u32[]{:S(2)}, u32[]{:S(2)}) collective-permute-start(f32[4,8256]{1,0:T(4,128)S(1)} %dynamic-slice_bitcast_fusion.2), channel_id=1, source_target_pairs={{0,8},{4,12},{8,0},{12,4},{1,9},{5,13},{9,1},{13,5},{2,10},{6,14},... | collective-permute-start | bytes 396296 | tf_op jit(solution)/shard_map/ppermute | solution.py:228
  163.9 23.1 %copy-start.1 = (bf16[64,2048]{1,0:T(8,128)(2,1)S(1)}, bf16[64,2048]{1,0:T(8,128)(2,1)}, u32[]{:S(2)}) copy-start(bf16[64,2048]{1,0:T(8,128)(2,1)} %param.8) | copy-start | bytes 786436
  168.9 8.6 %collective-permute-start.12 = (f32[2,16,2048]{2,1,0:T(8,128)S(1)}, f32[2,16,2048]{2,1,0:T(8,128)S(1)}, u32[]{:S(2)}, u32[]{:S(2)}) collective-permute-start(f32[2,16,2048]{2,1,0:T(8,128)S(1)} %dynamic-slice_bitcast_fusion.1), channel_id=1, source_target_pairs={{0,4},{4,0},{8,12},{12,8},{1,5},{5,1},{9,13},{13,9},{2,6},{6,2},{1... | collective-permute-start | bytes 786440 | tf_op jit(solution)/shard_map/ppermute | solution.py:228
  177.6 8.7 %collective-permute-start.13 = (f32[16,2048]{1,0:T(8,128)S(1)}, f32[16,2048]{1,0:T(8,128)S(1)}, u32[]{:S(2)}, u32[]{:S(2)}) collective-permute-start(f32[16,2048]{1,0:T(8,128)S(1)} %dynamic-slice_bitcast_fusion.3), channel_id=1, source_target_pairs={{0,8},{4,12},{8,0},{12,4},{1,9},{5,13},{9,1},{13,5},{2,10},{6,14},... | collective-permute-start | bytes 393224 | tf_op jit(solution)/shard_map/ppermute | solution.py:228

commit v12 on v11

--- a/solution.py
+++ b/solution.py
@@ -124,7 +124,8 @@
 MASK_FILL = -3e30
 
 
-def hist_kernel(kv0_ref, q_ref, k_ref, v_ref, bias_ref, cos_ref, sin_ref, acc_out, m_out, l_out, m_sc, l_sc, acc_sc, *, scale, blocks):
+def hist_kernel(kv0_ref, q_ref, k_ref, v_ref, bias_ref, cos_ref, sin_ref, *refs, scale, blocks):
+    acc_out, m_out, l_out, m_sc, l_sc, acc_sc = refs[-6:]
     j = pl.program_id(1)
 
     @pl.when(j == 0)
@@ -159,7 +160,7 @@
         l_out[0] = l_sc[...]
 
 
-def hist_attend(kv0, q_k, kv_local, bias, cos2, sin2, pb):
+def hist_attend(kv0, q_k, kv_local, bias, cos2, sin2, pb, prev=None):
     heads, rows, hd = q_k.shape
     slots, page_len, width = kv_local.shape
     kv_heads = width // (2 * hd)
@@ -179,11 +180,12 @@
             pl.BlockSpec((1, 1, pb * page_len), lambda h, j, r: (j, 0, 0)),
             pl.BlockSpec((1, hd), lambda h, j, r: (0, 0)),
             pl.BlockSpec((1, hd), lambda h, j, r: (0, 0)),
-        ],
+        ]
+        + ([pl.BlockSpec(memory_space=pl.ANY)] * 3 if prev is not None else []),
         out_specs=[
-            pl.BlockSpec((1, rows, hd), lambda h, j, r: (h, 0, 0)),
-            pl.BlockSpec((1, rows, 1), lambda h, j, r: (h, 0, 0)),
-            pl.BlockSpec((1, rows, 1), lambda h, j, r: (h, 0, 0)),
+            pl.BlockSpec((1, rows, hd), lambda h, j, r: (head_of(h, r), 0, 0)),
+            pl.BlockSpec((1, rows, 1), lambda h, j, r: (head_of(h, r), 0, 0)),
+            pl.BlockSpec((1, rows, 1), lambda h, j, r: (head_of(h, r), 0, 0)),
         ],
         scratch_shapes=[
             pltpu.VMEM((rows, 1), jnp.float32),
@@ -195,17 +197,18 @@
         kernel,
         grid_spec=grid_spec,
         out_shape=[
-            jax.ShapeDtypeStruct((heads, rows, hd), jnp.float32),
-            jax.ShapeDtypeStruct((heads, rows, 1), jnp.float32),
-            jax.ShapeDtypeStruct((heads, rows, 1), jnp.float32),
+            jax.ShapeDtypeStruct((kv_heads, rows, hd), jnp.float32),
+            jax.ShapeDtypeStruct((kv_heads, rows, 1), jnp.float32),
+            jax.ShapeDtypeStruct((kv_heads, rows, 1), jnp.float32),
         ],
+        input_output_aliases={7: 0, 8: 1, 9: 2} if prev is not None else {},
         compiler_params=pltpu.CompilerParams(dimension_semantics=("arbitrary", "arbitrary")),
         cost_estimate=pl.CostEstimate(
             flops=4 * heads * rows * slots * page_len * hd,
             transcendentals=heads * rows * slots * page_len,
             bytes_accessed=heads * (slots * page_len * 2 * hd * 2 + rows * hd * 6),
         ),
-    )(jnp.reshape(kv0, (1,)).astype(jnp.int32), q_k, kv_local, kv_local, bias, cos2, sin2)
+    )(jnp.reshape(kv0, (1,)).astype(jnp.int32), q_k, kv_local, kv_local, bias, cos2, sin2, *(prev or ()))
 
 
 def axis_reduce(x, axis, op):
@@ -332,12 +335,9 @@
         q_rest = lax.dynamic_slice_in_dim(
             jnp.concatenate([q_k, q_k], axis=0), rest_first % kv_heads, kv_heads - local_kv, 0
         )
-        rest = hist_attend(rest_first % kv_heads, q_rest, kv_local, bias, cos2, sin2, pb)
-        parts = []
-        for first, second in zip(own, rest):
-            rolled = jnp.concatenate([first, second, first, second], axis=0)
-            parts.append(lax.dynamic_slice_in_dim(rolled, kv_heads - kv_first, kv_heads, 0))
-        acc, top, total = parts
+        acc, top, total = hist_attend(
+            rest_first % kv_heads, q_rest, kv_local, bias, cos2, sin2, pb, prev=tuple(own)
+        )
     else:
         acc, top, total = hist_attend(jnp.int32(0), q_k, kv_local, bias, cos2, sin2, pb)
     acc = acc.reshape(HQ, tok_count, HD)

time: 187 us -> 189 us (1.011)
  waiting for transfers between devices: 71 us -> 79 us
  starting transfers between devices: 20.3 us -> 15.5 us
  local copies, waits for them, and re-layouts: 12 us -> 7.45 us
  other arithmetic: 16.1 us -> 19.4 us
    ppermute x6, starting transfers between devices: 8.54 us -> 2.52 us  [bit_scatter(): block = keep + lax.ppermute(send, axis, perm=[(i, i ^ d) for i in range(n)])]
    ppermute x6, waiting for transfers between devices: 40.6 us -> 46.5 us  [bit_scatter(): block = keep + lax.ppermute(send, axis, perm=[(i, i ^ d) for i in range(n)])]
    pallas_call x4 -> x0, local copies, waits for them, and re-layouts: 5.5 us -> none  [hist_attend(): pl.pallas_call(kernel, grid_spec=grid_spec, out_shape=[jax.ShapeDtypeStru...]
    pallas_call x0 -> x2, other arithmetic: none -> 4.55 us  [hist_attend(): pl.pallas_call(kernel, grid_spec=grid_spec, out_shape=[jax.ShapeDtypeStru...]
    concatenate x3 -> x0, other arithmetic: 2.17 us -> none  [body(): rolled = jnp.concatenate([first, second, first, second], axis=0)]
    ppermute x6, waiting for transfers between devices: 19.4 us -> 21.4 us  [axis_reduce(): x = op(x, lax.ppermute(x, axis, perm=[(i, i ^ d) for i in range(n)]))]
  transfers between devices with their start and end apart: 14 -> 14, of which waited for: 11 -> 11; matrix products, arithmetic and copies ran while one was open for 7% -> 5% of each run, Pallas kernels for 7% -> 7%
where the time goes in v12:
time: 189 us
  waiting for transfers between devices  79 us (42%)
  Pallas kernels  47.7 us (25%)
  other arithmetic  19.4 us (10%)
  starting transfers between devices  15.5 us (8%)
  matrix products  12.5 us (7%)
  local copies, waits for them, and re-layouts  7.45 us (4%)
  blocking collectives  5.79 us (3%)
    pallas_call x2, Pallas kernels, hist_attend(): pl.pallas_call(kernel, grid_spec=grid_spec, out_shape=[jax.ShapeDtypeStru...  47.7 us
    ppermute x6, waiting for transfers between devices, bit_scatter(): block = keep + lax.ppermute(send, axis, perm=[(i, i ^ d) for i in range(n)])  46.5 us
    ppermute x6, waiting for transfers between devices, axis_reduce(): x = op(x, lax.ppermute(x, axis, perm=[(i, i ^ d) for i in range(n)]))  21.4 us
    ppermute x2, waiting for transfers between devices, bit_gather(): other = lax.ppermute(x, axis, perm=[(i, i ^ d) for i in range(n)])  11 us
    ppermute x6, starting transfers between devices, axis_reduce(): x = op(x, lax.ppermute(x, axis, perm=[(i, i ^ d) for i in range(n)]))  9.33 us
    all_gather x1, blocking collectives, body(): attended = lax.all_gather(attended, 'store', axis=1, tiled=True)  5.79 us
    dot_general x1, matrix products, body(): jnp.dot(attended, w_out, preferred_element_type=jnp.float32)  4.99 us
    dot_general x1, matrix products, body(): query_part = jnp.dot(x_new, w_query, preferred_element_type=jnp.float32)  4.94 us
  transfers between devices with their start and end apart: 14, of which 11 were waited for; matrix products, arithmetic and copies ran while one was open for 5% of the time, Pallas kernels for 7%

profile of v12, /device:TPU:0, one launch (start us, length us, event | category | flops | bytes accessed | tf_op | source)
XLA Modules:
  0.0 189.0 jit_solution(15124418869238500703)
XLA Ops:
  0.0 0.9 copy-done
  1.0 4.9 %fusion.61 = f32[64,2048]{1,0:T(8,128)S(1)} fusion(bf16[64,2048]{1,0:T(8,128)(2,1)S(1)} %copy-done, bf16[2048,2048]{1,0:T(8,128)(2,1)} %param.10), kind=kOutput, calls=%fused_computation.131 | convolution fusion | flops 536870912 | bytes 9175040 | tf_op jit(solution)/shard_map/dot_general | solution.py:296
  5.9 2.1 %fusion.2 = f32[64,512]{1,0:T(8,128)S(1)} fusion(bf16[64,2048]{1,0:T(8,128)(2,1)S(1)} %copy-done, bf16[2048,2048]{1,0:T(8,128)(2,1)} %param.11, s32[]{:T(128)S(6)} %select_n.247), kind=kOutput, calls=%fused_computation.8 | convolution fusion | flops 134217728 | bytes 2490372 | tf_op jit(solution)/shard_map/dot_general | solution.py:297
  8.0 0.5 collective-permute-start
  10.0 1.2 reduce-window.6
  11.2 0.1 slice.52
  11.3 0.1 copy.32
  11.5 0.1 copy.33
  11.5 0.1 add_bitcast_fusion
  11.7 0.2 fusion.29
  11.9 2.6 %collective-permute-start.1 = (f32[64,2560]{1,0:T(8,128)S(1)}, f32[64,2560]{1,0:T(8,128)S(1)}, u32[]{:S(2)}, u32[]{:S(2)}) collective-permute-start(f32[64,2560]{1,0:T(8,128)S(1)} %fusion.55), channel_id=1, source_target_pairs={{0,2},{1,3},{2,0},{3,1},{4,6},{5,7},{6,4},{7,5},{8,10},{9,11},{10,... | collective-permute-start | bytes 1966088 | tf_op jit(solution)/shard_map/ppermute | solution.py:218
  14.5 0.2 multiply_cosine_fusion
  14.7 15.2 %collective-permute-done.1 = f32[64,2560]{1,0:T(8,128)S(1)} collective-permute-done((f32[64,2560]{1,0:T(8,128)S(1)}, f32[64,2560]{1,0:T(8,128)S(1)}, u32[]{:S(2)}, u32[]{:S(2)}) %collective-permute-start.1) | collective-permute-done | bytes 655392 | tf_op jit(solution)/shard_map/ppermute | solution.py:218
  30.0 0.1 copy.47
  30.1 0.2 fusion.59
  30.3 0.3 subtract_convert_fusion
  30.6 0.2 fusion.68
  30.8 2.9 %collective-permute-start.2 = (bf16[16,64,128]{2,1,0:T(8,128)(2,1)S(1)}, bf16[16,64,128]{2,1,0:T(8,128)(2,1)S(1)}, u32[]{:S(2)}, u32[]{:S(2)}) collective-permute-start(bf16[16,64,128]{2,1,0:T(8,128)(2,1)S(1)} %fusion.68), channel_id=1, source_target_pairs={{0,8},{4,12},{8,0},{12,4},{1,9},{5,13},{9,1},{13,5},{2,10},{6,14},... | collective-permute-start | bytes 786440 | tf_op jit(solution)/shard_map/ppermute | solution.py:242
  33.8 0.7 fusion.33
  34.5 11.0 %collective-permute-done.2 = bf16[16,64,128]{2,1,0:T(8,128)(2,1)S(1)} collective-permute-done((bf16[16,64,128]{2,1,0:T(8,128)(2,1)S(1)}, bf16[16,64,128]{2,1,0:T(8,128)(2,1)S(1)}, u32[]{:S(2)}, u32[]{:S(2)}) %collective-permute-start.2) | collective-permute-done | bytes 262176 | tf_op jit(solution)/shard_map/ppermute | solution.py:242
  45.5 0.2 select_bitcast_fusion.3
  45.8 0.8 collective-permute-start.3
  46.6 0.6 maximum_bitcast_fusion.1.cos_ref
  47.2 0.6 maximum_bitcast_fusion.2.sin_ref
  47.8 0.8 pad_maximum_fusion.2
  48.7 13.2 %shard_map.85 = (f32[8,512,128]{2,1,0:T(8,128)}, f32[8,512,1]{2,1,0:T(8,128)}, f32[8,512,1]{2,1,0:T(8,128)}) custom-call(s32[1]{0:T(128)} %bitcast.21.kv0_ref, bf16[2,512,128]{2,1,0:T(8,128)(2,1)} %bitcast.178, bf16[40,128,2048]{2,1,0:T(8,128)(2,1)} %bitcast.170, bf16[40,128,2048]{2,1,0:T(8,128)(2,1)} %bitcast.171, f32[1,1,5120]{2,1,0:T(1,128)} %bitcast.183, ...), custom_call_target="tpu_custom_call" | custom-call | flops 2684354560 | bytes 6029312 | tf_op jit(solution)/shard_map/pallas_call | solution.py:196
  62.0 0.1 maximum_bitcast_fusion
  62.2 1.2 fusion.17.q_ref
  63.4 34.4 %shard_map.86 = (f32[8,512,128]{2,1,0:T(8,128)}, f32[8,512,1]{2,1,0:T(8,128)}, f32[8,512,1]{2,1,0:T(8,128)}) custom-call(s32[1]{0:T(128)} %bitcast.kv0_ref, bf16[6,512,128]{2,1,0:T(8,128)(2,1)} %fusion.17.q_ref, bf16[40,128,2048]{2,1,0:T(8,128)(2,1)} %bitcast.172, ...), custom_call_target="tpu_custom_call", output_to_operand_aliasing={{0}: (7, {}), {1}: (8, {}), {2}: (9, {})} | custom-call | flops 8053063680 | bytes 18087936 | tf_op jit(solution)/shard_map/pallas_call | solution.py:196
  97.8 2.3 %reduce.2 = f32[8,512]{1,0:T(8,128)S(1)} reduce(f32[8,512,1]{2,1,0:T(8,128)} %get-tuple-element.15, f32[]{:T(128)} %constant.265), dimensions={2}, to_apply=%get-tuple-element.15.reduce_sub_computation | reduce | bytes 32772 | tf_op jit(solution)/shard_map/pallas_call | solution.py:196
  100.1 0.1 reshape.379
  100.2 1.2 collective-permute-done.4
  101.4 1.5 collective-permute-start.5
  102.9 2.4 %collective-permute-done.5 = f32[64,64]{1,0:T(8,128)S(1)} collective-permute-done((f32[64,64]{1,0:T(8,128)S(1)}, f32[64,64]{1,0:T(8,128)S(1)}, u32[]{:S(2)}, u32[]{:S(2)}) %collective-permute-start.5) | collective-permute-done | bytes 16416 | tf_op jit(solution)/shard_map/ppermute | solution.py:218
  105.4 1.3 collective-permute-start.6
  106.7 2.6 %collective-permute-done.6 = f32[64,64]{1,0:T(8,128)S(1)} collective-permute-done((f32[64,64]{1,0:T(8,128)S(1)}, f32[64,64]{1,0:T(8,128)S(1)}, u32[]{:S(2)}, u32[]{:S(2)}) %collective-permute-start.6) | collective-permute-done | bytes 16416 | tf_op jit(solution)/shard_map/ppermute | solution.py:218
  109.3 3.4 %collective-permute-start.7 = (f32[64,64]{1,0:T(8,128)S(1)}, f32[64,64]{1,0:T(8,128)S(1)}, u32[]{:S(2)}, u32[]{:S(2)}) collective-permute-start(f32[64,64]{1,0:T(8,128)S(1)} %max.17), channel_id=1, source_target_pairs={{0,8},{4,12},{8,0},{12,4},{1,9},{5,13},{9,1},{13,5},{2,10},{6,14},... | collective-permute-start | bytes 49160 | tf_op jit(solution)/shard_map/ppermute | solution.py:218
  112.7 1.9 reshape.378
  114.6 2.2 %reduce.3 = f32[8,512]{1,0:T(8,128)S(1)} reduce(f32[8,512,1]{2,1,0:T(8,128)} %get-tuple-element.16, f32[]{:T(128)} %constant.265), dimensions={2}, to_apply=%get-tuple-element.16.reduce_sub_computation | reduce | bytes 32772 | tf_op jit(solution)/shard_map/pallas_call | solution.py:196
  116.8 0.1 reshape.380
  116.9 0.6 mul.252
  117.5 1.8 mul.253
  119.3 2.8 %mul.254 = f32[2,2,2,2,4,8192]{5,4,3,2,1,0:T(4,128)S(1)} multiply(f32[2,2,2,2,4,8192]{5,4,3,2,1,0:T(4,128)} %reshape.378, f32[2,2,2,2,4,8192]{5,4,3,2,1,0:T(4,128)} %mul.253) | non-fusion elementwise | flops 524288 | bytes 6291456 | tf_op jit(solution)/shard_map/mul | solution.py:350
  122.1 1.2 fusion.13
  123.3 3.0 %collective-permute-done.8 = f32[2,2,2,4,8256]{4,3,0,1,2:T(4,128)} collective-permute-done((f32[2,2,2,4,8256]{4,3,0,1,2:T(4,128)}, f32[2,2,2,4,8256]{4,3,0,1,2:T(4,128)}, u32[]{:S(2)}, u32[]{:S(2)}) %collective-permute-start.8) | collective-permute-done | bytes 1056800 | tf_op jit(solution)/shard_map/ppermute | solution.py:231
  126.3 1.6 fusion.16
  128.0 1.0 copy-done.3
  129.0 1.6 collective-permute-start.9
  130.5 0.1 fusion.31
  130.6 0.1 reshape.382
  130.8 12.4 %collective-permute-done.9 = f32[2,2,4,8256]{3,2,0,1:T(4,128)S(1)} collective-permute-done((f32[2,2,4,8256]{3,2,0,1:T(4,128)S(1)}, f32[2,2,4,8256]{3,2,0,1:T(4,128)S(1)}, u32[]{:S(2)}, u32[]{:S(2)}) %collective-permute-start.9) | collective-permute-done | bytes 528416 | tf_op jit(solution)/shard_map/ppermute | solution.py:231
  143.2 1.2 bitcast_add_fusion
  144.4 0.1 collective-permute-start.10
  144.5 0.1 add_convert_fusion.1
  144.6 0.3 fusion.60
  144.9 7.1 %collective-permute-done.10 = f32[2,4,8256]{2,1,0:T(4,128)S(1)} collective-permute-done((f32[2,4,8256]{2,1,0:T(4,128)S(1)}, f32[2,4,8256]{2,1,0:T(4,128)S(1)}, u32[]{:S(2)}, u32[]{:S(2)}) %collective-permute-start.10) | collective-permute-done | bytes 264224 | tf_op jit(solution)/shard_map/ppermute | solution.py:231
  152.2 0.7 collective-permute-start.11
  153.0 6.8 %collective-permute-done.11 = f32[4,8256]{1,0:T(4,128)S(1)} collective-permute-done((f32[4,8256]{1,0:T(4,128)S(1)}, f32[4,8256]{1,0:T(4,128)S(1)}, u32[]{:S(2)}, u32[]{:S(2)}) %collective-permute-start.11) | collective-permute-done | bytes 132128 | tf_op jit(solution)/shard_map/ppermute | solution.py:231
  159.9 0.2 fusion.11
  160.2 5.8 %all_gather.3 = bf16[64,2048]{1,0:T(8,128)(2,1)S(1)} all-gather(bf16[64,512]{1,0:T(8,128)(2,1)S(1)} %bitcast.182), channel_id=1, replica_groups=mesh['groups'=2,'tensor'=4,'store'=4] {'store'}, dimensions={1}, use_global_device_ids=true | all-gather | bytes 327680 | tf_op jit(solution)/shard_map/all_gather | solution.py:392
  165.9 5.0 %fusion.62 = f32[64,2048]{1,0:T(8,128)S(1)} fusion(bf16[64,2048]{1,0:T(8,128)(2,1)S(1)} %all_gather.3, bf16[2048,2048]{1,0:T(8,128)(2,1)} %param.12), kind=kOutput, calls=%fused_computation.132 | convolution fusion | flops 536870912 | bytes 9175040 | tf_op jit(solution)/shard_map/dot_general | solution.py:418
  171.1 8.5 %collective-permute-done.12 = f32[2,16,2048]{2,1,0:T(8,128)S(1)} collective-permute-done((f32[2,16,2048]{2,1,0:T(8,128)S(1)}, f32[2,16,2048]{2,1,0:T(8,128)S(1)}, u32[]{:S(2)}, u32[]{:S(2)}) %collective-permute-start.12) | collective-permute-done | bytes 262176 | tf_op jit(solution)/shard_map/ppermute | solution.py:231
  179.7 8.6 %collective-permute-done.13 = f32[16,2048]{1,0:T(8,128)S(1)} collective-permute-done((f32[16,2048]{1,0:T(8,128)S(1)}, f32[16,2048]{1,0:T(8,128)S(1)}, u32[]{:S(2)}, u32[]{:S(2)}) %collective-permute-start.13) | collective-permute-done | bytes 131104 | tf_op jit(solution)/shard_map/ppermute | solution.py:231
  188.4 0.6 fusion.19
  (56 shorter events, 1.4 us)
Async XLA Ops:
  0.0 1.0 copy-start
  5.9 4.1 %copy-start.4 = (s32[256,1]{0,1:T(1,128)S(1)}, s32[256,1]{0,1:T(1,128)}, u32[]{:S(2)}) copy-start(s32[256,1]{0,1:T(1,128)} %param.14) | copy-start | bytes 3076
  8.0 3.8 %collective-permute-start = (f32[64,2560]{1,0:T(8,128)S(1)}, f32[64,2560]{1,0:T(8,128)S(1)}, u32[]{:S(2)}, u32[]{:S(2)}) collective-permute-start(f32[64,2560]{1,0:T(8,128)S(1)} %pad_maximum_fusion), channel_id=1, source_target_pairs={{0,1},{1,0},{2,3},{3,2},{4,5},{5,4},{6,7},{7,6},{8,9},{9,8},{10,11... | collective-permute-start | bytes 1966088 | tf_op jit(solution)/shard_map/ppermute | solution.py:218
  11.9 18.0 %collective-permute-start.1 = (f32[64,2560]{1,0:T(8,128)S(1)}, f32[64,2560]{1,0:T(8,128)S(1)}, u32[]{:S(2)}, u32[]{:S(2)}) collective-permute-start(f32[64,2560]{1,0:T(8,128)S(1)} %fusion.55), channel_id=1, source_target_pairs={{0,2},{1,3},{2,0},{3,1},{4,6},{5,7},{6,4},{7,5},{8,10},{9,11},{10,... | collective-permute-start | bytes 1966088 | tf_op jit(solution)/shard_map/ppermute | solution.py:218
  30.8 14.7 %collective-permute-start.2 = (bf16[16,64,128]{2,1,0:T(8,128)(2,1)S(1)}, bf16[16,64,128]{2,1,0:T(8,128)(2,1)S(1)}, u32[]{:S(2)}, u32[]{:S(2)}) collective-permute-start(bf16[16,64,128]{2,1,0:T(8,128)(2,1)S(1)} %fusion.68), channel_id=1, source_target_pairs={{0,8},{4,12},{8,0},{12,4},{1,9},{5,13},{9,1},{13,5},{2,10},{6,14},... | collective-permute-start | bytes 786440 | tf_op jit(solution)/shard_map/ppermute | solution.py:242
  45.8 16.1 %collective-permute-start.3 = (bf16[2,16,64,128]{3,2,1,0:T(8,128)(2,1)S(1)}, bf16[2,16,64,128]{3,2,1,0:T(8,128)(2,1)S(1)}, u32[]{:S(2)}, u32[]{:S(2)}) collective-permute-start(bf16[2,16,64,128]{3,2,1,0:T(8,128)(2,1)S(1)} %pad_maximum_fusion.1), channel_id=1, source_target_pairs={{0,4},{4,0},{8,12},{12,8},{1,5},{5,1},{9,13},{13,9},{2,6},{6,2},{1... | collective-permute-start | bytes 1572872 | tf_op jit(solution)/shard_map/ppermute | solution.py:242
  97.8 14.9 %copy-start.2 = (f32[8,512,128]{2,1,0:T(8,128)S(1)}, f32[8,512,128]{2,1,0:T(8,128)}, u32[]{:S(2)}) copy-start(f32[8,512,128]{2,1,0:T(8,128)} %get-tuple-element.14) | copy-start | bytes 6291460
  100.2 1.2 collective-permute-start.4
  101.4 3.9 %collective-permute-start.5 = (f32[64,64]{1,0:T(8,128)S(1)}, f32[64,64]{1,0:T(8,128)S(1)}, u32[]{:S(2)}, u32[]{:S(2)}) collective-permute-start(f32[64,64]{1,0:T(8,128)S(1)} %max.15), channel_id=1, source_target_pairs={{0,2},{1,3},{2,0},{3,1},{4,6},{5,7},{6,4},{7,5},{8,10},{9,11},{10,... | collective-permute-start | bytes 49160 | tf_op jit(solution)/shard_map/ppermute | solution.py:218
  105.4 3.9 %collective-permute-start.6 = (f32[64,64]{1,0:T(8,128)S(1)}, f32[64,64]{1,0:T(8,128)S(1)}, u32[]{:S(2)}, u32[]{:S(2)}) collective-permute-start(f32[64,64]{1,0:T(8,128)S(1)} %max.16), channel_id=1, source_target_pairs={{0,4},{4,0},{8,12},{12,8},{1,5},{5,1},{9,13},{13,9},{2,6},{6,2},{1... | collective-permute-start | bytes 49160 | tf_op jit(solution)/shard_map/ppermute | solution.py:218
  109.3 7.6 %collective-permute-start.7 = (f32[64,64]{1,0:T(8,128)S(1)}, f32[64,64]{1,0:T(8,128)S(1)}, u32[]{:S(2)}, u32[]{:S(2)}) collective-permute-start(f32[64,64]{1,0:T(8,128)S(1)} %max.17), channel_id=1, source_target_pairs={{0,8},{4,12},{8,0},{12,4},{1,9},{5,13},{9,1},{13,5},{2,10},{6,14},... | collective-permute-start | bytes 49160 | tf_op jit(solution)/shard_map/ppermute | solution.py:218
  123.3 3.0 %collective-permute-start.8 = (f32[2,2,2,4,8256]{4,3,0,1,2:T(4,128)}, f32[2,2,2,4,8256]{4,3,0,1,2:T(4,128)}, u32[]{:S(2)}, u32[]{:S(2)}) collective-permute-start(f32[2,2,2,4,8256]{4,3,0,1,2:T(4,128)} %fusion.13), channel_id=1, source_target_pairs={{0,1},{1,0},{2,3},{3,2},{4,5},{5,4},{6,7},{7,6},{8,9},{9,8},{10,11... | collective-permute-start | bytes 3170312 | tf_op jit(solution)/shard_map/ppermute | solution.py:231
  127.9 1.0 copy-start.3
  129.0 14.2 %collective-permute-start.9 = (f32[2,2,4,8256]{3,2,0,1:T(4,128)S(1)}, f32[2,2,4,8256]{3,2,0,1:T(4,128)S(1)}, u32[]{:S(2)}, u32[]{:S(2)}) collective-permute-start(f32[2,2,4,8256]{3,2,0,1:T(4,128)S(1)} %dynamic-slice_bitcast_fusion), channel_id=1, source_target_pairs={{0,2},{1,3},{2,0},{3,1},{4,6},{5,7},{6,4},{7,5},{8,10},{9,11},{10,... | collective-permute-start | bytes 1585160 | tf_op jit(solution)/shard_map/ppermute | solution.py:231
  144.4 7.7 %collective-permute-start.10 = (f32[2,4,8256]{2,1,0:T(4,128)S(1)}, f32[2,4,8256]{2,1,0:T(4,128)S(1)}, u32[]{:S(2)}, u32[]{:S(2)}) collective-permute-start(f32[2,4,8256]{2,1,0:T(4,128)S(1)} %dynamic-slice_bitcast_fusion.1), channel_id=1, source_target_pairs={{0,4},{4,0},{8,12},{12,8},{1,5},{5,1},{9,13},{13,9},{2,6},{6,2},{1... | collective-permute-start | bytes 792584 | tf_op jit(solution)/shard_map/ppermute | solution.py:231
  152.2 7.7 %collective-permute-start.11 = (f32[4,8256]{1,0:T(4,128)S(1)}, f32[4,8256]{1,0:T(4,128)S(1)}, u32[]{:S(2)}, u32[]{:S(2)}) collective-permute-start(f32[4,8256]{1,0:T(4,128)S(1)} %dynamic-slice_bitcast_fusion.3), channel_id=1, source_target_pairs={{0,8},{4,12},{8,0},{12,4},{1,9},{5,13},{9,1},{13,5},{2,10},{6,14},... | collective-permute-start | bytes 396296 | tf_op jit(solution)/shard_map/ppermute | solution.py:231
  165.9 23.1 %copy-start.1 = (bf16[64,2048]{1,0:T(8,128)(2,1)S(1)}, bf16[64,2048]{1,0:T(8,128)(2,1)}, u32[]{:S(2)}) copy-start(bf16[64,2048]{1,0:T(8,128)(2,1)} %param.8) | copy-start | bytes 786436
  171.0 8.6 %collective-permute-start.12 = (f32[2,16,2048]{2,1,0:T(8,128)S(1)}, f32[2,16,2048]{2,1,0:T(8,128)S(1)}, u32[]{:S(2)}, u32[]{:S(2)}) collective-permute-start(f32[2,16,2048]{2,1,0:T(8,128)S(1)} %dynamic-slice_bitcast_fusion.2), channel_id=1, source_target_pairs={{0,4},{4,0},{8,12},{12,8},{1,5},{5,1},{9,13},{13,9},{2,6},{6,2},{1... | collective-permute-start | bytes 786440 | tf_op jit(solution)/shard_map/ppermute | solution.py:231
  179.7 8.7 %collective-permute-start.13 = (f32[16,2048]{1,0:T(8,128)S(1)}, f32[16,2048]{1,0:T(8,128)S(1)}, u32[]{:S(2)}, u32[]{:S(2)}) collective-permute-start(f32[16,2048]{1,0:T(8,128)S(1)} %dynamic-slice_bitcast_fusion.4), channel_id=1, source_target_pairs={{0,8},{4,12},{8,0},{12,4},{1,9},{5,13},{9,1},{13,5},{2,10},{6,14},... | collective-permute-start | bytes 393224 | tf_op jit(solution)/shard_map/ppermute | solution.py:231

commit v13 on v11

--- a/solution.py
+++ b/solution.py
@@ -292,15 +292,25 @@
     keyval_cols = lax.dynamic_slice_in_dim(w_keyval, kv_first * (2 * HD), local_kv * 2 * HD, 1)
     query_part = jnp.dot(x_new, w_query, preferred_element_type=jnp.float32)
     keyval_part = jnp.dot(x_new, keyval_cols, preferred_element_type=jnp.float32)
-    width_q = query_part.shape[1]
-    both = axis_sum(jnp.concatenate([query_part, keyval_part], axis=1), "store")
-    query_sum, keyval_sum = both[:, :width_q], both[:, width_q:]
+    keyval_sum = axis_sum(keyval_part, "store")
     keyval_local = keyval_sum.reshape(tok_count, local_kv, 2, HD)
     tok_ids = jnp.arange(tok_count, dtype=jnp.int32)
     tok_sess = tok_ids // TURN
     tok_pos = table_lookup(lengths, tok_sess) + tok_ids % TURN
     tok_angle = tok_pos.astype(jnp.float32)[:, None, None] * freq_table
-    query_rot = to_half(rotate(query_sum.reshape(tok_count, local_heads, HD), tok_angle))
+    if local_heads % shards == 0 and not shards & (shards - 1):
+        s_bits = shards.bit_length() - 1
+        heads_major = jnp.transpose(query_part.reshape(tok_count, local_heads, HD), (1, 0, 2))
+        block = heads_major.reshape((2,) * s_bits + (local_heads // shards, tok_count, HD))
+        block = jnp.transpose(block, tuple(range(s_bits - 1, -1, -1)) + tuple(range(s_bits, s_bits + 3)))
+        block = bit_scatter(block, "store")
+        block = to_half(rotate(block, jnp.transpose(tok_angle, (1, 0, 2))))
+        q_heads = bit_gather(block, "store")
+        query_rot = jnp.transpose(q_heads, (1, 0, 2))
+    else:
+        query_sum = axis_sum(query_part, "store")
+        query_rot = to_half(rotate(query_sum.reshape(tok_count, local_heads, HD), tok_angle))
+        q_heads = jnp.transpose(query_rot, (1, 0, 2))
     key_new = to_half(rotate(keyval_local[:, :, 0], tok_angle))
     value_new = to_half(keyval_local[:, :, 1])
 
@@ -318,7 +328,6 @@
     cos2 = jnp.concatenate([cosine, cosine])[None, :]
     sin2 = jnp.concatenate([-sine, sine])[None, :]
 
-    q_heads = jnp.transpose(query_rot, (1, 0, 2))
     if tensors & (tensors - 1):
         q_all = lax.all_gather(q_heads, "tensor", axis=0, tiled=True)
     else:

time: 187 us -> 180 us (0.963)
  waiting for transfers between devices: 71 us -> 62.8 us
  other arithmetic: 16.1 us -> 13.5 us
  starting transfers between devices: 20.3 us -> 22.8 us
    ppermute x6 -> x8, waiting for transfers between devices: 40.6 us -> 31.3 us  [bit_scatter(): block = keep + lax.ppermute(send, axis, perm=[(i, i ^ d) for i in range(n)])]
    ppermute x2 -> x4, waiting for transfers between devices: 11 us -> 14.6 us  [bit_gather(): other = lax.ppermute(x, axis, perm=[(i, i ^ d) for i in range(n)])]
    ppermute x6 -> x8, starting transfers between devices: 8.54 us -> 11.6 us  [bit_scatter(): block = keep + lax.ppermute(send, axis, perm=[(i, i ^ d) for i in range(n)])]
    ppermute x6, waiting for transfers between devices: 19.4 us -> 16.8 us  [axis_reduce(): x = op(x, lax.ppermute(x, axis, perm=[(i, i ^ d) for i in range(n)]))]
    ppermute x6, starting transfers between devices: 8.05 us -> 5.55 us  [axis_reduce(): x = op(x, lax.ppermute(x, axis, perm=[(i, i ^ d) for i in range(n)]))]
    ppermute x2 -> x4, starting transfers between devices: 3.69 us -> 5.58 us  [bit_gather(): other = lax.ppermute(x, axis, perm=[(i, i ^ d) for i in range(n)])]
  transfers between devices with their start and end apart: 14 -> 18, of which waited for: 11 -> 14; matrix products, arithmetic and copies ran while one was open for 7% -> 8% of each run, Pallas kernels for 7% -> 7%
where the time goes in v13:
time: 180 us; the launch traced here: 179 us
  waiting for transfers between devices  62.8 us (35%)
  Pallas kernels  47.5 us (26%)
  starting transfers between devices  22.8 us (13%)
  other arithmetic  13.5 us (8%)
  matrix products  13.2 us (7%)
  local copies, waits for them, and re-layouts  12 us (7%)
  blocking collectives  5.79 us (3%)
  between operations  1.89 us (1%)
    pallas_call x2, Pallas kernels, hist_attend(): pl.pallas_call(kernel, grid_spec=grid_spec, out_shape=[jax.ShapeDtypeStru...  47.5 us
    ppermute x8, waiting for transfers between devices, bit_scatter(): block = keep + lax.ppermute(send, axis, perm=[(i, i ^ d) for i in range(n)])  31.3 us
    ppermute x6, waiting for transfers between devices, axis_reduce(): x = op(x, lax.ppermute(x, axis, perm=[(i, i ^ d) for i in range(n)]))  16.8 us
    ppermute x4, waiting for transfers between devices, bit_gather(): other = lax.ppermute(x, axis, perm=[(i, i ^ d) for i in range(n)])  14.6 us
    ppermute x8, starting transfers between devices, bit_scatter(): block = keep + lax.ppermute(send, axis, perm=[(i, i ^ d) for i in range(n)])  11.6 us
    all_gather x1, blocking collectives, body(): attended = lax.all_gather(attended, 'store', axis=1, tiled=True)  5.79 us
    ppermute x4, starting transfers between devices, bit_gather(): other = lax.ppermute(x, axis, perm=[(i, i ^ d) for i in range(n)])  5.58 us
    ppermute x6, starting transfers between devices, axis_reduce(): x = op(x, lax.ppermute(x, axis, perm=[(i, i ^ d) for i in range(n)]))  5.55 us
  transfers between devices with their start and end apart: 18, of which 14 were waited for; matrix products, arithmetic and copies ran while one was open for 8% of the time, Pallas kernels for 7%

profile of v13, /device:TPU:0, one launch (start us, length us, event | category | flops | bytes accessed | tf_op | source)
XLA Modules:
  0.0 179.4 jit_solution(17071772055983481463)
XLA Ops:
  0.0 0.9 copy-done
  1.0 4.9 %convolution_bitcast_fusion = f32[8,8,16,128]{3,1,2,0:T(8,128)S(1)} fusion(bf16[64,2048]{1,0:T(8,128)(2,1)S(1)} %copy-done, bf16[2048,2048]{1,0:T(8,128)(2,1)} %param.10), kind=kOutput, calls=%fused_computation.15 | convolution fusion | flops 536870912 | bytes 9175040 | tf_op jit(solution)/shard_map/dot_general | solution.py:293
  5.9 0.1 copy.79
  6.0 0.1 constant_dynamic-slice_fusion.5
  6.2 0.5 collective-permute-start
  7.4 1.2 reduce-window.6
  8.7 0.1 copy.55
  8.9 0.1 copy.56
  9.1 0.2 multiply_cosine_fusion
  9.4 2.6 %collective-permute-start.1 = (f32[4,64,128]{2,1,0:T(8,128)S(1)}, f32[4,64,128]{2,1,0:T(8,128)S(1)}, u32[]{:S(2)}, u32[]{:S(2)}) collective-permute-start(f32[4,64,128]{2,1,0:T(8,128)S(1)} %dynamic-slice_bitcast_fusion.4), channel_id=1, source_target_pairs={{0,2},{1,3},{2,0},{3,1},{4,6},{5,7},{6,4},{7,5},{8,10},{9,11},{10,... | collective-permute-start | bytes 393224 | tf_op jit(solution)/shard_map/ppermute | solution.py:228
  12.0 0.2 fusion.32
  12.2 4.0 %collective-permute-done.1 = f32[4,64,128]{2,1,0:T(8,128)S(1)} collective-permute-done((f32[4,64,128]{2,1,0:T(8,128)S(1)}, f32[4,64,128]{2,1,0:T(8,128)S(1)}, u32[]{:S(2)}, u32[]{:S(2)}) %collective-permute-start.1) | collective-permute-done | bytes 131104 | tf_op jit(solution)/shard_map/ppermute | solution.py:228
  16.2 0.1 subtract_convert_fusion
  16.4 1.8 %collective-permute-start.2 = (bf16[4,64,128]{2,1,0:T(8,128)(2,1)S(1)}, bf16[4,64,128]{2,1,0:T(8,128)(2,1)S(1)}, u32[]{:S(2)}, u32[]{:S(2)}) collective-permute-start(bf16[4,64,128]{2,1,0:T(8,128)(2,1)S(1)} %pad_maximum_fusion.3), channel_id=1, source_target_pairs={{0,2},{1,3},{2,0},{3,1},{4,6},{5,7},{6,4},{7,5},{8,10},{9,11},{10,... | collective-permute-start | bytes 196616 | tf_op jit(solution)/shard_map/ppermute | solution.py:239
  18.8 1.9 %collective-permute-done.2 = bf16[4,64,128]{2,1,0:T(8,128)(2,1)S(1)} collective-permute-done((bf16[4,64,128]{2,1,0:T(8,128)(2,1)S(1)}, bf16[4,64,128]{2,1,0:T(8,128)(2,1)S(1)}, u32[]{:S(2)}, u32[]{:S(2)}) %collective-permute-start.2) | collective-permute-done | bytes 65568 | tf_op jit(solution)/shard_map/ppermute | solution.py:239
  20.7 0.1 select_bitcast_fusion.7
  21.1 1.2 collective-permute-done.3
  22.3 2.9 %collective-permute-start.4 = (bf16[16,64,128]{2,1,0:T(8,128)(2,1)S(1)}, bf16[16,64,128]{2,1,0:T(8,128)(2,1)S(1)}, u32[]{:S(2)}, u32[]{:S(2)}) collective-permute-start(bf16[16,64,128]{2,1,0:T(8,128)(2,1)S(1)} %bitcast.209), channel_id=1, source_target_pairs={{0,8},{4,12},{8,0},{12,4},{1,9},{5,13},{9,1},{13,5},{2,10},{6,14},... | collective-permute-start | bytes 786440 | tf_op jit(solution)/shard_map/ppermute | solution.py:239
  25.2 0.7 maximum_bitcast_fusion.1.cos_ref
  25.9 11.6 %collective-permute-done.4 = bf16[16,64,128]{2,1,0:T(8,128)(2,1)S(1)} collective-permute-done((bf16[16,64,128]{2,1,0:T(8,128)(2,1)S(1)}, bf16[16,64,128]{2,1,0:T(8,128)(2,1)S(1)}, u32[]{:S(2)}, u32[]{:S(2)}) %collective-permute-start.4) | collective-permute-done | bytes 262176 | tf_op jit(solution)/shard_map/ppermute | solution.py:239
  37.6 0.8 collective-permute-start.5
  38.4 0.6 maximum_bitcast_fusion.2.sin_ref
  39.0 0.7 fusion.36
  39.7 13.2 %shard_map.85 = (f32[2,512,128]{2,1,0:T(8,128)}, f32[2,512,1]{2,1,0:T(8,128)}, f32[2,512,1]{2,1,0:T(8,128)}) custom-call(s32[1]{0:T(128)} %bitcast.kv0_ref, bf16[2,512,128]{2,1,0:T(8,128)(2,1)} %bitcast.210, bf16[40,128,2048]{2,1,0:T(8,128)(2,1)} %bitcast.204, bf16[40,128,2048]{2,1,0:T(8,128)(2,1)} %bitcast.205, f32[1,1,5120]{2,1,0:T(1,128)} %bitcast.221, ...), custom_call_target="tpu_custom_call" | custom-call | flops 2684354560 | bytes 6029312 | tf_op jit(solution)/shard_map/pallas_call | solution.py:194
  52.9 1.2 copy.58
  54.2 0.1 maximum_bitcast_fusion
  54.4 1.2 fusion.20.q_ref
  55.6 34.3 %shard_map.86 = (f32[6,512,128]{2,1,0:T(8,128)}, f32[6,512,1]{2,1,0:T(8,128)}, f32[6,512,1]{2,1,0:T(8,128)}) custom-call(s32[1]{0:T(128)} %bitcast.27.kv0_ref, bf16[6,512,128]{2,1,0:T(8,128)(2,1)} %fusion.20.q_ref, bf16[40,128,2048]{2,1,0:T(8,128)(2,1)} %bitcast.206, bf16[40,128,2048]{2,1,0:T(8,128)(2,1)} %bitcast.207, f32[1,1,5120]{2,1,0:T(1,128)} %bitcast.222, ...), custom_call_target="tpu_custom_call" | custom-call | flops 8053063680 | bytes 18087936 | tf_op jit(solution)/shard_map/pallas_call | solution.py:194
  90.0 2.1 %copy.59 = f32[6,512,1]{1,0,2:T(8,128)S(1)} copy(f32[6,512,1]{2,1,0:T(8,128)} %get-tuple-element.14) | data formatting | bytes 24576 | tf_op jit(solution)/shard_map/pallas_call | solution.py:194
  92.2 1.2 collective-permute-done.6
  93.4 1.5 collective-permute-start.7
  94.9 0.2 copy.62
  95.1 2.2 %collective-permute-done.7 = f32[64,64]{1,0:T(8,128)S(1)} collective-permute-done((f32[64,64]{1,0:T(8,128)S(1)}, f32[64,64]{1,0:T(8,128)S(1)}, u32[]{:S(2)}, u32[]{:S(2)}) %collective-permute-start.7) | collective-permute-done | bytes 16416 | tf_op jit(solution)/shard_map/ppermute | solution.py:215
  97.3 1.3 collective-permute-start.8
  98.6 1.9 %fusion.2 = f32[8,512,128]{2,1,0:T(8,128)S(1)} fusion(s32[]{:T(128)S(6)} %select_n.322, f32[2,512,128]{2,1,0:T(8,128)S(1)} %copy-done.2, f32[6,512,128]{2,1,0:T(8,128)} %get-tuple-element.12), kind=kLoop, calls=%fused_computation.8 | loop fusion | flops 1572864 | bytes 4194308 | tf_op jit(solution)/shard_map/concatenate | solution.py:347
  100.6 2.0 %copy.63 = f32[6,512,1]{1,0,2:T(8,128)S(1)} copy(f32[6,512,1]{2,1,0:T(8,128)} %get-tuple-element.16) | data formatting | bytes 24576 | tf_op jit(solution)/shard_map/pallas_call | solution.py:194
  102.6 2.1 %collective-permute-start.9 = (f32[64,64]{1,0:T(8,128)S(1)}, f32[64,64]{1,0:T(8,128)S(1)}, u32[]{:S(2)}, u32[]{:S(2)}) collective-permute-start(f32[64,64]{1,0:T(8,128)S(1)} %max.17), channel_id=1, source_target_pairs={{0,8},{4,12},{8,0},{12,4},{1,9},{5,13},{9,1},{13,5},{2,10},{6,14},... | collective-permute-start | bytes 49160 | tf_op jit(solution)/shard_map/ppermute | solution.py:215
  104.9 1.8 %reshape.439 = f32[2,2,2,2,4,8192]{5,4,3,2,1,0:T(4,128)} reshape(f32[8,512,128]{2,1,0:T(8,128)S(1)} %fusion.2) | data formatting | bytes 4194304 | tf_op jit(solution)/shard_map/reshape | solution.py:352
  106.7 0.8 collective-permute-done.9
  107.5 0.6 mul.261
  108.1 1.8 %mul.262 = f32[2,2,2,2,4,8192]{5,4,3,2,1,0:T(4,128)} reshape(f32[64,64,128]{2,1,0:T(8,128)S(1)} %mul.261) | data formatting | bytes 4194304 | tf_op jit(solution)/shard_map/mul | solution.py:359
  109.9 2.8 %mul.263 = f32[2,2,2,2,4,8192]{5,4,3,2,1,0:T(4,128)S(1)} multiply(f32[2,2,2,2,4,8192]{5,4,3,2,1,0:T(4,128)} %reshape.439, f32[2,2,2,2,4,8192]{5,4,3,2,1,0:T(4,128)} %mul.262) | non-fusion elementwise | flops 524288 | bytes 6291456 | tf_op jit(solution)/shard_map/mul | solution.py:359
  112.7 1.3 fusion.16
  114.0 2.9 %collective-permute-done.10 = f32[2,2,2,4,8256]{4,3,0,1,2:T(4,128)S(1)} collective-permute-done((f32[2,2,2,4,8256]{4,3,0,1,2:T(4,128)}, f32[2,2,2,4,8256]{4,3,0,1,2:T(4,128)S(1)}, u32[]{:S(2)}, u32[]{:S(2)}) %collective-permute-start.10) | collective-permute-done | bytes 1056800 | tf_op jit(solution)/shard_map/ppermute | solution.py:228
  116.9 0.4 fusion.19
  117.4 1.6 collective-permute-start.11
  119.0 2.1 %fusion.5 = f32[64,512]{1,0:T(8,128)S(1)} fusion(bf16[64,2048]{1,0:T(8,128)(2,1)S(1)} %copy-done, bf16[2048,2048]{1,0:T(8,128)(2,1)} %param.11, s32[]{:T(128)S(6)} %select_n.328), kind=kOutput, calls=%fused_computation.16 | convolution fusion | flops 134217728 | bytes 2490372 | tf_op jit(solution)/shard_map/dot_general | solution.py:294
  121.2 1.3 collective-permute-done.14
  122.5 0.5 collective-permute-start.15
  123.1 11.3 %collective-permute-done.15 = f32[64,512]{1,0:T(8,128)S(1)} collective-permute-done((f32[64,512]{1,0:T(8,128)S(1)}, f32[64,512]{1,0:T(8,128)S(1)}, u32[]{:S(2)}, u32[]{:S(2)}) %collective-permute-start.15) | collective-permute-done | bytes 131104 | tf_op jit(solution)/shard_map/ppermute | solution.py:215
  134.6 0.1 bitcast_add_fusion
  134.8 1.3 collective-permute-start.12
  136.3 6.2 %collective-permute-done.12 = f32[2,4,8256]{2,1,0:T(4,128)S(1)} collective-permute-done((f32[2,4,8256]{2,1,0:T(4,128)S(1)}, f32[2,4,8256]{2,1,0:T(4,128)S(1)}, u32[]{:S(2)}, u32[]{:S(2)}) %collective-permute-start.12) | collective-permute-done | bytes 264224 | tf_op jit(solution)/shard_map/ppermute | solution.py:228
  142.5 2.5 %collective-permute-start.13 = (f32[4,8256]{1,0:T(4,128)S(1)}, f32[4,8256]{1,0:T(4,128)S(1)}, u32[]{:S(2)}, u32[]{:S(2)}) collective-permute-start(f32[4,8256]{1,0:T(4,128)S(1)} %dynamic-slice_bitcast_fusion.2), channel_id=1, source_target_pairs={{0,8},{4,12},{8,0},{12,4},{1,9},{5,13},{9,1},{13,5},{2,10},{6,14},... | collective-permute-start | bytes 396296 | tf_op jit(solution)/shard_map/ppermute | solution.py:228
  145.0 1.1 fusion.67
  146.1 4.1 %collective-permute-done.13 = f32[4,8256]{1,0:T(4,128)S(1)} collective-permute-done((f32[4,8256]{1,0:T(4,128)S(1)}, f32[4,8256]{1,0:T(4,128)S(1)}, u32[]{:S(2)}, u32[]{:S(2)}) %collective-permute-start.13) | collective-permute-done | bytes 132128 | tf_op jit(solution)/shard_map/ppermute | solution.py:228
  150.3 0.2 fusion.14
  150.6 5.8 %all_gather.3 = bf16[64,2048]{1,0:T(8,128)(2,1)S(1)} all-gather(bf16[64,512]{1,0:T(8,128)(2,1)S(1)} %bitcast.219), channel_id=1, replica_groups=mesh['groups'=2,'tensor'=4,'store'=4] {'store'}, dimensions={1}, use_global_device_ids=true | all-gather | bytes 327680 | tf_op jit(solution)/shard_map/all_gather | solution.py:401
  156.4 4.9 %fusion.68 = f32[64,2048]{1,0:T(8,128)S(1)} fusion(bf16[64,2048]{1,0:T(8,128)(2,1)S(1)} %all_gather.3, bf16[2048,2048]{1,0:T(8,128)(2,1)} %param.12), kind=kOutput, calls=%fused_computation.162 | convolution fusion | flops 536870912 | bytes 9175040 | tf_op jit(solution)/shard_map/dot_general | solution.py:427
  161.4 0.8 collective-permute-start.16
  162.1 7.9 %collective-permute-done.16 = f32[2,16,2048]{2,1,0:T(8,128)S(1)} collective-permute-done((f32[2,16,2048]{2,1,0:T(8,128)S(1)}, f32[2,16,2048]{2,1,0:T(8,128)S(1)}, u32[]{:S(2)}, u32[]{:S(2)}) %collective-permute-start.16) | collective-permute-done | bytes 262176 | tf_op jit(solution)/shard_map/ppermute | solution.py:228
  170.1 2.4 %collective-permute-start.17 = (f32[16,2048]{1,0:T(8,128)S(1)}, f32[16,2048]{1,0:T(8,128)S(1)}, u32[]{:S(2)}, u32[]{:S(2)}) collective-permute-start(f32[16,2048]{1,0:T(8,128)S(1)} %dynamic-slice_bitcast_fusion.3), channel_id=1, source_target_pairs={{0,8},{4,12},{8,0},{12,4},{1,9},{5,13},{9,1},{13,5},{2,10},{6,14},... | collective-permute-start | bytes 393224 | tf_op jit(solution)/shard_map/ppermute | solution.py:228
  172.5 6.3 %collective-permute-done.17 = f32[16,2048]{1,0:T(8,128)S(1)} collective-permute-done((f32[16,2048]{1,0:T(8,128)S(1)}, f32[16,2048]{1,0:T(8,128)S(1)}, u32[]{:S(2)}, u32[]{:S(2)}) %collective-permute-start.17) | collective-permute-done | bytes 131104 | tf_op jit(solution)/shard_map/ppermute | solution.py:228
  178.8 0.6 fusion.22
  (74 shorter events, 2.3 us)
Async XLA Ops:
  0.0 1.0 copy-start
  5.9 1.5 copy-start.4
  6.2 3.1 %collective-permute-start = (f32[2,4,64,128]{3,2,1,0:T(8,128)S(1)}, f32[2,4,64,128]{3,2,1,0:T(8,128)S(1)}, u32[]{:S(2)}, u32[]{:S(2)}) collective-permute-start(f32[2,4,64,128]{3,2,1,0:T(8,128)S(1)} %bitcast.220), channel_id=1, source_target_pairs={{0,1},{1,0},{2,3},{3,2},{4,5},{5,4},{6,7},{7,6},{8,9},{9,8},{10,11... | collective-permute-start | bytes 786440 | tf_op jit(solution)/shard_map/ppermute | solution.py:228
  9.4 6.7 %collective-permute-start.1 = (f32[4,64,128]{2,1,0:T(8,128)S(1)}, f32[4,64,128]{2,1,0:T(8,128)S(1)}, u32[]{:S(2)}, u32[]{:S(2)}) collective-permute-start(f32[4,64,128]{2,1,0:T(8,128)S(1)} %dynamic-slice_bitcast_fusion.4), channel_id=1, source_target_pairs={{0,2},{1,3},{2,0},{3,1},{4,6},{5,7},{6,4},{7,5},{8,10},{9,11},{10,... | collective-permute-start | bytes 393224 | tf_op jit(solution)/shard_map/ppermute | solution.py:228
  16.4 4.3 %collective-permute-start.2 = (bf16[4,64,128]{2,1,0:T(8,128)(2,1)S(1)}, bf16[4,64,128]{2,1,0:T(8,128)(2,1)S(1)}, u32[]{:S(2)}, u32[]{:S(2)}) collective-permute-start(bf16[4,64,128]{2,1,0:T(8,128)(2,1)S(1)} %pad_maximum_fusion.3), channel_id=1, source_target_pairs={{0,2},{1,3},{2,0},{3,1},{4,6},{5,7},{6,4},{7,5},{8,10},{9,11},{10,... | collective-permute-start | bytes 196616 | tf_op jit(solution)/shard_map/ppermute | solution.py:239
  20.8 1.4 collective-permute-start.3
  22.3 17.4 %copy-start.1 = (bf16[2,2,4,64,128]{4,3,2,0,1:T(8,128)(2,1)}, bf16[2,2,4,64,128]{4,3,2,0,1:T(8,128)(2,1)S(1)}, u32[]{:S(2)}) copy-start(bf16[2,2,4,64,128]{4,3,2,0,1:T(8,128)(2,1)S(1)} %pad_maximum_fusion.1) | copy-start | bytes 786436
  22.3 15.1 %collective-permute-start.4 = (bf16[16,64,128]{2,1,0:T(8,128)(2,1)S(1)}, bf16[16,64,128]{2,1,0:T(8,128)(2,1)S(1)}, u32[]{:S(2)}, u32[]{:S(2)}) collective-permute-start(bf16[16,64,128]{2,1,0:T(8,128)(2,1)S(1)} %bitcast.209), channel_id=1, source_target_pairs={{0,8},{4,12},{8,0},{12,4},{1,9},{5,13},{9,1},{13,5},{2,10},{6,14},... | collective-permute-start | bytes 786440 | tf_op jit(solution)/shard_map/ppermute | solution.py:239
  37.6 16.5 %collective-permute-start.5 = (bf16[2,16,64,128]{3,2,1,0:T(8,128)(2,1)S(1)}, bf16[2,16,64,128]{3,2,1,0:T(8,128)(2,1)S(1)}, u32[]{:S(2)}, u32[]{:S(2)}) collective-permute-start(bf16[2,16,64,128]{3,2,1,0:T(8,128)(2,1)S(1)} %pad_maximum_fusion), channel_id=1, source_target_pairs={{0,4},{4,0},{8,12},{12,8},{1,5},{5,1},{9,13},{13,9},{2,6},{6,2},{1... | collective-permute-start | bytes 1572872 | tf_op jit(solution)/shard_map/ppermute | solution.py:239
  89.9 5.0 %copy-start.3 = (f32[2,512,1]{2,1,0:T(8,128)S(1)}, f32[2,512,1]{2,1,0:T(8,128)}, u32[]{:S(2)}) copy-start(f32[2,512,1]{2,1,0:T(8,128)} %get-tuple-element.15) | copy-start | bytes 12292
  89.9 8.7 %copy-start.2 = (f32[2,512,128]{2,1,0:T(8,128)S(1)}, f32[2,512,128]{2,1,0:T(8,128)}, u32[]{:S(2)}) copy-start(f32[2,512,128]{2,1,0:T(8,128)} %get-tuple-element.11) | copy-start | bytes 1572868
  92.2 1.2 collective-permute-start.6
  93.4 3.9 %collective-permute-start.7 = (f32[64,64]{1,0:T(8,128)S(1)}, f32[64,64]{1,0:T(8,128)S(1)}, u32[]{:S(2)}, u32[]{:S(2)}) collective-permute-start(f32[64,64]{1,0:T(8,128)S(1)} %max.15), channel_id=1, source_target_pairs={{0,2},{1,3},{2,0},{3,1},{4,6},{5,7},{6,4},{7,5},{8,10},{9,11},{10,... | collective-permute-start | bytes 49160 | tf_op jit(solution)/shard_map/ppermute | solution.py:215
  97.3 5.3 %collective-permute-start.8 = (f32[64,64]{1,0:T(8,128)S(1)}, f32[64,64]{1,0:T(8,128)S(1)}, u32[]{:S(2)}, u32[]{:S(2)}) collective-permute-start(f32[64,64]{1,0:T(8,128)S(1)} %max.16), channel_id=1, source_target_pairs={{0,4},{4,0},{8,12},{12,8},{1,5},{5,1},{9,13},{13,9},{2,6},{6,2},{1... | collective-permute-start | bytes 49160 | tf_op jit(solution)/shard_map/ppermute | solution.py:215
  102.6 4.9 %collective-permute-start.9 = (f32[64,64]{1,0:T(8,128)S(1)}, f32[64,64]{1,0:T(8,128)S(1)}, u32[]{:S(2)}, u32[]{:S(2)}) collective-permute-start(f32[64,64]{1,0:T(8,128)S(1)} %max.17), channel_id=1, source_target_pairs={{0,8},{4,12},{8,0},{12,4},{1,9},{5,13},{9,1},{13,5},{2,10},{6,14},... | collective-permute-start | bytes 49160 | tf_op jit(solution)/shard_map/ppermute | solution.py:215
  114.0 2.9 %collective-permute-start.10 = (f32[2,2,2,4,8256]{4,3,0,1,2:T(4,128)}, f32[2,2,2,4,8256]{4,3,0,1,2:T(4,128)S(1)}, u32[]{:S(2)}, u32[]{:S(2)}) collective-permute-start(f32[2,2,2,4,8256]{4,3,0,1,2:T(4,128)} %fusion.16), channel_id=1, source_target_pairs={{0,1},{1,0},{2,3},{3,2},{4,5},{5,4},{6,7},{7,6},{8,9},{9,8},{10,11... | collective-permute-start | bytes 3170312 | tf_op jit(solution)/shard_map/ppermute | solution.py:228
  117.4 17.2 %collective-permute-start.11 = (f32[2,2,4,8256]{3,2,1,0:T(4,128)S(1)}, f32[2,2,4,8256]{3,2,1,0:T(4,128)S(1)}, u32[]{:S(2)}, u32[]{:S(2)}) collective-permute-start(f32[2,2,4,8256]{3,2,1,0:T(4,128)S(1)} %bitcast.216), channel_id=1, source_target_pairs={{0,2},{1,3},{2,0},{3,1},{4,6},{5,7},{6,4},{7,5},{8,10},{9,11},{10,... | collective-permute-start | bytes 1585160 | tf_op jit(solution)/shard_map/ppermute | solution.py:228
  121.0 1.4 collective-permute-start.14
  122.5 11.9 %collective-permute-start.15 = (f32[64,512]{1,0:T(8,128)S(1)}, f32[64,512]{1,0:T(8,128)S(1)}, u32[]{:S(2)}, u32[]{:S(2)}) collective-permute-start(f32[64,512]{1,0:T(8,128)S(1)} %add.283), channel_id=1, source_target_pairs={{0,2},{1,3},{2,0},{3,1},{4,6},{5,7},{6,4},{7,5},{8,10},{9,11},{10,... | collective-permute-start | bytes 393224 | tf_op jit(solution)/shard_map/ppermute | solution.py:215
  134.8 7.7 %collective-permute-start.12 = (f32[2,4,8256]{2,1,0:T(4,128)S(1)}, f32[2,4,8256]{2,1,0:T(4,128)S(1)}, u32[]{:S(2)}, u32[]{:S(2)}) collective-permute-start(f32[2,4,8256]{2,1,0:T(4,128)S(1)} %dynamic-slice_bitcast_fusion), channel_id=1, source_target_pairs={{0,4},{4,0},{8,12},{12,8},{1,5},{5,1},{9,13},{13,9},{2,6},{6,2},{1... | collective-permute-start | bytes 792584 | tf_op jit(solution)/shard_map/ppermute | solution.py:228
  142.5 7.7 %collective-permute-start.13 = (f32[4,8256]{1,0:T(4,128)S(1)}, f32[4,8256]{1,0:T(4,128)S(1)}, u32[]{:S(2)}, u32[]{:S(2)}) collective-permute-start(f32[4,8256]{1,0:T(4,128)S(1)} %dynamic-slice_bitcast_fusion.2), channel_id=1, source_target_pairs={{0,8},{4,12},{8,0},{12,4},{1,9},{5,13},{9,1},{13,5},{2,10},{6,14},... | collective-permute-start | bytes 396296 | tf_op jit(solution)/shard_map/ppermute | solution.py:228
  161.4 8.6 %collective-permute-start.16 = (f32[2,16,2048]{2,1,0:T(8,128)S(1)}, f32[2,16,2048]{2,1,0:T(8,128)S(1)}, u32[]{:S(2)}, u32[]{:S(2)}) collective-permute-start(f32[2,16,2048]{2,1,0:T(8,128)S(1)} %dynamic-slice_bitcast_fusion.1), channel_id=1, source_target_pairs={{0,4},{4,0},{8,12},{12,8},{1,5},{5,1},{9,13},{13,9},{2,6},{6,2},{1... | collective-permute-start | bytes 786440 | tf_op jit(solution)/shard_map/ppermute | solution.py:228
  170.1 8.7 %collective-permute-start.17 = (f32[16,2048]{1,0:T(8,128)S(1)}, f32[16,2048]{1,0:T(8,128)S(1)}, u32[]{:S(2)}, u32[]{:S(2)}) collective-permute-start(f32[16,2048]{1,0:T(8,128)S(1)} %dynamic-slice_bitcast_fusion.3), channel_id=1, source_target_pairs={{0,8},{4,12},{8,0},{12,4},{1,9},{5,13},{9,1},{13,5},{2,10},{6,14},... | collective-permute-start | bytes 393224 | tf_op jit(solution)/shard_map/ppermute | solution.py:228

commit v14 on v13

--- a/solution.py
+++ b/solution.py
@@ -307,10 +307,17 @@
         block = to_half(rotate(block, jnp.transpose(tok_angle, (1, 0, 2))))
         q_heads = bit_gather(block, "store")
         query_rot = jnp.transpose(q_heads, (1, 0, 2))
+        q_all = bit_gather(block, "tensor")
+        if tensors & (tensors - 1):
+            q_all = None
+        else:
+            q_all = bit_gather(q_all, "store").reshape((shards, tensors) + block.shape)
+            q_all = jnp.transpose(q_all, (1, 0, 2, 3, 4)).reshape((HQ,) + block.shape[1:])
     else:
         query_sum = axis_sum(query_part, "store")
         query_rot = to_half(rotate(query_sum.reshape(tok_count, local_heads, HD), tok_angle))
         q_heads = jnp.transpose(query_rot, (1, 0, 2))
+        q_all = None
     key_new = to_half(rotate(keyval_local[:, :, 0], tok_angle))
     value_new = to_half(keyval_local[:, :, 1])
 
@@ -328,9 +335,9 @@
     cos2 = jnp.concatenate([cosine, cosine])[None, :]
     sin2 = jnp.concatenate([-sine, sine])[None, :]
 
-    if tensors & (tensors - 1):
+    if q_all is None and tensors & (tensors - 1):
         q_all = lax.all_gather(q_heads, "tensor", axis=0, tiled=True)
-    else:
+    elif q_all is None:
         q_all = bit_gather(q_heads, "tensor")
     q_k = q_all.reshape(kv_heads, group_size * tok_count, HD)
     if local_heads % group_size == 0:

time: 180 us -> 177 us (0.983)
  waiting for transfers between devices: 62.8 us -> 59.9 us
    ppermute x4 -> x6, waiting for transfers between devices: 14.6 us -> 9.37 us  [bit_gather(): other = lax.ppermute(x, axis, perm=[(i, i ^ d) for i in range(n)])]
    ppermute x8, starting transfers between devices: 11.6 us -> 8.37 us  [bit_scatter(): block = keep + lax.ppermute(send, axis, perm=[(i, i ^ d) for i in range(n)])]
    ppermute x8, waiting for transfers between devices: 31.3 us -> 33.8 us  [bit_scatter(): block = keep + lax.ppermute(send, axis, perm=[(i, i ^ d) for i in range(n)])]
    ppermute x4 -> x6, starting transfers between devices: 5.58 us -> 6.6 us  [bit_gather(): other = lax.ppermute(x, axis, perm=[(i, i ^ d) for i in range(n)])]
  transfers between devices with their start and end apart: 18 -> 20, of which waited for: 14 -> 14; matrix products, arithmetic and copies ran while one was open for 8% -> 9% of each run, Pallas kernels for 7% -> 7%
where the time goes in v14:
time: 177 us
  waiting for transfers between devices  59.9 us (34%)
  Pallas kernels  47.5 us (27%)
  starting transfers between devices  22.2 us (13%)
  other arithmetic  13.5 us (8%)
  matrix products  13.2 us (7%)
  local copies, waits for them, and re-layouts  12.8 us (7%)
  blocking collectives  5.79 us (3%)
  between operations  1.96 us (1%)
    pallas_call x2, Pallas kernels, hist_attend(): pl.pallas_call(kernel, grid_spec=grid_spec, out_shape=[jax.ShapeDtypeStru...  47.5 us
    ppermute x8, waiting for transfers between devices, bit_scatter(): block = keep + lax.ppermute(send, axis, perm=[(i, i ^ d) for i in range(n)])  33.8 us
    ppermute x6, waiting for transfers between devices, axis_reduce(): x = op(x, lax.ppermute(x, axis, perm=[(i, i ^ d) for i in range(n)]))  16.8 us
    ppermute x6, waiting for transfers between devices, bit_gather(): other = lax.ppermute(x, axis, perm=[(i, i ^ d) for i in range(n)])  9.37 us
    ppermute x8, starting transfers between devices, bit_scatter(): block = keep + lax.ppermute(send, axis, perm=[(i, i ^ d) for i in range(n)])  8.37 us
    ppermute x6, starting transfers between devices, axis_reduce(): x = op(x, lax.ppermute(x, axis, perm=[(i, i ^ d) for i in range(n)]))  7.27 us
    ppermute x6, starting transfers between devices, bit_gather(): other = lax.ppermute(x, axis, perm=[(i, i ^ d) for i in range(n)])  6.6 us
    all_gather x1, blocking collectives, body(): attended = lax.all_gather(attended, 'store', axis=1, tiled=True)  5.79 us
  transfers between devices with their start and end apart: 20, of which 14 were waited for; matrix products, arithmetic and copies ran while one was open for 9% of the time, Pallas kernels for 7%

profile of v14, /device:TPU:0, one launch (start us, length us, event | category | flops | bytes accessed | tf_op | source)
XLA Modules:
  0.0 176.9 jit_solution(6548718679421009821)
XLA Ops:
  0.0 0.9 copy-done
  1.0 4.9 %convolution_bitcast_fusion = f32[8,8,16,128]{3,1,2,0:T(8,128)S(1)} fusion(bf16[64,2048]{1,0:T(8,128)(2,1)S(1)} %copy-done, bf16[2048,2048]{1,0:T(8,128)(2,1)} %param.10), kind=kOutput, calls=%fused_computation.15 | convolution fusion | flops 536870912 | bytes 9175040 | tf_op jit(solution)/shard_map/dot_general | solution.py:293
  6.0 0.1 constant_dynamic-slice_fusion.5
  6.2 0.5 collective-permute-start
  7.4 1.2 reduce-window.6
  8.7 0.1 copy.60
  9.1 0.2 fusion.32
  9.3 0.2 multiply_cosine_fusion
  9.6 2.6 %collective-permute-start.1 = (f32[4,64,128]{2,1,0:T(8,128)S(1)}, f32[4,64,128]{2,1,0:T(8,128)S(1)}, u32[]{:S(2)}, u32[]{:S(2)}) collective-permute-start(f32[4,64,128]{2,1,0:T(8,128)S(1)} %dynamic-slice_bitcast_fusion.4), channel_id=1, source_target_pairs={{0,2},{1,3},{2,0},{3,1},{4,6},{5,7},{6,4},{7,5},{8,10},{9,11},{10,... | collective-permute-start | bytes 393224 | tf_op jit(solution)/shard_map/ppermute | solution.py:228
  12.2 4.2 %collective-permute-done.1 = f32[4,64,128]{2,1,0:T(8,128)S(1)} collective-permute-done((f32[4,64,128]{2,1,0:T(8,128)S(1)}, f32[4,64,128]{2,1,0:T(8,128)S(1)}, u32[]{:S(2)}, u32[]{:S(2)}) %collective-permute-start.1) | collective-permute-done | bytes 131104 | tf_op jit(solution)/shard_map/ppermute | solution.py:228
  16.4 0.1 subtract_convert_fusion
  16.6 1.8 %collective-permute-start.2 = (bf16[4,64,128]{2,1,0:T(8,128)(2,1)S(1)}, bf16[4,64,128]{2,1,0:T(8,128)(2,1)S(1)}, u32[]{:S(2)}, u32[]{:S(2)}) collective-permute-start(bf16[4,64,128]{2,1,0:T(8,128)(2,1)S(1)} %pad_maximum_fusion.4), channel_id=1, source_target_pairs={{0,2},{1,3},{2,0},{3,1},{4,6},{5,7},{6,4},{7,5},{8,10},{9,11},{10,... | collective-permute-start | bytes 196616 | tf_op jit(solution)/shard_map/ppermute | solution.py:239
  18.4 2.6 %collective-permute-start.4 = (bf16[4,64,128]{2,1,0:T(8,128)(2,1)S(1)}, bf16[4,64,128]{2,1,0:T(8,128)(2,1)S(1)}, u32[]{:S(2)}, u32[]{:S(2)}) collective-permute-start(bf16[4,64,128]{2,1,0:T(8,128)(2,1)S(1)} %pad_maximum_fusion.4), channel_id=1, source_target_pairs={{0,8},{4,12},{8,0},{12,4},{1,9},{5,13},{9,1},{13,5},{2,10},{6,14},... | collective-permute-start | bytes 196616 | tf_op jit(solution)/shard_map/ppermute | solution.py:239
  21.0 0.7 fusion.36
  22.4 1.4 collective-permute-done.4
  23.8 0.1 select_bitcast_fusion.9
  23.9 1.5 collective-permute-start.5
  25.5 3.4 %collective-permute-done.5 = bf16[2,4,64,128]{3,2,1,0:T(8,128)(2,1)S(1)} collective-permute-done((bf16[2,4,64,128]{3,2,1,0:T(8,128)(2,1)S(1)}, bf16[2,4,64,128]{3,2,1,0:T(8,128)(2,1)S(1)}, u32[]{:S(2)}, u32[]{:S(2)}) %collective-permute-start.5) | collective-permute-done | bytes 131104 | tf_op jit(solution)/shard_map/ppermute | solution.py:239
  29.0 0.6 collective-permute-start.6
  29.6 0.6 maximum_bitcast_fusion.2.cos_ref
  30.3 0.6 maximum_bitcast_fusion.3.sin_ref
  30.9 4.5 %collective-permute-done.6 = bf16[16,64,128]{2,1,0:T(8,128)(2,1)S(1)} collective-permute-done((bf16[16,64,128]{2,1,0:T(8,128)(2,1)S(1)}, bf16[16,64,128]{2,1,0:T(8,128)(2,1)S(1)}, u32[]{:S(2)}, u32[]{:S(2)}) %collective-permute-start.6) | collective-permute-done | bytes 262176 | tf_op jit(solution)/shard_map/ppermute | solution.py:239
  35.7 0.7 copy.59
  36.5 13.2 %shard_map.85 = (f32[2,512,128]{2,1,0:T(8,128)}, f32[2,512,1]{2,1,0:T(8,128)}, f32[2,512,1]{2,1,0:T(8,128)}) custom-call(s32[1]{0:T(128)} %bitcast.kv0_ref, bf16[2,512,128]{2,1,0:T(8,128)(2,1)} %bitcast.226, bf16[40,128,2048]{2,1,0:T(8,128)(2,1)} %bitcast.217, bf16[40,128,2048]{2,1,0:T(8,128)(2,1)} %bitcast.218, f32[1,1,5120]{2,1,0:T(1,128)} %bitcast.235, ...), custom_call_target="tpu_custom_call" | custom-call | flops 2684354560 | bytes 6029312 | tf_op jit(solution)/shard_map/pallas_call | solution.py:194
  49.6 1.2 copy.65
  51.0 0.1 maximum_bitcast_fusion
  51.2 1.2 fusion.20.q_ref
  52.4 34.3 %shard_map.86 = (f32[6,512,128]{2,1,0:T(8,128)}, f32[6,512,1]{2,1,0:T(8,128)}, f32[6,512,1]{2,1,0:T(8,128)}) custom-call(s32[1]{0:T(128)} %bitcast.26.kv0_ref, bf16[6,512,128]{2,1,0:T(8,128)(2,1)} %fusion.20.q_ref, bf16[40,128,2048]{2,1,0:T(8,128)(2,1)} %bitcast.219, bf16[40,128,2048]{2,1,0:T(8,128)(2,1)} %bitcast.220, f32[1,1,5120]{2,1,0:T(1,128)} %bitcast.236, ...), custom_call_target="tpu_custom_call" | custom-call | flops 8053063680 | bytes 18087936 | tf_op jit(solution)/shard_map/pallas_call | solution.py:194
  86.8 2.1 %copy.66 = f32[6,512,1]{1,0,2:T(8,128)S(1)} copy(f32[6,512,1]{2,1,0:T(8,128)} %get-tuple-element.14) | data formatting | bytes 24576 | tf_op jit(solution)/shard_map/pallas_call | solution.py:194
  89.0 0.5 collective-permute-start.8
  89.5 0.9 collective-permute-done.8
  90.3 0.5 collective-permute-start.9
  90.9 0.2 copy.69
  91.1 3.2 %collective-permute-done.9 = f32[64,64]{1,0:T(8,128)S(1)} collective-permute-done((f32[64,64]{1,0:T(8,128)S(1)}, f32[64,64]{1,0:T(8,128)S(1)}, u32[]{:S(2)}, u32[]{:S(2)}) %collective-permute-start.9) | collective-permute-done | bytes 16416 | tf_op jit(solution)/shard_map/ppermute | solution.py:215
  94.3 1.4 collective-permute-start.10
  95.7 1.9 %fusion.2 = f32[8,512,128]{2,1,0:T(8,128)S(1)} fusion(s32[]{:T(128)S(6)} %select_n.354, f32[2,512,128]{2,1,0:T(8,128)S(1)} %copy-done.1, f32[6,512,128]{2,1,0:T(8,128)} %get-tuple-element.12), kind=kLoop, calls=%fused_computation.8 | loop fusion | flops 1572864 | bytes 4194308 | tf_op jit(solution)/shard_map/concatenate | solution.py:354
  97.6 2.0 %copy.70 = f32[6,512,1]{1,0,2:T(8,128)S(1)} copy(f32[6,512,1]{2,1,0:T(8,128)} %get-tuple-element.16) | data formatting | bytes 24576 | tf_op jit(solution)/shard_map/pallas_call | solution.py:194
  99.7 3.2 %collective-permute-start.11 = (f32[64,64]{1,0:T(8,128)S(1)}, f32[64,64]{1,0:T(8,128)S(1)}, u32[]{:S(2)}, u32[]{:S(2)}) collective-permute-start(f32[64,64]{1,0:T(8,128)S(1)} %max.17), channel_id=1, source_target_pairs={{0,8},{4,12},{8,0},{12,4},{1,9},{5,13},{9,1},{13,5},{2,10},{6,14},... | collective-permute-start | bytes 49160 | tf_op jit(solution)/shard_map/ppermute | solution.py:215
  103.0 1.8 %reshape.442 = f32[2,2,2,2,4,8192]{5,4,3,2,1,0:T(4,128)} reshape(f32[8,512,128]{2,1,0:T(8,128)S(1)} %fusion.2) | data formatting | bytes 4194304 | tf_op jit(solution)/shard_map/reshape | solution.py:359
  104.8 0.1 collective-permute-done.11
  105.0 0.6 mul.261
  105.6 1.8 %mul.262 = f32[2,2,2,2,4,8192]{5,4,3,2,1,0:T(4,128)} reshape(f32[64,64,128]{2,1,0:T(8,128)S(1)} %mul.261) | data formatting | bytes 4194304 | tf_op jit(solution)/shard_map/mul | solution.py:366
  107.4 2.8 %mul.263 = f32[2,2,2,2,4,8192]{5,4,3,2,1,0:T(4,128)S(1)} multiply(f32[2,2,2,2,4,8192]{5,4,3,2,1,0:T(4,128)} %reshape.442, f32[2,2,2,2,4,8192]{5,4,3,2,1,0:T(4,128)} %mul.262) | non-fusion elementwise | flops 524288 | bytes 6291456 | tf_op jit(solution)/shard_map/mul | solution.py:366
  110.1 1.3 fusion.16
  111.4 2.9 %collective-permute-done.12 = f32[2,2,2,4,8256]{4,3,0,1,2:T(4,128)S(1)} collective-permute-done((f32[2,2,2,4,8256]{4,3,0,1,2:T(4,128)}, f32[2,2,2,4,8256]{4,3,0,1,2:T(4,128)S(1)}, u32[]{:S(2)}, u32[]{:S(2)}) %collective-permute-start.12) | collective-permute-done | bytes 1056800 | tf_op jit(solution)/shard_map/ppermute | solution.py:228
  114.3 0.4 fusion.19
  114.8 0.6 collective-permute-start.13
  115.4 2.1 %fusion.5 = f32[64,512]{1,0:T(8,128)S(1)} fusion(bf16[64,2048]{1,0:T(8,128)(2,1)S(1)} %copy-done, bf16[2048,2048]{1,0:T(8,128)(2,1)} %param.11, s32[]{:T(128)S(6)} %select_n.360), kind=kOutput, calls=%fused_computation.16 | convolution fusion | flops 134217728 | bytes 2490372 | tf_op jit(solution)/shard_map/dot_general | solution.py:294
  117.6 1.3 collective-permute-done.16
  118.9 1.5 collective-permute-start.17
  120.5 11.3 %collective-permute-done.17 = f32[64,512]{1,0:T(8,128)S(1)} collective-permute-done((f32[64,512]{1,0:T(8,128)S(1)}, f32[64,512]{1,0:T(8,128)S(1)}, u32[]{:S(2)}, u32[]{:S(2)}) %collective-permute-start.17) | collective-permute-done | bytes 131104 | tf_op jit(solution)/shard_map/ppermute | solution.py:215
  132.0 0.1 bitcast_add_fusion
  132.2 0.3 collective-permute-start.14
  132.7 7.2 %collective-permute-done.14 = f32[2,4,8256]{2,1,0:T(4,128)S(1)} collective-permute-done((f32[2,4,8256]{2,1,0:T(4,128)S(1)}, f32[2,4,8256]{2,1,0:T(4,128)S(1)}, u32[]{:S(2)}, u32[]{:S(2)}) %collective-permute-start.14) | collective-permute-done | bytes 264224 | tf_op jit(solution)/shard_map/ppermute | solution.py:228
  140.0 2.9 %collective-permute-start.15 = (f32[4,8256]{1,0:T(4,128)S(1)}, f32[4,8256]{1,0:T(4,128)S(1)}, u32[]{:S(2)}, u32[]{:S(2)}) collective-permute-start(f32[4,8256]{1,0:T(4,128)S(1)} %dynamic-slice_bitcast_fusion.2), channel_id=1, source_target_pairs={{0,8},{4,12},{8,0},{12,4},{1,9},{5,13},{9,1},{13,5},{2,10},{6,14},... | collective-permute-start | bytes 396296 | tf_op jit(solution)/shard_map/ppermute | solution.py:228
  142.8 1.1 fusion.67
  144.0 3.8 %collective-permute-done.15 = f32[4,8256]{1,0:T(4,128)S(1)} collective-permute-done((f32[4,8256]{1,0:T(4,128)S(1)}, f32[4,8256]{1,0:T(4,128)S(1)}, u32[]{:S(2)}, u32[]{:S(2)}) %collective-permute-start.15) | collective-permute-done | bytes 132128 | tf_op jit(solution)/shard_map/ppermute | solution.py:228
  147.8 0.2 fusion.14
  148.1 5.8 %all_gather.3 = bf16[64,2048]{1,0:T(8,128)(2,1)S(1)} all-gather(bf16[64,512]{1,0:T(8,128)(2,1)S(1)} %bitcast.233), channel_id=1, replica_groups=mesh['groups'=2,'tensor'=4,'store'=4] {'store'}, dimensions={1}, use_global_device_ids=true | all-gather | bytes 327680 | tf_op jit(solution)/shard_map/all_gather | solution.py:408
  153.9 5.0 %fusion.68 = f32[64,2048]{1,0:T(8,128)S(1)} fusion(bf16[64,2048]{1,0:T(8,128)(2,1)S(1)} %all_gather.3, bf16[2048,2048]{1,0:T(8,128)(2,1)} %param.12), kind=kOutput, calls=%fused_computation.168 | convolution fusion | flops 536870912 | bytes 9175040 | tf_op jit(solution)/shard_map/dot_general | solution.py:434
  159.0 8.5 %collective-permute-done.18 = f32[2,16,2048]{2,1,0:T(8,128)S(1)} collective-permute-done((f32[2,16,2048]{2,1,0:T(8,128)S(1)}, f32[2,16,2048]{2,1,0:T(8,128)S(1)}, u32[]{:S(2)}, u32[]{:S(2)}) %collective-permute-start.18) | collective-permute-done | bytes 262176 | tf_op jit(solution)/shard_map/ppermute | solution.py:228
  167.6 1.5 collective-permute-start.19
  169.0 7.3 %collective-permute-done.19 = f32[16,2048]{1,0:T(8,128)S(1)} collective-permute-done((f32[16,2048]{1,0:T(8,128)S(1)}, f32[16,2048]{1,0:T(8,128)S(1)}, u32[]{:S(2)}, u32[]{:S(2)}) %collective-permute-start.19) | collective-permute-done | bytes 131104 | tf_op jit(solution)/shard_map/ppermute | solution.py:228
  176.3 0.6 fusion.22
  (81 shorter events, 2.8 us)
Async XLA Ops:
  0.0 1.0 copy-start
  5.9 1.5 copy-start.3
  6.2 3.4 %collective-permute-start = (f32[2,4,64,128]{3,2,1,0:T(8,128)S(1)}, f32[2,4,64,128]{3,2,1,0:T(8,128)S(1)}, u32[]{:S(2)}, u32[]{:S(2)}) collective-permute-start(f32[2,4,64,128]{3,2,1,0:T(8,128)S(1)} %bitcast.234), channel_id=1, source_target_pairs={{0,1},{1,0},{2,3},{3,2},{4,5},{5,4},{6,7},{7,6},{8,9},{9,8},{10,11... | collective-permute-start | bytes 786440 | tf_op jit(solution)/shard_map/ppermute | solution.py:228
  9.6 6.7 %collective-permute-start.1 = (f32[4,64,128]{2,1,0:T(8,128)S(1)}, f32[4,64,128]{2,1,0:T(8,128)S(1)}, u32[]{:S(2)}, u32[]{:S(2)}) collective-permute-start(f32[4,64,128]{2,1,0:T(8,128)S(1)} %dynamic-slice_bitcast_fusion.4), channel_id=1, source_target_pairs={{0,2},{1,3},{2,0},{3,1},{4,6},{5,7},{6,4},{7,5},{8,10},{9,11},{10,... | collective-permute-start | bytes 393224 | tf_op jit(solution)/shard_map/ppermute | solution.py:228
  16.6 5.7 %collective-permute-start.2 = (bf16[4,64,128]{2,1,0:T(8,128)(2,1)S(1)}, bf16[4,64,128]{2,1,0:T(8,128)(2,1)S(1)}, u32[]{:S(2)}, u32[]{:S(2)}) collective-permute-start(bf16[4,64,128]{2,1,0:T(8,128)(2,1)S(1)} %pad_maximum_fusion.4), channel_id=1, source_target_pairs={{0,2},{1,3},{2,0},{3,1},{4,6},{5,7},{6,4},{7,5},{8,10},{9,11},{10,... | collective-permute-start | bytes 196616 | tf_op jit(solution)/shard_map/ppermute | solution.py:239
  18.4 5.3 %collective-permute-start.4 = (bf16[4,64,128]{2,1,0:T(8,128)(2,1)S(1)}, bf16[4,64,128]{2,1,0:T(8,128)(2,1)S(1)}, u32[]{:S(2)}, u32[]{:S(2)}) collective-permute-start(bf16[4,64,128]{2,1,0:T(8,128)(2,1)S(1)} %pad_maximum_fusion.4), channel_id=1, source_target_pairs={{0,8},{4,12},{8,0},{12,4},{1,9},{5,13},{9,1},{13,5},{2,10},{6,14},... | collective-permute-start | bytes 196616 | tf_op jit(solution)/shard_map/ppermute | solution.py:239
  23.9 5.0 %collective-permute-start.5 = (bf16[2,4,64,128]{3,2,1,0:T(8,128)(2,1)S(1)}, bf16[2,4,64,128]{3,2,1,0:T(8,128)(2,1)S(1)}, u32[]{:S(2)}, u32[]{:S(2)}) collective-permute-start(bf16[2,4,64,128]{3,2,1,0:T(8,128)(2,1)S(1)} %pad_maximum_fusion.3), channel_id=1, source_target_pairs={{0,4},{4,0},{8,12},{12,8},{1,5},{5,1},{9,13},{13,9},{2,6},{6,2},{1... | collective-permute-start | bytes 393224 | tf_op jit(solution)/shard_map/ppermute | solution.py:239
  29.0 6.4 %collective-permute-start.6 = (bf16[16,64,128]{2,1,0:T(8,128)(2,1)S(1)}, bf16[16,64,128]{2,1,0:T(8,128)(2,1)S(1)}, u32[]{:S(2)}, u32[]{:S(2)}) collective-permute-start(bf16[16,64,128]{2,1,0:T(8,128)(2,1)S(1)} %bitcast.228), channel_id=1, source_target_pairs={{0,2},{1,3},{2,0},{3,1},{4,6},{5,7},{6,4},{7,5},{8,10},{9,11},{10,... | collective-permute-start | bytes 786440 | tf_op jit(solution)/shard_map/ppermute | solution.py:239
  30.8 4.8 %collective-permute-start.3 = (bf16[2,4,64,128]{3,2,1,0:T(8,128)(2,1)S(1)}, bf16[2,4,64,128]{3,2,1,0:T(8,128)(2,1)S(1)}, u32[]{:S(2)}, u32[]{:S(2)}) collective-permute-start(bf16[2,4,64,128]{3,2,1,0:T(8,128)(2,1)S(1)} %pad_maximum_fusion.2), channel_id=1, source_target_pairs={{0,1},{1,0},{2,3},{3,2},{4,5},{5,4},{6,7},{7,6},{8,9},{9,8},{10,11... | collective-permute-start | bytes 393224 | tf_op jit(solution)/shard_map/ppermute | solution.py:239
  35.6 15.3 %collective-permute-start.7 = (bf16[2,16,64,128]{3,2,1,0:T(8,128)(2,1)S(1)}, bf16[2,16,64,128]{3,2,1,0:T(8,128)(2,1)S(1)}, u32[]{:S(2)}, u32[]{:S(2)}) collective-permute-start(bf16[2,16,64,128]{3,2,1,0:T(8,128)(2,1)S(1)} %pad_maximum_fusion), channel_id=1, source_target_pairs={{0,1},{1,0},{2,3},{3,2},{4,5},{5,4},{6,7},{7,6},{8,9},{9,8},{10,11... | collective-permute-start | bytes 1572872 | tf_op jit(solution)/shard_map/ppermute | solution.py:239
  86.7 4.1 %copy-start.2 = (f32[2,512,1]{2,1,0:T(8,128)S(1)}, f32[2,512,1]{2,1,0:T(8,128)}, u32[]{:S(2)}) copy-start(f32[2,512,1]{2,1,0:T(8,128)} %get-tuple-element.15) | copy-start | bytes 12292
  86.8 8.9 %copy-start.1 = (f32[2,512,128]{2,1,0:T(8,128)S(1)}, f32[2,512,128]{2,1,0:T(8,128)}, u32[]{:S(2)}) copy-start(f32[2,512,128]{2,1,0:T(8,128)} %get-tuple-element.11) | copy-start | bytes 1572868
  89.0 1.4 collective-permute-start.8
  90.3 3.9 %collective-permute-start.9 = (f32[64,64]{1,0:T(8,128)S(1)}, f32[64,64]{1,0:T(8,128)S(1)}, u32[]{:S(2)}, u32[]{:S(2)}) collective-permute-start(f32[64,64]{1,0:T(8,128)S(1)} %max.15), channel_id=1, source_target_pairs={{0,2},{1,3},{2,0},{3,1},{4,6},{5,7},{6,4},{7,5},{8,10},{9,11},{10,... | collective-permute-start | bytes 49160 | tf_op jit(solution)/shard_map/ppermute | solution.py:215
  94.3 5.4 %collective-permute-start.10 = (f32[64,64]{1,0:T(8,128)S(1)}, f32[64,64]{1,0:T(8,128)S(1)}, u32[]{:S(2)}, u32[]{:S(2)}) collective-permute-start(f32[64,64]{1,0:T(8,128)S(1)} %max.16), channel_id=1, source_target_pairs={{0,4},{4,0},{8,12},{12,8},{1,5},{5,1},{9,13},{13,9},{2,6},{6,2},{1... | collective-permute-start | bytes 49160 | tf_op jit(solution)/shard_map/ppermute | solution.py:215
  99.7 5.3 %collective-permute-start.11 = (f32[64,64]{1,0:T(8,128)S(1)}, f32[64,64]{1,0:T(8,128)S(1)}, u32[]{:S(2)}, u32[]{:S(2)}) collective-permute-start(f32[64,64]{1,0:T(8,128)S(1)} %max.17), channel_id=1, source_target_pairs={{0,8},{4,12},{8,0},{12,4},{1,9},{5,13},{9,1},{13,5},{2,10},{6,14},... | collective-permute-start | bytes 49160 | tf_op jit(solution)/shard_map/ppermute | solution.py:215
  111.4 2.9 %collective-permute-start.12 = (f32[2,2,2,4,8256]{4,3,0,1,2:T(4,128)}, f32[2,2,2,4,8256]{4,3,0,1,2:T(4,128)S(1)}, u32[]{:S(2)}, u32[]{:S(2)}) collective-permute-start(f32[2,2,2,4,8256]{4,3,0,1,2:T(4,128)} %fusion.16), channel_id=1, source_target_pairs={{0,1},{1,0},{2,3},{3,2},{4,5},{5,4},{6,7},{7,6},{8,9},{9,8},{10,11... | collective-permute-start | bytes 3170312 | tf_op jit(solution)/shard_map/ppermute | solution.py:228
  114.8 17.2 %collective-permute-start.13 = (f32[2,2,4,8256]{3,2,1,0:T(4,128)S(1)}, f32[2,2,4,8256]{3,2,1,0:T(4,128)S(1)}, u32[]{:S(2)}, u32[]{:S(2)}) collective-permute-start(f32[2,2,4,8256]{3,2,1,0:T(4,128)S(1)} %bitcast.230), channel_id=1, source_target_pairs={{0,2},{1,3},{2,0},{3,1},{4,6},{5,7},{6,4},{7,5},{8,10},{9,11},{10,... | collective-permute-start | bytes 1585160 | tf_op jit(solution)/shard_map/ppermute | solution.py:228
  117.5 1.4 collective-permute-start.16
  118.9 12.9 %collective-permute-start.17 = (f32[64,512]{1,0:T(8,128)S(1)}, f32[64,512]{1,0:T(8,128)S(1)}, u32[]{:S(2)}, u32[]{:S(2)}) collective-permute-start(f32[64,512]{1,0:T(8,128)S(1)} %add.285), channel_id=1, source_target_pairs={{0,2},{1,3},{2,0},{3,1},{4,6},{5,7},{6,4},{7,5},{8,10},{9,11},{10,... | collective-permute-start | bytes 393224 | tf_op jit(solution)/shard_map/ppermute | solution.py:215
  132.2 7.7 %collective-permute-start.14 = (f32[2,4,8256]{2,1,0:T(4,128)S(1)}, f32[2,4,8256]{2,1,0:T(4,128)S(1)}, u32[]{:S(2)}, u32[]{:S(2)}) collective-permute-start(f32[2,4,8256]{2,1,0:T(4,128)S(1)} %dynamic-slice_bitcast_fusion), channel_id=1, source_target_pairs={{0,4},{4,0},{8,12},{12,8},{1,5},{5,1},{9,13},{13,9},{2,6},{6,2},{1... | collective-permute-start | bytes 792584 | tf_op jit(solution)/shard_map/ppermute | solution.py:228
  140.0 7.8 %collective-permute-start.15 = (f32[4,8256]{1,0:T(4,128)S(1)}, f32[4,8256]{1,0:T(4,128)S(1)}, u32[]{:S(2)}, u32[]{:S(2)}) collective-permute-start(f32[4,8256]{1,0:T(4,128)S(1)} %dynamic-slice_bitcast_fusion.2), channel_id=1, source_target_pairs={{0,8},{4,12},{8,0},{12,4},{1,9},{5,13},{9,1},{13,5},{2,10},{6,14},... | collective-permute-start | bytes 396296 | tf_op jit(solution)/shard_map/ppermute | solution.py:228
  158.9 8.6 %collective-permute-start.18 = (f32[2,16,2048]{2,1,0:T(8,128)S(1)}, f32[2,16,2048]{2,1,0:T(8,128)S(1)}, u32[]{:S(2)}, u32[]{:S(2)}) collective-permute-start(f32[2,16,2048]{2,1,0:T(8,128)S(1)} %dynamic-slice_bitcast_fusion.1), channel_id=1, source_target_pairs={{0,4},{4,0},{8,12},{12,8},{1,5},{5,1},{9,13},{13,9},{2,6},{6,2},{1... | collective-permute-start | bytes 786440 | tf_op jit(solution)/shard_map/ppermute | solution.py:228
  167.6 8.7 %collective-permute-start.19 = (f32[16,2048]{1,0:T(8,128)S(1)}, f32[16,2048]{1,0:T(8,128)S(1)}, u32[]{:S(2)}, u32[]{:S(2)}) collective-permute-start(f32[16,2048]{1,0:T(8,128)S(1)} %dynamic-slice_bitcast_fusion.3), channel_id=1, source_target_pairs={{0,8},{4,12},{8,0},{12,4},{1,9},{5,13},{9,1},{13,5},{2,10},{6,14},... | collective-permute-start | bytes 393224 | tf_op jit(solution)/shard_map/ppermute | solution.py:228

commit v15 on v14

--- a/solution.py
+++ b/solution.py
@@ -405,7 +405,7 @@
             .reshape(tok_count, chunk_heads * HD)
             .astype(jnp.bfloat16)
         )
-        attended = lax.all_gather(attended, "store", axis=1, tiled=True)
+        attended = jnp.transpose(bit_gather(jnp.transpose(attended), "store"))
     else:
         packed = lax.psum_scatter(packed, "tensor", scatter_dimension=0, tiled=True)
         packed = axis_sum(packed, "store")

time: 177 us -> 177 us (level)
  blocking collectives: 5.79 us -> 0 us
  waiting for transfers between devices: 59.9 us -> 64.6 us
    all_gather x1 -> x0, blocking collectives: 5.79 us -> none  [body(): attended = lax.all_gather(attended, 'store', axis=1, tiled=True)]
    ppermute x6 -> x8, waiting for transfers between devices: 9.37 us -> 14.4 us  [bit_gather(): other = lax.ppermute(x, axis, perm=[(i, i ^ d) for i in range(n)])]
    ppermute x6 -> x8, starting transfers between devices: 6.6 us -> 7.28 us  [bit_gather(): other = lax.ppermute(x, axis, perm=[(i, i ^ d) for i in range(n)])]
  transfers between devices with their start and end apart: 20 -> 22, of which waited for: 14 -> 16; matrix products, arithmetic and copies ran while one was open for 9% -> 9% of each run, Pallas kernels for 7% -> 7%
where the time goes in v15:
time: 177 us
  waiting for transfers between devices  64.6 us (36%)
  Pallas kernels  47.5 us (27%)
  starting transfers between devices  22.9 us (13%)
  other arithmetic  13.6 us (8%)
  local copies, waits for them, and re-layouts  13.2 us (7%)
  matrix products  13.2 us (7%)
  between operations  2 us (1%)
    pallas_call x2, Pallas kernels, hist_attend(): pl.pallas_call(kernel, grid_spec=grid_spec, out_shape=[jax.ShapeDtypeStru...  47.5 us
    ppermute x8, waiting for transfers between devices, bit_scatter(): block = keep + lax.ppermute(send, axis, perm=[(i, i ^ d) for i in range(n)])  33.4 us
    ppermute x6, waiting for transfers between devices, axis_reduce(): x = op(x, lax.ppermute(x, axis, perm=[(i, i ^ d) for i in range(n)]))  16.8 us
    ppermute x8, waiting for transfers between devices, bit_gather(): other = lax.ppermute(x, axis, perm=[(i, i ^ d) for i in range(n)])  14.4 us
    ppermute x8, starting transfers between devices, bit_scatter(): block = keep + lax.ppermute(send, axis, perm=[(i, i ^ d) for i in range(n)])  8.37 us
    ppermute x8, starting transfers between devices, bit_gather(): other = lax.ppermute(x, axis, perm=[(i, i ^ d) for i in range(n)])  7.28 us
    ppermute x6, starting transfers between devices, axis_reduce(): x = op(x, lax.ppermute(x, axis, perm=[(i, i ^ d) for i in range(n)]))  7.26 us
    pallas_call x4, local copies, waits for them, and re-layouts, hist_attend(): pl.pallas_call(kernel, grid_spec=grid_spec, out_shape=[jax.ShapeDtypeStru...  5.53 us
  transfers between devices with their start and end apart: 22, of which 16 were waited for; matrix products, arithmetic and copies ran while one was open for 9% of the time, Pallas kernels for 7%

profile of v15, /device:TPU:0, one launch (start us, length us, event | category | flops | bytes accessed | tf_op | source)
XLA Modules:
  0.0 177.0 jit_solution(4688236536916095979)
XLA Ops:
  0.0 0.9 copy-done
  1.0 4.9 %convolution_bitcast_fusion = f32[8,8,16,128]{3,1,2,0:T(8,128)S(1)} fusion(bf16[64,2048]{1,0:T(8,128)(2,1)S(1)} %copy-done, bf16[2048,2048]{1,0:T(8,128)(2,1)} %param.10), kind=kOutput, calls=%fused_computation.17 | convolution fusion | flops 536870912 | bytes 9175040 | tf_op jit(solution)/shard_map/dot_general | solution.py:293
  6.2 0.5 collective-permute-start
  7.4 1.2 reduce-window.6
  9.1 0.2 fusion.34
  9.3 0.2 multiply_cosine_fusion
  9.6 2.6 %collective-permute-start.1 = (f32[4,64,128]{2,1,0:T(8,128)S(1)}, f32[4,64,128]{2,1,0:T(8,128)S(1)}, u32[]{:S(2)}, u32[]{:S(2)}) collective-permute-start(f32[4,64,128]{2,1,0:T(8,128)S(1)} %dynamic-slice_bitcast_fusion.4), channel_id=1, source_target_pairs={{0,2},{1,3},{2,0},{3,1},{4,6},{5,7},{6,4},{7,5},{8,10},{9,11},{10,... | collective-permute-start | bytes 393224 | tf_op jit(solution)/shard_map/ppermute | solution.py:228
  12.2 4.2 %collective-permute-done.1 = f32[4,64,128]{2,1,0:T(8,128)S(1)} collective-permute-done((f32[4,64,128]{2,1,0:T(8,128)S(1)}, f32[4,64,128]{2,1,0:T(8,128)S(1)}, u32[]{:S(2)}, u32[]{:S(2)}) %collective-permute-start.1) | collective-permute-done | bytes 131104 | tf_op jit(solution)/shard_map/ppermute | solution.py:228
  16.6 1.8 %collective-permute-start.2 = (bf16[4,64,128]{2,1,0:T(8,128)(2,1)S(1)}, bf16[4,64,128]{2,1,0:T(8,128)(2,1)S(1)}, u32[]{:S(2)}, u32[]{:S(2)}) collective-permute-start(bf16[4,64,128]{2,1,0:T(8,128)(2,1)S(1)} %pad_maximum_fusion.5), channel_id=1, source_target_pairs={{0,2},{1,3},{2,0},{3,1},{4,6},{5,7},{6,4},{7,5},{8,10},{9,11},{10,... | collective-permute-start | bytes 196616 | tf_op jit(solution)/shard_map/ppermute | solution.py:239
  18.4 2.6 %collective-permute-start.4 = (bf16[4,64,128]{2,1,0:T(8,128)(2,1)S(1)}, bf16[4,64,128]{2,1,0:T(8,128)(2,1)S(1)}, u32[]{:S(2)}, u32[]{:S(2)}) collective-permute-start(bf16[4,64,128]{2,1,0:T(8,128)(2,1)S(1)} %pad_maximum_fusion.5), channel_id=1, source_target_pairs={{0,8},{4,12},{8,0},{12,4},{1,9},{5,13},{9,1},{13,5},{2,10},{6,14},... | collective-permute-start | bytes 196616 | tf_op jit(solution)/shard_map/ppermute | solution.py:239
  21.0 0.7 fusion.38
  22.4 1.4 collective-permute-done.4
  23.8 0.1 select_bitcast_fusion.13
  23.9 1.5 collective-permute-start.5
  25.5 3.4 %collective-permute-done.5 = bf16[2,4,64,128]{3,2,1,0:T(8,128)(2,1)S(1)} collective-permute-done((bf16[2,4,64,128]{3,2,1,0:T(8,128)(2,1)S(1)}, bf16[2,4,64,128]{3,2,1,0:T(8,128)(2,1)S(1)}, u32[]{:S(2)}, u32[]{:S(2)}) %collective-permute-start.5) | collective-permute-done | bytes 131104 | tf_op jit(solution)/shard_map/ppermute | solution.py:239
  29.0 0.6 collective-permute-start.6
  29.6 0.6 maximum_bitcast_fusion.3.cos_ref
  30.2 0.6 maximum_bitcast_fusion.4.sin_ref
  31.0 4.5 %collective-permute-done.6 = bf16[16,64,128]{2,1,0:T(8,128)(2,1)S(1)} collective-permute-done((bf16[16,64,128]{2,1,0:T(8,128)(2,1)S(1)}, bf16[16,64,128]{2,1,0:T(8,128)(2,1)S(1)}, u32[]{:S(2)}, u32[]{:S(2)}) %collective-permute-start.6) | collective-permute-done | bytes 262176 | tf_op jit(solution)/shard_map/ppermute | solution.py:239
  35.7 0.7 copy.79
  36.5 13.2 %shard_map.85 = (f32[2,512,128]{2,1,0:T(8,128)}, f32[2,512,1]{2,1,0:T(8,128)}, f32[2,512,1]{2,1,0:T(8,128)}) custom-call(s32[1]{0:T(128)} %bitcast.kv0_ref, bf16[2,512,128]{2,1,0:T(8,128)(2,1)} %bitcast.254, bf16[40,128,2048]{2,1,0:T(8,128)(2,1)} %bitcast.246, bf16[40,128,2048]{2,1,0:T(8,128)(2,1)} %bitcast.247, f32[1,1,5120]{2,1,0:T(1,128)} %bitcast.262, ...), custom_call_target="tpu_custom_call" | custom-call | flops 2684354560 | bytes 6029312 | tf_op jit(solution)/shard_map/pallas_call | solution.py:194
  49.7 1.2 copy.85
  51.2 1.2 fusion.22.q_ref
  52.4 34.3 %shard_map.86 = (f32[6,512,128]{2,1,0:T(8,128)}, f32[6,512,1]{2,1,0:T(8,128)}, f32[6,512,1]{2,1,0:T(8,128)}) custom-call(s32[1]{0:T(128)} %bitcast.26.kv0_ref, bf16[6,512,128]{2,1,0:T(8,128)(2,1)} %fusion.22.q_ref, bf16[40,128,2048]{2,1,0:T(8,128)(2,1)} %bitcast.248, bf16[40,128,2048]{2,1,0:T(8,128)(2,1)} %bitcast.249, f32[1,1,5120]{2,1,0:T(1,128)} %bitcast.263, ...), custom_call_target="tpu_custom_call" | custom-call | flops 8053063680 | bytes 18087936 | tf_op jit(solution)/shard_map/pallas_call | solution.py:194
  86.8 2.1 %copy.86 = f32[6,512,1]{1,0,2:T(8,128)S(1)} copy(f32[6,512,1]{2,1,0:T(8,128)} %get-tuple-element.14) | data formatting | bytes 24576 | tf_op jit(solution)/shard_map/pallas_call | solution.py:194
  89.0 0.5 collective-permute-start.8
  89.5 0.9 collective-permute-done.8
  90.4 0.5 collective-permute-start.9
  90.9 0.2 copy.89
  91.1 3.2 %collective-permute-done.9 = f32[64,64]{1,0:T(8,128)S(1)} collective-permute-done((f32[64,64]{1,0:T(8,128)S(1)}, f32[64,64]{1,0:T(8,128)S(1)}, u32[]{:S(2)}, u32[]{:S(2)}) %collective-permute-start.9) | collective-permute-done | bytes 16416 | tf_op jit(solution)/shard_map/ppermute | solution.py:215
  94.3 1.4 collective-permute-start.10
  95.7 1.9 %fusion.4 = f32[8,512,128]{2,1,0:T(8,128)S(1)} fusion(s32[]{:T(128)S(6)} %select_n.386, f32[2,512,128]{2,1,0:T(8,128)S(1)} %copy-done.1, f32[6,512,128]{2,1,0:T(8,128)} %get-tuple-element.12), kind=kLoop, calls=%fused_computation.10 | loop fusion | flops 1572864 | bytes 4194308 | tf_op jit(solution)/shard_map/concatenate | solution.py:354
  97.7 2.0 %copy.90 = f32[6,512,1]{1,0,2:T(8,128)S(1)} copy(f32[6,512,1]{2,1,0:T(8,128)} %get-tuple-element.16) | data formatting | bytes 24576 | tf_op jit(solution)/shard_map/pallas_call | solution.py:194
  99.7 3.2 %collective-permute-start.11 = (f32[64,64]{1,0:T(8,128)S(1)}, f32[64,64]{1,0:T(8,128)S(1)}, u32[]{:S(2)}, u32[]{:S(2)}) collective-permute-start(f32[64,64]{1,0:T(8,128)S(1)} %max.17), channel_id=1, source_target_pairs={{0,8},{4,12},{8,0},{12,4},{1,9},{5,13},{9,1},{13,5},{2,10},{6,14},... | collective-permute-start | bytes 49160 | tf_op jit(solution)/shard_map/ppermute | solution.py:215
  103.0 1.8 %reshape.444 = f32[2,2,2,2,4,8192]{5,4,3,2,1,0:T(4,128)} reshape(f32[8,512,128]{2,1,0:T(8,128)S(1)} %fusion.4) | data formatting | bytes 4194304 | tf_op jit(solution)/shard_map/reshape | solution.py:359
  104.8 0.2 collective-permute-done.11
  105.0 0.6 mul.261
  105.6 1.8 %mul.262 = f32[2,2,2,2,4,8192]{5,4,3,2,1,0:T(4,128)} reshape(f32[64,64,128]{2,1,0:T(8,128)S(1)} %mul.261) | data formatting | bytes 4194304 | tf_op jit(solution)/shard_map/mul | solution.py:366
  107.4 2.8 %mul.263 = f32[2,2,2,2,4,8192]{5,4,3,2,1,0:T(4,128)S(1)} multiply(f32[2,2,2,2,4,8192]{5,4,3,2,1,0:T(4,128)} %reshape.444, f32[2,2,2,2,4,8192]{5,4,3,2,1,0:T(4,128)} %mul.262) | non-fusion elementwise | flops 524288 | bytes 6291456 | tf_op jit(solution)/shard_map/mul | solution.py:366
  110.1 1.3 fusion.18
  111.4 2.9 %collective-permute-done.12 = f32[2,2,2,4,8256]{4,3,0,1,2:T(4,128)S(1)} collective-permute-done((f32[2,2,2,4,8256]{4,3,0,1,2:T(4,128)}, f32[2,2,2,4,8256]{4,3,0,1,2:T(4,128)S(1)}, u32[]{:S(2)}, u32[]{:S(2)}) %collective-permute-start.12) | collective-permute-done | bytes 1056800 | tf_op jit(solution)/shard_map/ppermute | solution.py:228
  114.3 0.4 fusion.21
  114.8 0.6 collective-permute-start.13
  115.4 2.1 %fusion.7 = f32[64,512]{1,0:T(8,128)S(1)} fusion(bf16[64,2048]{1,0:T(8,128)(2,1)S(1)} %copy-done, bf16[2048,2048]{1,0:T(8,128)(2,1)} %param.11, s32[]{:T(128)S(6)} %select_n.392), kind=kOutput, calls=%fused_computation.18 | convolution fusion | flops 134217728 | bytes 2490372 | tf_op jit(solution)/shard_map/dot_general | solution.py:294
  117.6 1.3 collective-permute-done.16
  118.9 1.5 collective-permute-start.17
  120.6 11.3 %collective-permute-done.17 = f32[64,512]{1,0:T(8,128)S(1)} collective-permute-done((f32[64,512]{1,0:T(8,128)S(1)}, f32[64,512]{1,0:T(8,128)S(1)}, u32[]{:S(2)}, u32[]{:S(2)}) %collective-permute-start.17) | collective-permute-done | bytes 131104 | tf_op jit(solution)/shard_map/ppermute | solution.py:215
  132.0 0.1 bitcast_add_fusion
  132.2 0.3 collective-permute-start.14
  132.7 7.2 %collective-permute-done.14 = f32[2,4,8256]{2,1,0:T(4,128)S(1)} collective-permute-done((f32[2,4,8256]{2,1,0:T(4,128)S(1)}, f32[2,4,8256]{2,1,0:T(4,128)S(1)}, u32[]{:S(2)}, u32[]{:S(2)}) %collective-permute-start.14) | collective-permute-done | bytes 264224 | tf_op jit(solution)/shard_map/ppermute | solution.py:228
  140.0 2.9 %collective-permute-start.15 = (f32[4,8256]{1,0:T(4,128)S(1)}, f32[4,8256]{1,0:T(4,128)S(1)}, u32[]{:S(2)}, u32[]{:S(2)}) collective-permute-start(f32[4,8256]{1,0:T(4,128)S(1)} %dynamic-slice_bitcast_fusion.2), channel_id=1, source_target_pairs={{0,8},{4,12},{8,0},{12,4},{1,9},{5,13},{9,1},{13,5},{2,10},{6,14},... | collective-permute-start | bytes 396296 | tf_op jit(solution)/shard_map/ppermute | solution.py:228
  142.9 1.1 fusion.69
  144.0 3.8 %collective-permute-done.15 = f32[4,8256]{1,0:T(4,128)S(1)} collective-permute-done((f32[4,8256]{1,0:T(4,128)S(1)}, f32[4,8256]{1,0:T(4,128)S(1)}, u32[]{:S(2)}, u32[]{:S(2)}) %collective-permute-start.15) | collective-permute-done | bytes 132128 | tf_op jit(solution)/shard_map/ppermute | solution.py:228
  147.9 0.2 fusion.16
  148.1 0.6 collective-permute-start.18
  148.7 3.7 %collective-permute-done.18 = bf16[512,64]{0,1:T(8,128)(2,1)S(1)} collective-permute-done((bf16[512,64]{0,1:T(8,128)(2,1)S(1)}, bf16[512,64]{0,1:T(8,128)(2,1)S(1)}, u32[]{:S(2)}, u32[]{:S(2)}) %collective-permute-start.18) | collective-permute-done | bytes 65568 | tf_op jit(solution)/shard_map/ppermute | solution.py:239
  152.6 1.3 collective-permute-done.19
  154.0 0.3 copy.101
  154.2 0.2 reshape.454
  154.4 4.9 %fusion = f32[2,2,16,2048]{3,2,1,0:T(8,128)S(1)} fusion(bf16[2,2,16,2048]{3,2,1,0:T(8,128)(2,1)S(1)} %bitcast.253, bf16[2048,2048]{1,0:T(8,128)(2,1)} %param.12), kind=kOutput, calls=%fused_computation | convolution fusion | flops 536870912 | bytes 9175040 | tf_op jit(solution)/shard_map/dot_general | solution.py:434
  159.5 8.3 %collective-permute-done.20 = f32[2,16,2048]{2,1,0:T(8,128)S(1)} collective-permute-done((f32[2,16,2048]{2,1,0:T(8,128)S(1)}, f32[2,16,2048]{2,1,0:T(8,128)S(1)}, u32[]{:S(2)}, u32[]{:S(2)}) %collective-permute-start.20) | collective-permute-done | bytes 262176 | tf_op jit(solution)/shard_map/ppermute | solution.py:228
  167.9 1.5 collective-permute-start.21
  169.4 7.0 %collective-permute-done.21 = f32[16,2048]{1,0:T(8,128)S(1)} collective-permute-done((f32[16,2048]{1,0:T(8,128)S(1)}, f32[16,2048]{1,0:T(8,128)S(1)}, u32[]{:S(2)}, u32[]{:S(2)}) %collective-permute-start.21) | collective-permute-done | bytes 131104 | tf_op jit(solution)/shard_map/ppermute | solution.py:228
  176.4 0.6 fusion.24
  (90 shorter events, 3.3 us)
Async XLA Ops:
  0.0 1.0 copy-start
  5.9 1.5 copy-start.3
  6.2 3.4 %collective-permute-start = (f32[2,4,64,128]{3,2,1,0:T(8,128)S(1)}, f32[2,4,64,128]{3,2,1,0:T(8,128)S(1)}, u32[]{:S(2)}, u32[]{:S(2)}) collective-permute-start(f32[2,4,64,128]{3,2,1,0:T(8,128)S(1)} %bitcast.261), channel_id=1, source_target_pairs={{0,1},{1,0},{2,3},{3,2},{4,5},{5,4},{6,7},{7,6},{8,9},{9,8},{10,11... | collective-permute-start | bytes 786440 | tf_op jit(solution)/shard_map/ppermute | solution.py:228
  9.6 6.7 %collective-permute-start.1 = (f32[4,64,128]{2,1,0:T(8,128)S(1)}, f32[4,64,128]{2,1,0:T(8,128)S(1)}, u32[]{:S(2)}, u32[]{:S(2)}) collective-permute-start(f32[4,64,128]{2,1,0:T(8,128)S(1)} %dynamic-slice_bitcast_fusion.4), channel_id=1, source_target_pairs={{0,2},{1,3},{2,0},{3,1},{4,6},{5,7},{6,4},{7,5},{8,10},{9,11},{10,... | collective-permute-start | bytes 393224 | tf_op jit(solution)/shard_map/ppermute | solution.py:228
  16.6 5.7 %collective-permute-start.2 = (bf16[4,64,128]{2,1,0:T(8,128)(2,1)S(1)}, bf16[4,64,128]{2,1,0:T(8,128)(2,1)S(1)}, u32[]{:S(2)}, u32[]{:S(2)}) collective-permute-start(bf16[4,64,128]{2,1,0:T(8,128)(2,1)S(1)} %pad_maximum_fusion.5), channel_id=1, source_target_pairs={{0,2},{1,3},{2,0},{3,1},{4,6},{5,7},{6,4},{7,5},{8,10},{9,11},{10,... | collective-permute-start | bytes 196616 | tf_op jit(solution)/shard_map/ppermute | solution.py:239
  18.4 5.3 %collective-permute-start.4 = (bf16[4,64,128]{2,1,0:T(8,128)(2,1)S(1)}, bf16[4,64,128]{2,1,0:T(8,128)(2,1)S(1)}, u32[]{:S(2)}, u32[]{:S(2)}) collective-permute-start(bf16[4,64,128]{2,1,0:T(8,128)(2,1)S(1)} %pad_maximum_fusion.5), channel_id=1, source_target_pairs={{0,8},{4,12},{8,0},{12,4},{1,9},{5,13},{9,1},{13,5},{2,10},{6,14},... | collective-permute-start | bytes 196616 | tf_op jit(solution)/shard_map/ppermute | solution.py:239
  23.9 5.0 %collective-permute-start.5 = (bf16[2,4,64,128]{3,2,1,0:T(8,128)(2,1)S(1)}, bf16[2,4,64,128]{3,2,1,0:T(8,128)(2,1)S(1)}, u32[]{:S(2)}, u32[]{:S(2)}) collective-permute-start(bf16[2,4,64,128]{3,2,1,0:T(8,128)(2,1)S(1)} %pad_maximum_fusion.3), channel_id=1, source_target_pairs={{0,4},{4,0},{8,12},{12,8},{1,5},{5,1},{9,13},{13,9},{2,6},{6,2},{1... | collective-permute-start | bytes 393224 | tf_op jit(solution)/shard_map/ppermute | solution.py:239
  29.0 6.4 %collective-permute-start.6 = (bf16[16,64,128]{2,1,0:T(8,128)(2,1)S(1)}, bf16[16,64,128]{2,1,0:T(8,128)(2,1)S(1)}, u32[]{:S(2)}, u32[]{:S(2)}) collective-permute-start(bf16[16,64,128]{2,1,0:T(8,128)(2,1)S(1)} %bitcast.256), channel_id=1, source_target_pairs={{0,2},{1,3},{2,0},{3,1},{4,6},{5,7},{6,4},{7,5},{8,10},{9,11},{10,... | collective-permute-start | bytes 786440 | tf_op jit(solution)/shard_map/ppermute | solution.py:239
  30.9 4.8 %collective-permute-start.3 = (bf16[2,4,64,128]{3,2,1,0:T(8,128)(2,1)S(1)}, bf16[2,4,64,128]{3,2,1,0:T(8,128)(2,1)S(1)}, u32[]{:S(2)}, u32[]{:S(2)}) collective-permute-start(bf16[2,4,64,128]{3,2,1,0:T(8,128)(2,1)S(1)} %pad_maximum_fusion.2), channel_id=1, source_target_pairs={{0,1},{1,0},{2,3},{3,2},{4,5},{5,4},{6,7},{7,6},{8,9},{9,8},{10,11... | collective-permute-start | bytes 393224 | tf_op jit(solution)/shard_map/ppermute | solution.py:239
  35.6 15.3 %collective-permute-start.7 = (bf16[2,16,64,128]{3,2,1,0:T(8,128)(2,1)S(1)}, bf16[2,16,64,128]{3,2,1,0:T(8,128)(2,1)S(1)}, u32[]{:S(2)}, u32[]{:S(2)}) collective-permute-start(bf16[2,16,64,128]{3,2,1,0:T(8,128)(2,1)S(1)} %pad_maximum_fusion), channel_id=1, source_target_pairs={{0,1},{1,0},{2,3},{3,2},{4,5},{5,4},{6,7},{7,6},{8,9},{9,8},{10,11... | collective-permute-start | bytes 1572872 | tf_op jit(solution)/shard_map/ppermute | solution.py:239
  86.8 4.1 %copy-start.2 = (f32[2,512,1]{2,1,0:T(8,128)S(1)}, f32[2,512,1]{2,1,0:T(8,128)}, u32[]{:S(2)}) copy-start(f32[2,512,1]{2,1,0:T(8,128)} %get-tuple-element.15) | copy-start | bytes 12292
  86.8 8.9 %copy-start.1 = (f32[2,512,128]{2,1,0:T(8,128)S(1)}, f32[2,512,128]{2,1,0:T(8,128)}, u32[]{:S(2)}) copy-start(f32[2,512,128]{2,1,0:T(8,128)} %get-tuple-element.11) | copy-start | bytes 1572868
  89.0 1.4 collective-permute-start.8
  90.4 3.9 %collective-permute-start.9 = (f32[64,64]{1,0:T(8,128)S(1)}, f32[64,64]{1,0:T(8,128)S(1)}, u32[]{:S(2)}, u32[]{:S(2)}) collective-permute-start(f32[64,64]{1,0:T(8,128)S(1)} %max.15), channel_id=1, source_target_pairs={{0,2},{1,3},{2,0},{3,1},{4,6},{5,7},{6,4},{7,5},{8,10},{9,11},{10,... | collective-permute-start | bytes 49160 | tf_op jit(solution)/shard_map/ppermute | solution.py:215
  94.3 5.4 %collective-permute-start.10 = (f32[64,64]{1,0:T(8,128)S(1)}, f32[64,64]{1,0:T(8,128)S(1)}, u32[]{:S(2)}, u32[]{:S(2)}) collective-permute-start(f32[64,64]{1,0:T(8,128)S(1)} %max.16), channel_id=1, source_target_pairs={{0,4},{4,0},{8,12},{12,8},{1,5},{5,1},{9,13},{13,9},{2,6},{6,2},{1... | collective-permute-start | bytes 49160 | tf_op jit(solution)/shard_map/ppermute | solution.py:215
  99.7 5.3 %collective-permute-start.11 = (f32[64,64]{1,0:T(8,128)S(1)}, f32[64,64]{1,0:T(8,128)S(1)}, u32[]{:S(2)}, u32[]{:S(2)}) collective-permute-start(f32[64,64]{1,0:T(8,128)S(1)} %max.17), channel_id=1, source_target_pairs={{0,8},{4,12},{8,0},{12,4},{1,9},{5,13},{9,1},{13,5},{2,10},{6,14},... | collective-permute-start | bytes 49160 | tf_op jit(solution)/shard_map/ppermute | solution.py:215
  111.4 2.9 %collective-permute-start.12 = (f32[2,2,2,4,8256]{4,3,0,1,2:T(4,128)}, f32[2,2,2,4,8256]{4,3,0,1,2:T(4,128)S(1)}, u32[]{:S(2)}, u32[]{:S(2)}) collective-permute-start(f32[2,2,2,4,8256]{4,3,0,1,2:T(4,128)} %fusion.18), channel_id=1, source_target_pairs={{0,1},{1,0},{2,3},{3,2},{4,5},{5,4},{6,7},{7,6},{8,9},{9,8},{10,11... | collective-permute-start | bytes 3170312 | tf_op jit(solution)/shard_map/ppermute | solution.py:228
  114.8 17.2 %collective-permute-start.13 = (f32[2,2,4,8256]{3,2,1,0:T(4,128)S(1)}, f32[2,2,4,8256]{3,2,1,0:T(4,128)S(1)}, u32[]{:S(2)}, u32[]{:S(2)}) collective-permute-start(f32[2,2,4,8256]{3,2,1,0:T(4,128)S(1)} %bitcast.258), channel_id=1, source_target_pairs={{0,2},{1,3},{2,0},{3,1},{4,6},{5,7},{6,4},{7,5},{8,10},{9,11},{10,... | collective-permute-start | bytes 1585160 | tf_op jit(solution)/shard_map/ppermute | solution.py:228
  117.5 1.4 collective-permute-start.16
  118.9 12.9 %collective-permute-start.17 = (f32[64,512]{1,0:T(8,128)S(1)}, f32[64,512]{1,0:T(8,128)S(1)}, u32[]{:S(2)}, u32[]{:S(2)}) collective-permute-start(f32[64,512]{1,0:T(8,128)S(1)} %add.287), channel_id=1, source_target_pairs={{0,2},{1,3},{2,0},{3,1},{4,6},{5,7},{6,4},{7,5},{8,10},{9,11},{10,... | collective-permute-start | bytes 393224 | tf_op jit(solution)/shard_map/ppermute | solution.py:215
  132.2 7.7 %collective-permute-start.14 = (f32[2,4,8256]{2,1,0:T(4,128)S(1)}, f32[2,4,8256]{2,1,0:T(4,128)S(1)}, u32[]{:S(2)}, u32[]{:S(2)}) collective-permute-start(f32[2,4,8256]{2,1,0:T(4,128)S(1)} %dynamic-slice_bitcast_fusion), channel_id=1, source_target_pairs={{0,4},{4,0},{8,12},{12,8},{1,5},{5,1},{9,13},{13,9},{2,6},{6,2},{1... | collective-permute-start | bytes 792584 | tf_op jit(solution)/shard_map/ppermute | solution.py:228
  140.0 7.8 %collective-permute-start.15 = (f32[4,8256]{1,0:T(4,128)S(1)}, f32[4,8256]{1,0:T(4,128)S(1)}, u32[]{:S(2)}, u32[]{:S(2)}) collective-permute-start(f32[4,8256]{1,0:T(4,128)S(1)} %dynamic-slice_bitcast_fusion.2), channel_id=1, source_target_pairs={{0,8},{4,12},{8,0},{12,4},{1,9},{5,13},{9,1},{13,5},{2,10},{6,14},... | collective-permute-start | bytes 396296 | tf_op jit(solution)/shard_map/ppermute | solution.py:228
  148.1 4.3 %collective-permute-start.18 = (bf16[512,64]{0,1:T(8,128)(2,1)S(1)}, bf16[512,64]{0,1:T(8,128)(2,1)S(1)}, u32[]{:S(2)}, u32[]{:S(2)}) collective-permute-start(bf16[512,64]{0,1:T(8,128)(2,1)S(1)} %bitcast.264), channel_id=1, source_target_pairs={{0,2},{1,3},{2,0},{3,1},{4,6},{5,7},{6,4},{7,5},{8,10},{9,11},{10,... | collective-permute-start | bytes 196616 | tf_op jit(solution)/shard_map/ppermute | solution.py:239
  152.5 1.4 collective-permute-start.19
  159.4 8.4 %collective-permute-start.20 = (f32[2,16,2048]{2,1,0:T(8,128)S(1)}, f32[2,16,2048]{2,1,0:T(8,128)S(1)}, u32[]{:S(2)}, u32[]{:S(2)}) collective-permute-start(f32[2,16,2048]{2,1,0:T(8,128)S(1)} %dynamic-slice_bitcast_fusion.1), channel_id=1, source_target_pairs={{0,4},{4,0},{8,12},{12,8},{1,5},{5,1},{9,13},{13,9},{2,6},{6,2},{1... | collective-permute-start | bytes 786440 | tf_op jit(solution)/shard_map/ppermute | solution.py:228
  167.9 8.5 %collective-permute-start.21 = (f32[16,2048]{1,0:T(8,128)S(1)}, f32[16,2048]{1,0:T(8,128)S(1)}, u32[]{:S(2)}, u32[]{:S(2)}) collective-permute-start(f32[16,2048]{1,0:T(8,128)S(1)} %dynamic-slice_bitcast_fusion.3), channel_id=1, source_target_pairs={{0,8},{4,12},{8,0},{12,4},{1,9},{5,13},{9,1},{13,5},{2,10},{6,14},... | collective-permute-start | bytes 393224 | tf_op jit(solution)/shard_map/ppermute | solution.py:228

commit v16 on v14

--- a/solution.py
+++ b/solution.py
@@ -141,11 +141,11 @@
     scores = lax.dot_general(
         q_ref[0], keys, (((1,), (1,)), ((), ())), preferred_element_type=jnp.float32
     )
-    scores = scores * scale + bias_ref[0]
+    scores = scores + bias_ref[0]
     m_old = m_sc[...]
     m_new = jnp.maximum(m_old, jnp.max(scores, axis=1, keepdims=True))
-    alpha = jnp.exp(m_old - m_new)
-    weights = jnp.exp(scores - m_new)
+    alpha = jnp.exp((m_old - m_new) * scale)
+    weights = jnp.exp((scores - m_new) * scale)
     l_sc[...] = alpha * l_sc[...] + jnp.sum(weights, axis=1, keepdims=True)
     acc_sc[...] = alpha * acc_sc[...] + jnp.dot(
         weights.astype(jnp.bfloat16), vals, preferred_element_type=jnp.float32
@@ -155,7 +155,7 @@
     @pl.when(j == blocks - 1)
     def _():
         acc_out[0] = acc_sc[...]
-        m_out[0] = m_sc[...]
+        m_out[0] = m_sc[...] * scale
         l_out[0] = l_sc[...]
 
 

time: 177 us -> 179 us (1.011)
  Pallas kernels: 47.5 us -> 49.5 us
    pallas_call x2, Pallas kernels: 47.5 us -> 49.5 us  [hist_attend(): pl.pallas_call(kernel, grid_spec=grid_spec, out_shape=[jax.ShapeDtypeStru...]
  transfers between devices with their start and end apart: 20 -> 20, of which waited for: 14 -> 14; matrix products, arithmetic and copies ran while one was open for 9% -> 9% of each run, Pallas kernels for 7% -> 8%
where the time goes in v16:
time: 179 us
  waiting for transfers between devices  59.9 us (33%)
  Pallas kernels  49.5 us (28%)
  starting transfers between devices  22.2 us (12%)
  other arithmetic  13.5 us (8%)
  matrix products  13.2 us (7%)
  local copies, waits for them, and re-layouts  12.8 us (7%)
  blocking collectives  5.79 us (3%)
  between operations  1.96 us (1%)
    pallas_call x2, Pallas kernels, hist_attend(): pl.pallas_call(kernel, grid_spec=grid_spec, out_shape=[jax.ShapeDtypeStru...  49.5 us
    ppermute x8, waiting for transfers between devices, bit_scatter(): block = keep + lax.ppermute(send, axis, perm=[(i, i ^ d) for i in range(n)])  33.8 us
    ppermute x6, waiting for transfers between devices, axis_reduce(): x = op(x, lax.ppermute(x, axis, perm=[(i, i ^ d) for i in range(n)]))  16.8 us
    ppermute x6, waiting for transfers between devices, bit_gather(): other = lax.ppermute(x, axis, perm=[(i, i ^ d) for i in range(n)])  9.37 us
    ppermute x8, starting transfers between devices, bit_scatter(): block = keep + lax.ppermute(send, axis, perm=[(i, i ^ d) for i in range(n)])  8.38 us
    ppermute x6, starting transfers between devices, axis_reduce(): x = op(x, lax.ppermute(x, axis, perm=[(i, i ^ d) for i in range(n)]))  7.27 us
    ppermute x6, starting transfers between devices, bit_gather(): other = lax.ppermute(x, axis, perm=[(i, i ^ d) for i in range(n)])  6.6 us
    all_gather x1, blocking collectives, body(): attended = lax.all_gather(attended, 'store', axis=1, tiled=True)  5.79 us
  transfers between devices with their start and end apart: 20, of which 14 were waited for; matrix products, arithmetic and copies ran while one was open for 9% of the time, Pallas kernels for 8%

profile of v16, /device:TPU:0, one launch (start us, length us, event | category | flops | bytes accessed | tf_op | source)
XLA Modules:
  0.0 179.0 jit_solution(15107840932454034452)
XLA Ops:
  0.0 0.9 copy-done
  1.0 4.9 %convolution_bitcast_fusion = f32[8,8,16,128]{3,1,2,0:T(8,128)S(1)} fusion(bf16[64,2048]{1,0:T(8,128)(2,1)S(1)} %copy-done, bf16[2048,2048]{1,0:T(8,128)(2,1)} %param.10), kind=kOutput, calls=%fused_computation.15 | convolution fusion | flops 536870912 | bytes 9175040 | tf_op jit(solution)/shard_map/dot_general | solution.py:293
  6.0 0.1 constant_dynamic-slice_fusion.5
  6.2 0.5 collective-permute-start
  7.4 1.2 reduce-window.6
  8.7 0.1 copy.60
  9.1 0.2 fusion.32
  9.3 0.2 multiply_cosine_fusion
  9.6 2.6 %collective-permute-start.1 = (f32[4,64,128]{2,1,0:T(8,128)S(1)}, f32[4,64,128]{2,1,0:T(8,128)S(1)}, u32[]{:S(2)}, u32[]{:S(2)}) collective-permute-start(f32[4,64,128]{2,1,0:T(8,128)S(1)} %dynamic-slice_bitcast_fusion.4), channel_id=1, source_target_pairs={{0,2},{1,3},{2,0},{3,1},{4,6},{5,7},{6,4},{7,5},{8,10},{9,11},{10,... | collective-permute-start | bytes 393224 | tf_op jit(solution)/shard_map/ppermute | solution.py:228
  12.2 4.2 %collective-permute-done.1 = f32[4,64,128]{2,1,0:T(8,128)S(1)} collective-permute-done((f32[4,64,128]{2,1,0:T(8,128)S(1)}, f32[4,64,128]{2,1,0:T(8,128)S(1)}, u32[]{:S(2)}, u32[]{:S(2)}) %collective-permute-start.1) | collective-permute-done | bytes 131104 | tf_op jit(solution)/shard_map/ppermute | solution.py:228
  16.4 0.1 subtract_convert_fusion
  16.6 1.8 %collective-permute-start.2 = (bf16[4,64,128]{2,1,0:T(8,128)(2,1)S(1)}, bf16[4,64,128]{2,1,0:T(8,128)(2,1)S(1)}, u32[]{:S(2)}, u32[]{:S(2)}) collective-permute-start(bf16[4,64,128]{2,1,0:T(8,128)(2,1)S(1)} %pad_maximum_fusion.4), channel_id=1, source_target_pairs={{0,2},{1,3},{2,0},{3,1},{4,6},{5,7},{6,4},{7,5},{8,10},{9,11},{10,... | collective-permute-start | bytes 196616 | tf_op jit(solution)/shard_map/ppermute | solution.py:239
  18.4 2.6 %collective-permute-start.4 = (bf16[4,64,128]{2,1,0:T(8,128)(2,1)S(1)}, bf16[4,64,128]{2,1,0:T(8,128)(2,1)S(1)}, u32[]{:S(2)}, u32[]{:S(2)}) collective-permute-start(bf16[4,64,128]{2,1,0:T(8,128)(2,1)S(1)} %pad_maximum_fusion.4), channel_id=1, source_target_pairs={{0,8},{4,12},{8,0},{12,4},{1,9},{5,13},{9,1},{13,5},{2,10},{6,14},... | collective-permute-start | bytes 196616 | tf_op jit(solution)/shard_map/ppermute | solution.py:239
  21.0 0.7 fusion.36
  22.4 1.4 collective-permute-done.4
  23.8 0.1 select_bitcast_fusion.9
  23.9 1.5 collective-permute-start.5
  25.5 3.4 %collective-permute-done.5 = bf16[2,4,64,128]{3,2,1,0:T(8,128)(2,1)S(1)} collective-permute-done((bf16[2,4,64,128]{3,2,1,0:T(8,128)(2,1)S(1)}, bf16[2,4,64,128]{3,2,1,0:T(8,128)(2,1)S(1)}, u32[]{:S(2)}, u32[]{:S(2)}) %collective-permute-start.5) | collective-permute-done | bytes 131104 | tf_op jit(solution)/shard_map/ppermute | solution.py:239
  29.0 0.6 collective-permute-start.6
  29.6 0.6 maximum_bitcast_fusion.2.cos_ref
  30.3 0.6 maximum_bitcast_fusion.3.sin_ref
  30.9 4.5 %collective-permute-done.6 = bf16[16,64,128]{2,1,0:T(8,128)(2,1)S(1)} collective-permute-done((bf16[16,64,128]{2,1,0:T(8,128)(2,1)S(1)}, bf16[16,64,128]{2,1,0:T(8,128)(2,1)S(1)}, u32[]{:S(2)}, u32[]{:S(2)}) %collective-permute-start.6) | collective-permute-done | bytes 262176 | tf_op jit(solution)/shard_map/ppermute | solution.py:239
  35.7 0.7 copy.59
  36.5 13.7 %shard_map.85 = (f32[2,512,128]{2,1,0:T(8,128)}, f32[2,512,1]{2,1,0:T(8,128)}, f32[2,512,1]{2,1,0:T(8,128)}) custom-call(s32[1]{0:T(128)} %bitcast.kv0_ref, bf16[2,512,128]{2,1,0:T(8,128)(2,1)} %bitcast.226, bf16[40,128,2048]{2,1,0:T(8,128)(2,1)} %bitcast.217, bf16[40,128,2048]{2,1,0:T(8,128)(2,1)} %bitcast.218, f32[1,1,5120]{2,1,0:T(1,128)} %bitcast.235, ...), custom_call_target="tpu_custom_call" | custom-call | flops 2684354560 | bytes 6029312 | tf_op jit(solution)/shard_map/pallas_call | solution.py:194
  50.2 1.2 copy.65
  51.5 0.1 maximum_bitcast_fusion
  51.8 1.2 fusion.20.q_ref
  53.0 35.8 %shard_map.86 = (f32[6,512,128]{2,1,0:T(8,128)}, f32[6,512,1]{2,1,0:T(8,128)}, f32[6,512,1]{2,1,0:T(8,128)}) custom-call(s32[1]{0:T(128)} %bitcast.26.kv0_ref, bf16[6,512,128]{2,1,0:T(8,128)(2,1)} %fusion.20.q_ref, bf16[40,128,2048]{2,1,0:T(8,128)(2,1)} %bitcast.219, bf16[40,128,2048]{2,1,0:T(8,128)(2,1)} %bitcast.220, f32[1,1,5120]{2,1,0:T(1,128)} %bitcast.236, ...), custom_call_target="tpu_custom_call" | custom-call | flops 8053063680 | bytes 18087936 | tf_op jit(solution)/shard_map/pallas_call | solution.py:194
  88.8 2.1 %copy.66 = f32[6,512,1]{1,0,2:T(8,128)S(1)} copy(f32[6,512,1]{2,1,0:T(8,128)} %get-tuple-element.14) | data formatting | bytes 24576 | tf_op jit(solution)/shard_map/pallas_call | solution.py:194
  91.0 0.5 collective-permute-start.8
  91.5 0.9 collective-permute-done.8
  92.4 0.5 collective-permute-start.9
  92.9 0.2 copy.69
  93.1 3.2 %collective-permute-done.9 = f32[64,64]{1,0:T(8,128)S(1)} collective-permute-done((f32[64,64]{1,0:T(8,128)S(1)}, f32[64,64]{1,0:T(8,128)S(1)}, u32[]{:S(2)}, u32[]{:S(2)}) %collective-permute-start.9) | collective-permute-done | bytes 16416 | tf_op jit(solution)/shard_map/ppermute | solution.py:215
  96.3 1.4 collective-permute-start.10
  97.7 1.9 %fusion.2 = f32[8,512,128]{2,1,0:T(8,128)S(1)} fusion(s32[]{:T(128)S(6)} %select_n.354, f32[2,512,128]{2,1,0:T(8,128)S(1)} %copy-done.1, f32[6,512,128]{2,1,0:T(8,128)} %get-tuple-element.12), kind=kLoop, calls=%fused_computation.8 | loop fusion | flops 1572864 | bytes 4194308 | tf_op jit(solution)/shard_map/concatenate | solution.py:354
  99.6 2.0 %copy.70 = f32[6,512,1]{1,0,2:T(8,128)S(1)} copy(f32[6,512,1]{2,1,0:T(8,128)} %get-tuple-element.16) | data formatting | bytes 24576 | tf_op jit(solution)/shard_map/pallas_call | solution.py:194
  101.7 3.2 %collective-permute-start.11 = (f32[64,64]{1,0:T(8,128)S(1)}, f32[64,64]{1,0:T(8,128)S(1)}, u32[]{:S(2)}, u32[]{:S(2)}) collective-permute-start(f32[64,64]{1,0:T(8,128)S(1)} %max.17), channel_id=1, source_target_pairs={{0,8},{4,12},{8,0},{12,4},{1,9},{5,13},{9,1},{13,5},{2,10},{6,14},... | collective-permute-start | bytes 49160 | tf_op jit(solution)/shard_map/ppermute | solution.py:215
  105.0 1.8 %reshape.442 = f32[2,2,2,2,4,8192]{5,4,3,2,1,0:T(4,128)} reshape(f32[8,512,128]{2,1,0:T(8,128)S(1)} %fusion.2) | data formatting | bytes 4194304 | tf_op jit(solution)/shard_map/reshape | solution.py:359
  106.8 0.2 collective-permute-done.11
  107.0 0.6 mul.261
  107.6 1.8 %mul.262 = f32[2,2,2,2,4,8192]{5,4,3,2,1,0:T(4,128)} reshape(f32[64,64,128]{2,1,0:T(8,128)S(1)} %mul.261) | data formatting | bytes 4194304 | tf_op jit(solution)/shard_map/mul | solution.py:366
  109.4 2.8 %mul.263 = f32[2,2,2,2,4,8192]{5,4,3,2,1,0:T(4,128)S(1)} multiply(f32[2,2,2,2,4,8192]{5,4,3,2,1,0:T(4,128)} %reshape.442, f32[2,2,2,2,4,8192]{5,4,3,2,1,0:T(4,128)} %mul.262) | non-fusion elementwise | flops 524288 | bytes 6291456 | tf_op jit(solution)/shard_map/mul | solution.py:366
  112.2 1.3 fusion.16
  113.4 2.9 %collective-permute-done.12 = f32[2,2,2,4,8256]{4,3,0,1,2:T(4,128)S(1)} collective-permute-done((f32[2,2,2,4,8256]{4,3,0,1,2:T(4,128)}, f32[2,2,2,4,8256]{4,3,0,1,2:T(4,128)S(1)}, u32[]{:S(2)}, u32[]{:S(2)}) %collective-permute-start.12) | collective-permute-done | bytes 1056800 | tf_op jit(solution)/shard_map/ppermute | solution.py:228
  116.3 0.4 fusion.19
  116.8 0.6 collective-permute-start.13
  117.5 2.1 %fusion.5 = f32[64,512]{1,0:T(8,128)S(1)} fusion(bf16[64,2048]{1,0:T(8,128)(2,1)S(1)} %copy-done, bf16[2048,2048]{1,0:T(8,128)(2,1)} %param.11, s32[]{:T(128)S(6)} %select_n.360), kind=kOutput, calls=%fused_computation.16 | convolution fusion | flops 134217728 | bytes 2490372 | tf_op jit(solution)/shard_map/dot_general | solution.py:294
  119.7 1.3 collective-permute-done.16
  121.0 1.5 collective-permute-start.17
  122.6 11.3 %collective-permute-done.17 = f32[64,512]{1,0:T(8,128)S(1)} collective-permute-done((f32[64,512]{1,0:T(8,128)S(1)}, f32[64,512]{1,0:T(8,128)S(1)}, u32[]{:S(2)}, u32[]{:S(2)}) %collective-permute-start.17) | collective-permute-done | bytes 131104 | tf_op jit(solution)/shard_map/ppermute | solution.py:215
  134.1 0.1 bitcast_add_fusion
  134.2 0.3 collective-permute-start.14
  134.7 7.2 %collective-permute-done.14 = f32[2,4,8256]{2,1,0:T(4,128)S(1)} collective-permute-done((f32[2,4,8256]{2,1,0:T(4,128)S(1)}, f32[2,4,8256]{2,1,0:T(4,128)S(1)}, u32[]{:S(2)}, u32[]{:S(2)}) %collective-permute-start.14) | collective-permute-done | bytes 264224 | tf_op jit(solution)/shard_map/ppermute | solution.py:228
  142.0 2.9 %collective-permute-start.15 = (f32[4,8256]{1,0:T(4,128)S(1)}, f32[4,8256]{1,0:T(4,128)S(1)}, u32[]{:S(2)}, u32[]{:S(2)}) collective-permute-start(f32[4,8256]{1,0:T(4,128)S(1)} %dynamic-slice_bitcast_fusion.2), channel_id=1, source_target_pairs={{0,8},{4,12},{8,0},{12,4},{1,9},{5,13},{9,1},{13,5},{2,10},{6,14},... | collective-permute-start | bytes 396296 | tf_op jit(solution)/shard_map/ppermute | solution.py:228
  144.9 1.1 fusion.67
  146.0 3.8 %collective-permute-done.15 = f32[4,8256]{1,0:T(4,128)S(1)} collective-permute-done((f32[4,8256]{1,0:T(4,128)S(1)}, f32[4,8256]{1,0:T(4,128)S(1)}, u32[]{:S(2)}, u32[]{:S(2)}) %collective-permute-start.15) | collective-permute-done | bytes 132128 | tf_op jit(solution)/shard_map/ppermute | solution.py:228
  149.9 0.2 fusion.14
  150.1 5.8 %all_gather.3 = bf16[64,2048]{1,0:T(8,128)(2,1)S(1)} all-gather(bf16[64,512]{1,0:T(8,128)(2,1)S(1)} %bitcast.233), channel_id=1, replica_groups=mesh['groups'=2,'tensor'=4,'store'=4] {'store'}, dimensions={1}, use_global_device_ids=true | all-gather | bytes 327680 | tf_op jit(solution)/shard_map/all_gather | solution.py:408
  155.9 5.0 %fusion.68 = f32[64,2048]{1,0:T(8,128)S(1)} fusion(bf16[64,2048]{1,0:T(8,128)(2,1)S(1)} %all_gather.3, bf16[2048,2048]{1,0:T(8,128)(2,1)} %param.12), kind=kOutput, calls=%fused_computation.168 | convolution fusion | flops 536870912 | bytes 9175040 | tf_op jit(solution)/shard_map/dot_general | solution.py:434
  161.0 8.5 %collective-permute-done.18 = f32[2,16,2048]{2,1,0:T(8,128)S(1)} collective-permute-done((f32[2,16,2048]{2,1,0:T(8,128)S(1)}, f32[2,16,2048]{2,1,0:T(8,128)S(1)}, u32[]{:S(2)}, u32[]{:S(2)}) %collective-permute-start.18) | collective-permute-done | bytes 262176 | tf_op jit(solution)/shard_map/ppermute | solution.py:228
  169.6 1.5 collective-permute-start.19
  171.1 7.3 %collective-permute-done.19 = f32[16,2048]{1,0:T(8,128)S(1)} collective-permute-done((f32[16,2048]{1,0:T(8,128)S(1)}, f32[16,2048]{1,0:T(8,128)S(1)}, u32[]{:S(2)}, u32[]{:S(2)}) %collective-permute-start.19) | collective-permute-done | bytes 131104 | tf_op jit(solution)/shard_map/ppermute | solution.py:228
  178.3 0.6 fusion.22
  (81 shorter events, 2.8 us)
Async XLA Ops:
  0.0 1.0 copy-start
  5.9 1.5 copy-start.3
  6.2 3.4 %collective-permute-start = (f32[2,4,64,128]{3,2,1,0:T(8,128)S(1)}, f32[2,4,64,128]{3,2,1,0:T(8,128)S(1)}, u32[]{:S(2)}, u32[]{:S(2)}) collective-permute-start(f32[2,4,64,128]{3,2,1,0:T(8,128)S(1)} %bitcast.234), channel_id=1, source_target_pairs={{0,1},{1,0},{2,3},{3,2},{4,5},{5,4},{6,7},{7,6},{8,9},{9,8},{10,11... | collective-permute-start | bytes 786440 | tf_op jit(solution)/shard_map/ppermute | solution.py:228
  9.6 6.7 %collective-permute-start.1 = (f32[4,64,128]{2,1,0:T(8,128)S(1)}, f32[4,64,128]{2,1,0:T(8,128)S(1)}, u32[]{:S(2)}, u32[]{:S(2)}) collective-permute-start(f32[4,64,128]{2,1,0:T(8,128)S(1)} %dynamic-slice_bitcast_fusion.4), channel_id=1, source_target_pairs={{0,2},{1,3},{2,0},{3,1},{4,6},{5,7},{6,4},{7,5},{8,10},{9,11},{10,... | collective-permute-start | bytes 393224 | tf_op jit(solution)/shard_map/ppermute | solution.py:228
  16.6 5.7 %collective-permute-start.2 = (bf16[4,64,128]{2,1,0:T(8,128)(2,1)S(1)}, bf16[4,64,128]{2,1,0:T(8,128)(2,1)S(1)}, u32[]{:S(2)}, u32[]{:S(2)}) collective-permute-start(bf16[4,64,128]{2,1,0:T(8,128)(2,1)S(1)} %pad_maximum_fusion.4), channel_id=1, source_target_pairs={{0,2},{1,3},{2,0},{3,1},{4,6},{5,7},{6,4},{7,5},{8,10},{9,11},{10,... | collective-permute-start | bytes 196616 | tf_op jit(solution)/shard_map/ppermute | solution.py:239
  18.4 5.3 %collective-permute-start.4 = (bf16[4,64,128]{2,1,0:T(8,128)(2,1)S(1)}, bf16[4,64,128]{2,1,0:T(8,128)(2,1)S(1)}, u32[]{:S(2)}, u32[]{:S(2)}) collective-permute-start(bf16[4,64,128]{2,1,0:T(8,128)(2,1)S(1)} %pad_maximum_fusion.4), channel_id=1, source_target_pairs={{0,8},{4,12},{8,0},{12,4},{1,9},{5,13},{9,1},{13,5},{2,10},{6,14},... | collective-permute-start | bytes 196616 | tf_op jit(solution)/shard_map/ppermute | solution.py:239
  23.9 5.0 %collective-permute-start.5 = (bf16[2,4,64,128]{3,2,1,0:T(8,128)(2,1)S(1)}, bf16[2,4,64,128]{3,2,1,0:T(8,128)(2,1)S(1)}, u32[]{:S(2)}, u32[]{:S(2)}) collective-permute-start(bf16[2,4,64,128]{3,2,1,0:T(8,128)(2,1)S(1)} %pad_maximum_fusion.3), channel_id=1, source_target_pairs={{0,4},{4,0},{8,12},{12,8},{1,5},{5,1},{9,13},{13,9},{2,6},{6,2},{1... | collective-permute-start | bytes 393224 | tf_op jit(solution)/shard_map/ppermute | solution.py:239
  29.0 6.4 %collective-permute-start.6 = (bf16[16,64,128]{2,1,0:T(8,128)(2,1)S(1)}, bf16[16,64,128]{2,1,0:T(8,128)(2,1)S(1)}, u32[]{:S(2)}, u32[]{:S(2)}) collective-permute-start(bf16[16,64,128]{2,1,0:T(8,128)(2,1)S(1)} %bitcast.228), channel_id=1, source_target_pairs={{0,2},{1,3},{2,0},{3,1},{4,6},{5,7},{6,4},{7,5},{8,10},{9,11},{10,... | collective-permute-start | bytes 786440 | tf_op jit(solution)/shard_map/ppermute | solution.py:239
  30.8 4.8 %collective-permute-start.3 = (bf16[2,4,64,128]{3,2,1,0:T(8,128)(2,1)S(1)}, bf16[2,4,64,128]{3,2,1,0:T(8,128)(2,1)S(1)}, u32[]{:S(2)}, u32[]{:S(2)}) collective-permute-start(bf16[2,4,64,128]{3,2,1,0:T(8,128)(2,1)S(1)} %pad_maximum_fusion.2), channel_id=1, source_target_pairs={{0,1},{1,0},{2,3},{3,2},{4,5},{5,4},{6,7},{7,6},{8,9},{9,8},{10,11... | collective-permute-start | bytes 393224 | tf_op jit(solution)/shard_map/ppermute | solution.py:239
  35.6 15.8 %collective-permute-start.7 = (bf16[2,16,64,128]{3,2,1,0:T(8,128)(2,1)S(1)}, bf16[2,16,64,128]{3,2,1,0:T(8,128)(2,1)S(1)}, u32[]{:S(2)}, u32[]{:S(2)}) collective-permute-start(bf16[2,16,64,128]{3,2,1,0:T(8,128)(2,1)S(1)} %pad_maximum_fusion), channel_id=1, source_target_pairs={{0,1},{1,0},{2,3},{3,2},{4,5},{5,4},{6,7},{7,6},{8,9},{9,8},{10,11... | collective-permute-start | bytes 1572872 | tf_op jit(solution)/shard_map/ppermute | solution.py:239
  88.8 4.1 %copy-start.2 = (f32[2,512,1]{2,1,0:T(8,128)S(1)}, f32[2,512,1]{2,1,0:T(8,128)}, u32[]{:S(2)}) copy-start(f32[2,512,1]{2,1,0:T(8,128)} %get-tuple-element.15) | copy-start | bytes 12292
  88.8 8.9 %copy-start.1 = (f32[2,512,128]{2,1,0:T(8,128)S(1)}, f32[2,512,128]{2,1,0:T(8,128)}, u32[]{:S(2)}) copy-start(f32[2,512,128]{2,1,0:T(8,128)} %get-tuple-element.11) | copy-start | bytes 1572868
  91.0 1.4 collective-permute-start.8
  92.4 3.9 %collective-permute-start.9 = (f32[64,64]{1,0:T(8,128)S(1)}, f32[64,64]{1,0:T(8,128)S(1)}, u32[]{:S(2)}, u32[]{:S(2)}) collective-permute-start(f32[64,64]{1,0:T(8,128)S(1)} %max.15), channel_id=1, source_target_pairs={{0,2},{1,3},{2,0},{3,1},{4,6},{5,7},{6,4},{7,5},{8,10},{9,11},{10,... | collective-permute-start | bytes 49160 | tf_op jit(solution)/shard_map/ppermute | solution.py:215
  96.3 5.4 %collective-permute-start.10 = (f32[64,64]{1,0:T(8,128)S(1)}, f32[64,64]{1,0:T(8,128)S(1)}, u32[]{:S(2)}, u32[]{:S(2)}) collective-permute-start(f32[64,64]{1,0:T(8,128)S(1)} %max.16), channel_id=1, source_target_pairs={{0,4},{4,0},{8,12},{12,8},{1,5},{5,1},{9,13},{13,9},{2,6},{6,2},{1... | collective-permute-start | bytes 49160 | tf_op jit(solution)/shard_map/ppermute | solution.py:215
  101.7 5.3 %collective-permute-start.11 = (f32[64,64]{1,0:T(8,128)S(1)}, f32[64,64]{1,0:T(8,128)S(1)}, u32[]{:S(2)}, u32[]{:S(2)}) collective-permute-start(f32[64,64]{1,0:T(8,128)S(1)} %max.17), channel_id=1, source_target_pairs={{0,8},{4,12},{8,0},{12,4},{1,9},{5,13},{9,1},{13,5},{2,10},{6,14},... | collective-permute-start | bytes 49160 | tf_op jit(solution)/shard_map/ppermute | solution.py:215
  113.4 2.9 %collective-permute-start.12 = (f32[2,2,2,4,8256]{4,3,0,1,2:T(4,128)}, f32[2,2,2,4,8256]{4,3,0,1,2:T(4,128)S(1)}, u32[]{:S(2)}, u32[]{:S(2)}) collective-permute-start(f32[2,2,2,4,8256]{4,3,0,1,2:T(4,128)} %fusion.16), channel_id=1, source_target_pairs={{0,1},{1,0},{2,3},{3,2},{4,5},{5,4},{6,7},{7,6},{8,9},{9,8},{10,11... | collective-permute-start | bytes 3170312 | tf_op jit(solution)/shard_map/ppermute | solution.py:228
  116.8 17.2 %collective-permute-start.13 = (f32[2,2,4,8256]{3,2,1,0:T(4,128)S(1)}, f32[2,2,4,8256]{3,2,1,0:T(4,128)S(1)}, u32[]{:S(2)}, u32[]{:S(2)}) collective-permute-start(f32[2,2,4,8256]{3,2,1,0:T(4,128)S(1)} %bitcast.230), channel_id=1, source_target_pairs={{0,2},{1,3},{2,0},{3,1},{4,6},{5,7},{6,4},{7,5},{8,10},{9,11},{10,... | collective-permute-start | bytes 1585160 | tf_op jit(solution)/shard_map/ppermute | solution.py:228
  119.5 1.4 collective-permute-start.16
  121.0 12.9 %collective-permute-start.17 = (f32[64,512]{1,0:T(8,128)S(1)}, f32[64,512]{1,0:T(8,128)S(1)}, u32[]{:S(2)}, u32[]{:S(2)}) collective-permute-start(f32[64,512]{1,0:T(8,128)S(1)} %add.285), channel_id=1, source_target_pairs={{0,2},{1,3},{2,0},{3,1},{4,6},{5,7},{6,4},{7,5},{8,10},{9,11},{10,... | collective-permute-start | bytes 393224 | tf_op jit(solution)/shard_map/ppermute | solution.py:215
  134.2 7.7 %collective-permute-start.14 = (f32[2,4,8256]{2,1,0:T(4,128)S(1)}, f32[2,4,8256]{2,1,0:T(4,128)S(1)}, u32[]{:S(2)}, u32[]{:S(2)}) collective-permute-start(f32[2,4,8256]{2,1,0:T(4,128)S(1)} %dynamic-slice_bitcast_fusion), channel_id=1, source_target_pairs={{0,4},{4,0},{8,12},{12,8},{1,5},{5,1},{9,13},{13,9},{2,6},{6,2},{1... | collective-permute-start | bytes 792584 | tf_op jit(solution)/shard_map/ppermute | solution.py:228
  142.0 7.8 %collective-permute-start.15 = (f32[4,8256]{1,0:T(4,128)S(1)}, f32[4,8256]{1,0:T(4,128)S(1)}, u32[]{:S(2)}, u32[]{:S(2)}) collective-permute-start(f32[4,8256]{1,0:T(4,128)S(1)} %dynamic-slice_bitcast_fusion.2), channel_id=1, source_target_pairs={{0,8},{4,12},{8,0},{12,4},{1,9},{5,13},{9,1},{13,5},{2,10},{6,14},... | collective-permute-start | bytes 396296 | tf_op jit(solution)/shard_map/ppermute | solution.py:228
  160.9 8.6 %collective-permute-start.18 = (f32[2,16,2048]{2,1,0:T(8,128)S(1)}, f32[2,16,2048]{2,1,0:T(8,128)S(1)}, u32[]{:S(2)}, u32[]{:S(2)}) collective-permute-start(f32[2,16,2048]{2,1,0:T(8,128)S(1)} %dynamic-slice_bitcast_fusion.1), channel_id=1, source_target_pairs={{0,4},{4,0},{8,12},{12,8},{1,5},{5,1},{9,13},{13,9},{2,6},{6,2},{1... | collective-permute-start | bytes 786440 | tf_op jit(solution)/shard_map/ppermute | solution.py:228
  169.6 8.7 %collective-permute-start.19 = (f32[16,2048]{1,0:T(8,128)S(1)}, f32[16,2048]{1,0:T(8,128)S(1)}, u32[]{:S(2)}, u32[]{:S(2)}) collective-permute-start(f32[16,2048]{1,0:T(8,128)S(1)} %dynamic-slice_bitcast_fusion.3), channel_id=1, source_target_pairs={{0,8},{4,12},{8,0},{12,4},{1,9},{5,13},{9,1},{13,5},{2,10},{6,14},... | collective-permute-start | bytes 393224 | tf_op jit(solution)/shard_map/ppermute | solution.py:228

commit v17 on v14

--- a/solution.py
+++ b/solution.py
@@ -268,7 +268,10 @@
     if any(lax.axis_size(a) & (lax.axis_size(a) - 1) for a in axes):
         return jnp.max(lax.all_gather(x, axes), axis=0)
     for a in axes:
-        x = axis_reduce(x, a, jnp.maximum)
+        n = lax.axis_size(a)
+        others = [lax.ppermute(x, a, perm=[(i, (i + k) % n) for i in range(n)]) for k in range(1, n)]
+        for other in others:
+            x = jnp.maximum(x, other)
     return x
 
 

time: 177 us -> 177 us (level)
    ppermute x0 -> x6, starting transfers between devices: none -> 7.65 us  [axis_max(): lax.ppermute(x, a, perm=[(i, (i + k) % n) for i in range(n)])]
    ppermute x6 -> x2, starting transfers between devices: 7.27 us -> 1.45 us  [axis_reduce(): x = op(x, lax.ppermute(x, axis, perm=[(i, i ^ d) for i in range(n)]))]
    ppermute x6 -> x2, waiting for transfers between devices: 16.8 us -> 12.6 us  [axis_reduce(): x = op(x, lax.ppermute(x, axis, perm=[(i, i ^ d) for i in range(n)]))]
  transfers between devices with their start and end apart: 20 -> 22, of which waited for: 14 -> 12; matrix products, arithmetic and copies ran while one was open for 9% -> 10% of each run, Pallas kernels for 7% -> 7%
where the time goes in v17:
time: 177 us
  waiting for transfers between devices  58.2 us (33%)
  Pallas kernels  47.5 us (27%)
  starting transfers between devices  22.8 us (13%)
  local copies, waits for them, and re-layouts  13.7 us (8%)
  other arithmetic  13.6 us (8%)
  matrix products  13.2 us (7%)
  blocking collectives  5.79 us (3%)
  between operations  1.96 us (1%)
    pallas_call x2, Pallas kernels, hist_attend(): pl.pallas_call(kernel, grid_spec=grid_spec, out_shape=[jax.ShapeDtypeStru...  47.5 us
    ppermute x8, waiting for transfers between devices, bit_scatter(): block = keep + lax.ppermute(send, axis, perm=[(i, i ^ d) for i in range(n)])  35.1 us
    ppermute x2, waiting for transfers between devices, axis_reduce(): x = op(x, lax.ppermute(x, axis, perm=[(i, i ^ d) for i in range(n)]))  12.6 us
    ppermute x6, waiting for transfers between devices, bit_gather(): other = lax.ppermute(x, axis, perm=[(i, i ^ d) for i in range(n)])  9.31 us
    ppermute x6, starting transfers between devices, axis_max(): lax.ppermute(x, a, perm=[(i, (i + k) % n) for i in range(n)])  7.65 us
    ppermute x8, starting transfers between devices, bit_scatter(): block = keep + lax.ppermute(send, axis, perm=[(i, i ^ d) for i in range(n)])  7.1 us
    ppermute x6, starting transfers between devices, bit_gather(): other = lax.ppermute(x, axis, perm=[(i, i ^ d) for i in range(n)])  6.6 us
    pallas_call x4, local copies, waits for them, and re-layouts, hist_attend(): pl.pallas_call(kernel, grid_spec=grid_spec, out_shape=[jax.ShapeDtypeStru...  6.49 us
  transfers between devices with their start and end apart: 22, of which 12 were waited for; matrix products, arithmetic and copies ran while one was open for 10% of the time, Pallas kernels for 7%

profile of v17, /device:TPU:0, one launch (start us, length us, event | category | flops | bytes accessed | tf_op | source)
XLA Modules:
  0.0 176.8 jit_solution(14338103062530760007)
XLA Ops:
  0.0 0.9 copy-done
  1.0 4.9 %convolution_bitcast_fusion = f32[8,8,16,128]{3,1,2,0:T(8,128)S(1)} fusion(bf16[64,2048]{1,0:T(8,128)(2,1)S(1)} %copy-done, bf16[2048,2048]{1,0:T(8,128)(2,1)} %param.10), kind=kOutput, calls=%fused_computation.15 | convolution fusion | flops 536870912 | bytes 9175040 | tf_op jit(solution)/shard_map/dot_general | solution.py:296
  5.9 0.1 copy.87
  6.0 0.1 constant_dynamic-slice_fusion.5
  6.2 0.5 collective-permute-start
  7.4 1.2 reduce-window.6
  8.7 0.1 copy.60
  9.1 0.2 fusion.32
  9.3 0.2 multiply_cosine_fusion
  9.6 2.6 %collective-permute-start.1 = (f32[4,64,128]{2,1,0:T(8,128)S(1)}, f32[4,64,128]{2,1,0:T(8,128)S(1)}, u32[]{:S(2)}, u32[]{:S(2)}) collective-permute-start(f32[4,64,128]{2,1,0:T(8,128)S(1)} %dynamic-slice_bitcast_fusion.4), channel_id=1, source_target_pairs={{0,2},{1,3},{2,0},{3,1},{4,6},{5,7},{6,4},{7,5},{8,10},{9,11},{10,... | collective-permute-start | bytes 393224 | tf_op jit(solution)/shard_map/ppermute | solution.py:228
  12.2 4.2 %collective-permute-done.1 = f32[4,64,128]{2,1,0:T(8,128)S(1)} collective-permute-done((f32[4,64,128]{2,1,0:T(8,128)S(1)}, f32[4,64,128]{2,1,0:T(8,128)S(1)}, u32[]{:S(2)}, u32[]{:S(2)}) %collective-permute-start.1) | collective-permute-done | bytes 131104 | tf_op jit(solution)/shard_map/ppermute | solution.py:228
  16.4 0.1 subtract_convert_fusion
  16.6 1.8 %collective-permute-start.2 = (bf16[4,64,128]{2,1,0:T(8,128)(2,1)S(1)}, bf16[4,64,128]{2,1,0:T(8,128)(2,1)S(1)}, u32[]{:S(2)}, u32[]{:S(2)}) collective-permute-start(bf16[4,64,128]{2,1,0:T(8,128)(2,1)S(1)} %pad_maximum_fusion.4), channel_id=1, source_target_pairs={{0,2},{1,3},{2,0},{3,1},{4,6},{5,7},{6,4},{7,5},{8,10},{9,11},{10,... | collective-permute-start | bytes 196616 | tf_op jit(solution)/shard_map/ppermute | solution.py:239
  18.4 2.6 %collective-permute-start.4 = (bf16[4,64,128]{2,1,0:T(8,128)(2,1)S(1)}, bf16[4,64,128]{2,1,0:T(8,128)(2,1)S(1)}, u32[]{:S(2)}, u32[]{:S(2)}) collective-permute-start(bf16[4,64,128]{2,1,0:T(8,128)(2,1)S(1)} %pad_maximum_fusion.4), channel_id=1, source_target_pairs={{0,8},{4,12},{8,0},{12,4},{1,9},{5,13},{9,1},{13,5},{2,10},{6,14},... | collective-permute-start | bytes 196616 | tf_op jit(solution)/shard_map/ppermute | solution.py:239
  21.0 0.7 fusion.36
  22.4 1.4 collective-permute-done.4
  23.8 0.1 select_bitcast_fusion.9
  23.9 1.5 collective-permute-start.5
  25.5 3.4 %collective-permute-done.5 = bf16[2,4,64,128]{3,2,1,0:T(8,128)(2,1)S(1)} collective-permute-done((bf16[2,4,64,128]{3,2,1,0:T(8,128)(2,1)S(1)}, bf16[2,4,64,128]{3,2,1,0:T(8,128)(2,1)S(1)}, u32[]{:S(2)}, u32[]{:S(2)}) %collective-permute-start.5) | collective-permute-done | bytes 131104 | tf_op jit(solution)/shard_map/ppermute | solution.py:239
  29.0 0.6 collective-permute-start.6
  29.6 0.7 maximum_bitcast_fusion.2.cos_ref
  30.3 0.6 maximum_bitcast_fusion.3.sin_ref
  31.0 4.5 %collective-permute-done.6 = bf16[16,64,128]{2,1,0:T(8,128)(2,1)S(1)} collective-permute-done((bf16[16,64,128]{2,1,0:T(8,128)(2,1)S(1)}, bf16[16,64,128]{2,1,0:T(8,128)(2,1)S(1)}, u32[]{:S(2)}, u32[]{:S(2)}) %collective-permute-start.6) | collective-permute-done | bytes 262176 | tf_op jit(solution)/shard_map/ppermute | solution.py:239
  35.7 0.7 copy.59
  36.4 13.2 %shard_map.85 = (f32[2,512,128]{2,1,0:T(8,128)}, f32[2,512,1]{2,1,0:T(8,128)}, f32[2,512,1]{2,1,0:T(8,128)}) custom-call(s32[1]{0:T(128)} %bitcast.kv0_ref, bf16[2,512,128]{2,1,0:T(8,128)(2,1)} %bitcast.226, bf16[40,128,2048]{2,1,0:T(8,128)(2,1)} %bitcast.217, bf16[40,128,2048]{2,1,0:T(8,128)(2,1)} %bitcast.218, f32[1,1,5120]{2,1,0:T(1,128)} %bitcast.235, ...), custom_call_target="tpu_custom_call" | custom-call | flops 2684354560 | bytes 6029312 | tf_op jit(solution)/shard_map/pallas_call | solution.py:194
  49.6 1.2 copy.65
  50.9 1.2 copy.69
  52.2 0.1 maximum_bitcast_fusion
  52.5 1.2 fusion.20.q_ref
  53.7 34.3 %shard_map.86 = (f32[6,512,128]{2,1,0:T(8,128)}, f32[6,512,1]{2,1,0:T(8,128)}, f32[6,512,1]{2,1,0:T(8,128)}) custom-call(s32[1]{0:T(128)} %bitcast.26.kv0_ref, bf16[6,512,128]{2,1,0:T(8,128)(2,1)} %fusion.20.q_ref, bf16[40,128,2048]{2,1,0:T(8,128)(2,1)} %bitcast.219, bf16[40,128,2048]{2,1,0:T(8,128)(2,1)} %bitcast.220, f32[1,1,5120]{2,1,0:T(1,128)} %bitcast.236, ...), custom_call_target="tpu_custom_call" | custom-call | flops 8053063680 | bytes 18087936 | tf_op jit(solution)/shard_map/pallas_call | solution.py:194
  88.0 2.0 %copy.66 = f32[6,512,1]{1,0,2:T(8,128)S(1)} copy(f32[6,512,1]{2,1,0:T(8,128)} %get-tuple-element.14) | data formatting | bytes 24576 | tf_op jit(solution)/shard_map/pallas_call | solution.py:194
  90.2 0.6 collective-permute-start.10
  90.8 1.5 collective-permute-start.9
  92.3 1.9 %fusion.2 = f32[8,512,128]{2,1,0:T(8,128)S(1)} fusion(s32[]{:T(128)S(6)} %select_n.354, f32[2,512,128]{2,1,0:T(8,128)S(1)} %copy-done.1, f32[6,512,128]{2,1,0:T(8,128)} %get-tuple-element.12), kind=kLoop, calls=%fused_computation.8 | loop fusion | flops 1572864 | bytes 4194308 | tf_op jit(solution)/shard_map/concatenate | solution.py:357
  94.3 2.0 %copy.70 = f32[6,512,1]{1,0,2:T(8,128)S(1)} copy(f32[6,512,1]{2,1,0:T(8,128)} %get-tuple-element.16) | data formatting | bytes 24576 | tf_op jit(solution)/shard_map/pallas_call | solution.py:194
  96.3 1.4 collective-permute-start.11
  97.8 3.3 %collective-permute-start.12 = (f32[64,64]{1,0:T(8,128)S(1)}, f32[64,64]{1,0:T(8,128)S(1)}, u32[]{:S(2)}, u32[]{:S(2)}) collective-permute-start(f32[64,64]{1,0:T(8,128)S(1)} %maximum_maximum_fusion.1), channel_id=1, source_target_pairs={{0,8},{4,12},{8,0},{12,4},{1,9},{5,13},{9,1},{13,5},{2,10},{6,14},... | collective-permute-start | bytes 49160 | tf_op jit(solution)/shard_map/ppermute | solution.py:272
  101.0 0.8 collective-permute-start.13
  101.9 1.8 %reshape.442 = f32[2,2,2,2,4,8192]{5,4,3,2,1,0:T(4,128)} reshape(f32[8,512,128]{2,1,0:T(8,128)S(1)} %fusion.2) | data formatting | bytes 4194304 | tf_op jit(solution)/shard_map/reshape | solution.py:362
  103.7 1.2 collective-permute-done.13
  105.0 0.6 mul.261
  105.6 1.8 %mul.262 = f32[2,2,2,2,4,8192]{5,4,3,2,1,0:T(4,128)} reshape(f32[64,64,128]{2,1,0:T(8,128)S(1)} %mul.261) | data formatting | bytes 4194304 | tf_op jit(solution)/shard_map/mul | solution.py:369
  107.4 2.8 %mul.263 = f32[2,2,2,2,4,8192]{5,4,3,2,1,0:T(4,128)S(1)} multiply(f32[2,2,2,2,4,8192]{5,4,3,2,1,0:T(4,128)} %reshape.442, f32[2,2,2,2,4,8192]{5,4,3,2,1,0:T(4,128)} %mul.262) | non-fusion elementwise | flops 524288 | bytes 6291456 | tf_op jit(solution)/shard_map/mul | solution.py:369
  110.1 1.3 fusion.16
  111.4 2.9 %collective-permute-done.14 = f32[2,2,2,4,8256]{4,3,0,1,2:T(4,128)S(1)} collective-permute-done((f32[2,2,2,4,8256]{4,3,0,1,2:T(4,128)}, f32[2,2,2,4,8256]{4,3,0,1,2:T(4,128)S(1)}, u32[]{:S(2)}, u32[]{:S(2)}) %collective-permute-start.14) | collective-permute-done | bytes 1056800 | tf_op jit(solution)/shard_map/ppermute | solution.py:228
  114.3 0.4 fusion.19
  114.8 0.8 collective-permute-start.15
  115.6 2.1 %fusion.5 = f32[64,512]{1,0:T(8,128)S(1)} fusion(bf16[64,2048]{1,0:T(8,128)(2,1)S(1)} %copy-done, bf16[2048,2048]{1,0:T(8,128)(2,1)} %param.11, s32[]{:T(128)S(6)} %select_n.360), kind=kOutput, calls=%fused_computation.16 | convolution fusion | flops 134217728 | bytes 2490372 | tf_op jit(solution)/shard_map/dot_general | solution.py:297
  117.8 1.3 collective-permute-done.18
  119.1 1.4 collective-permute-start.19
  120.5 11.3 %collective-permute-done.19 = f32[64,512]{1,0:T(8,128)S(1)} collective-permute-done((f32[64,512]{1,0:T(8,128)S(1)}, f32[64,512]{1,0:T(8,128)S(1)}, u32[]{:S(2)}, u32[]{:S(2)}) %collective-permute-start.19) | collective-permute-done | bytes 131104 | tf_op jit(solution)/shard_map/ppermute | solution.py:215
  132.0 0.1 bitcast_add_fusion
  132.2 0.2 collective-permute-start.16
  132.6 7.3 %collective-permute-done.16 = f32[2,4,8256]{2,1,0:T(4,128)S(1)} collective-permute-done((f32[2,4,8256]{2,1,0:T(4,128)S(1)}, f32[2,4,8256]{2,1,0:T(4,128)S(1)}, u32[]{:S(2)}, u32[]{:S(2)}) %collective-permute-start.16) | collective-permute-done | bytes 264224 | tf_op jit(solution)/shard_map/ppermute | solution.py:228
  140.0 1.5 collective-permute-start.17
  141.5 1.1 fusion.67
  142.6 5.0 %collective-permute-done.17 = f32[4,8256]{1,0:T(4,128)S(1)} collective-permute-done((f32[4,8256]{1,0:T(4,128)S(1)}, f32[4,8256]{1,0:T(4,128)S(1)}, u32[]{:S(2)}, u32[]{:S(2)}) %collective-permute-start.17) | collective-permute-done | bytes 132128 | tf_op jit(solution)/shard_map/ppermute | solution.py:228
  147.7 0.2 fusion.14
  147.9 5.8 %all_gather.3 = bf16[64,2048]{1,0:T(8,128)(2,1)S(1)} all-gather(bf16[64,512]{1,0:T(8,128)(2,1)S(1)} %bitcast.233), channel_id=1, replica_groups=mesh['groups'=2,'tensor'=4,'store'=4] {'store'}, dimensions={1}, use_global_device_ids=true | all-gather | bytes 327680 | tf_op jit(solution)/shard_map/all_gather | solution.py:411
  153.7 5.0 %fusion.68 = f32[64,2048]{1,0:T(8,128)S(1)} fusion(bf16[64,2048]{1,0:T(8,128)(2,1)S(1)} %all_gather.3, bf16[2048,2048]{1,0:T(8,128)(2,1)} %param.12), kind=kOutput, calls=%fused_computation.170 | convolution fusion | flops 536870912 | bytes 9175040 | tf_op jit(solution)/shard_map/dot_general | solution.py:437
  158.8 8.5 %collective-permute-done.20 = f32[2,16,2048]{2,1,0:T(8,128)S(1)} collective-permute-done((f32[2,16,2048]{2,1,0:T(8,128)S(1)}, f32[2,16,2048]{2,1,0:T(8,128)S(1)}, u32[]{:S(2)}, u32[]{:S(2)}) %collective-permute-start.20) | collective-permute-done | bytes 262176 | tf_op jit(solution)/shard_map/ppermute | solution.py:228
  167.4 1.5 collective-permute-start.21
  168.9 7.2 %collective-permute-done.21 = f32[16,2048]{1,0:T(8,128)S(1)} collective-permute-done((f32[16,2048]{1,0:T(8,128)S(1)}, f32[16,2048]{1,0:T(8,128)S(1)}, u32[]{:S(2)}, u32[]{:S(2)}) %collective-permute-start.21) | collective-permute-done | bytes 131104 | tf_op jit(solution)/shard_map/ppermute | solution.py:228
  176.1 0.6 fusion.22
  (81 shorter events, 2.7 us)
Async XLA Ops:
  0.0 1.0 copy-start
  5.9 1.5 copy-start.2
  6.2 3.3 %collective-permute-start = (f32[2,4,64,128]{3,2,1,0:T(8,128)S(1)}, f32[2,4,64,128]{3,2,1,0:T(8,128)S(1)}, u32[]{:S(2)}, u32[]{:S(2)}) collective-permute-start(f32[2,4,64,128]{3,2,1,0:T(8,128)S(1)} %bitcast.234), channel_id=1, source_target_pairs={{0,1},{1,0},{2,3},{3,2},{4,5},{5,4},{6,7},{7,6},{8,9},{9,8},{10,11... | collective-permute-start | bytes 786440 | tf_op jit(solution)/shard_map/ppermute | solution.py:228
  9.6 6.7 %collective-permute-start.1 = (f32[4,64,128]{2,1,0:T(8,128)S(1)}, f32[4,64,128]{2,1,0:T(8,128)S(1)}, u32[]{:S(2)}, u32[]{:S(2)}) collective-permute-start(f32[4,64,128]{2,1,0:T(8,128)S(1)} %dynamic-slice_bitcast_fusion.4), channel_id=1, source_target_pairs={{0,2},{1,3},{2,0},{3,1},{4,6},{5,7},{6,4},{7,5},{8,10},{9,11},{10,... | collective-permute-start | bytes 393224 | tf_op jit(solution)/shard_map/ppermute | solution.py:228
  16.6 5.7 %collective-permute-start.2 = (bf16[4,64,128]{2,1,0:T(8,128)(2,1)S(1)}, bf16[4,64,128]{2,1,0:T(8,128)(2,1)S(1)}, u32[]{:S(2)}, u32[]{:S(2)}) collective-permute-start(bf16[4,64,128]{2,1,0:T(8,128)(2,1)S(1)} %pad_maximum_fusion.4), channel_id=1, source_target_pairs={{0,2},{1,3},{2,0},{3,1},{4,6},{5,7},{6,4},{7,5},{8,10},{9,11},{10,... | collective-permute-start | bytes 196616 | tf_op jit(solution)/shard_map/ppermute | solution.py:239
  18.4 5.3 %collective-permute-start.4 = (bf16[4,64,128]{2,1,0:T(8,128)(2,1)S(1)}, bf16[4,64,128]{2,1,0:T(8,128)(2,1)S(1)}, u32[]{:S(2)}, u32[]{:S(2)}) collective-permute-start(bf16[4,64,128]{2,1,0:T(8,128)(2,1)S(1)} %pad_maximum_fusion.4), channel_id=1, source_target_pairs={{0,8},{4,12},{8,0},{12,4},{1,9},{5,13},{9,1},{13,5},{2,10},{6,14},... | collective-permute-start | bytes 196616 | tf_op jit(solution)/shard_map/ppermute | solution.py:239
  23.9 5.0 %collective-permute-start.5 = (bf16[2,4,64,128]{3,2,1,0:T(8,128)(2,1)S(1)}, bf16[2,4,64,128]{3,2,1,0:T(8,128)(2,1)S(1)}, u32[]{:S(2)}, u32[]{:S(2)}) collective-permute-start(bf16[2,4,64,128]{3,2,1,0:T(8,128)(2,1)S(1)} %pad_maximum_fusion.3), channel_id=1, source_target_pairs={{0,4},{4,0},{8,12},{12,8},{1,5},{5,1},{9,13},{13,9},{2,6},{6,2},{1... | collective-permute-start | bytes 393224 | tf_op jit(solution)/shard_map/ppermute | solution.py:239
  29.0 6.4 %collective-permute-start.6 = (bf16[16,64,128]{2,1,0:T(8,128)(2,1)S(1)}, bf16[16,64,128]{2,1,0:T(8,128)(2,1)S(1)}, u32[]{:S(2)}, u32[]{:S(2)}) collective-permute-start(bf16[16,64,128]{2,1,0:T(8,128)(2,1)S(1)} %bitcast.228), channel_id=1, source_target_pairs={{0,2},{1,3},{2,0},{3,1},{4,6},{5,7},{6,4},{7,5},{8,10},{9,11},{10,... | collective-permute-start | bytes 786440 | tf_op jit(solution)/shard_map/ppermute | solution.py:239
  30.9 4.7 %collective-permute-start.3 = (bf16[2,4,64,128]{3,2,1,0:T(8,128)(2,1)S(1)}, bf16[2,4,64,128]{3,2,1,0:T(8,128)(2,1)S(1)}, u32[]{:S(2)}, u32[]{:S(2)}) collective-permute-start(bf16[2,4,64,128]{3,2,1,0:T(8,128)(2,1)S(1)} %pad_maximum_fusion.2), channel_id=1, source_target_pairs={{0,1},{1,0},{2,3},{3,2},{4,5},{5,4},{6,7},{7,6},{8,9},{9,8},{10,11... | collective-permute-start | bytes 393224 | tf_op jit(solution)/shard_map/ppermute | solution.py:239
  35.6 16.5 %collective-permute-start.7 = (bf16[2,16,64,128]{3,2,1,0:T(8,128)(2,1)S(1)}, bf16[2,16,64,128]{3,2,1,0:T(8,128)(2,1)S(1)}, u32[]{:S(2)}, u32[]{:S(2)}) collective-permute-start(bf16[2,16,64,128]{3,2,1,0:T(8,128)(2,1)S(1)} %pad_maximum_fusion), channel_id=1, source_target_pairs={{0,1},{1,0},{2,3},{3,2},{4,5},{5,4},{6,7},{7,6},{8,9},{9,8},{10,11... | collective-permute-start | bytes 1572872 | tf_op jit(solution)/shard_map/ppermute | solution.py:239
  53.7 38.6 %copy-start.1 = (f32[2,512,128]{2,1,0:T(8,128)S(1)}, f32[2,512,128]{2,1,0:T(8,128)}, u32[]{:S(2)}) copy-start(f32[2,512,128]{2,1,0:T(8,128)} %get-tuple-element.11) | copy-start | bytes 1572868
  90.2 6.1 %collective-permute-start.10 = (f32[64,64]{1,0:T(8,128)S(1)}, f32[64,64]{1,0:T(8,128)S(1)}, u32[]{:S(2)}, u32[]{:S(2)}) collective-permute-start(f32[64,64]{1,0:T(8,128)S(1)} %reshape.443), channel_id=1, source_target_pairs={{0,3},{1,0},{2,1},{3,2},{4,7},{5,4},{6,5},{7,6},{8,11},{9,8},{10,9... | collective-permute-start | bytes 49160 | tf_op jit(solution)/shard_map/ppermute | solution.py:272
  90.8 5.5 %collective-permute-start.8 = (f32[64,64]{1,0:T(8,128)S(1)}, f32[64,64]{1,0:T(8,128)S(1)}, u32[]{:S(2)}, u32[]{:S(2)}) collective-permute-start(f32[64,64]{1,0:T(8,128)S(1)} %reshape.443), channel_id=1, source_target_pairs={{0,1},{1,2},{2,3},{3,0},{4,5},{5,6},{6,7},{7,4},{8,9},{9,10},{10,1... | collective-permute-start | bytes 49160 | tf_op jit(solution)/shard_map/ppermute | solution.py:272
  90.8 5.5 %collective-permute-start.9 = (f32[64,64]{1,0:T(8,128)S(1)}, f32[64,64]{1,0:T(8,128)S(1)}, u32[]{:S(2)}, u32[]{:S(2)}) collective-permute-start(f32[64,64]{1,0:T(8,128)S(1)} %reshape.443), channel_id=1, source_target_pairs={{0,2},{1,3},{2,0},{3,1},{4,6},{5,7},{6,4},{7,5},{8,10},{9,11},{10,... | collective-permute-start | bytes 49160 | tf_op jit(solution)/shard_map/ppermute | solution.py:272
  96.3 7.4 %collective-permute-start.11 = (f32[64,64]{1,0:T(8,128)S(1)}, f32[64,64]{1,0:T(8,128)S(1)}, u32[]{:S(2)}, u32[]{:S(2)}) collective-permute-start(f32[64,64]{1,0:T(8,128)S(1)} %maximum_maximum_fusion.1), channel_id=1, source_target_pairs={{0,4},{4,8},{8,12},{12,0},{1,5},{5,9},{9,13},{13,1},{2,6},{6,10},{... | collective-permute-start | bytes 49160 | tf_op jit(solution)/shard_map/ppermute | solution.py:272
  97.8 6.0 %collective-permute-start.12 = (f32[64,64]{1,0:T(8,128)S(1)}, f32[64,64]{1,0:T(8,128)S(1)}, u32[]{:S(2)}, u32[]{:S(2)}) collective-permute-start(f32[64,64]{1,0:T(8,128)S(1)} %maximum_maximum_fusion.1), channel_id=1, source_target_pairs={{0,8},{4,12},{8,0},{12,4},{1,9},{5,13},{9,1},{13,5},{2,10},{6,14},... | collective-permute-start | bytes 49160 | tf_op jit(solution)/shard_map/ppermute | solution.py:272
  101.0 3.9 %collective-permute-start.13 = (f32[64,64]{1,0:T(8,128)S(1)}, f32[64,64]{1,0:T(8,128)S(1)}, u32[]{:S(2)}, u32[]{:S(2)}) collective-permute-start(f32[64,64]{1,0:T(8,128)S(1)} %maximum_maximum_fusion.1), channel_id=1, source_target_pairs={{0,12},{4,0},{8,4},{12,8},{1,13},{5,1},{9,5},{13,9},{2,14},{6,2},{... | collective-permute-start | bytes 49160 | tf_op jit(solution)/shard_map/ppermute | solution.py:272
  111.4 2.9 %collective-permute-start.14 = (f32[2,2,2,4,8256]{4,3,0,1,2:T(4,128)}, f32[2,2,2,4,8256]{4,3,0,1,2:T(4,128)S(1)}, u32[]{:S(2)}, u32[]{:S(2)}) collective-permute-start(f32[2,2,2,4,8256]{4,3,0,1,2:T(4,128)} %fusion.16), channel_id=1, source_target_pairs={{0,1},{1,0},{2,3},{3,2},{4,5},{5,4},{6,7},{7,6},{8,9},{9,8},{10,11... | collective-permute-start | bytes 3170312 | tf_op jit(solution)/shard_map/ppermute | solution.py:228
  114.8 17.2 %collective-permute-start.15 = (f32[2,2,4,8256]{3,2,1,0:T(4,128)S(1)}, f32[2,2,4,8256]{3,2,1,0:T(4,128)S(1)}, u32[]{:S(2)}, u32[]{:S(2)}) collective-permute-start(f32[2,2,4,8256]{3,2,1,0:T(4,128)S(1)} %bitcast.230), channel_id=1, source_target_pairs={{0,2},{1,3},{2,0},{3,1},{4,6},{5,7},{6,4},{7,5},{8,10},{9,11},{10,... | collective-permute-start | bytes 1585160 | tf_op jit(solution)/shard_map/ppermute | solution.py:228
  117.6 1.4 collective-permute-start.18
  119.1 12.7 %collective-permute-start.19 = (f32[64,512]{1,0:T(8,128)S(1)}, f32[64,512]{1,0:T(8,128)S(1)}, u32[]{:S(2)}, u32[]{:S(2)}) collective-permute-start(f32[64,512]{1,0:T(8,128)S(1)} %add.285), channel_id=1, source_target_pairs={{0,2},{1,3},{2,0},{3,1},{4,6},{5,7},{6,4},{7,5},{8,10},{9,11},{10,... | collective-permute-start | bytes 393224 | tf_op jit(solution)/shard_map/ppermute | solution.py:215
  132.2 7.7 %collective-permute-start.16 = (f32[2,4,8256]{2,1,0:T(4,128)S(1)}, f32[2,4,8256]{2,1,0:T(4,128)S(1)}, u32[]{:S(2)}, u32[]{:S(2)}) collective-permute-start(f32[2,4,8256]{2,1,0:T(4,128)S(1)} %dynamic-slice_bitcast_fusion), channel_id=1, source_target_pairs={{0,4},{4,0},{8,12},{12,8},{1,5},{5,1},{9,13},{13,9},{2,6},{6,2},{1... | collective-permute-start | bytes 792584 | tf_op jit(solution)/shard_map/ppermute | solution.py:228
  140.0 7.6 %collective-permute-start.17 = (f32[4,8256]{1,0:T(4,128)S(1)}, f32[4,8256]{1,0:T(4,128)S(1)}, u32[]{:S(2)}, u32[]{:S(2)}) collective-permute-start(f32[4,8256]{1,0:T(4,128)S(1)} %dynamic-slice_bitcast_fusion.2), channel_id=1, source_target_pairs={{0,8},{4,12},{8,0},{12,4},{1,9},{5,13},{9,1},{13,5},{2,10},{6,14},... | collective-permute-start | bytes 396296 | tf_op jit(solution)/shard_map/ppermute | solution.py:228
  158.7 8.6 %collective-permute-start.20 = (f32[2,16,2048]{2,1,0:T(8,128)S(1)}, f32[2,16,2048]{2,1,0:T(8,128)S(1)}, u32[]{:S(2)}, u32[]{:S(2)}) collective-permute-start(f32[2,16,2048]{2,1,0:T(8,128)S(1)} %dynamic-slice_bitcast_fusion.1), channel_id=1, source_target_pairs={{0,4},{4,0},{8,12},{12,8},{1,5},{5,1},{9,13},{13,9},{2,6},{6,2},{1... | collective-permute-start | bytes 786440 | tf_op jit(solution)/shard_map/ppermute | solution.py:228
  167.4 8.7 %collective-permute-start.21 = (f32[16,2048]{1,0:T(8,128)S(1)}, f32[16,2048]{1,0:T(8,128)S(1)}, u32[]{:S(2)}, u32[]{:S(2)}) collective-permute-start(f32[16,2048]{1,0:T(8,128)S(1)} %dynamic-slice_bitcast_fusion.3), channel_id=1, source_target_pairs={{0,8},{4,12},{8,0},{12,4},{1,9},{5,13},{9,1},{13,5},{2,10},{6,14},... | collective-permute-start | bytes 393224 | tf_op jit(solution)/shard_map/ppermute | solution.py:228

commit v18 on v17

--- a/solution.py
+++ b/solution.py
@@ -255,6 +255,17 @@
     x = x.reshape((2,) * bits + (x.shape[0] // n,) + x.shape[1:])
     x = jnp.transpose(x, tuple(range(bits - 1, -1, -1)) + tuple(range(bits, x.ndim)))
     return bit_scatter(x, axis)
+
+
+def direct_scatter(x, axis):
+    n = lax.axis_size(axis)
+    idx = lax.axis_index(axis)
+    blocks = x.reshape((n, x.shape[0] // n) + x.shape[1:])
+    total = lax.dynamic_index_in_dim(blocks, idx, 0, keepdims=False)
+    for k in range(1, n):
+        piece = lax.dynamic_index_in_dim(blocks, (idx + k) % n, 0, keepdims=False)
+        total = total + lax.ppermute(piece, axis, perm=[(i, (i + k) % n) for i in range(n)])
+    return total
 
 
 def axis_sum(x, axis):
@@ -434,7 +445,7 @@
             .reshape(tok_count, local_heads * HD)
             .astype(jnp.bfloat16)
         )
-    result = scatter_rows(jnp.dot(attended, w_out, preferred_element_type=jnp.float32), "tensor")
+    result = direct_scatter(jnp.dot(attended, w_out, preferred_element_type=jnp.float32), "tensor")
     return result.astype(jnp.bfloat16)
 
 

time: 177 us -> 173 us (0.977)
  waiting for transfers between devices: 58.2 us -> 51.7 us
  starting transfers between devices: 22.8 us -> 25.1 us
    ppermute x8 -> x6, waiting for transfers between devices: 35.1 us -> 19.4 us  [bit_scatter(): block = keep + lax.ppermute(send, axis, perm=[(i, i ^ d) for i in range(n)])]
    ppermute x0 -> x3, waiting for transfers between devices: none -> 9.28 us  [direct_scatter(): lax.ppermute(piece, axis, perm=[(i, (i + k) % n) for i in range(n)])]
    ppermute x0 -> x3, starting transfers between devices: none -> 3.87 us  [direct_scatter(): lax.ppermute(piece, axis, perm=[(i, (i + k) % n) for i in range(n)])]
    ppermute x8 -> x6, starting transfers between devices: 7.1 us -> 5.48 us  [bit_scatter(): block = keep + lax.ppermute(send, axis, perm=[(i, i ^ d) for i in range(n)])]
  transfers between devices with their start and end apart: 22 -> 23, of which waited for: 12 -> 12; matrix products, arithmetic and copies ran while one was open for 10% -> 10% of each run, Pallas kernels for 7% -> 8%
where the time goes in v18:
time: 173 us
  waiting for transfers between devices  51.7 us (30%)
  Pallas kernels  47.5 us (27%)
  starting transfers between devices  25.1 us (15%)
  local copies, waits for them, and re-layouts  13.7 us (8%)
  other arithmetic  13.6 us (8%)
  matrix products  13.2 us (8%)
  blocking collectives  5.79 us (3%)
  between operations  1.99 us (1%)
    pallas_call x2, Pallas kernels, hist_attend(): pl.pallas_call(kernel, grid_spec=grid_spec, out_shape=[jax.ShapeDtypeStru...  47.5 us
    ppermute x6, waiting for transfers between devices, bit_scatter(): block = keep + lax.ppermute(send, axis, perm=[(i, i ^ d) for i in range(n)])  19.4 us
    ppermute x2, waiting for transfers between devices, axis_reduce(): x = op(x, lax.ppermute(x, axis, perm=[(i, i ^ d) for i in range(n)]))  12.5 us
    ppermute x6, waiting for transfers between devices, bit_gather(): other = lax.ppermute(x, axis, perm=[(i, i ^ d) for i in range(n)])  9.28 us
    ppermute x3, waiting for transfers between devices, direct_scatter(): lax.ppermute(piece, axis, perm=[(i, (i + k) % n) for i in range(n)])  9.28 us
    ppermute x6, starting transfers between devices, axis_max(): lax.ppermute(x, a, perm=[(i, (i + k) % n) for i in range(n)])  7.66 us
    ppermute x6, starting transfers between devices, bit_gather(): other = lax.ppermute(x, axis, perm=[(i, i ^ d) for i in range(n)])  6.6 us
    pallas_call x4, local copies, waits for them, and re-layouts, hist_attend(): pl.pallas_call(kernel, grid_spec=grid_spec, out_shape=[jax.ShapeDtypeStru...  6.49 us
  transfers between devices with their start and end apart: 23, of which 12 were waited for; matrix products, arithmetic and copies ran while one was open for 10% of the time, Pallas kernels for 8%

profile of v18, /device:TPU:0, one launch (start us, length us, event | category | flops | bytes accessed | tf_op | source)
XLA Modules:
  0.0 172.6 jit_solution(5924021021901209739)
XLA Ops:
  0.0 0.9 copy-done
  1.0 4.9 %convolution_bitcast_fusion = f32[8,8,16,128]{3,1,2,0:T(8,128)S(1)} fusion(bf16[64,2048]{1,0:T(8,128)(2,1)S(1)} %copy-done, bf16[2048,2048]{1,0:T(8,128)(2,1)} %param.10), kind=kOutput, calls=%fused_computation.15 | convolution fusion | flops 536870912 | bytes 9175040 | tf_op jit(solution)/shard_map/dot_general | solution.py:307
  6.0 0.1 constant_dynamic-slice_fusion.5
  6.2 0.5 collective-permute-start
  7.4 1.2 reduce-window.6
  8.7 0.1 copy.60
  9.1 0.2 fusion.34
  9.3 0.2 multiply_cosine_fusion
  9.6 2.6 %collective-permute-start.1 = (f32[4,64,128]{2,1,0:T(8,128)S(1)}, f32[4,64,128]{2,1,0:T(8,128)S(1)}, u32[]{:S(2)}, u32[]{:S(2)}) collective-permute-start(f32[4,64,128]{2,1,0:T(8,128)S(1)} %dynamic-slice_bitcast_fusion.5), channel_id=1, source_target_pairs={{0,2},{1,3},{2,0},{3,1},{4,6},{5,7},{6,4},{7,5},{8,10},{9,11},{10,... | collective-permute-start | bytes 393224 | tf_op jit(solution)/shard_map/ppermute | solution.py:228
  12.2 4.2 %collective-permute-done.1 = f32[4,64,128]{2,1,0:T(8,128)S(1)} collective-permute-done((f32[4,64,128]{2,1,0:T(8,128)S(1)}, f32[4,64,128]{2,1,0:T(8,128)S(1)}, u32[]{:S(2)}, u32[]{:S(2)}) %collective-permute-start.1) | collective-permute-done | bytes 131104 | tf_op jit(solution)/shard_map/ppermute | solution.py:228
  16.4 0.1 subtract_convert_fusion
  16.6 1.8 %collective-permute-start.2 = (bf16[4,64,128]{2,1,0:T(8,128)(2,1)S(1)}, bf16[4,64,128]{2,1,0:T(8,128)(2,1)S(1)}, u32[]{:S(2)}, u32[]{:S(2)}) collective-permute-start(bf16[4,64,128]{2,1,0:T(8,128)(2,1)S(1)} %pad_maximum_fusion.4), channel_id=1, source_target_pairs={{0,2},{1,3},{2,0},{3,1},{4,6},{5,7},{6,4},{7,5},{8,10},{9,11},{10,... | collective-permute-start | bytes 196616 | tf_op jit(solution)/shard_map/ppermute | solution.py:239
  18.4 2.6 %collective-permute-start.4 = (bf16[4,64,128]{2,1,0:T(8,128)(2,1)S(1)}, bf16[4,64,128]{2,1,0:T(8,128)(2,1)S(1)}, u32[]{:S(2)}, u32[]{:S(2)}) collective-permute-start(bf16[4,64,128]{2,1,0:T(8,128)(2,1)S(1)} %pad_maximum_fusion.4), channel_id=1, source_target_pairs={{0,8},{4,12},{8,0},{12,4},{1,9},{5,13},{9,1},{13,5},{2,10},{6,14},... | collective-permute-start | bytes 196616 | tf_op jit(solution)/shard_map/ppermute | solution.py:239
  21.0 0.7 fusion.38
  22.4 1.4 collective-permute-done.4
  23.8 0.1 select_bitcast_fusion.9
  23.9 1.5 collective-permute-start.5
  25.5 3.4 %collective-permute-done.5 = bf16[2,4,64,128]{3,2,1,0:T(8,128)(2,1)S(1)} collective-permute-done((bf16[2,4,64,128]{3,2,1,0:T(8,128)(2,1)S(1)}, bf16[2,4,64,128]{3,2,1,0:T(8,128)(2,1)S(1)}, u32[]{:S(2)}, u32[]{:S(2)}) %collective-permute-start.5) | collective-permute-done | bytes 131104 | tf_op jit(solution)/shard_map/ppermute | solution.py:239
  29.0 0.6 collective-permute-start.6
  29.6 0.6 maximum_bitcast_fusion.2.cos_ref
  30.3 0.7 maximum_bitcast_fusion.3.sin_ref
  31.0 4.4 %collective-permute-done.6 = bf16[16,64,128]{2,1,0:T(8,128)(2,1)S(1)} collective-permute-done((bf16[16,64,128]{2,1,0:T(8,128)(2,1)S(1)}, bf16[16,64,128]{2,1,0:T(8,128)(2,1)S(1)}, u32[]{:S(2)}, u32[]{:S(2)}) %collective-permute-start.6) | collective-permute-done | bytes 262176 | tf_op jit(solution)/shard_map/ppermute | solution.py:239
  35.7 0.7 copy.59
  36.5 13.2 %shard_map.85 = (f32[2,512,128]{2,1,0:T(8,128)}, f32[2,512,1]{2,1,0:T(8,128)}, f32[2,512,1]{2,1,0:T(8,128)}) custom-call(s32[1]{0:T(128)} %bitcast.kv0_ref, bf16[2,512,128]{2,1,0:T(8,128)(2,1)} %bitcast.230, bf16[40,128,2048]{2,1,0:T(8,128)(2,1)} %bitcast.221, bf16[40,128,2048]{2,1,0:T(8,128)(2,1)} %bitcast.222, f32[1,1,5120]{2,1,0:T(1,128)} %bitcast.239, ...), custom_call_target="tpu_custom_call" | custom-call | flops 2684354560 | bytes 6029312 | tf_op jit(solution)/shard_map/pallas_call | solution.py:194
  49.6 1.2 copy.65
  50.9 1.2 copy.69
  52.2 0.1 maximum_bitcast_fusion
  52.5 1.2 fusion.20.q_ref
  53.7 34.3 %shard_map.86 = (f32[6,512,128]{2,1,0:T(8,128)}, f32[6,512,1]{2,1,0:T(8,128)}, f32[6,512,1]{2,1,0:T(8,128)}) custom-call(s32[1]{0:T(128)} %bitcast.26.kv0_ref, bf16[6,512,128]{2,1,0:T(8,128)(2,1)} %fusion.20.q_ref, bf16[40,128,2048]{2,1,0:T(8,128)(2,1)} %bitcast.223, bf16[40,128,2048]{2,1,0:T(8,128)(2,1)} %bitcast.224, f32[1,1,5120]{2,1,0:T(1,128)} %bitcast.240, ...), custom_call_target="tpu_custom_call" | custom-call | flops 8053063680 | bytes 18087936 | tf_op jit(solution)/shard_map/pallas_call | solution.py:194
  88.0 2.0 %copy.66 = f32[6,512,1]{1,0,2:T(8,128)S(1)} copy(f32[6,512,1]{2,1,0:T(8,128)} %get-tuple-element.14) | data formatting | bytes 24576 | tf_op jit(solution)/shard_map/pallas_call | solution.py:194
  90.2 0.6 collective-permute-start.10
  90.8 1.5 collective-permute-start.9
  92.3 1.9 %fusion.2 = f32[8,512,128]{2,1,0:T(8,128)S(1)} fusion(s32[]{:T(128)S(6)} %select_n.367, f32[2,512,128]{2,1,0:T(8,128)S(1)} %copy-done.1, f32[6,512,128]{2,1,0:T(8,128)} %get-tuple-element.12), kind=kLoop, calls=%fused_computation.8 | loop fusion | flops 1572864 | bytes 4194308 | tf_op jit(solution)/shard_map/concatenate | solution.py:368
  94.3 2.0 %copy.70 = f32[6,512,1]{1,0,2:T(8,128)S(1)} copy(f32[6,512,1]{2,1,0:T(8,128)} %get-tuple-element.16) | data formatting | bytes 24576 | tf_op jit(solution)/shard_map/pallas_call | solution.py:194
  96.3 1.4 collective-permute-start.11
  97.8 3.3 %collective-permute-start.12 = (f32[64,64]{1,0:T(8,128)S(1)}, f32[64,64]{1,0:T(8,128)S(1)}, u32[]{:S(2)}, u32[]{:S(2)}) collective-permute-start(f32[64,64]{1,0:T(8,128)S(1)} %maximum_maximum_fusion.1), channel_id=1, source_target_pairs={{0,8},{4,12},{8,0},{12,4},{1,9},{5,13},{9,1},{13,5},{2,10},{6,14},... | collective-permute-start | bytes 49160 | tf_op jit(solution)/shard_map/ppermute | solution.py:283
  101.1 0.8 collective-permute-start.13
  101.9 1.8 %reshape.438 = f32[2,2,2,2,4,8192]{5,4,3,2,1,0:T(4,128)} reshape(f32[8,512,128]{2,1,0:T(8,128)S(1)} %fusion.2) | data formatting | bytes 4194304 | tf_op jit(solution)/shard_map/reshape | solution.py:373
  103.7 1.2 collective-permute-done.13
  105.0 0.6 mul.261
  105.6 1.8 %mul.262 = f32[2,2,2,2,4,8192]{5,4,3,2,1,0:T(4,128)} reshape(f32[64,64,128]{2,1,0:T(8,128)S(1)} %mul.261) | data formatting | bytes 4194304 | tf_op jit(solution)/shard_map/mul | solution.py:380
  107.4 2.8 %mul.263 = f32[2,2,2,2,4,8192]{5,4,3,2,1,0:T(4,128)S(1)} multiply(f32[2,2,2,2,4,8192]{5,4,3,2,1,0:T(4,128)} %reshape.438, f32[2,2,2,2,4,8192]{5,4,3,2,1,0:T(4,128)} %mul.262) | non-fusion elementwise | flops 524288 | bytes 6291456 | tf_op jit(solution)/shard_map/mul | solution.py:380
  110.2 1.3 fusion.16
  111.4 2.9 %collective-permute-done.14 = f32[2,2,2,4,8256]{4,3,0,1,2:T(4,128)S(1)} collective-permute-done((f32[2,2,2,4,8256]{4,3,0,1,2:T(4,128)}, f32[2,2,2,4,8256]{4,3,0,1,2:T(4,128)S(1)}, u32[]{:S(2)}, u32[]{:S(2)}) %collective-permute-start.14) | collective-permute-done | bytes 1056800 | tf_op jit(solution)/shard_map/ppermute | solution.py:228
  114.3 0.4 fusion.19
  114.8 0.8 collective-permute-start.15
  115.6 2.1 %fusion.5 = f32[64,512]{1,0:T(8,128)S(1)} fusion(bf16[64,2048]{1,0:T(8,128)(2,1)S(1)} %copy-done, bf16[2048,2048]{1,0:T(8,128)(2,1)} %param.11, s32[]{:T(128)S(6)} %select_n.373), kind=kOutput, calls=%fused_computation.16 | convolution fusion | flops 134217728 | bytes 2490372 | tf_op jit(solution)/shard_map/dot_general | solution.py:308
  117.9 1.2 collective-permute-done.18
  119.1 1.4 collective-permute-start.19
  120.6 11.3 %collective-permute-done.19 = f32[64,512]{1,0:T(8,128)S(1)} collective-permute-done((f32[64,512]{1,0:T(8,128)S(1)}, f32[64,512]{1,0:T(8,128)S(1)}, u32[]{:S(2)}, u32[]{:S(2)}) %collective-permute-start.19) | collective-permute-done | bytes 131104 | tf_op jit(solution)/shard_map/ppermute | solution.py:215
  132.1 0.1 bitcast_add_fusion
  132.2 0.2 collective-permute-start.16
  132.6 7.3 %collective-permute-done.16 = f32[2,4,8256]{2,1,0:T(4,128)S(1)} collective-permute-done((f32[2,4,8256]{2,1,0:T(4,128)S(1)}, f32[2,4,8256]{2,1,0:T(4,128)S(1)}, u32[]{:S(2)}, u32[]{:S(2)}) %collective-permute-start.16) | collective-permute-done | bytes 264224 | tf_op jit(solution)/shard_map/ppermute | solution.py:228
  140.0 1.5 collective-permute-start.17
  141.5 1.1 fusion.69
  142.6 5.0 %collective-permute-done.17 = f32[4,8256]{1,0:T(4,128)S(1)} collective-permute-done((f32[4,8256]{1,0:T(4,128)S(1)}, f32[4,8256]{1,0:T(4,128)S(1)}, u32[]{:S(2)}, u32[]{:S(2)}) %collective-permute-start.17) | collective-permute-done | bytes 132128 | tf_op jit(solution)/shard_map/ppermute | solution.py:228
  147.7 0.2 fusion.14
  148.0 5.8 %all_gather.3 = bf16[64,2048]{1,0:T(8,128)(2,1)S(1)} all-gather(bf16[64,512]{1,0:T(8,128)(2,1)S(1)} %bitcast.237), channel_id=1, replica_groups=mesh['groups'=2,'tensor'=4,'store'=4] {'store'}, dimensions={1}, use_global_device_ids=true | all-gather | bytes 327680 | tf_op jit(solution)/shard_map/all_gather | solution.py:422
  153.7 5.0 %fusion.70 = f32[64,2048]{1,0:T(8,128)S(1)} fusion(bf16[64,2048]{1,0:T(8,128)(2,1)S(1)} %all_gather.3, bf16[2048,2048]{1,0:T(8,128)(2,1)} %param.12), kind=kOutput, calls=%fused_computation.172 | convolution fusion | flops 536870912 | bytes 9175040 | tf_op jit(solution)/shard_map/dot_general | solution.py:448
  158.8 3.2 %collective-permute-start.21 = (f32[16,2048]{1,0:T(8,128)S(1)}, f32[16,2048]{1,0:T(8,128)S(1)}, u32[]{:S(2)}, u32[]{:S(2)}) collective-permute-start(f32[16,2048]{1,0:T(8,128)S(1)} %get-tuple-element.31), channel_id=1, source_target_pairs={{0,8},{4,12},{8,0},{12,4},{1,9},{5,13},{9,1},{13,5},{2,10},{6,14},... | collective-permute-start | bytes 393224 | tf_op jit(solution)/shard_map/ppermute | solution.py:267
  162.0 0.6 collective-permute-start.22
  162.6 4.4 %collective-permute-done.20 = f32[16,2048]{1,0:T(8,128)S(1)} collective-permute-done((f32[16,2048]{1,0:T(8,128)S(1)}, f32[16,2048]{1,0:T(8,128)S(1)}, u32[]{:S(2)}, u32[]{:S(2)}) %collective-permute-start.20) | collective-permute-done | bytes 131104 | tf_op jit(solution)/shard_map/ppermute | solution.py:267
  167.0 4.9 %collective-permute-done.21 = f32[16,2048]{1,0:T(8,128)S(1)} collective-permute-done((f32[16,2048]{1,0:T(8,128)S(1)}, f32[16,2048]{1,0:T(8,128)S(1)}, u32[]{:S(2)}, u32[]{:S(2)}) %collective-permute-start.21) | collective-permute-done | bytes 131104 | tf_op jit(solution)/shard_map/ppermute | solution.py:267
  171.9 0.7 fusion.24
  (81 shorter events, 2.7 us)
Async XLA Ops:
  0.0 1.0 copy-start
  5.9 1.5 copy-start.2
  6.2 3.3 %collective-permute-start = (f32[2,4,64,128]{3,2,1,0:T(8,128)S(1)}, f32[2,4,64,128]{3,2,1,0:T(8,128)S(1)}, u32[]{:S(2)}, u32[]{:S(2)}) collective-permute-start(f32[2,4,64,128]{3,2,1,0:T(8,128)S(1)} %bitcast.238), channel_id=1, source_target_pairs={{0,1},{1,0},{2,3},{3,2},{4,5},{5,4},{6,7},{7,6},{8,9},{9,8},{10,11... | collective-permute-start | bytes 786440 | tf_op jit(solution)/shard_map/ppermute | solution.py:228
  9.6 6.7 %collective-permute-start.1 = (f32[4,64,128]{2,1,0:T(8,128)S(1)}, f32[4,64,128]{2,1,0:T(8,128)S(1)}, u32[]{:S(2)}, u32[]{:S(2)}) collective-permute-start(f32[4,64,128]{2,1,0:T(8,128)S(1)} %dynamic-slice_bitcast_fusion.5), channel_id=1, source_target_pairs={{0,2},{1,3},{2,0},{3,1},{4,6},{5,7},{6,4},{7,5},{8,10},{9,11},{10,... | collective-permute-start | bytes 393224 | tf_op jit(solution)/shard_map/ppermute | solution.py:228
  16.6 5.7 %collective-permute-start.2 = (bf16[4,64,128]{2,1,0:T(8,128)(2,1)S(1)}, bf16[4,64,128]{2,1,0:T(8,128)(2,1)S(1)}, u32[]{:S(2)}, u32[]{:S(2)}) collective-permute-start(bf16[4,64,128]{2,1,0:T(8,128)(2,1)S(1)} %pad_maximum_fusion.4), channel_id=1, source_target_pairs={{0,2},{1,3},{2,0},{3,1},{4,6},{5,7},{6,4},{7,5},{8,10},{9,11},{10,... | collective-permute-start | bytes 196616 | tf_op jit(solution)/shard_map/ppermute | solution.py:239
  18.4 5.3 %collective-permute-start.4 = (bf16[4,64,128]{2,1,0:T(8,128)(2,1)S(1)}, bf16[4,64,128]{2,1,0:T(8,128)(2,1)S(1)}, u32[]{:S(2)}, u32[]{:S(2)}) collective-permute-start(bf16[4,64,128]{2,1,0:T(8,128)(2,1)S(1)} %pad_maximum_fusion.4), channel_id=1, source_target_pairs={{0,8},{4,12},{8,0},{12,4},{1,9},{5,13},{9,1},{13,5},{2,10},{6,14},... | collective-permute-start | bytes 196616 | tf_op jit(solution)/shard_map/ppermute | solution.py:239
  23.9 5.0 %collective-permute-start.5 = (bf16[2,4,64,128]{3,2,1,0:T(8,128)(2,1)S(1)}, bf16[2,4,64,128]{3,2,1,0:T(8,128)(2,1)S(1)}, u32[]{:S(2)}, u32[]{:S(2)}) collective-permute-start(bf16[2,4,64,128]{3,2,1,0:T(8,128)(2,1)S(1)} %pad_maximum_fusion.3), channel_id=1, source_target_pairs={{0,4},{4,0},{8,12},{12,8},{1,5},{5,1},{9,13},{13,9},{2,6},{6,2},{1... | collective-permute-start | bytes 393224 | tf_op jit(solution)/shard_map/ppermute | solution.py:239
  29.0 6.4 %collective-permute-start.6 = (bf16[16,64,128]{2,1,0:T(8,128)(2,1)S(1)}, bf16[16,64,128]{2,1,0:T(8,128)(2,1)S(1)}, u32[]{:S(2)}, u32[]{:S(2)}) collective-permute-start(bf16[16,64,128]{2,1,0:T(8,128)(2,1)S(1)} %bitcast.232), channel_id=1, source_target_pairs={{0,2},{1,3},{2,0},{3,1},{4,6},{5,7},{6,4},{7,5},{8,10},{9,11},{10,... | collective-permute-start | bytes 786440 | tf_op jit(solution)/shard_map/ppermute | solution.py:239
  30.9 4.7 %collective-permute-start.3 = (bf16[2,4,64,128]{3,2,1,0:T(8,128)(2,1)S(1)}, bf16[2,4,64,128]{3,2,1,0:T(8,128)(2,1)S(1)}, u32[]{:S(2)}, u32[]{:S(2)}) collective-permute-start(bf16[2,4,64,128]{3,2,1,0:T(8,128)(2,1)S(1)} %pad_maximum_fusion.2), channel_id=1, source_target_pairs={{0,1},{1,0},{2,3},{3,2},{4,5},{5,4},{6,7},{7,6},{8,9},{9,8},{10,11... | collective-permute-start | bytes 393224 | tf_op jit(solution)/shard_map/ppermute | solution.py:239
  35.6 16.5 %collective-permute-start.7 = (bf16[2,16,64,128]{3,2,1,0:T(8,128)(2,1)S(1)}, bf16[2,16,64,128]{3,2,1,0:T(8,128)(2,1)S(1)}, u32[]{:S(2)}, u32[]{:S(2)}) collective-permute-start(bf16[2,16,64,128]{3,2,1,0:T(8,128)(2,1)S(1)} %pad_maximum_fusion), channel_id=1, source_target_pairs={{0,1},{1,0},{2,3},{3,2},{4,5},{5,4},{6,7},{7,6},{8,9},{9,8},{10,11... | collective-permute-start | bytes 1572872 | tf_op jit(solution)/shard_map/ppermute | solution.py:239
  53.7 38.6 %copy-start.1 = (f32[2,512,128]{2,1,0:T(8,128)S(1)}, f32[2,512,128]{2,1,0:T(8,128)}, u32[]{:S(2)}) copy-start(f32[2,512,128]{2,1,0:T(8,128)} %get-tuple-element.11) | copy-start | bytes 1572868
  90.2 6.1 %collective-permute-start.10 = (f32[64,64]{1,0:T(8,128)S(1)}, f32[64,64]{1,0:T(8,128)S(1)}, u32[]{:S(2)}, u32[]{:S(2)}) collective-permute-start(f32[64,64]{1,0:T(8,128)S(1)} %reshape.439), channel_id=1, source_target_pairs={{0,3},{1,0},{2,1},{3,2},{4,7},{5,4},{6,5},{7,6},{8,11},{9,8},{10,9... | collective-permute-start | bytes 49160 | tf_op jit(solution)/shard_map/ppermute | solution.py:283
  90.8 5.5 %collective-permute-start.8 = (f32[64,64]{1,0:T(8,128)S(1)}, f32[64,64]{1,0:T(8,128)S(1)}, u32[]{:S(2)}, u32[]{:S(2)}) collective-permute-start(f32[64,64]{1,0:T(8,128)S(1)} %reshape.439), channel_id=1, source_target_pairs={{0,1},{1,2},{2,3},{3,0},{4,5},{5,6},{6,7},{7,4},{8,9},{9,10},{10,1... | collective-permute-start | bytes 49160 | tf_op jit(solution)/shard_map/ppermute | solution.py:283
  90.8 5.5 %collective-permute-start.9 = (f32[64,64]{1,0:T(8,128)S(1)}, f32[64,64]{1,0:T(8,128)S(1)}, u32[]{:S(2)}, u32[]{:S(2)}) collective-permute-start(f32[64,64]{1,0:T(8,128)S(1)} %reshape.439), channel_id=1, source_target_pairs={{0,2},{1,3},{2,0},{3,1},{4,6},{5,7},{6,4},{7,5},{8,10},{9,11},{10,... | collective-permute-start | bytes 49160 | tf_op jit(solution)/shard_map/ppermute | solution.py:283
  96.3 7.4 %collective-permute-start.11 = (f32[64,64]{1,0:T(8,128)S(1)}, f32[64,64]{1,0:T(8,128)S(1)}, u32[]{:S(2)}, u32[]{:S(2)}) collective-permute-start(f32[64,64]{1,0:T(8,128)S(1)} %maximum_maximum_fusion.1), channel_id=1, source_target_pairs={{0,4},{4,8},{8,12},{12,0},{1,5},{5,9},{9,13},{13,1},{2,6},{6,10},{... | collective-permute-start | bytes 49160 | tf_op jit(solution)/shard_map/ppermute | solution.py:283
  97.8 6.0 %collective-permute-start.12 = (f32[64,64]{1,0:T(8,128)S(1)}, f32[64,64]{1,0:T(8,128)S(1)}, u32[]{:S(2)}, u32[]{:S(2)}) collective-permute-start(f32[64,64]{1,0:T(8,128)S(1)} %maximum_maximum_fusion.1), channel_id=1, source_target_pairs={{0,8},{4,12},{8,0},{12,4},{1,9},{5,13},{9,1},{13,5},{2,10},{6,14},... | collective-permute-start | bytes 49160 | tf_op jit(solution)/shard_map/ppermute | solution.py:283
  101.1 3.9 %collective-permute-start.13 = (f32[64,64]{1,0:T(8,128)S(1)}, f32[64,64]{1,0:T(8,128)S(1)}, u32[]{:S(2)}, u32[]{:S(2)}) collective-permute-start(f32[64,64]{1,0:T(8,128)S(1)} %maximum_maximum_fusion.1), channel_id=1, source_target_pairs={{0,12},{4,0},{8,4},{12,8},{1,13},{5,1},{9,5},{13,9},{2,14},{6,2},{... | collective-permute-start | bytes 49160 | tf_op jit(solution)/shard_map/ppermute | solution.py:283
  111.4 2.9 %collective-permute-start.14 = (f32[2,2,2,4,8256]{4,3,0,1,2:T(4,128)}, f32[2,2,2,4,8256]{4,3,0,1,2:T(4,128)S(1)}, u32[]{:S(2)}, u32[]{:S(2)}) collective-permute-start(f32[2,2,2,4,8256]{4,3,0,1,2:T(4,128)} %fusion.16), channel_id=1, source_target_pairs={{0,1},{1,0},{2,3},{3,2},{4,5},{5,4},{6,7},{7,6},{8,9},{9,8},{10,11... | collective-permute-start | bytes 3170312 | tf_op jit(solution)/shard_map/ppermute | solution.py:228
  114.8 17.2 %collective-permute-start.15 = (f32[2,2,4,8256]{3,2,1,0:T(4,128)S(1)}, f32[2,2,4,8256]{3,2,1,0:T(4,128)S(1)}, u32[]{:S(2)}, u32[]{:S(2)}) collective-permute-start(f32[2,2,4,8256]{3,2,1,0:T(4,128)S(1)} %bitcast.234), channel_id=1, source_target_pairs={{0,2},{1,3},{2,0},{3,1},{4,6},{5,7},{6,4},{7,5},{8,10},{9,11},{10,... | collective-permute-start | bytes 1585160 | tf_op jit(solution)/shard_map/ppermute | solution.py:228
  117.7 1.4 collective-permute-start.18
  119.1 12.7 %collective-permute-start.19 = (f32[64,512]{1,0:T(8,128)S(1)}, f32[64,512]{1,0:T(8,128)S(1)}, u32[]{:S(2)}, u32[]{:S(2)}) collective-permute-start(f32[64,512]{1,0:T(8,128)S(1)} %add.311), channel_id=1, source_target_pairs={{0,2},{1,3},{2,0},{3,1},{4,6},{5,7},{6,4},{7,5},{8,10},{9,11},{10,... | collective-permute-start | bytes 393224 | tf_op jit(solution)/shard_map/ppermute | solution.py:215
  132.2 7.7 %collective-permute-start.16 = (f32[2,4,8256]{2,1,0:T(4,128)S(1)}, f32[2,4,8256]{2,1,0:T(4,128)S(1)}, u32[]{:S(2)}, u32[]{:S(2)}) collective-permute-start(f32[2,4,8256]{2,1,0:T(4,128)S(1)} %dynamic-slice_bitcast_fusion), channel_id=1, source_target_pairs={{0,4},{4,0},{8,12},{12,8},{1,5},{5,1},{9,13},{13,9},{2,6},{6,2},{1... | collective-permute-start | bytes 792584 | tf_op jit(solution)/shard_map/ppermute | solution.py:228
  140.0 7.6 %collective-permute-start.17 = (f32[4,8256]{1,0:T(4,128)S(1)}, f32[4,8256]{1,0:T(4,128)S(1)}, u32[]{:S(2)}, u32[]{:S(2)}) collective-permute-start(f32[4,8256]{1,0:T(4,128)S(1)} %dynamic-slice_bitcast_fusion.1), channel_id=1, source_target_pairs={{0,8},{4,12},{8,0},{12,4},{1,9},{5,13},{9,1},{13,5},{2,10},{6,14},... | collective-permute-start | bytes 396296 | tf_op jit(solution)/shard_map/ppermute | solution.py:228
  158.8 8.3 %collective-permute-start.20 = (f32[16,2048]{1,0:T(8,128)S(1)}, f32[16,2048]{1,0:T(8,128)S(1)}, u32[]{:S(2)}, u32[]{:S(2)}) collective-permute-start(f32[16,2048]{1,0:T(8,128)S(1)} %get-tuple-element.29), channel_id=1, source_target_pairs={{0,4},{4,8},{8,12},{12,0},{1,5},{5,9},{9,13},{13,1},{2,6},{6,10},{... | collective-permute-start | bytes 393224 | tf_op jit(solution)/shard_map/ppermute | solution.py:267
  158.8 13.1 %collective-permute-start.21 = (f32[16,2048]{1,0:T(8,128)S(1)}, f32[16,2048]{1,0:T(8,128)S(1)}, u32[]{:S(2)}, u32[]{:S(2)}) collective-permute-start(f32[16,2048]{1,0:T(8,128)S(1)} %get-tuple-element.31), channel_id=1, source_target_pairs={{0,8},{4,12},{8,0},{12,4},{1,9},{5,13},{9,1},{13,5},{2,10},{6,14},... | collective-permute-start | bytes 393224 | tf_op jit(solution)/shard_map/ppermute | solution.py:267
  162.0 9.9 %collective-permute-start.22 = (f32[16,2048]{1,0:T(8,128)S(1)}, f32[16,2048]{1,0:T(8,128)S(1)}, u32[]{:S(2)}, u32[]{:S(2)}) collective-permute-start(f32[16,2048]{1,0:T(8,128)S(1)} %get-tuple-element.30), channel_id=1, source_target_pairs={{0,12},{4,0},{8,4},{12,8},{1,13},{5,1},{9,5},{13,9},{2,14},{6,2},{... | collective-permute-start | bytes 393224 | tf_op jit(solution)/shard_map/ppermute | solution.py:267

commit v19 on v18

--- a/solution.py
+++ b/solution.py
@@ -391,10 +391,10 @@
         s_bits = shards.bit_length() - 1
         t_bits = tensors.bit_length() - 1
         block = packed.reshape((2,) * t_bits + (2,) * s_bits + (chunk_heads, width))
-        order = tuple(range(t_bits + s_bits - 1, t_bits - 1, -1)) + tuple(range(t_bits - 1, -1, -1))
+        order = tuple(range(t_bits + s_bits - 1, t_bits - 1, -1)) + tuple(range(t_bits))
         block = jnp.transpose(block, order + (t_bits + s_bits, t_bits + s_bits + 1))
         block = bit_scatter(block, "store")
-        block = bit_scatter(block, "tensor")
+        block = direct_scatter(block.reshape(tensors * chunk_heads, width), "tensor")
         acc = block[:, : tok_count * HD].reshape(chunk_heads, tok_count, HD)
         total = block[:, tok_count * HD :]
         chunk_first = (tensor_idx * shards + store_idx) * chunk_heads

time: 173 us -> 173 us (level)
  waiting for transfers between devices: 51.7 us -> 44.6 us
  starting transfers between devices: 25.1 us -> 29.1 us
  other arithmetic: 13.6 us -> 15.8 us
    ppermute x2, waiting for transfers between devices: 12.5 us -> 3.58 us  [axis_reduce(): x = op(x, lax.ppermute(x, axis, perm=[(i, i ^ d) for i in range(n)]))]
    ppermute x3 -> x6, waiting for transfers between devices: 9.28 us -> 15.8 us  [direct_scatter(): lax.ppermute(piece, axis, perm=[(i, (i + k) % n) for i in range(n)])]
    ppermute x3 -> x6, starting transfers between devices: 3.87 us -> 9.05 us  [direct_scatter(): lax.ppermute(piece, axis, perm=[(i, (i + k) % n) for i in range(n)])]
    ppermute x6 -> x4, waiting for transfers between devices: 19.4 us -> 14.6 us  [bit_scatter(): block = keep + lax.ppermute(send, axis, perm=[(i, i ^ d) for i in range(n)])]
    ppermute x6 -> x4, starting transfers between devices: 5.48 us -> 4.54 us  [bit_scatter(): block = keep + lax.ppermute(send, axis, perm=[(i, i ^ d) for i in range(n)])]
  transfers between devices with their start and end apart: 23 -> 24, of which waited for: 12 -> 12; matrix products, arithmetic and copies ran while one was open for 10% -> 11% of each run, Pallas kernels for 8% -> 8%
where the time goes in v19:
time: 173 us; the launch traced here: 172 us
  Pallas kernels  47.6 us (28%)
  waiting for transfers between devices  44.6 us (26%)
  starting transfers between devices  29.1 us (17%)
  other arithmetic  15.8 us (9%)
  local copies, waits for them, and re-layouts  13.6 us (8%)
  matrix products  13.3 us (8%)
  blocking collectives  5.79 us (3%)
  between operations  1.93 us (1%)
    pallas_call x2, Pallas kernels, hist_attend(): pl.pallas_call(kernel, grid_spec=grid_spec, out_shape=[jax.ShapeDtypeStru...  47.6 us
    ppermute x6, waiting for transfers between devices, direct_scatter(): lax.ppermute(piece, axis, perm=[(i, (i + k) % n) for i in range(n)])  15.8 us
    ppermute x4, waiting for transfers between devices, bit_scatter(): block = keep + lax.ppermute(send, axis, perm=[(i, i ^ d) for i in range(n)])  14.6 us
    ppermute x6, waiting for transfers between devices, bit_gather(): other = lax.ppermute(x, axis, perm=[(i, i ^ d) for i in range(n)])  9.39 us
    ppermute x6, starting transfers between devices, direct_scatter(): lax.ppermute(piece, axis, perm=[(i, (i + k) % n) for i in range(n)])  9.05 us
    ppermute x6, starting transfers between devices, axis_max(): lax.ppermute(x, a, perm=[(i, (i + k) % n) for i in range(n)])  7.62 us
    ppermute x6, starting transfers between devices, bit_gather(): other = lax.ppermute(x, axis, perm=[(i, i ^ d) for i in range(n)])  6.6 us
    pallas_call x4, local copies, waits for them, and re-layouts, hist_attend(): pl.pallas_call(kernel, grid_spec=grid_spec, out_shape=[jax.ShapeDtypeStru...  6.49 us
  transfers between devices with their start and end apart: 24, of which 12 were waited for; matrix products, arithmetic and copies ran while one was open for 11% of the time, Pallas kernels for 8%

profile of v19, /device:TPU:0, one launch (start us, length us, event | category | flops | bytes accessed | tf_op | source)
XLA Modules:
  0.0 171.8 jit_solution(6236801979812804073)
XLA Ops:
  0.0 0.9 copy-done
  1.0 4.9 %convolution_bitcast_fusion = f32[8,8,16,128]{3,1,2,0:T(8,128)S(1)} fusion(bf16[64,2048]{1,0:T(8,128)(2,1)S(1)} %copy-done, bf16[2048,2048]{1,0:T(8,128)(2,1)} %param.10), kind=kOutput, calls=%fused_computation.15 | convolution fusion | flops 536870912 | bytes 9175040 | tf_op jit(solution)/shard_map/dot_general | solution.py:307
  6.2 0.5 collective-permute-start
  7.4 1.2 reduce-window.6
  9.1 0.2 fusion.36
  9.3 0.2 multiply_cosine_fusion
  9.7 2.6 %collective-permute-start.1 = (f32[4,64,128]{2,1,0:T(8,128)S(1)}, f32[4,64,128]{2,1,0:T(8,128)S(1)}, u32[]{:S(2)}, u32[]{:S(2)}) collective-permute-start(f32[4,64,128]{2,1,0:T(8,128)S(1)} %dynamic-slice_bitcast_fusion.7), channel_id=1, source_target_pairs={{0,2},{1,3},{2,0},{3,1},{4,6},{5,7},{6,4},{7,5},{8,10},{9,11},{10,... | collective-permute-start | bytes 393224 | tf_op jit(solution)/shard_map/ppermute | solution.py:228
  12.2 4.2 %collective-permute-done.1 = f32[4,64,128]{2,1,0:T(8,128)S(1)} collective-permute-done((f32[4,64,128]{2,1,0:T(8,128)S(1)}, f32[4,64,128]{2,1,0:T(8,128)S(1)}, u32[]{:S(2)}, u32[]{:S(2)}) %collective-permute-start.1) | collective-permute-done | bytes 131104 | tf_op jit(solution)/shard_map/ppermute | solution.py:228
  16.6 1.8 %collective-permute-start.2 = (bf16[4,64,128]{2,1,0:T(8,128)(2,1)S(1)}, bf16[4,64,128]{2,1,0:T(8,128)(2,1)S(1)}, u32[]{:S(2)}, u32[]{:S(2)}) collective-permute-start(bf16[4,64,128]{2,1,0:T(8,128)(2,1)S(1)} %pad_maximum_fusion.4), channel_id=1, source_target_pairs={{0,2},{1,3},{2,0},{3,1},{4,6},{5,7},{6,4},{7,5},{8,10},{9,11},{10,... | collective-permute-start | bytes 196616 | tf_op jit(solution)/shard_map/ppermute | solution.py:239
  18.4 2.6 %collective-permute-start.4 = (bf16[4,64,128]{2,1,0:T(8,128)(2,1)S(1)}, bf16[4,64,128]{2,1,0:T(8,128)(2,1)S(1)}, u32[]{:S(2)}, u32[]{:S(2)}) collective-permute-start(bf16[4,64,128]{2,1,0:T(8,128)(2,1)S(1)} %pad_maximum_fusion.4), channel_id=1, source_target_pairs={{0,8},{4,12},{8,0},{12,4},{1,9},{5,13},{9,1},{13,5},{2,10},{6,14},... | collective-permute-start | bytes 196616 | tf_op jit(solution)/shard_map/ppermute | solution.py:239
  21.0 0.7 fusion.40
  22.4 1.4 collective-permute-done.4
  23.8 0.1 select_bitcast_fusion.9
  23.9 1.5 collective-permute-start.5
  25.6 3.4 %collective-permute-done.5 = bf16[2,4,64,128]{3,2,1,0:T(8,128)(2,1)S(1)} collective-permute-done((bf16[2,4,64,128]{3,2,1,0:T(8,128)(2,1)S(1)}, bf16[2,4,64,128]{3,2,1,0:T(8,128)(2,1)S(1)}, u32[]{:S(2)}, u32[]{:S(2)}) %collective-permute-start.5) | collective-permute-done | bytes 131104 | tf_op jit(solution)/shard_map/ppermute | solution.py:239
  29.0 0.6 collective-permute-start.6
  29.6 0.6 maximum_bitcast_fusion.2.cos_ref
  30.2 0.6 maximum_bitcast_fusion.3.sin_ref
  30.9 4.6 %collective-permute-done.6 = bf16[16,64,128]{2,1,0:T(8,128)(2,1)S(1)} collective-permute-done((bf16[16,64,128]{2,1,0:T(8,128)(2,1)S(1)}, bf16[16,64,128]{2,1,0:T(8,128)(2,1)S(1)}, u32[]{:S(2)}, u32[]{:S(2)}) %collective-permute-start.6) | collective-permute-done | bytes 262176 | tf_op jit(solution)/shard_map/ppermute | solution.py:239
  35.8 0.7 copy.55
  36.5 13.2 %shard_map.85 = (f32[2,512,128]{2,1,0:T(8,128)}, f32[2,512,1]{2,1,0:T(8,128)}, f32[2,512,1]{2,1,0:T(8,128)}) custom-call(s32[1]{0:T(128)} %bitcast.kv0_ref, bf16[2,512,128]{2,1,0:T(8,128)(2,1)} %bitcast.236, bf16[40,128,2048]{2,1,0:T(8,128)(2,1)} %bitcast.225, bf16[40,128,2048]{2,1,0:T(8,128)(2,1)} %bitcast.226, f32[1,1,5120]{2,1,0:T(1,128)} %bitcast.244, ...), custom_call_target="tpu_custom_call" | custom-call | flops 2684354560 | bytes 6029312 | tf_op jit(solution)/shard_map/pallas_call | solution.py:194
  49.7 1.2 copy.61
  50.9 1.2 copy.65
  52.5 1.2 fusion.20.q_ref
  53.7 34.4 %shard_map.86 = (f32[6,512,128]{2,1,0:T(8,128)}, f32[6,512,1]{2,1,0:T(8,128)}, f32[6,512,1]{2,1,0:T(8,128)}) custom-call(s32[1]{0:T(128)} %bitcast.26.kv0_ref, bf16[6,512,128]{2,1,0:T(8,128)(2,1)} %fusion.20.q_ref, bf16[40,128,2048]{2,1,0:T(8,128)(2,1)} %bitcast.227, bf16[40,128,2048]{2,1,0:T(8,128)(2,1)} %bitcast.228, f32[1,1,5120]{2,1,0:T(1,128)} %bitcast.245, ...), custom_call_target="tpu_custom_call" | custom-call | flops 8053063680 | bytes 18087936 | tf_op jit(solution)/shard_map/pallas_call | solution.py:194
  88.1 2.0 %copy.62 = f32[6,512,1]{1,0,2:T(8,128)S(1)} copy(f32[6,512,1]{2,1,0:T(8,128)} %get-tuple-element.14) | data formatting | bytes 24576 | tf_op jit(solution)/shard_map/pallas_call | solution.py:194
  90.2 0.6 collective-permute-start.10
  90.9 1.5 collective-permute-start.9
  92.4 1.9 %fusion.2 = f32[8,512,128]{2,1,0:T(8,128)S(1)} fusion(s32[]{:T(128)S(6)} %select_n.358, f32[2,512,128]{2,1,0:T(8,128)S(1)} %copy-done.1, f32[6,512,128]{2,1,0:T(8,128)} %get-tuple-element.12), kind=kLoop, calls=%fused_computation.8 | loop fusion | flops 1572864 | bytes 4194308 | tf_op jit(solution)/shard_map/concatenate | solution.py:368
  94.3 2.0 %copy.66 = f32[6,512,1]{1,0,2:T(8,128)S(1)} copy(f32[6,512,1]{2,1,0:T(8,128)} %get-tuple-element.16) | data formatting | bytes 24576 | tf_op jit(solution)/shard_map/pallas_call | solution.py:194
  96.4 1.4 collective-permute-start.11
  97.9 3.2 %collective-permute-start.12 = (f32[64,64]{1,0:T(8,128)S(1)}, f32[64,64]{1,0:T(8,128)S(1)}, u32[]{:S(2)}, u32[]{:S(2)}) collective-permute-start(f32[64,64]{1,0:T(8,128)S(1)} %maximum_maximum_fusion.1), channel_id=1, source_target_pairs={{0,8},{4,12},{8,0},{12,4},{1,9},{5,13},{9,1},{13,5},{2,10},{6,14},... | collective-permute-start | bytes 49160 | tf_op jit(solution)/shard_map/ppermute | solution.py:283
  101.1 0.8 collective-permute-start.13
  102.0 1.8 %reshape.438 = f32[2,2,2,2,4,8192]{5,4,3,2,1,0:T(4,128)} reshape(f32[8,512,128]{2,1,0:T(8,128)S(1)} %fusion.2) | data formatting | bytes 4194304 | tf_op jit(solution)/shard_map/reshape | solution.py:373
  103.8 1.2 collective-permute-done.13
  105.0 0.6 fusion.70
  105.6 0.6 mul.261
  106.2 1.8 %mul.262 = f32[2,2,2,2,4,8192]{5,4,3,2,1,0:T(4,128)} reshape(f32[64,64,128]{2,1,0:T(8,128)S(1)} %mul.261) | data formatting | bytes 4194304 | tf_op jit(solution)/shard_map/mul | solution.py:380
  108.0 2.8 %mul.263 = f32[2,2,2,2,4,8192]{5,4,3,2,1,0:T(4,128)S(1)} multiply(f32[2,2,2,2,4,8192]{5,4,3,2,1,0:T(4,128)} %reshape.438, f32[2,2,2,2,4,8192]{5,4,3,2,1,0:T(4,128)} %mul.262) | non-fusion elementwise | flops 524288 | bytes 6291456 | tf_op jit(solution)/shard_map/mul | solution.py:380
  110.8 0.3 fusion.16
  111.2 2.1 %fusion.5 = f32[64,512]{1,0:T(8,128)S(1)} fusion(bf16[64,2048]{1,0:T(8,128)(2,1)S(1)} %copy-done, bf16[2048,2048]{1,0:T(8,128)(2,1)} %param.11, s32[]{:T(128)S(6)} %select_n.367), kind=kOutput, calls=%fused_computation.16 | convolution fusion | flops 134217728 | bytes 2490372 | tf_op jit(solution)/shard_map/dot_general | solution.py:308
  113.2 0.5 collective-permute-start.19
  113.8 1.1 collective-permute-done.19
  114.9 0.9 add.314
  115.8 0.8 collective-permute-start.20
  116.6 1.6 fusion.19
  118.3 1.4 collective-permute-start.15
  119.8 2.5 %collective-permute-done.20 = f32[64,512]{1,0:T(8,128)S(1)} collective-permute-done((f32[64,512]{1,0:T(8,128)S(1)}, f32[64,512]{1,0:T(8,128)S(1)}, u32[]{:S(2)}, u32[]{:S(2)}) %collective-permute-start.20) | collective-permute-done | bytes 131104 | tf_op jit(solution)/shard_map/ppermute | solution.py:215
  122.7 10.4 %collective-permute-done.15 = f32[2,2,4,8256]{3,2,1,0:T(4,128)S(1)} collective-permute-done((f32[2,2,4,8256]{3,2,1,0:T(4,128)S(1)}, f32[2,2,4,8256]{3,2,1,0:T(4,128)S(1)}, u32[]{:S(2)}, u32[]{:S(2)}) %collective-permute-start.15) | collective-permute-done | bytes 528416 | tf_op jit(solution)/shard_map/ppermute | solution.py:228
  133.4 3.1 %collective-permute-start.17 = (f32[4,8256]{1,0:T(4,128)S(1)}, f32[4,8256]{1,0:T(4,128)S(1)}, u32[]{:S(2)}, u32[]{:S(2)}) collective-permute-start(f32[4,8256]{1,0:T(4,128)S(1)} %get-tuple-element.29), channel_id=1, source_target_pairs={{0,8},{4,12},{8,0},{12,4},{1,9},{5,13},{9,1},{13,5},{2,10},{6,14},... | collective-permute-start | bytes 396296 | tf_op jit(solution)/shard_map/ppermute | solution.py:267
  136.5 0.7 collective-permute-start.18
  137.1 1.1 fusion.71
  138.3 3.4 %collective-permute-done.16 = f32[4,8256]{1,0:T(4,128)S(1)} collective-permute-done((f32[4,8256]{1,0:T(4,128)S(1)}, f32[4,8256]{1,0:T(4,128)S(1)}, u32[]{:S(2)}, u32[]{:S(2)}) %collective-permute-start.16) | collective-permute-done | bytes 132128 | tf_op jit(solution)/shard_map/ppermute | solution.py:267
  141.6 4.3 %collective-permute-done.17 = f32[4,8256]{1,0:T(4,128)S(1)} collective-permute-done((f32[4,8256]{1,0:T(4,128)S(1)}, f32[4,8256]{1,0:T(4,128)S(1)}, u32[]{:S(2)}, u32[]{:S(2)}) %collective-permute-start.17) | collective-permute-done | bytes 132128 | tf_op jit(solution)/shard_map/ppermute | solution.py:267
  146.1 0.7 fusion.61
  146.8 0.2 fusion.14
  147.0 5.8 %all_gather.3 = bf16[64,2048]{1,0:T(8,128)(2,1)S(1)} all-gather(bf16[64,512]{1,0:T(8,128)(2,1)S(1)} %bitcast.242), channel_id=1, replica_groups=mesh['groups'=2,'tensor'=4,'store'=4] {'store'}, dimensions={1}, use_global_device_ids=true | all-gather | bytes 327680 | tf_op jit(solution)/shard_map/all_gather | solution.py:422
  152.8 5.0 %fusion.72 = f32[64,2048]{1,0:T(8,128)S(1)} fusion(bf16[64,2048]{1,0:T(8,128)(2,1)S(1)} %all_gather.3, bf16[2048,2048]{1,0:T(8,128)(2,1)} %param.12), kind=kOutput, calls=%fused_computation.172 | convolution fusion | flops 536870912 | bytes 9175040 | tf_op jit(solution)/shard_map/dot_general | solution.py:448
  157.8 2.7 %collective-permute-start.21 = (f32[16,2048]{1,0:T(8,128)S(1)}, f32[16,2048]{1,0:T(8,128)S(1)}, u32[]{:S(2)}, u32[]{:S(2)}) collective-permute-start(f32[16,2048]{1,0:T(8,128)S(1)} %get-tuple-element.30), channel_id=1, source_target_pairs={{0,4},{4,8},{8,12},{12,0},{1,5},{5,9},{9,13},{13,1},{2,6},{6,10},{... | collective-permute-start | bytes 393224 | tf_op jit(solution)/shard_map/ppermute | solution.py:267
  160.5 0.7 collective-permute-start.22
  161.3 1.7 %collective-permute-start.23 = (f32[16,2048]{1,0:T(8,128)S(1)}, f32[16,2048]{1,0:T(8,128)S(1)}, u32[]{:S(2)}, u32[]{:S(2)}) collective-permute-start(f32[16,2048]{1,0:T(8,128)S(1)} %get-tuple-element.31), channel_id=1, source_target_pairs={{0,12},{4,0},{8,4},{12,8},{1,13},{5,1},{9,5},{13,9},{2,14},{6,2},{... | collective-permute-start | bytes 393224 | tf_op jit(solution)/shard_map/ppermute | solution.py:267
  163.0 3.1 %collective-permute-done.21 = f32[16,2048]{1,0:T(8,128)S(1)} collective-permute-done((f32[16,2048]{1,0:T(8,128)S(1)}, f32[16,2048]{1,0:T(8,128)S(1)}, u32[]{:S(2)}, u32[]{:S(2)}) %collective-permute-start.21) | collective-permute-done | bytes 131104 | tf_op jit(solution)/shard_map/ppermute | solution.py:267
  166.1 5.0 %collective-permute-done.22 = f32[16,2048]{1,0:T(8,128)S(1)} collective-permute-done((f32[16,2048]{1,0:T(8,128)S(1)}, f32[16,2048]{1,0:T(8,128)S(1)}, u32[]{:S(2)}, u32[]{:S(2)}) %collective-permute-start.22) | collective-permute-done | bytes 131104 | tf_op jit(solution)/shard_map/ppermute | solution.py:267
  171.1 0.7 fusion.26
  (90 shorter events, 3.2 us)
Async XLA Ops:
  0.0 1.0 copy-start
  5.9 1.5 copy-start.7
  6.2 3.4 %collective-permute-start = (f32[2,4,64,128]{3,2,1,0:T(8,128)S(1)}, f32[2,4,64,128]{3,2,1,0:T(8,128)S(1)}, u32[]{:S(2)}, u32[]{:S(2)}) collective-permute-start(f32[2,4,64,128]{3,2,1,0:T(8,128)S(1)} %bitcast.243), channel_id=1, source_target_pairs={{0,1},{1,0},{2,3},{3,2},{4,5},{5,4},{6,7},{7,6},{8,9},{9,8},{10,11... | collective-permute-start | bytes 786440 | tf_op jit(solution)/shard_map/ppermute | solution.py:228
  9.5 12.8 %copy-start.3 = (f32[64,64]{1,0:T(8,128)}, f32[64,64]{1,0:T(8,128)S(1)}, u32[]{:S(2)}) copy-start(f32[64,64]{1,0:T(8,128)S(1)} %get-tuple-element.51) | copy-start | bytes 49156
  9.6 12.8 %copy-start.5 = (f32[64,64]{1,0:T(8,128)}, f32[64,64]{1,0:T(8,128)S(1)}, u32[]{:S(2)}) copy-start(f32[64,64]{1,0:T(8,128)S(1)} %get-tuple-element.52) | copy-start | bytes 49156
  9.7 6.7 %collective-permute-start.1 = (f32[4,64,128]{2,1,0:T(8,128)S(1)}, f32[4,64,128]{2,1,0:T(8,128)S(1)}, u32[]{:S(2)}, u32[]{:S(2)}) collective-permute-start(f32[4,64,128]{2,1,0:T(8,128)S(1)} %dynamic-slice_bitcast_fusion.7), channel_id=1, source_target_pairs={{0,2},{1,3},{2,0},{3,1},{4,6},{5,7},{6,4},{7,5},{8,10},{9,11},{10,... | collective-permute-start | bytes 393224 | tf_op jit(solution)/shard_map/ppermute | solution.py:228
  16.6 5.7 %collective-permute-start.2 = (bf16[4,64,128]{2,1,0:T(8,128)(2,1)S(1)}, bf16[4,64,128]{2,1,0:T(8,128)(2,1)S(1)}, u32[]{:S(2)}, u32[]{:S(2)}) collective-permute-start(bf16[4,64,128]{2,1,0:T(8,128)(2,1)S(1)} %pad_maximum_fusion.4), channel_id=1, source_target_pairs={{0,2},{1,3},{2,0},{3,1},{4,6},{5,7},{6,4},{7,5},{8,10},{9,11},{10,... | collective-permute-start | bytes 196616 | tf_op jit(solution)/shard_map/ppermute | solution.py:239
  18.4 5.3 %collective-permute-start.4 = (bf16[4,64,128]{2,1,0:T(8,128)(2,1)S(1)}, bf16[4,64,128]{2,1,0:T(8,128)(2,1)S(1)}, u32[]{:S(2)}, u32[]{:S(2)}) collective-permute-start(bf16[4,64,128]{2,1,0:T(8,128)(2,1)S(1)} %pad_maximum_fusion.4), channel_id=1, source_target_pairs={{0,8},{4,12},{8,0},{12,4},{1,9},{5,13},{9,1},{13,5},{2,10},{6,14},... | collective-permute-start | bytes 196616 | tf_op jit(solution)/shard_map/ppermute | solution.py:239
  23.9 5.0 %collective-permute-start.5 = (bf16[2,4,64,128]{3,2,1,0:T(8,128)(2,1)S(1)}, bf16[2,4,64,128]{3,2,1,0:T(8,128)(2,1)S(1)}, u32[]{:S(2)}, u32[]{:S(2)}) collective-permute-start(bf16[2,4,64,128]{3,2,1,0:T(8,128)(2,1)S(1)} %pad_maximum_fusion.3), channel_id=1, source_target_pairs={{0,4},{4,0},{8,12},{12,8},{1,5},{5,1},{9,13},{13,9},{2,6},{6,2},{1... | collective-permute-start | bytes 393224 | tf_op jit(solution)/shard_map/ppermute | solution.py:239
  29.0 6.4 %collective-permute-start.6 = (bf16[16,64,128]{2,1,0:T(8,128)(2,1)S(1)}, bf16[16,64,128]{2,1,0:T(8,128)(2,1)S(1)}, u32[]{:S(2)}, u32[]{:S(2)}) collective-permute-start(bf16[16,64,128]{2,1,0:T(8,128)(2,1)S(1)} %bitcast.238), channel_id=1, source_target_pairs={{0,2},{1,3},{2,0},{3,1},{4,6},{5,7},{6,4},{7,5},{8,10},{9,11},{10,... | collective-permute-start | bytes 786440 | tf_op jit(solution)/shard_map/ppermute | solution.py:239
  30.8 4.8 %collective-permute-start.3 = (bf16[2,4,64,128]{3,2,1,0:T(8,128)(2,1)S(1)}, bf16[2,4,64,128]{3,2,1,0:T(8,128)(2,1)S(1)}, u32[]{:S(2)}, u32[]{:S(2)}) collective-permute-start(bf16[2,4,64,128]{3,2,1,0:T(8,128)(2,1)S(1)} %pad_maximum_fusion.2), channel_id=1, source_target_pairs={{0,1},{1,0},{2,3},{3,2},{4,5},{5,4},{6,7},{7,6},{8,9},{9,8},{10,11... | collective-permute-start | bytes 393224 | tf_op jit(solution)/shard_map/ppermute | solution.py:239
  35.6 16.5 %collective-permute-start.7 = (bf16[2,16,64,128]{3,2,1,0:T(8,128)(2,1)S(1)}, bf16[2,16,64,128]{3,2,1,0:T(8,128)(2,1)S(1)}, u32[]{:S(2)}, u32[]{:S(2)}) collective-permute-start(bf16[2,16,64,128]{3,2,1,0:T(8,128)(2,1)S(1)} %pad_maximum_fusion), channel_id=1, source_target_pairs={{0,1},{1,0},{2,3},{3,2},{4,5},{5,4},{6,7},{7,6},{8,9},{9,8},{10,11... | collective-permute-start | bytes 1572872 | tf_op jit(solution)/shard_map/ppermute | solution.py:239
  53.7 38.7 %copy-start.1 = (f32[2,512,128]{2,1,0:T(8,128)S(1)}, f32[2,512,128]{2,1,0:T(8,128)}, u32[]{:S(2)}) copy-start(f32[2,512,128]{2,1,0:T(8,128)} %get-tuple-element.11) | copy-start | bytes 1572868
  90.2 6.1 %collective-permute-start.10 = (f32[64,64]{1,0:T(8,128)S(1)}, f32[64,64]{1,0:T(8,128)S(1)}, u32[]{:S(2)}, u32[]{:S(2)}) collective-permute-start(f32[64,64]{1,0:T(8,128)S(1)} %reshape.439), channel_id=1, source_target_pairs={{0,3},{1,0},{2,1},{3,2},{4,7},{5,4},{6,5},{7,6},{8,11},{9,8},{10,9... | collective-permute-start | bytes 49160 | tf_op jit(solution)/shard_map/ppermute | solution.py:283
  90.9 5.5 %collective-permute-start.8 = (f32[64,64]{1,0:T(8,128)S(1)}, f32[64,64]{1,0:T(8,128)S(1)}, u32[]{:S(2)}, u32[]{:S(2)}) collective-permute-start(f32[64,64]{1,0:T(8,128)S(1)} %reshape.439), channel_id=1, source_target_pairs={{0,1},{1,2},{2,3},{3,0},{4,5},{5,6},{6,7},{7,4},{8,9},{9,10},{10,1... | collective-permute-start | bytes 49160 | tf_op jit(solution)/shard_map/ppermute | solution.py:283
  90.9 5.5 %collective-permute-start.9 = (f32[64,64]{1,0:T(8,128)S(1)}, f32[64,64]{1,0:T(8,128)S(1)}, u32[]{:S(2)}, u32[]{:S(2)}) collective-permute-start(f32[64,64]{1,0:T(8,128)S(1)} %reshape.439), channel_id=1, source_target_pairs={{0,2},{1,3},{2,0},{3,1},{4,6},{5,7},{6,4},{7,5},{8,10},{9,11},{10,... | collective-permute-start | bytes 49160 | tf_op jit(solution)/shard_map/ppermute | solution.py:283
  96.4 7.4 %collective-permute-start.11 = (f32[64,64]{1,0:T(8,128)S(1)}, f32[64,64]{1,0:T(8,128)S(1)}, u32[]{:S(2)}, u32[]{:S(2)}) collective-permute-start(f32[64,64]{1,0:T(8,128)S(1)} %maximum_maximum_fusion.1), channel_id=1, source_target_pairs={{0,4},{4,8},{8,12},{12,0},{1,5},{5,9},{9,13},{13,1},{2,6},{6,10},{... | collective-permute-start | bytes 49160 | tf_op jit(solution)/shard_map/ppermute | solution.py:283
  97.9 5.9 %collective-permute-start.12 = (f32[64,64]{1,0:T(8,128)S(1)}, f32[64,64]{1,0:T(8,128)S(1)}, u32[]{:S(2)}, u32[]{:S(2)}) collective-permute-start(f32[64,64]{1,0:T(8,128)S(1)} %maximum_maximum_fusion.1), channel_id=1, source_target_pairs={{0,8},{4,12},{8,0},{12,4},{1,9},{5,13},{9,1},{13,5},{2,10},{6,14},... | collective-permute-start | bytes 49160 | tf_op jit(solution)/shard_map/ppermute | solution.py:283
  101.1 3.9 %collective-permute-start.13 = (f32[64,64]{1,0:T(8,128)S(1)}, f32[64,64]{1,0:T(8,128)S(1)}, u32[]{:S(2)}, u32[]{:S(2)}) collective-permute-start(f32[64,64]{1,0:T(8,128)S(1)} %maximum_maximum_fusion.1), channel_id=1, source_target_pairs={{0,12},{4,0},{8,4},{12,8},{1,13},{5,1},{9,5},{13,9},{2,14},{6,2},{... | collective-permute-start | bytes 49160 | tf_op jit(solution)/shard_map/ppermute | solution.py:283
  105.6 5.2 %copy-start.2 = (f32[64,64]{1,0:T(8,128)}, f32[64,64]{1,0:T(8,128)S(1)}, u32[]{:S(2)}) copy-start(f32[64,64]{1,0:T(8,128)S(1)} %get-tuple-element.22) | copy-start | bytes 49156
  111.1 5.5 %collective-permute-start.14 = (f32[2,2,2,4,8256]{4,3,0,2,1:T(4,128)S(1)}, f32[2,2,2,4,8256]{4,3,0,2,1:T(4,128)}, u32[]{:S(2)}, u32[]{:S(2)}) collective-permute-start(f32[2,2,2,4,8256]{4,3,0,2,1:T(4,128)S(1)} %fusion.16), channel_id=1, source_target_pairs={{0,1},{1,0},{2,3},{3,2},{4,5},{5,4},{6,7},{7,6},{8,9},{9,8},{10,11... | collective-permute-start | bytes 3170312 | tf_op jit(solution)/shard_map/ppermute | solution.py:228
  113.2 1.7 collective-permute-start.19
  115.8 6.4 %collective-permute-start.20 = (f32[64,512]{1,0:T(8,128)S(1)}, f32[64,512]{1,0:T(8,128)S(1)}, u32[]{:S(2)}, u32[]{:S(2)}) collective-permute-start(f32[64,512]{1,0:T(8,128)S(1)} %add.314), channel_id=1, source_target_pairs={{0,2},{1,3},{2,0},{3,1},{4,6},{5,7},{6,4},{7,5},{8,10},{9,11},{10,... | collective-permute-start | bytes 393224 | tf_op jit(solution)/shard_map/ppermute | solution.py:215
  118.2 4.3 %copy-start.4 = (f32[64,64]{1,0:T(8,128)S(1)}, f32[64,64]{1,0:T(8,128)}, u32[]{:S(2)}) copy-start(f32[64,64]{1,0:T(8,128)} %copy-done.3) | copy-start | bytes 49156
  118.2 4.3 %copy-start.6 = (f32[64,64]{1,0:T(8,128)S(1)}, f32[64,64]{1,0:T(8,128)}, u32[]{:S(2)}) copy-start(f32[64,64]{1,0:T(8,128)} %copy-done.5) | copy-start | bytes 49156
  118.3 14.8 %collective-permute-start.15 = (f32[2,2,4,8256]{3,2,1,0:T(4,128)S(1)}, f32[2,2,4,8256]{3,2,1,0:T(4,128)S(1)}, u32[]{:S(2)}, u32[]{:S(2)}) collective-permute-start(f32[2,2,4,8256]{3,2,1,0:T(4,128)S(1)} %dynamic-slice_bitcast_fusion), channel_id=1, source_target_pairs={{0,2},{1,3},{2,0},{3,1},{4,6},{5,7},{6,4},{7,5},{8,10},{9,11},{10,... | collective-permute-start | bytes 1585160 | tf_op jit(solution)/shard_map/ppermute | solution.py:228
  133.3 8.4 %collective-permute-start.16 = (f32[4,8256]{1,0:T(4,128)S(1)}, f32[4,8256]{1,0:T(4,128)S(1)}, u32[]{:S(2)}, u32[]{:S(2)}) collective-permute-start(f32[4,8256]{1,0:T(4,128)S(1)} %get-tuple-element.27), channel_id=1, source_target_pairs={{0,4},{4,8},{8,12},{12,0},{1,5},{5,9},{9,13},{13,1},{2,6},{6,10},{... | collective-permute-start | bytes 396296 | tf_op jit(solution)/shard_map/ppermute | solution.py:267
  133.4 12.6 %collective-permute-start.17 = (f32[4,8256]{1,0:T(4,128)S(1)}, f32[4,8256]{1,0:T(4,128)S(1)}, u32[]{:S(2)}, u32[]{:S(2)}) collective-permute-start(f32[4,8256]{1,0:T(4,128)S(1)} %get-tuple-element.29), channel_id=1, source_target_pairs={{0,8},{4,12},{8,0},{12,4},{1,9},{5,13},{9,1},{13,5},{2,10},{6,14},... | collective-permute-start | bytes 396296 | tf_op jit(solution)/shard_map/ppermute | solution.py:267
  136.5 9.5 %collective-permute-start.18 = (f32[4,8256]{1,0:T(4,128)S(1)}, f32[4,8256]{1,0:T(4,128)S(1)}, u32[]{:S(2)}, u32[]{:S(2)}) collective-permute-start(f32[4,8256]{1,0:T(4,128)S(1)} %get-tuple-element.28), channel_id=1, source_target_pairs={{0,12},{4,0},{8,4},{12,8},{1,13},{5,1},{9,5},{13,9},{2,14},{6,2},{... | collective-permute-start | bytes 396296 | tf_op jit(solution)/shard_map/ppermute | solution.py:267
  157.8 8.3 %collective-permute-start.21 = (f32[16,2048]{1,0:T(8,128)S(1)}, f32[16,2048]{1,0:T(8,128)S(1)}, u32[]{:S(2)}, u32[]{:S(2)}) collective-permute-start(f32[16,2048]{1,0:T(8,128)S(1)} %get-tuple-element.30), channel_id=1, source_target_pairs={{0,4},{4,8},{8,12},{12,0},{1,5},{5,9},{9,13},{13,1},{2,6},{6,10},{... | collective-permute-start | bytes 393224 | tf_op jit(solution)/shard_map/ppermute | solution.py:267
  160.5 10.6 %collective-permute-start.22 = (f32[16,2048]{1,0:T(8,128)S(1)}, f32[16,2048]{1,0:T(8,128)S(1)}, u32[]{:S(2)}, u32[]{:S(2)}) collective-permute-start(f32[16,2048]{1,0:T(8,128)S(1)} %get-tuple-element.32), channel_id=1, source_target_pairs={{0,8},{4,12},{8,0},{12,4},{1,9},{5,13},{9,1},{13,5},{2,10},{6,14},... | collective-permute-start | bytes 393224 | tf_op jit(solution)/shard_map/ppermute | solution.py:267
  161.3 9.8 %collective-permute-start.23 = (f32[16,2048]{1,0:T(8,128)S(1)}, f32[16,2048]{1,0:T(8,128)S(1)}, u32[]{:S(2)}, u32[]{:S(2)}) collective-permute-start(f32[16,2048]{1,0:T(8,128)S(1)} %get-tuple-element.31), channel_id=1, source_target_pairs={{0,12},{4,0},{8,4},{12,8},{1,13},{5,1},{9,5},{13,9},{2,14},{6,2},{... | collective-permute-start | bytes 393224 | tf_op jit(solution)/shard_map/ppermute | solution.py:267

commit v20 on v19

--- a/solution.py
+++ b/solution.py
@@ -266,6 +266,17 @@
         piece = lax.dynamic_index_in_dim(blocks, (idx + k) % n, 0, keepdims=False)
         total = total + lax.ppermute(piece, axis, perm=[(i, (i + k) % n) for i in range(n)])
     return total
+
+
+def direct_gather(x, axis):
+    n = lax.axis_size(axis)
+    idx = lax.axis_index(axis)
+    out = jnp.zeros((n,) + x.shape, x.dtype)
+    out = lax.dynamic_update_index_in_dim(out, x, idx, 0)
+    for k in range(1, n):
+        got = lax.ppermute(x, axis, perm=[(i, (i + k) % n) for i in range(n)])
+        out = lax.dynamic_update_index_in_dim(out, got, (idx - k) % n, 0)
+    return out.reshape((n * x.shape[0],) + x.shape[1:])
 
 
 def axis_sum(x, axis):
@@ -321,7 +332,7 @@
         block = to_half(rotate(block, jnp.transpose(tok_angle, (1, 0, 2))))
         q_heads = bit_gather(block, "store")
         query_rot = jnp.transpose(q_heads, (1, 0, 2))
-        q_all = bit_gather(block, "tensor")
+        q_all = direct_gather(block, "tensor")
         if tensors & (tensors - 1):
             q_all = None
         else:

time: 173 us -> 171 us (0.988)
  waiting for transfers between devices: 44.6 us -> 40 us
  starting transfers between devices: 29.1 us -> 31.7 us
    ppermute x0 -> x3, starting transfers between devices: none -> 5.82 us  [direct_gather(): got = lax.ppermute(x, axis, perm=[(i, (i + k) % n) for i in range(n)])]
    ppermute x6 -> x4, waiting for transfers between devices: 9.39 us -> 5.77 us  [bit_gather(): other = lax.ppermute(x, axis, perm=[(i, i ^ d) for i in range(n)])]
    ppermute x6 -> x4, starting transfers between devices: 6.6 us -> 3.5 us  [bit_gather(): other = lax.ppermute(x, axis, perm=[(i, i ^ d) for i in range(n)])]
  transfers between devices with their start and end apart: 24 -> 25, of which waited for: 12 -> 12; matrix products, arithmetic and copies ran while one was open for 11% -> 12% of each run, Pallas kernels for 8% -> 8%
where the time goes in v20:
time: 171 us; the launch traced here: 170 us
  Pallas kernels  47.6 us (28%)
  waiting for transfers between devices  40 us (23%)
  starting transfers between devices  31.7 us (19%)
  other arithmetic  16.5 us (10%)
  matrix products  13.2 us (8%)
  local copies, waits for them, and re-layouts  12.9 us (8%)
  blocking collectives  5.79 us (3%)
  between operations  1.85 us (1%)
    pallas_call x2, Pallas kernels, hist_attend(): pl.pallas_call(kernel, grid_spec=grid_spec, out_shape=[jax.ShapeDtypeStru...  47.6 us
    ppermute x6, waiting for transfers between devices, direct_scatter(): lax.ppermute(piece, axis, perm=[(i, (i + k) % n) for i in range(n)])  14.6 us
    ppermute x4, waiting for transfers between devices, bit_scatter(): block = keep + lax.ppermute(send, axis, perm=[(i, i ^ d) for i in range(n)])  13.8 us
    ppermute x6, starting transfers between devices, direct_scatter(): lax.ppermute(piece, axis, perm=[(i, (i + k) % n) for i in range(n)])  10.2 us
    pallas_call x4, local copies, waits for them, and re-layouts, hist_attend(): pl.pallas_call(kernel, grid_spec=grid_spec, out_shape=[jax.ShapeDtypeStru...  6.49 us
    ppermute x6, starting transfers between devices, axis_max(): lax.ppermute(x, a, perm=[(i, (i + k) % n) for i in range(n)])  6.28 us
    ppermute x3, starting transfers between devices, direct_gather(): got = lax.ppermute(x, axis, perm=[(i, (i + k) % n) for i in range(n)])  5.82 us
    all_gather x1, blocking collectives, body(): attended = lax.all_gather(attended, 'store', axis=1, tiled=True)  5.79 us
  transfers between devices with their start and end apart: 25, of which 12 were waited for; matrix products, arithmetic and copies ran while one was open for 12% of the time, Pallas kernels for 8%

profile of v20, /device:TPU:0, one launch (start us, length us, event | category | flops | bytes accessed | tf_op | source)
XLA Modules:
  0.0 169.6 jit_solution(5063776071837398673)
XLA Ops:
  0.0 0.9 copy-done
  1.0 4.9 %convolution_bitcast_fusion = f32[8,8,16,128]{3,1,2,0:T(8,128)S(1)} fusion(bf16[64,2048]{1,0:T(8,128)(2,1)S(1)} %copy-done, bf16[2048,2048]{1,0:T(8,128)(2,1)} %param.10), kind=kOutput, calls=%fused_computation.15 | convolution fusion | flops 536870912 | bytes 9175040 | tf_op jit(solution)/shard_map/dot_general | solution.py:318
  6.2 0.5 collective-permute-start
  8.2 1.2 reduce-window.6
  9.9 0.2 fusion.36
  10.1 0.7 fusion.40
  10.8 0.2 multiply_cosine_fusion
  11.1 2.6 %collective-permute-start.1 = (f32[4,64,128]{2,1,0:T(8,128)S(1)}, f32[4,64,128]{2,1,0:T(8,128)S(1)}, u32[]{:S(2)}, u32[]{:S(2)}) collective-permute-start(f32[4,64,128]{2,1,0:T(8,128)S(1)} %dynamic-slice_bitcast_fusion.7), channel_id=1, source_target_pairs={{0,2},{1,3},{2,0},{3,1},{4,6},{5,7},{6,4},{7,5},{8,10},{9,11},{10,... | collective-permute-start | bytes 393224 | tf_op jit(solution)/shard_map/ppermute | solution.py:228
  13.7 0.6 maximum_bitcast_fusion.cos_ref
  14.3 0.6 maximum_bitcast_fusion.1.sin_ref
  14.8 3.0 %collective-permute-done.1 = f32[4,64,128]{2,1,0:T(8,128)S(1)} collective-permute-done((f32[4,64,128]{2,1,0:T(8,128)S(1)}, f32[4,64,128]{2,1,0:T(8,128)S(1)}, u32[]{:S(2)}, u32[]{:S(2)}) %collective-permute-start.1) | collective-permute-done | bytes 131104 | tf_op jit(solution)/shard_map/ppermute | solution.py:228
  18.1 1.9 %collective-permute-start.4 = (bf16[4,64,128]{2,1,0:T(8,128)(2,1)S(1)}, bf16[4,64,128]{2,1,0:T(8,128)(2,1)S(1)}, u32[]{:S(2)}, u32[]{:S(2)}) collective-permute-start(bf16[4,64,128]{2,1,0:T(8,128)(2,1)S(1)} %pad_maximum_fusion.4), channel_id=1, source_target_pairs={{0,4},{4,8},{8,12},{12,0},{1,5},{5,9},{9,13},{13,1},{2,6},{6,10},{... | collective-permute-start | bytes 196616 | tf_op jit(solution)/shard_map/ppermute | solution.py:277
  19.9 2.6 %collective-permute-start.5 = (bf16[4,64,128]{2,1,0:T(8,128)(2,1)S(1)}, bf16[4,64,128]{2,1,0:T(8,128)(2,1)S(1)}, u32[]{:S(2)}, u32[]{:S(2)}) collective-permute-start(bf16[4,64,128]{2,1,0:T(8,128)(2,1)S(1)} %pad_maximum_fusion.4), channel_id=1, source_target_pairs={{0,8},{4,12},{8,0},{12,4},{1,9},{5,13},{9,1},{13,5},{2,10},{6,14},... | collective-permute-start | bytes 196616 | tf_op jit(solution)/shard_map/ppermute | solution.py:277
  22.5 1.3 collective-permute-start.6
  23.9 1.5 collective-permute-start.2
  25.6 1.4 collective-permute-done.5
  27.1 1.9 %collective-permute-start.7 = (bf16[16,64,128]{2,1,0:T(8,128)(2,1)S(1)}, bf16[16,64,128]{2,1,0:T(8,128)(2,1)S(1)}, u32[]{:S(2)}, u32[]{:S(2)}) collective-permute-start(bf16[16,64,128]{2,1,0:T(8,128)(2,1)S(1)} %bitcast.239), channel_id=1, source_target_pairs={{0,2},{1,3},{2,0},{3,1},{4,6},{5,7},{6,4},{7,5},{8,10},{9,11},{10,... | collective-permute-start | bytes 786440 | tf_op jit(solution)/shard_map/ppermute | solution.py:239
  29.2 5.8 %collective-permute-done.7 = bf16[16,64,128]{2,1,0:T(8,128)(2,1)S(1)} collective-permute-done((bf16[16,64,128]{2,1,0:T(8,128)(2,1)S(1)}, bf16[16,64,128]{2,1,0:T(8,128)(2,1)S(1)}, u32[]{:S(2)}, u32[]{:S(2)}) %collective-permute-start.7) | collective-permute-done | bytes 262176 | tf_op jit(solution)/shard_map/ppermute | solution.py:239
  35.2 0.7 pad_maximum_fusion.2
  35.9 13.2 %shard_map.85 = (f32[2,512,128]{2,1,0:T(8,128)}, f32[2,512,1]{2,1,0:T(8,128)}, f32[2,512,1]{2,1,0:T(8,128)}) custom-call(s32[1]{0:T(128)} %bitcast.kv0_ref, bf16[2,512,128]{2,1,0:T(8,128)(2,1)} %bitcast.237, bf16[40,128,2048]{2,1,0:T(8,128)(2,1)} %bitcast.226, bf16[40,128,2048]{2,1,0:T(8,128)(2,1)} %bitcast.227, f32[1,1,5120]{2,1,0:T(1,128)} %bitcast.247, ...), custom_call_target="tpu_custom_call" | custom-call | flops 2684354560 | bytes 6029312 | tf_op jit(solution)/shard_map/pallas_call | solution.py:194
  49.1 1.2 copy.56
  50.3 1.2 copy.60
  51.8 1.2 fusion.20.q_ref
  53.1 34.4 %shard_map.86 = (f32[6,512,128]{2,1,0:T(8,128)}, f32[6,512,1]{2,1,0:T(8,128)}, f32[6,512,1]{2,1,0:T(8,128)}) custom-call(s32[1]{0:T(128)} %bitcast.27.kv0_ref, bf16[6,512,128]{2,1,0:T(8,128)(2,1)} %fusion.20.q_ref, bf16[40,128,2048]{2,1,0:T(8,128)(2,1)} %bitcast.228, bf16[40,128,2048]{2,1,0:T(8,128)(2,1)} %bitcast.229, f32[1,1,5120]{2,1,0:T(1,128)} %bitcast.248, ...), custom_call_target="tpu_custom_call" | custom-call | flops 8053063680 | bytes 18087936 | tf_op jit(solution)/shard_map/pallas_call | solution.py:194
  87.4 2.0 %copy.57 = f32[6,512,1]{1,0,2:T(8,128)S(1)} copy(f32[6,512,1]{2,1,0:T(8,128)} %get-tuple-element.14) | data formatting | bytes 24576 | tf_op jit(solution)/shard_map/pallas_call | solution.py:194
  89.6 0.6 collective-permute-start.10
  90.2 1.2 collective-permute-start.11
  91.4 1.9 %fusion.2 = f32[8,512,128]{2,1,0:T(8,128)S(1)} fusion(s32[]{:T(128)S(6)} %select_n.347, f32[2,512,128]{2,1,0:T(8,128)S(1)} %copy-done.1, f32[6,512,128]{2,1,0:T(8,128)} %get-tuple-element.12), kind=kLoop, calls=%fused_computation.8 | loop fusion | flops 1572864 | bytes 4194308 | tf_op jit(solution)/shard_map/concatenate | solution.py:379
  93.4 2.0 %copy.61 = f32[6,512,1]{1,0,2:T(8,128)S(1)} copy(f32[6,512,1]{2,1,0:T(8,128)} %get-tuple-element.16) | data formatting | bytes 24576 | tf_op jit(solution)/shard_map/pallas_call | solution.py:194
  95.4 2.0 %collective-permute-start.12 = (f32[64,64]{1,0:T(8,128)S(1)}, f32[64,64]{1,0:T(8,128)S(1)}, u32[]{:S(2)}, u32[]{:S(2)}) collective-permute-start(f32[64,64]{1,0:T(8,128)S(1)} %maximum_maximum_fusion.1), channel_id=1, source_target_pairs={{0,4},{4,8},{8,12},{12,0},{1,5},{5,9},{9,13},{13,1},{2,6},{6,10},{... | collective-permute-start | bytes 49160 | tf_op jit(solution)/shard_map/ppermute | solution.py:294
  97.4 0.6 collective-permute-start.13
  98.0 1.8 %collective-permute-start.14 = (f32[64,64]{1,0:T(8,128)S(1)}, f32[64,64]{1,0:T(8,128)S(1)}, u32[]{:S(2)}, u32[]{:S(2)}) collective-permute-start(f32[64,64]{1,0:T(8,128)S(1)} %maximum_maximum_fusion.1), channel_id=1, source_target_pairs={{0,12},{4,0},{8,4},{12,8},{1,13},{5,1},{9,5},{13,9},{2,14},{6,2},{... | collective-permute-start | bytes 49160 | tf_op jit(solution)/shard_map/ppermute | solution.py:294
  100.0 1.8 %reshape.469 = f32[2,2,2,2,4,8192]{5,4,3,2,1,0:T(4,128)} reshape(f32[8,512,128]{2,1,0:T(8,128)S(1)} %fusion.2) | data formatting | bytes 4194304 | tf_op jit(solution)/shard_map/reshape | solution.py:384
  101.8 1.1 collective-permute-done.13
  102.9 0.6 fusion.70
  103.5 0.6 mul.261
  104.1 1.8 %mul.262 = f32[2,2,2,2,4,8192]{5,4,3,2,1,0:T(4,128)} reshape(f32[64,64,128]{2,1,0:T(8,128)S(1)} %mul.261) | data formatting | bytes 4194304 | tf_op jit(solution)/shard_map/mul | solution.py:391
  105.9 2.8 %mul.263 = f32[2,2,2,2,4,8192]{5,4,3,2,1,0:T(4,128)S(1)} multiply(f32[2,2,2,2,4,8192]{5,4,3,2,1,0:T(4,128)} %reshape.469, f32[2,2,2,2,4,8192]{5,4,3,2,1,0:T(4,128)} %mul.262) | non-fusion elementwise | flops 524288 | bytes 6291456 | tf_op jit(solution)/shard_map/mul | solution.py:391
  108.7 0.3 fusion.16
  109.1 2.1 %fusion.5 = f32[64,512]{1,0:T(8,128)S(1)} fusion(bf16[64,2048]{1,0:T(8,128)(2,1)S(1)} %copy-done, bf16[2048,2048]{1,0:T(8,128)(2,1)} %param.11, s32[]{:T(128)S(6)} %select_n.355), kind=kOutput, calls=%fused_computation.16 | convolution fusion | flops 134217728 | bytes 2490372 | tf_op jit(solution)/shard_map/dot_general | solution.py:319
  111.1 0.5 collective-permute-start.20
  111.7 1.1 collective-permute-done.20
  112.8 0.9 add.333
  113.7 1.2 collective-permute-start.21
  114.9 1.6 fusion.19
  116.5 1.0 collective-permute-start.16
  117.6 2.1 %collective-permute-done.21 = f32[64,512]{1,0:T(8,128)S(1)} collective-permute-done((f32[64,512]{1,0:T(8,128)S(1)}, f32[64,512]{1,0:T(8,128)S(1)}, u32[]{:S(2)}, u32[]{:S(2)}) %collective-permute-start.21) | collective-permute-done | bytes 131104 | tf_op jit(solution)/shard_map/ppermute | solution.py:215
  120.2 10.8 %collective-permute-done.16 = f32[2,2,4,8256]{3,2,1,0:T(4,128)S(1)} collective-permute-done((f32[2,2,4,8256]{3,2,1,0:T(4,128)S(1)}, f32[2,2,4,8256]{3,2,1,0:T(4,128)S(1)}, u32[]{:S(2)}, u32[]{:S(2)}) %collective-permute-start.16) | collective-permute-done | bytes 528416 | tf_op jit(solution)/shard_map/ppermute | solution.py:228
  131.2 1.2 collective-permute-start.17
  132.4 2.4 %collective-permute-start.18 = (f32[4,8256]{1,0:T(4,128)S(1)}, f32[4,8256]{1,0:T(4,128)S(1)}, u32[]{:S(2)}, u32[]{:S(2)}) collective-permute-start(f32[4,8256]{1,0:T(4,128)S(1)} %get-tuple-element.29), channel_id=1, source_target_pairs={{0,8},{4,12},{8,0},{12,4},{1,9},{5,13},{9,1},{13,5},{2,10},{6,14},... | collective-permute-start | bytes 396296 | tf_op jit(solution)/shard_map/ppermute | solution.py:267
  134.8 0.8 collective-permute-start.19
  135.5 1.1 fusion.71
  136.7 2.8 %collective-permute-done.17 = f32[4,8256]{1,0:T(4,128)S(1)} collective-permute-done((f32[4,8256]{1,0:T(4,128)S(1)}, f32[4,8256]{1,0:T(4,128)S(1)}, u32[]{:S(2)}, u32[]{:S(2)}) %collective-permute-start.17) | collective-permute-done | bytes 132128 | tf_op jit(solution)/shard_map/ppermute | solution.py:267
  139.5 4.3 %collective-permute-done.18 = f32[4,8256]{1,0:T(4,128)S(1)} collective-permute-done((f32[4,8256]{1,0:T(4,128)S(1)}, f32[4,8256]{1,0:T(4,128)S(1)}, u32[]{:S(2)}, u32[]{:S(2)}) %collective-permute-start.18) | collective-permute-done | bytes 132128 | tf_op jit(solution)/shard_map/ppermute | solution.py:267
  143.8 0.7 fusion.61
  144.5 0.2 fusion.14
  144.8 5.8 %all_gather.3 = bf16[64,2048]{1,0:T(8,128)(2,1)S(1)} all-gather(bf16[64,512]{1,0:T(8,128)(2,1)S(1)} %bitcast.245), channel_id=1, replica_groups=mesh['groups'=2,'tensor'=4,'store'=4] {'store'}, dimensions={1}, use_global_device_ids=true | all-gather | bytes 327680 | tf_op jit(solution)/shard_map/all_gather | solution.py:433
  150.6 5.0 %fusion.72 = f32[64,2048]{1,0:T(8,128)S(1)} fusion(bf16[64,2048]{1,0:T(8,128)(2,1)S(1)} %all_gather.3, bf16[2048,2048]{1,0:T(8,128)(2,1)} %param.12), kind=kOutput, calls=%fused_computation.170 | convolution fusion | flops 536870912 | bytes 9175040 | tf_op jit(solution)/shard_map/dot_general | solution.py:459
  155.6 3.3 %collective-permute-start.22 = (f32[16,2048]{1,0:T(8,128)S(1)}, f32[16,2048]{1,0:T(8,128)S(1)}, u32[]{:S(2)}, u32[]{:S(2)}) collective-permute-start(f32[16,2048]{1,0:T(8,128)S(1)} %get-tuple-element.30), channel_id=1, source_target_pairs={{0,4},{4,8},{8,12},{12,0},{1,5},{5,9},{9,13},{13,1},{2,6},{6,10},{... | collective-permute-start | bytes 393224 | tf_op jit(solution)/shard_map/ppermute | solution.py:267
  158.9 0.6 collective-permute-start.23
  159.5 1.9 %collective-permute-start.24 = (f32[16,2048]{1,0:T(8,128)S(1)}, f32[16,2048]{1,0:T(8,128)S(1)}, u32[]{:S(2)}, u32[]{:S(2)}) collective-permute-start(f32[16,2048]{1,0:T(8,128)S(1)} %get-tuple-element.31), channel_id=1, source_target_pairs={{0,12},{4,0},{8,4},{12,8},{1,13},{5,1},{9,5},{13,9},{2,14},{6,2},{... | collective-permute-start | bytes 393224 | tf_op jit(solution)/shard_map/ppermute | solution.py:267
  161.4 2.5 %collective-permute-done.22 = f32[16,2048]{1,0:T(8,128)S(1)} collective-permute-done((f32[16,2048]{1,0:T(8,128)S(1)}, f32[16,2048]{1,0:T(8,128)S(1)}, u32[]{:S(2)}, u32[]{:S(2)}) %collective-permute-start.22) | collective-permute-done | bytes 131104 | tf_op jit(solution)/shard_map/ppermute | solution.py:267
  163.9 5.0 %collective-permute-done.23 = f32[16,2048]{1,0:T(8,128)S(1)} collective-permute-done((f32[16,2048]{1,0:T(8,128)S(1)}, f32[16,2048]{1,0:T(8,128)S(1)}, u32[]{:S(2)}, u32[]{:S(2)}) %collective-permute-start.23) | collective-permute-done | bytes 131104 | tf_op jit(solution)/shard_map/ppermute | solution.py:267
  168.9 0.7 fusion.26
  (92 shorter events, 3.3 us)
Async XLA Ops:
  0.0 1.0 copy-start
  5.9 2.3 %copy-start.7 = (s32[256,1]{0,1:T(1,128)S(1)}, s32[256,1]{0,1:T(1,128)}, u32[]{:S(2)}) copy-start(s32[256,1]{0,1:T(1,128)} %param.14) | copy-start | bytes 3076
  6.2 4.8 %collective-permute-start = (f32[2,4,64,128]{3,2,1,0:T(8,128)S(1)}, f32[2,4,64,128]{3,2,1,0:T(8,128)S(1)}, u32[]{:S(2)}, u32[]{:S(2)}) collective-permute-start(f32[2,4,64,128]{3,2,1,0:T(8,128)S(1)} %bitcast.246), channel_id=1, source_target_pairs={{0,1},{1,0},{2,3},{3,2},{4,5},{5,4},{6,7},{7,6},{8,9},{9,8},{10,11... | collective-permute-start | bytes 786440 | tf_op jit(solution)/shard_map/ppermute | solution.py:228
  11.0 18.1 %copy-start.3 = (f32[64,64]{1,0:T(8,128)}, f32[64,64]{1,0:T(8,128)S(1)}, u32[]{:S(2)}) copy-start(f32[64,64]{1,0:T(8,128)S(1)} %get-tuple-element.45) | copy-start | bytes 49156
  11.0 18.1 %copy-start.5 = (f32[64,64]{1,0:T(8,128)}, f32[64,64]{1,0:T(8,128)S(1)}, u32[]{:S(2)}) copy-start(f32[64,64]{1,0:T(8,128)S(1)} %get-tuple-element.46) | copy-start | bytes 49156
  11.1 6.7 %collective-permute-start.1 = (f32[4,64,128]{2,1,0:T(8,128)S(1)}, f32[4,64,128]{2,1,0:T(8,128)S(1)}, u32[]{:S(2)}, u32[]{:S(2)}) collective-permute-start(f32[4,64,128]{2,1,0:T(8,128)S(1)} %dynamic-slice_bitcast_fusion.7), channel_id=1, source_target_pairs={{0,2},{1,3},{2,0},{3,1},{4,6},{5,7},{6,4},{7,5},{8,10},{9,11},{10,... | collective-permute-start | bytes 393224 | tf_op jit(solution)/shard_map/ppermute | solution.py:228
  18.1 7.5 %collective-permute-start.4 = (bf16[4,64,128]{2,1,0:T(8,128)(2,1)S(1)}, bf16[4,64,128]{2,1,0:T(8,128)(2,1)S(1)}, u32[]{:S(2)}, u32[]{:S(2)}) collective-permute-start(bf16[4,64,128]{2,1,0:T(8,128)(2,1)S(1)} %pad_maximum_fusion.4), channel_id=1, source_target_pairs={{0,4},{4,8},{8,12},{12,0},{1,5},{5,9},{9,13},{13,1},{2,6},{6,10},{... | collective-permute-start | bytes 196616 | tf_op jit(solution)/shard_map/ppermute | solution.py:277
  19.9 7.1 %collective-permute-start.5 = (bf16[4,64,128]{2,1,0:T(8,128)(2,1)S(1)}, bf16[4,64,128]{2,1,0:T(8,128)(2,1)S(1)}, u32[]{:S(2)}, u32[]{:S(2)}) collective-permute-start(bf16[4,64,128]{2,1,0:T(8,128)(2,1)S(1)} %pad_maximum_fusion.4), channel_id=1, source_target_pairs={{0,8},{4,12},{8,0},{12,4},{1,9},{5,13},{9,1},{13,5},{2,10},{6,14},... | collective-permute-start | bytes 196616 | tf_op jit(solution)/shard_map/ppermute | solution.py:277
  22.5 4.6 %collective-permute-start.6 = (bf16[4,64,128]{2,1,0:T(8,128)(2,1)S(1)}, bf16[4,64,128]{2,1,0:T(8,128)(2,1)S(1)}, u32[]{:S(2)}, u32[]{:S(2)}) collective-permute-start(bf16[4,64,128]{2,1,0:T(8,128)(2,1)S(1)} %pad_maximum_fusion.4), channel_id=1, source_target_pairs={{0,12},{4,0},{8,4},{12,8},{1,13},{5,1},{9,5},{13,9},{2,14},{6,2},{... | collective-permute-start | bytes 196616 | tf_op jit(solution)/shard_map/ppermute | solution.py:277
  23.9 5.1 %collective-permute-start.2 = (bf16[4,64,128]{2,1,0:T(8,128)(2,1)S(1)}, bf16[4,64,128]{2,1,0:T(8,128)(2,1)S(1)}, u32[]{:S(2)}, u32[]{:S(2)}) collective-permute-start(bf16[4,64,128]{2,1,0:T(8,128)(2,1)S(1)} %pad_maximum_fusion.4), channel_id=1, source_target_pairs={{0,2},{1,3},{2,0},{3,1},{4,6},{5,7},{6,4},{7,5},{8,10},{9,11},{10,... | collective-permute-start | bytes 196616 | tf_op jit(solution)/shard_map/ppermute | solution.py:239
  27.1 7.8 %collective-permute-start.7 = (bf16[16,64,128]{2,1,0:T(8,128)(2,1)S(1)}, bf16[16,64,128]{2,1,0:T(8,128)(2,1)S(1)}, u32[]{:S(2)}, u32[]{:S(2)}) collective-permute-start(bf16[16,64,128]{2,1,0:T(8,128)(2,1)S(1)} %bitcast.239), channel_id=1, source_target_pairs={{0,2},{1,3},{2,0},{3,1},{4,6},{5,7},{6,4},{7,5},{8,10},{9,11},{10,... | collective-permute-start | bytes 786440 | tf_op jit(solution)/shard_map/ppermute | solution.py:239
  29.1 6.1 %collective-permute-start.3 = (bf16[2,4,64,128]{3,2,1,0:T(8,128)(2,1)S(1)}, bf16[2,4,64,128]{3,2,1,0:T(8,128)(2,1)S(1)}, u32[]{:S(2)}, u32[]{:S(2)}) collective-permute-start(bf16[2,4,64,128]{3,2,1,0:T(8,128)(2,1)S(1)} %pad_maximum_fusion.3), channel_id=1, source_target_pairs={{0,1},{1,0},{2,3},{3,2},{4,5},{5,4},{6,7},{7,6},{8,9},{9,8},{10,11... | collective-permute-start | bytes 393224 | tf_op jit(solution)/shard_map/ppermute | solution.py:239
  35.0 16.5 %collective-permute-start.8 = (bf16[2,16,64,128]{3,2,1,0:T(8,128)(2,1)S(1)}, bf16[2,16,64,128]{3,2,1,0:T(8,128)(2,1)S(1)}, u32[]{:S(2)}, u32[]{:S(2)}) collective-permute-start(bf16[2,16,64,128]{3,2,1,0:T(8,128)(2,1)S(1)} %pad_maximum_fusion.1), channel_id=1, source_target_pairs={{0,1},{1,0},{2,3},{3,2},{4,5},{5,4},{6,7},{7,6},{8,9},{9,8},{10,11... | collective-permute-start | bytes 1572872 | tf_op jit(solution)/shard_map/ppermute | solution.py:239
  53.1 38.4 %copy-start.1 = (f32[2,512,128]{2,1,0:T(8,128)S(1)}, f32[2,512,128]{2,1,0:T(8,128)}, u32[]{:S(2)}) copy-start(f32[2,512,128]{2,1,0:T(8,128)} %get-tuple-element.11) | copy-start | bytes 1572868
  89.6 5.8 %collective-permute-start.10 = (f32[64,64]{1,0:T(8,128)S(1)}, f32[64,64]{1,0:T(8,128)S(1)}, u32[]{:S(2)}, u32[]{:S(2)}) collective-permute-start(f32[64,64]{1,0:T(8,128)S(1)} %reshape.470), channel_id=1, source_target_pairs={{0,2},{1,3},{2,0},{3,1},{4,6},{5,7},{6,4},{7,5},{8,10},{9,11},{10,... | collective-permute-start | bytes 49160 | tf_op jit(solution)/shard_map/ppermute | solution.py:294
  90.2 5.2 %collective-permute-start.11 = (f32[64,64]{1,0:T(8,128)S(1)}, f32[64,64]{1,0:T(8,128)S(1)}, u32[]{:S(2)}, u32[]{:S(2)}) collective-permute-start(f32[64,64]{1,0:T(8,128)S(1)} %reshape.470), channel_id=1, source_target_pairs={{0,3},{1,0},{2,1},{3,2},{4,7},{5,4},{6,5},{7,6},{8,11},{9,8},{10,9... | collective-permute-start | bytes 49160 | tf_op jit(solution)/shard_map/ppermute | solution.py:294
  91.4 4.0 %collective-permute-start.9 = (f32[64,64]{1,0:T(8,128)S(1)}, f32[64,64]{1,0:T(8,128)S(1)}, u32[]{:S(2)}, u32[]{:S(2)}) collective-permute-start(f32[64,64]{1,0:T(8,128)S(1)} %reshape.470), channel_id=1, source_target_pairs={{0,1},{1,2},{2,3},{3,0},{4,5},{5,6},{6,7},{7,4},{8,9},{9,10},{10,1... | collective-permute-start | bytes 49160 | tf_op jit(solution)/shard_map/ppermute | solution.py:294
  95.4 6.3 %collective-permute-start.12 = (f32[64,64]{1,0:T(8,128)S(1)}, f32[64,64]{1,0:T(8,128)S(1)}, u32[]{:S(2)}, u32[]{:S(2)}) collective-permute-start(f32[64,64]{1,0:T(8,128)S(1)} %maximum_maximum_fusion.1), channel_id=1, source_target_pairs={{0,4},{4,8},{8,12},{12,0},{1,5},{5,9},{9,13},{13,1},{2,6},{6,10},{... | collective-permute-start | bytes 49160 | tf_op jit(solution)/shard_map/ppermute | solution.py:294
  97.4 5.5 %collective-permute-start.13 = (f32[64,64]{1,0:T(8,128)S(1)}, f32[64,64]{1,0:T(8,128)S(1)}, u32[]{:S(2)}, u32[]{:S(2)}) collective-permute-start(f32[64,64]{1,0:T(8,128)S(1)} %maximum_maximum_fusion.1), channel_id=1, source_target_pairs={{0,8},{4,12},{8,0},{12,4},{1,9},{5,13},{9,1},{13,5},{2,10},{6,14},... | collective-permute-start | bytes 49160 | tf_op jit(solution)/shard_map/ppermute | solution.py:294
  98.0 4.9 %collective-permute-start.14 = (f32[64,64]{1,0:T(8,128)S(1)}, f32[64,64]{1,0:T(8,128)S(1)}, u32[]{:S(2)}, u32[]{:S(2)}) collective-permute-start(f32[64,64]{1,0:T(8,128)S(1)} %maximum_maximum_fusion.1), channel_id=1, source_target_pairs={{0,12},{4,0},{8,4},{12,8},{1,13},{5,1},{9,5},{13,9},{2,14},{6,2},{... | collective-permute-start | bytes 49160 | tf_op jit(solution)/shard_map/ppermute | solution.py:294
  103.5 5.2 %copy-start.2 = (f32[64,64]{1,0:T(8,128)}, f32[64,64]{1,0:T(8,128)S(1)}, u32[]{:S(2)}) copy-start(f32[64,64]{1,0:T(8,128)S(1)} %get-tuple-element.22) | copy-start | bytes 49156
  109.0 5.9 %collective-permute-start.15 = (f32[2,2,2,4,8256]{4,3,0,2,1:T(4,128)S(1)}, f32[2,2,2,4,8256]{4,3,0,2,1:T(4,128)}, u32[]{:S(2)}, u32[]{:S(2)}) collective-permute-start(f32[2,2,2,4,8256]{4,3,0,2,1:T(4,128)S(1)} %fusion.16), channel_id=1, source_target_pairs={{0,1},{1,0},{2,3},{3,2},{4,5},{5,4},{6,7},{7,6},{8,9},{9,8},{10,11... | collective-permute-start | bytes 3170312 | tf_op jit(solution)/shard_map/ppermute | solution.py:228
  111.1 1.7 collective-permute-start.20
  113.7 6.0 %collective-permute-start.21 = (f32[64,512]{1,0:T(8,128)S(1)}, f32[64,512]{1,0:T(8,128)S(1)}, u32[]{:S(2)}, u32[]{:S(2)}) collective-permute-start(f32[64,512]{1,0:T(8,128)S(1)} %add.333), channel_id=1, source_target_pairs={{0,2},{1,3},{2,0},{3,1},{4,6},{5,7},{6,4},{7,5},{8,10},{9,11},{10,... | collective-permute-start | bytes 393224 | tf_op jit(solution)/shard_map/ppermute | solution.py:215
  116.5 3.6 %copy-start.4 = (f32[64,64]{1,0:T(8,128)S(1)}, f32[64,64]{1,0:T(8,128)}, u32[]{:S(2)}) copy-start(f32[64,64]{1,0:T(8,128)} %copy-done.3) | copy-start | bytes 49156
  116.5 3.6 %copy-start.6 = (f32[64,64]{1,0:T(8,128)S(1)}, f32[64,64]{1,0:T(8,128)}, u32[]{:S(2)}) copy-start(f32[64,64]{1,0:T(8,128)} %copy-done.5) | copy-start | bytes 49156
  116.5 14.4 %collective-permute-start.16 = (f32[2,2,4,8256]{3,2,1,0:T(4,128)S(1)}, f32[2,2,4,8256]{3,2,1,0:T(4,128)S(1)}, u32[]{:S(2)}, u32[]{:S(2)}) collective-permute-start(f32[2,2,4,8256]{3,2,1,0:T(4,128)S(1)} %dynamic-slice_bitcast_fusion), channel_id=1, source_target_pairs={{0,2},{1,3},{2,0},{3,1},{4,6},{5,7},{6,4},{7,5},{8,10},{9,11},{10,... | collective-permute-start | bytes 1585160 | tf_op jit(solution)/shard_map/ppermute | solution.py:228
  131.2 8.3 %collective-permute-start.17 = (f32[4,8256]{1,0:T(4,128)S(1)}, f32[4,8256]{1,0:T(4,128)S(1)}, u32[]{:S(2)}, u32[]{:S(2)}) collective-permute-start(f32[4,8256]{1,0:T(4,128)S(1)} %get-tuple-element.27), channel_id=1, source_target_pairs={{0,4},{4,8},{8,12},{12,0},{1,5},{5,9},{9,13},{13,1},{2,6},{6,10},{... | collective-permute-start | bytes 396296 | tf_op jit(solution)/shard_map/ppermute | solution.py:267
  132.4 11.4 %collective-permute-start.18 = (f32[4,8256]{1,0:T(4,128)S(1)}, f32[4,8256]{1,0:T(4,128)S(1)}, u32[]{:S(2)}, u32[]{:S(2)}) collective-permute-start(f32[4,8256]{1,0:T(4,128)S(1)} %get-tuple-element.29), channel_id=1, source_target_pairs={{0,8},{4,12},{8,0},{12,4},{1,9},{5,13},{9,1},{13,5},{2,10},{6,14},... | collective-permute-start | bytes 396296 | tf_op jit(solution)/shard_map/ppermute | solution.py:267
  134.8 9.0 %collective-permute-start.19 = (f32[4,8256]{1,0:T(4,128)S(1)}, f32[4,8256]{1,0:T(4,128)S(1)}, u32[]{:S(2)}, u32[]{:S(2)}) collective-permute-start(f32[4,8256]{1,0:T(4,128)S(1)} %get-tuple-element.28), channel_id=1, source_target_pairs={{0,12},{4,0},{8,4},{12,8},{1,13},{5,1},{9,5},{13,9},{2,14},{6,2},{... | collective-permute-start | bytes 396296 | tf_op jit(solution)/shard_map/ppermute | solution.py:267
  155.6 8.3 %collective-permute-start.22 = (f32[16,2048]{1,0:T(8,128)S(1)}, f32[16,2048]{1,0:T(8,128)S(1)}, u32[]{:S(2)}, u32[]{:S(2)}) collective-permute-start(f32[16,2048]{1,0:T(8,128)S(1)} %get-tuple-element.30), channel_id=1, source_target_pairs={{0,4},{4,8},{8,12},{12,0},{1,5},{5,9},{9,13},{13,1},{2,6},{6,10},{... | collective-permute-start | bytes 393224 | tf_op jit(solution)/shard_map/ppermute | solution.py:267
  158.9 9.9 %collective-permute-start.23 = (f32[16,2048]{1,0:T(8,128)S(1)}, f32[16,2048]{1,0:T(8,128)S(1)}, u32[]{:S(2)}, u32[]{:S(2)}) collective-permute-start(f32[16,2048]{1,0:T(8,128)S(1)} %get-tuple-element.32), channel_id=1, source_target_pairs={{0,8},{4,12},{8,0},{12,4},{1,9},{5,13},{9,1},{13,5},{2,10},{6,14},... | collective-permute-start | bytes 393224 | tf_op jit(solution)/shard_map/ppermute | solution.py:267
  159.5 9.4 %collective-permute-start.24 = (f32[16,2048]{1,0:T(8,128)S(1)}, f32[16,2048]{1,0:T(8,128)S(1)}, u32[]{:S(2)}, u32[]{:S(2)}) collective-permute-start(f32[16,2048]{1,0:T(8,128)S(1)} %get-tuple-element.31), channel_id=1, source_target_pairs={{0,12},{4,0},{8,4},{12,8},{1,13},{5,1},{9,5},{13,9},{2,14},{6,2},{... | collective-permute-start | bytes 393224 | tf_op jit(solution)/shard_map/ppermute | solution.py:267

commit v21 on v20

--- a/solution.py
+++ b/solution.py
@@ -330,7 +330,7 @@
         block = jnp.transpose(block, tuple(range(s_bits - 1, -1, -1)) + tuple(range(s_bits, s_bits + 3)))
         block = bit_scatter(block, "store")
         block = to_half(rotate(block, jnp.transpose(tok_angle, (1, 0, 2))))
-        q_heads = bit_gather(block, "store")
+        q_heads = direct_gather(block, "store")
         query_rot = jnp.transpose(q_heads, (1, 0, 2))
         q_all = direct_gather(block, "tensor")
         if tensors & (tensors - 1):

time: 171 us -> 172 us (level)
    ppermute x3 -> x6, starting transfers between devices: 5.82 us -> 9 us  [direct_gather(): got = lax.ppermute(x, axis, perm=[(i, (i + k) % n) for i in range(n)])]
    ppermute x4 -> x2, starting transfers between devices: 3.5 us -> 1.75 us  [bit_gather(): other = lax.ppermute(x, axis, perm=[(i, i ^ d) for i in range(n)])]
    ppermute x4 -> x2, waiting for transfers between devices: 5.77 us -> 6.39 us  [bit_gather(): other = lax.ppermute(x, axis, perm=[(i, i ^ d) for i in range(n)])]
  transfers between devices with their start and end apart: 25 -> 26, of which waited for: 12 -> 11; matrix products, arithmetic and copies ran while one was open for 12% -> 11% of each run, Pallas kernels for 8% -> 8%
where the time goes in v21:
time: 172 us; the launch traced here: 171 us
  Pallas kernels  47.6 us (28%)
  waiting for transfers between devices  39.4 us (23%)
  starting transfers between devices  33.4 us (19%)
  other arithmetic  15.8 us (9%)
  local copies, waits for them, and re-layouts  13.7 us (8%)
  matrix products  13.3 us (8%)
  blocking collectives  5.79 us (3%)
  between operations  1.91 us (1%)
    pallas_call x2, Pallas kernels, hist_attend(): pl.pallas_call(kernel, grid_spec=grid_spec, out_shape=[jax.ShapeDtypeStru...  47.6 us
    ppermute x6, waiting for transfers between devices, direct_scatter(): lax.ppermute(piece, axis, perm=[(i, (i + k) % n) for i in range(n)])  15 us
    ppermute x4, waiting for transfers between devices, bit_scatter(): block = keep + lax.ppermute(send, axis, perm=[(i, i ^ d) for i in range(n)])  13.6 us
    ppermute x6, starting transfers between devices, direct_scatter(): lax.ppermute(piece, axis, perm=[(i, (i + k) % n) for i in range(n)])  10 us
    ppermute x6, starting transfers between devices, direct_gather(): got = lax.ppermute(x, axis, perm=[(i, (i + k) % n) for i in range(n)])  9 us
    ppermute x6, starting transfers between devices, axis_max(): lax.ppermute(x, a, perm=[(i, (i + k) % n) for i in range(n)])  6.73 us
    pallas_call x4, local copies, waits for them, and re-layouts, hist_attend(): pl.pallas_call(kernel, grid_spec=grid_spec, out_shape=[jax.ShapeDtypeStru...  6.49 us
    ppermute x2, waiting for transfers between devices, bit_gather(): other = lax.ppermute(x, axis, perm=[(i, i ^ d) for i in range(n)])  6.39 us
  transfers between devices with their start and end apart: 26, of which 11 were waited for; matrix products, arithmetic and copies ran while one was open for 11% of the time, Pallas kernels for 8%

profile of v21, /device:TPU:0, one launch (start us, length us, event | category | flops | bytes accessed | tf_op | source)
XLA Modules:
  0.0 170.9 jit_solution(566074493527881427)
XLA Ops:
  0.0 0.9 copy-done
  1.0 4.9 %convolution_bitcast_fusion = f32[8,8,16,128]{3,1,2,0:T(8,128)S(1)} fusion(bf16[64,2048]{1,0:T(8,128)(2,1)S(1)} %copy-done, bf16[2048,2048]{1,0:T(8,128)(2,1)} %param.10), kind=kOutput, calls=%fused_computation.15 | convolution fusion | flops 536870912 | bytes 9175040 | tf_op jit(solution)/shard_map/dot_general | solution.py:318
  6.2 0.5 collective-permute-start
  8.2 1.2 reduce-window.6
  10.1 0.7 fusion.40
  10.8 0.2 multiply_cosine_fusion
  11.1 2.6 %collective-permute-start.1 = (f32[4,64,128]{2,1,0:T(8,128)S(1)}, f32[4,64,128]{2,1,0:T(8,128)S(1)}, u32[]{:S(2)}, u32[]{:S(2)}) collective-permute-start(f32[4,64,128]{2,1,0:T(8,128)S(1)} %dynamic-slice_bitcast_fusion.7), channel_id=1, source_target_pairs={{0,2},{1,3},{2,0},{3,1},{4,6},{5,7},{6,4},{7,5},{8,10},{9,11},{10,... | collective-permute-start | bytes 393224 | tf_op jit(solution)/shard_map/ppermute | solution.py:228
  13.7 0.6 maximum_bitcast_fusion.cos_ref
  14.3 0.6 maximum_bitcast_fusion.1.sin_ref
  14.8 3.0 %collective-permute-done.1 = f32[4,64,128]{2,1,0:T(8,128)S(1)} collective-permute-done((f32[4,64,128]{2,1,0:T(8,128)S(1)}, f32[4,64,128]{2,1,0:T(8,128)S(1)}, u32[]{:S(2)}, u32[]{:S(2)}) %collective-permute-start.1) | collective-permute-done | bytes 131104 | tf_op jit(solution)/shard_map/ppermute | solution.py:228
  18.1 1.9 %collective-permute-start.5 = (bf16[4,64,128]{2,1,0:T(8,128)(2,1)S(1)}, bf16[4,64,128]{2,1,0:T(8,128)(2,1)S(1)}, u32[]{:S(2)}, u32[]{:S(2)}) collective-permute-start(bf16[4,64,128]{2,1,0:T(8,128)(2,1)S(1)} %pad_maximum_fusion.3), channel_id=1, source_target_pairs={{0,4},{4,8},{8,12},{12,0},{1,5},{5,9},{9,13},{13,1},{2,6},{6,10},{... | collective-permute-start | bytes 196616 | tf_op jit(solution)/shard_map/ppermute | solution.py:277
  19.9 2.6 %collective-permute-start.6 = (bf16[4,64,128]{2,1,0:T(8,128)(2,1)S(1)}, bf16[4,64,128]{2,1,0:T(8,128)(2,1)S(1)}, u32[]{:S(2)}, u32[]{:S(2)}) collective-permute-start(bf16[4,64,128]{2,1,0:T(8,128)(2,1)S(1)} %pad_maximum_fusion.3), channel_id=1, source_target_pairs={{0,8},{4,12},{8,0},{12,4},{1,9},{5,13},{9,1},{13,5},{2,10},{6,14},... | collective-permute-start | bytes 196616 | tf_op jit(solution)/shard_map/ppermute | solution.py:277
  22.5 1.3 collective-permute-start.7
  23.9 1.5 collective-permute-start.3
  25.6 1.7 collective-permute-start.4
  27.3 1.7 collective-permute-start.8
  29.2 6.4 %collective-permute-done.8 = bf16[16,64,128]{2,1,0:T(8,128)(2,1)S(1)} collective-permute-done((bf16[16,64,128]{2,1,0:T(8,128)(2,1)S(1)}, bf16[16,64,128]{2,1,0:T(8,128)(2,1)S(1)}, u32[]{:S(2)}, u32[]{:S(2)}) %collective-permute-start.8) | collective-permute-done | bytes 262176 | tf_op jit(solution)/shard_map/ppermute | solution.py:239
  35.9 0.7 copy-done.1
  36.6 13.2 %shard_map.85 = (f32[2,512,128]{2,1,0:T(8,128)}, f32[2,512,1]{2,1,0:T(8,128)}, f32[2,512,1]{2,1,0:T(8,128)}) custom-call(s32[1]{0:T(128)} %bitcast.kv0_ref, bf16[2,512,128]{2,1,0:T(8,128)(2,1)} %bitcast.230, bf16[40,128,2048]{2,1,0:T(8,128)(2,1)} %bitcast.219, bf16[40,128,2048]{2,1,0:T(8,128)(2,1)} %bitcast.220, f32[1,1,5120]{2,1,0:T(1,128)} %bitcast.242, ...), custom_call_target="tpu_custom_call" | custom-call | flops 2684354560 | bytes 6029312 | tf_op jit(solution)/shard_map/pallas_call | solution.py:194
  49.8 1.2 copy.52
  51.0 1.2 copy.56
  52.5 1.2 fusion.20.q_ref
  53.8 34.4 %shard_map.86 = (f32[6,512,128]{2,1,0:T(8,128)}, f32[6,512,1]{2,1,0:T(8,128)}, f32[6,512,1]{2,1,0:T(8,128)}) custom-call(s32[1]{0:T(128)} %bitcast.26.kv0_ref, bf16[6,512,128]{2,1,0:T(8,128)(2,1)} %fusion.20.q_ref, bf16[40,128,2048]{2,1,0:T(8,128)(2,1)} %bitcast.221, bf16[40,128,2048]{2,1,0:T(8,128)(2,1)} %bitcast.222, f32[1,1,5120]{2,1,0:T(1,128)} %bitcast.243, ...), custom_call_target="tpu_custom_call" | custom-call | flops 8053063680 | bytes 18087936 | tf_op jit(solution)/shard_map/pallas_call | solution.py:194
  88.1 2.0 %copy.53 = f32[6,512,1]{1,0,2:T(8,128)S(1)} copy(f32[6,512,1]{2,1,0:T(8,128)} %get-tuple-element.14) | data formatting | bytes 24576 | tf_op jit(solution)/shard_map/pallas_call | solution.py:194
  90.3 0.7 collective-permute-start.10
  91.0 1.2 collective-permute-start.11
  92.1 1.0 collective-permute-start.12
  93.1 1.9 %fusion.2 = f32[8,512,128]{2,1,0:T(8,128)S(1)} fusion(s32[]{:T(128)S(6)} %select_n.342, f32[2,512,128]{2,1,0:T(8,128)S(1)} %copy-done.2, f32[6,512,128]{2,1,0:T(8,128)} %get-tuple-element.12), kind=kLoop, calls=%fused_computation.8 | loop fusion | flops 1572864 | bytes 4194308 | tf_op jit(solution)/shard_map/concatenate | solution.py:379
  95.1 2.0 %copy.57 = f32[6,512,1]{1,0,2:T(8,128)S(1)} copy(f32[6,512,1]{2,1,0:T(8,128)} %get-tuple-element.16) | data formatting | bytes 24576 | tf_op jit(solution)/shard_map/pallas_call | solution.py:194
  97.1 1.2 collective-permute-start.13
  98.4 0.8 collective-permute-start.14
  99.2 1.8 %collective-permute-start.15 = (f32[64,64]{1,0:T(8,128)S(1)}, f32[64,64]{1,0:T(8,128)S(1)}, u32[]{:S(2)}, u32[]{:S(2)}) collective-permute-start(f32[64,64]{1,0:T(8,128)S(1)} %maximum_maximum_fusion.1), channel_id=1, source_target_pairs={{0,12},{4,0},{8,4},{12,8},{1,13},{5,1},{9,5},{13,9},{2,14},{6,2},{... | collective-permute-start | bytes 49160 | tf_op jit(solution)/shard_map/ppermute | solution.py:294
  101.1 1.8 %reshape.469 = f32[2,2,2,2,4,8192]{5,4,3,2,1,0:T(4,128)} reshape(f32[8,512,128]{2,1,0:T(8,128)S(1)} %fusion.2) | data formatting | bytes 4194304 | tf_op jit(solution)/shard_map/reshape | solution.py:384
  103.1 0.9 collective-permute-done.14
  104.0 0.6 fusion.70
  104.6 0.6 mul.261
  105.2 1.8 %mul.262 = f32[2,2,2,2,4,8192]{5,4,3,2,1,0:T(4,128)} reshape(f32[64,64,128]{2,1,0:T(8,128)S(1)} %mul.261) | data formatting | bytes 4194304 | tf_op jit(solution)/shard_map/mul | solution.py:391
  107.0 2.8 %mul.263 = f32[2,2,2,2,4,8192]{5,4,3,2,1,0:T(4,128)S(1)} multiply(f32[2,2,2,2,4,8192]{5,4,3,2,1,0:T(4,128)} %reshape.469, f32[2,2,2,2,4,8192]{5,4,3,2,1,0:T(4,128)} %mul.262) | non-fusion elementwise | flops 524288 | bytes 6291456 | tf_op jit(solution)/shard_map/mul | solution.py:391
  109.8 0.3 fusion.16
  110.1 2.1 %fusion.5 = f32[64,512]{1,0:T(8,128)S(1)} fusion(bf16[64,2048]{1,0:T(8,128)(2,1)S(1)} %copy-done, bf16[2048,2048]{1,0:T(8,128)(2,1)} %param.11, s32[]{:T(128)S(6)} %select_n.350), kind=kOutput, calls=%fused_computation.16 | convolution fusion | flops 134217728 | bytes 2490372 | tf_op jit(solution)/shard_map/dot_general | solution.py:319
  112.2 0.5 collective-permute-start.21
  112.8 1.1 collective-permute-done.21
  113.9 0.9 add.362
  114.8 0.9 collective-permute-start.22
  115.7 1.6 fusion.19
  117.4 1.2 collective-permute-start.17
  118.7 2.3 %collective-permute-done.22 = f32[64,512]{1,0:T(8,128)S(1)} collective-permute-done((f32[64,512]{1,0:T(8,128)S(1)}, f32[64,512]{1,0:T(8,128)S(1)}, u32[]{:S(2)}, u32[]{:S(2)}) %collective-permute-start.22) | collective-permute-done | bytes 131104 | tf_op jit(solution)/shard_map/ppermute | solution.py:215
  121.5 10.6 %collective-permute-done.17 = f32[2,2,4,8256]{3,2,1,0:T(4,128)S(1)} collective-permute-done((f32[2,2,4,8256]{3,2,1,0:T(4,128)S(1)}, f32[2,2,4,8256]{3,2,1,0:T(4,128)S(1)}, u32[]{:S(2)}, u32[]{:S(2)}) %collective-permute-start.17) | collective-permute-done | bytes 528416 | tf_op jit(solution)/shard_map/ppermute | solution.py:228
  132.2 1.6 collective-permute-start.18
  133.8 1.8 %collective-permute-start.19 = (f32[4,8256]{1,0:T(4,128)S(1)}, f32[4,8256]{1,0:T(4,128)S(1)}, u32[]{:S(2)}, u32[]{:S(2)}) collective-permute-start(f32[4,8256]{1,0:T(4,128)S(1)} %get-tuple-element.29), channel_id=1, source_target_pairs={{0,8},{4,12},{8,0},{12,4},{1,9},{5,13},{9,1},{13,5},{2,10},{6,14},... | collective-permute-start | bytes 396296 | tf_op jit(solution)/shard_map/ppermute | solution.py:267
  135.6 0.8 collective-permute-start.20
  136.4 1.1 fusion.71
  137.6 3.1 %collective-permute-done.18 = f32[4,8256]{1,0:T(4,128)S(1)} collective-permute-done((f32[4,8256]{1,0:T(4,128)S(1)}, f32[4,8256]{1,0:T(4,128)S(1)}, u32[]{:S(2)}, u32[]{:S(2)}) %collective-permute-start.18) | collective-permute-done | bytes 132128 | tf_op jit(solution)/shard_map/ppermute | solution.py:267
  140.6 4.4 %collective-permute-done.19 = f32[4,8256]{1,0:T(4,128)S(1)} collective-permute-done((f32[4,8256]{1,0:T(4,128)S(1)}, f32[4,8256]{1,0:T(4,128)S(1)}, u32[]{:S(2)}, u32[]{:S(2)}) %collective-permute-start.19) | collective-permute-done | bytes 132128 | tf_op jit(solution)/shard_map/ppermute | solution.py:267
  145.1 0.7 fusion.61
  145.8 0.2 fusion.14
  146.1 5.8 %all_gather.3 = bf16[64,2048]{1,0:T(8,128)(2,1)S(1)} all-gather(bf16[64,512]{1,0:T(8,128)(2,1)S(1)} %bitcast.240), channel_id=1, replica_groups=mesh['groups'=2,'tensor'=4,'store'=4] {'store'}, dimensions={1}, use_global_device_ids=true | all-gather | bytes 327680 | tf_op jit(solution)/shard_map/all_gather | solution.py:433
  151.9 5.0 %fusion.72 = f32[64,2048]{1,0:T(8,128)S(1)} fusion(bf16[64,2048]{1,0:T(8,128)(2,1)S(1)} %all_gather.3, bf16[2048,2048]{1,0:T(8,128)(2,1)} %param.12), kind=kOutput, calls=%fused_computation.169 | convolution fusion | flops 536870912 | bytes 9175040 | tf_op jit(solution)/shard_map/dot_general | solution.py:459
  156.9 3.4 %collective-permute-start.23 = (f32[16,2048]{1,0:T(8,128)S(1)}, f32[16,2048]{1,0:T(8,128)S(1)}, u32[]{:S(2)}, u32[]{:S(2)}) collective-permute-start(f32[16,2048]{1,0:T(8,128)S(1)} %get-tuple-element.30), channel_id=1, source_target_pairs={{0,4},{4,8},{8,12},{12,0},{1,5},{5,9},{9,13},{13,1},{2,6},{6,10},{... | collective-permute-start | bytes 393224 | tf_op jit(solution)/shard_map/ppermute | solution.py:267
  160.3 0.3 collective-permute-start.24
  160.6 2.1 %collective-permute-start.25 = (f32[16,2048]{1,0:T(8,128)S(1)}, f32[16,2048]{1,0:T(8,128)S(1)}, u32[]{:S(2)}, u32[]{:S(2)}) collective-permute-start(f32[16,2048]{1,0:T(8,128)S(1)} %get-tuple-element.31), channel_id=1, source_target_pairs={{0,12},{4,0},{8,4},{12,8},{1,13},{5,1},{9,5},{13,9},{2,14},{6,2},{... | collective-permute-start | bytes 393224 | tf_op jit(solution)/shard_map/ppermute | solution.py:267
  162.7 2.5 %collective-permute-done.23 = f32[16,2048]{1,0:T(8,128)S(1)} collective-permute-done((f32[16,2048]{1,0:T(8,128)S(1)}, f32[16,2048]{1,0:T(8,128)S(1)}, u32[]{:S(2)}, u32[]{:S(2)}) %collective-permute-start.23) | collective-permute-done | bytes 131104 | tf_op jit(solution)/shard_map/ppermute | solution.py:267
  165.2 5.0 %collective-permute-done.24 = f32[16,2048]{1,0:T(8,128)S(1)} collective-permute-done((f32[16,2048]{1,0:T(8,128)S(1)}, f32[16,2048]{1,0:T(8,128)S(1)}, u32[]{:S(2)}, u32[]{:S(2)}) %collective-permute-start.24) | collective-permute-done | bytes 131104 | tf_op jit(solution)/shard_map/ppermute | solution.py:267
  170.2 0.7 fusion.26
  (97 shorter events, 3.6 us)
Async XLA Ops:
  0.0 1.0 copy-start
  5.9 2.3 %copy-start.8 = (s32[256,1]{0,1:T(1,128)S(1)}, s32[256,1]{0,1:T(1,128)}, u32[]{:S(2)}) copy-start(s32[256,1]{0,1:T(1,128)} %param.14) | copy-start | bytes 3076
  6.2 4.8 %collective-permute-start = (f32[2,4,64,128]{3,2,1,0:T(8,128)S(1)}, f32[2,4,64,128]{3,2,1,0:T(8,128)S(1)}, u32[]{:S(2)}, u32[]{:S(2)}) collective-permute-start(f32[2,4,64,128]{3,2,1,0:T(8,128)S(1)} %bitcast.241), channel_id=1, source_target_pairs={{0,1},{1,0},{2,3},{3,2},{4,5},{5,4},{6,7},{7,6},{8,9},{9,8},{10,11... | collective-permute-start | bytes 786440 | tf_op jit(solution)/shard_map/ppermute | solution.py:228
  11.0 18.2 %copy-start.4 = (f32[64,64]{1,0:T(8,128)}, f32[64,64]{1,0:T(8,128)S(1)}, u32[]{:S(2)}) copy-start(f32[64,64]{1,0:T(8,128)S(1)} %get-tuple-element.41) | copy-start | bytes 49156
  11.0 18.2 %copy-start.6 = (f32[64,64]{1,0:T(8,128)}, f32[64,64]{1,0:T(8,128)S(1)}, u32[]{:S(2)}) copy-start(f32[64,64]{1,0:T(8,128)S(1)} %get-tuple-element.42) | copy-start | bytes 49156
  11.1 6.7 %collective-permute-start.1 = (f32[4,64,128]{2,1,0:T(8,128)S(1)}, f32[4,64,128]{2,1,0:T(8,128)S(1)}, u32[]{:S(2)}, u32[]{:S(2)}) collective-permute-start(f32[4,64,128]{2,1,0:T(8,128)S(1)} %dynamic-slice_bitcast_fusion.7), channel_id=1, source_target_pairs={{0,2},{1,3},{2,0},{3,1},{4,6},{5,7},{6,4},{7,5},{8,10},{9,11},{10,... | collective-permute-start | bytes 393224 | tf_op jit(solution)/shard_map/ppermute | solution.py:228
  18.1 7.5 %collective-permute-start.5 = (bf16[4,64,128]{2,1,0:T(8,128)(2,1)S(1)}, bf16[4,64,128]{2,1,0:T(8,128)(2,1)S(1)}, u32[]{:S(2)}, u32[]{:S(2)}) collective-permute-start(bf16[4,64,128]{2,1,0:T(8,128)(2,1)S(1)} %pad_maximum_fusion.3), channel_id=1, source_target_pairs={{0,4},{4,8},{8,12},{12,0},{1,5},{5,9},{9,13},{13,1},{2,6},{6,10},{... | collective-permute-start | bytes 196616 | tf_op jit(solution)/shard_map/ppermute | solution.py:277
  19.9 7.3 %collective-permute-start.6 = (bf16[4,64,128]{2,1,0:T(8,128)(2,1)S(1)}, bf16[4,64,128]{2,1,0:T(8,128)(2,1)S(1)}, u32[]{:S(2)}, u32[]{:S(2)}) collective-permute-start(bf16[4,64,128]{2,1,0:T(8,128)(2,1)S(1)} %pad_maximum_fusion.3), channel_id=1, source_target_pairs={{0,8},{4,12},{8,0},{12,4},{1,9},{5,13},{9,1},{13,5},{2,10},{6,14},... | collective-permute-start | bytes 196616 | tf_op jit(solution)/shard_map/ppermute | solution.py:277
  22.5 4.8 %collective-permute-start.7 = (bf16[4,64,128]{2,1,0:T(8,128)(2,1)S(1)}, bf16[4,64,128]{2,1,0:T(8,128)(2,1)S(1)}, u32[]{:S(2)}, u32[]{:S(2)}) collective-permute-start(bf16[4,64,128]{2,1,0:T(8,128)(2,1)S(1)} %pad_maximum_fusion.3), channel_id=1, source_target_pairs={{0,12},{4,0},{8,4},{12,8},{1,13},{5,1},{9,5},{13,9},{2,14},{6,2},{... | collective-permute-start | bytes 196616 | tf_op jit(solution)/shard_map/ppermute | solution.py:277
  23.9 5.3 %collective-permute-start.2 = (bf16[4,64,128]{2,1,0:T(8,128)(2,1)S(1)}, bf16[4,64,128]{2,1,0:T(8,128)(2,1)S(1)}, u32[]{:S(2)}, u32[]{:S(2)}) collective-permute-start(bf16[4,64,128]{2,1,0:T(8,128)(2,1)S(1)} %pad_maximum_fusion.3), channel_id=1, source_target_pairs={{0,1},{1,2},{2,3},{3,0},{4,5},{5,6},{6,7},{7,4},{8,9},{9,10},{10,1... | collective-permute-start | bytes 196616 | tf_op jit(solution)/shard_map/ppermute | solution.py:277
  23.9 11.9 %collective-permute-start.3 = (bf16[4,64,128]{2,1,0:T(8,128)(2,1)S(1)}, bf16[4,64,128]{2,1,0:T(8,128)(2,1)S(1)}, u32[]{:S(2)}, u32[]{:S(2)}) collective-permute-start(bf16[4,64,128]{2,1,0:T(8,128)(2,1)S(1)} %pad_maximum_fusion.3), channel_id=1, source_target_pairs={{0,2},{1,3},{2,0},{3,1},{4,6},{5,7},{6,4},{7,5},{8,10},{9,11},{10,... | collective-permute-start | bytes 196616 | tf_op jit(solution)/shard_map/ppermute | solution.py:277
  25.6 10.3 %collective-permute-start.4 = (bf16[4,64,128]{2,1,0:T(8,128)(2,1)S(1)}, bf16[4,64,128]{2,1,0:T(8,128)(2,1)S(1)}, u32[]{:S(2)}, u32[]{:S(2)}) collective-permute-start(bf16[4,64,128]{2,1,0:T(8,128)(2,1)S(1)} %pad_maximum_fusion.3), channel_id=1, source_target_pairs={{0,3},{1,0},{2,1},{3,2},{4,7},{5,4},{6,5},{7,6},{8,11},{9,8},{10,9... | collective-permute-start | bytes 196616 | tf_op jit(solution)/shard_map/ppermute | solution.py:277
  27.3 8.3 %collective-permute-start.8 = (bf16[16,64,128]{2,1,0:T(8,128)(2,1)S(1)}, bf16[16,64,128]{2,1,0:T(8,128)(2,1)S(1)}, u32[]{:S(2)}, u32[]{:S(2)}) collective-permute-start(bf16[16,64,128]{2,1,0:T(8,128)(2,1)S(1)} %bitcast.236), channel_id=1, source_target_pairs={{0,2},{1,3},{2,0},{3,1},{4,6},{5,7},{6,4},{7,5},{8,10},{9,11},{10,... | collective-permute-start | bytes 786440 | tf_op jit(solution)/shard_map/ppermute | solution.py:239
  35.7 16.5 %collective-permute-start.9 = (bf16[2,16,64,128]{3,2,1,0:T(8,128)(2,1)S(1)}, bf16[2,16,64,128]{3,2,1,0:T(8,128)(2,1)S(1)}, u32[]{:S(2)}, u32[]{:S(2)}) collective-permute-start(bf16[2,16,64,128]{3,2,1,0:T(8,128)(2,1)S(1)} %pad_maximum_fusion.1), channel_id=1, source_target_pairs={{0,1},{1,0},{2,3},{3,2},{4,5},{5,4},{6,7},{7,6},{8,9},{9,8},{10,11... | collective-permute-start | bytes 1572872 | tf_op jit(solution)/shard_map/ppermute | solution.py:239
  35.9 0.7 copy-start.1
  53.8 39.4 %copy-start.2 = (f32[2,512,128]{2,1,0:T(8,128)S(1)}, f32[2,512,128]{2,1,0:T(8,128)}, u32[]{:S(2)}) copy-start(f32[2,512,128]{2,1,0:T(8,128)} %get-tuple-element.11) | copy-start | bytes 1572868
  90.3 6.8 %collective-permute-start.10 = (f32[64,64]{1,0:T(8,128)S(1)}, f32[64,64]{1,0:T(8,128)S(1)}, u32[]{:S(2)}, u32[]{:S(2)}) collective-permute-start(f32[64,64]{1,0:T(8,128)S(1)} %reshape.470), channel_id=1, source_target_pairs={{0,1},{1,2},{2,3},{3,0},{4,5},{5,6},{6,7},{7,4},{8,9},{9,10},{10,1... | collective-permute-start | bytes 49160 | tf_op jit(solution)/shard_map/ppermute | solution.py:294
  91.0 6.1 %collective-permute-start.11 = (f32[64,64]{1,0:T(8,128)S(1)}, f32[64,64]{1,0:T(8,128)S(1)}, u32[]{:S(2)}, u32[]{:S(2)}) collective-permute-start(f32[64,64]{1,0:T(8,128)S(1)} %reshape.470), channel_id=1, source_target_pairs={{0,2},{1,3},{2,0},{3,1},{4,6},{5,7},{6,4},{7,5},{8,10},{9,11},{10,... | collective-permute-start | bytes 49160 | tf_op jit(solution)/shard_map/ppermute | solution.py:294
  92.1 5.0 %collective-permute-start.12 = (f32[64,64]{1,0:T(8,128)S(1)}, f32[64,64]{1,0:T(8,128)S(1)}, u32[]{:S(2)}, u32[]{:S(2)}) collective-permute-start(f32[64,64]{1,0:T(8,128)S(1)} %reshape.470), channel_id=1, source_target_pairs={{0,3},{1,0},{2,1},{3,2},{4,7},{5,4},{6,5},{7,6},{8,11},{9,8},{10,9... | collective-permute-start | bytes 49160 | tf_op jit(solution)/shard_map/ppermute | solution.py:294
  97.1 6.0 %collective-permute-start.13 = (f32[64,64]{1,0:T(8,128)S(1)}, f32[64,64]{1,0:T(8,128)S(1)}, u32[]{:S(2)}, u32[]{:S(2)}) collective-permute-start(f32[64,64]{1,0:T(8,128)S(1)} %maximum_maximum_fusion.1), channel_id=1, source_target_pairs={{0,4},{4,8},{8,12},{12,0},{1,5},{5,9},{9,13},{13,1},{2,6},{6,10},{... | collective-permute-start | bytes 49160 | tf_op jit(solution)/shard_map/ppermute | solution.py:294
  98.4 5.6 %collective-permute-start.14 = (f32[64,64]{1,0:T(8,128)S(1)}, f32[64,64]{1,0:T(8,128)S(1)}, u32[]{:S(2)}, u32[]{:S(2)}) collective-permute-start(f32[64,64]{1,0:T(8,128)S(1)} %maximum_maximum_fusion.1), channel_id=1, source_target_pairs={{0,8},{4,12},{8,0},{12,4},{1,9},{5,13},{9,1},{13,5},{2,10},{6,14},... | collective-permute-start | bytes 49160 | tf_op jit(solution)/shard_map/ppermute | solution.py:294
  99.2 4.8 %collective-permute-start.15 = (f32[64,64]{1,0:T(8,128)S(1)}, f32[64,64]{1,0:T(8,128)S(1)}, u32[]{:S(2)}, u32[]{:S(2)}) collective-permute-start(f32[64,64]{1,0:T(8,128)S(1)} %maximum_maximum_fusion.1), channel_id=1, source_target_pairs={{0,12},{4,0},{8,4},{12,8},{1,13},{5,1},{9,5},{13,9},{2,14},{6,2},{... | collective-permute-start | bytes 49160 | tf_op jit(solution)/shard_map/ppermute | solution.py:294
  104.6 5.2 %copy-start.3 = (f32[64,64]{1,0:T(8,128)}, f32[64,64]{1,0:T(8,128)S(1)}, u32[]{:S(2)}) copy-start(f32[64,64]{1,0:T(8,128)S(1)} %get-tuple-element.22) | copy-start | bytes 49156
  110.0 5.7 %collective-permute-start.16 = (f32[2,2,2,4,8256]{4,3,0,2,1:T(4,128)S(1)}, f32[2,2,2,4,8256]{4,3,0,2,1:T(4,128)}, u32[]{:S(2)}, u32[]{:S(2)}) collective-permute-start(f32[2,2,2,4,8256]{4,3,0,2,1:T(4,128)S(1)} %fusion.16), channel_id=1, source_target_pairs={{0,1},{1,0},{2,3},{3,2},{4,5},{5,4},{6,7},{7,6},{8,9},{9,8},{10,11... | collective-permute-start | bytes 3170312 | tf_op jit(solution)/shard_map/ppermute | solution.py:228
  112.2 1.7 collective-permute-start.21
  114.8 6.2 %collective-permute-start.22 = (f32[64,512]{1,0:T(8,128)S(1)}, f32[64,512]{1,0:T(8,128)S(1)}, u32[]{:S(2)}, u32[]{:S(2)}) collective-permute-start(f32[64,512]{1,0:T(8,128)S(1)} %add.362), channel_id=1, source_target_pairs={{0,2},{1,3},{2,0},{3,1},{4,6},{5,7},{6,4},{7,5},{8,10},{9,11},{10,... | collective-permute-start | bytes 393224 | tf_op jit(solution)/shard_map/ppermute | solution.py:215
  117.3 4.0 %copy-start.5 = (f32[64,64]{1,0:T(8,128)S(1)}, f32[64,64]{1,0:T(8,128)}, u32[]{:S(2)}) copy-start(f32[64,64]{1,0:T(8,128)} %copy-done.4) | copy-start | bytes 49156
  117.4 4.0 %copy-start.7 = (f32[64,64]{1,0:T(8,128)S(1)}, f32[64,64]{1,0:T(8,128)}, u32[]{:S(2)}) copy-start(f32[64,64]{1,0:T(8,128)} %copy-done.6) | copy-start | bytes 49156
  117.4 14.6 %collective-permute-start.17 = (f32[2,2,4,8256]{3,2,1,0:T(4,128)S(1)}, f32[2,2,4,8256]{3,2,1,0:T(4,128)S(1)}, u32[]{:S(2)}, u32[]{:S(2)}) collective-permute-start(f32[2,2,4,8256]{3,2,1,0:T(4,128)S(1)} %dynamic-slice_bitcast_fusion), channel_id=1, source_target_pairs={{0,2},{1,3},{2,0},{3,1},{4,6},{5,7},{6,4},{7,5},{8,10},{9,11},{10,... | collective-permute-start | bytes 1585160 | tf_op jit(solution)/shard_map/ppermute | solution.py:228
  132.2 8.4 %collective-permute-start.18 = (f32[4,8256]{1,0:T(4,128)S(1)}, f32[4,8256]{1,0:T(4,128)S(1)}, u32[]{:S(2)}, u32[]{:S(2)}) collective-permute-start(f32[4,8256]{1,0:T(4,128)S(1)} %get-tuple-element.27), channel_id=1, source_target_pairs={{0,4},{4,8},{8,12},{12,0},{1,5},{5,9},{9,13},{13,1},{2,6},{6,10},{... | collective-permute-start | bytes 396296 | tf_op jit(solution)/shard_map/ppermute | solution.py:267
  133.8 11.2 %collective-permute-start.19 = (f32[4,8256]{1,0:T(4,128)S(1)}, f32[4,8256]{1,0:T(4,128)S(1)}, u32[]{:S(2)}, u32[]{:S(2)}) collective-permute-start(f32[4,8256]{1,0:T(4,128)S(1)} %get-tuple-element.29), channel_id=1, source_target_pairs={{0,8},{4,12},{8,0},{12,4},{1,9},{5,13},{9,1},{13,5},{2,10},{6,14},... | collective-permute-start | bytes 396296 | tf_op jit(solution)/shard_map/ppermute | solution.py:267
  135.6 9.4 %collective-permute-start.20 = (f32[4,8256]{1,0:T(4,128)S(1)}, f32[4,8256]{1,0:T(4,128)S(1)}, u32[]{:S(2)}, u32[]{:S(2)}) collective-permute-start(f32[4,8256]{1,0:T(4,128)S(1)} %get-tuple-element.28), channel_id=1, source_target_pairs={{0,12},{4,0},{8,4},{12,8},{1,13},{5,1},{9,5},{13,9},{2,14},{6,2},{... | collective-permute-start | bytes 396296 | tf_op jit(solution)/shard_map/ppermute | solution.py:267
  156.9 8.3 %collective-permute-start.23 = (f32[16,2048]{1,0:T(8,128)S(1)}, f32[16,2048]{1,0:T(8,128)S(1)}, u32[]{:S(2)}, u32[]{:S(2)}) collective-permute-start(f32[16,2048]{1,0:T(8,128)S(1)} %get-tuple-element.30), channel_id=1, source_target_pairs={{0,4},{4,8},{8,12},{12,0},{1,5},{5,9},{9,13},{13,1},{2,6},{6,10},{... | collective-permute-start | bytes 393224 | tf_op jit(solution)/shard_map/ppermute | solution.py:267
  160.3 9.9 %collective-permute-start.24 = (f32[16,2048]{1,0:T(8,128)S(1)}, f32[16,2048]{1,0:T(8,128)S(1)}, u32[]{:S(2)}, u32[]{:S(2)}) collective-permute-start(f32[16,2048]{1,0:T(8,128)S(1)} %get-tuple-element.32), channel_id=1, source_target_pairs={{0,8},{4,12},{8,0},{12,4},{1,9},{5,13},{9,1},{13,5},{2,10},{6,14},... | collective-permute-start | bytes 393224 | tf_op jit(solution)/shard_map/ppermute | solution.py:267
  160.6 9.6 %collective-permute-start.25 = (f32[16,2048]{1,0:T(8,128)S(1)}, f32[16,2048]{1,0:T(8,128)S(1)}, u32[]{:S(2)}, u32[]{:S(2)}) collective-permute-start(f32[16,2048]{1,0:T(8,128)S(1)} %get-tuple-element.31), channel_id=1, source_target_pairs={{0,12},{4,0},{8,4},{12,8},{1,13},{5,1},{9,5},{13,9},{2,14},{6,2},{... | collective-permute-start | bytes 393224 | tf_op jit(solution)/shard_map/ppermute | solution.py:267
